TPU v7x, 128 devices: a whole 4x4x4 slice. The times are simulated.
128 devices in a mesh: ctx: 32 (over x, y, core), head: 4 (over z).
Axes of the slice: x: 4, y: 4, z: 4, core: 2. Of those that a mesh axis runs over, the one named last changes fastest.
Arguments:
- queries: bfloat16 [32768, 4096], P('ctx', 'head'), may hold values from -4.5 to 4.5
- keys: bfloat16 [32768, 4096], P('ctx', 'head'), may hold values from -6 to 6
- values: bfloat16 [32768, 4096], P('ctx', 'head'), may hold values from -5.5 to 5.5
- row_target: int32 [32768], replicated, may hold values from 0 to 32767, as said below
- seg_doc: int32 [32], replicated, may hold values from 0 to 3, as said below
- mem_gate: float32 [32], P('head'), may hold values from -2 to 2
- out_weight: bfloat16 [4096, 4096], P(None, 'head'), may hold values from -0.09375 to 0.09375
Outputs:
- layer_out: bfloat16 [32768, 4096], P('ctx', 'head')
Inputs may be any that keep to these rules, and one draw needn't show every extreme that they name: `row_target`: a permutation of the token indices; the rows of one ctx shard of the loader order hold at most 48 tokens of any one segment, and exactly 48 of some. `seg_doc`: never falling along the segments, every document present with one or more segments.
All inputs are finite; a program needn't handle non-finite values.
Results may differ from a plain program's by a relative error of at most 0.0051.
Values may be sent and summed in bfloat16 or wider, within the bound.
No kernel may reach another device: no remote copies, remote signals or barrier semaphores. Data moves between devices by JAX's collectives and lax.ppermute only.
A program may use at most 128 MiB of HBM per device.

v0:
```python
import jax
import jax.numpy as jnp
from jax import lax
from jax.sharding import PartitionSpec as P


def entering(part, axis, combine, identity):
    place = lax.axis_index(axis)
    gathered = jax.tree.map(lambda a: lax.all_gather(a, axis), part)
    state = jax.tree.map(lambda a, e: jnp.zeros_like(a) + jnp.asarray(e, a.dtype), part, identity)

    def one(step, state):
        return combine(
            state, jax.tree.map(lambda a: lax.dynamic_index_in_dim(a, step, 0, False), gathered)
        )

    return lax.fori_loop(0, place, one, state)


def feature(inputs):
    return jax.nn.elu(inputs) + 1.0


def combine(earlier, later):
    restart = later[2] > 0.5
    return (
        jnp.where(restart, later[0], earlier[0] + later[0]),
        jnp.where(restart, later[1], earlier[1] + later[1]),
        jnp.maximum(earlier[2], later[2]),
    )


def per_device(queries, keys, values, row_target, seg_doc, mem_gate, out_weight):
    highest = lax.Precision.HIGHEST
    ctx_count = lax.axis_size("ctx")
    my_index = lax.axis_index("ctx")
    seg_rows, feat_width = queries.shape
    head_count = mem_gate.shape[0]
    head_size = feat_width // head_count
    share_rows = seg_rows // ctx_count
    capacity = share_rows + share_rows // 2
    targets = row_target.reshape(ctx_count, seg_rows)
    my_targets = lax.dynamic_index_in_dim(targets, my_index, 0, keepdims=False)
    owners = my_targets // seg_rows
    indices = jnp.arange(ctx_count, dtype=jnp.int32)
    matches = (owners[:, None] == indices[None, :]).astype(jnp.int32)
    within = jnp.sum(jnp.cumsum(matches, axis=0) * matches, axis=1) - 1
    send_slot = owners * capacity + within

    def scatter_rows(source):
        buffer = (
            jnp.zeros((ctx_count * capacity, feat_width), source.dtype).at[send_slot].set(source)
        )
        return buffer.reshape(ctx_count, capacity, feat_width)

    got_query, got_key, got_value = (
        lax.all_to_all(scatter_rows(queries), "ctx", split_axis=0, concat_axis=0, tiled=True),
        lax.all_to_all(scatter_rows(keys), "ctx", split_axis=0, concat_axis=0, tiled=True),
        lax.all_to_all(scatter_rows(values), "ctx", split_axis=0, concat_axis=0, tiled=True),
    )
    arrived = targets // seg_rows == my_index
    arrival = jnp.cumsum(arrived.astype(jnp.int32), axis=1) - 1
    columns = jnp.where(arrived, arrival, capacity)
    where_to = (
        jnp.full((ctx_count, capacity), seg_rows, jnp.int32)
        .at[indices[:, None], columns]
        .set(targets % seg_rows, mode="drop")
    )
    positions = where_to.reshape(-1)

    def place_rows(received):
        return (
            jnp.zeros((seg_rows, feat_width), received.dtype)
            .at[positions]
            .set(received.reshape(-1, feat_width), mode="drop")
        )

    query_heads = place_rows(got_query).reshape(seg_rows, head_count, head_size)
    key_heads = place_rows(got_key).reshape(seg_rows, head_count, head_size)
    value_heads = place_rows(got_value).reshape(seg_rows, head_count, head_size)
    key_feat = feature(key_heads.astype(jnp.float32))
    delta_m = jnp.einsum(
        "khd,khe->hde", key_feat, value_heads.astype(jnp.float32), precision=highest
    )
    delta_z = jnp.sum(key_feat, axis=0)
    doc_now = seg_doc[my_index]
    doc_before = seg_doc[jnp.maximum(my_index - 1, 0)]
    begins = (
        jnp.where((my_index == 0) | (doc_now != doc_before), 1.0, 0.0)
        .astype(jnp.float32)
        .reshape(1)
    )
    zero_m = jnp.zeros_like(delta_m)
    zero_z = jnp.zeros_like(delta_z)
    prior_m, prior_z, prior_flag = entering(
        (delta_m, delta_z, begins), "ctx", combine, (zero_m, zero_z, jnp.zeros((1,), jnp.float32))
    )
    keep_prior = 1.0 - begins[0]
    mem_m = keep_prior * prior_m
    mem_z = keep_prior * prior_z
    score_scale = head_size ** (-0.5)
    position = jnp.arange(seg_rows)
    causal = position[:, None] >= position[None, :]

    def one_head(items):
        query_one, key_one, value_one = items
        scores = jnp.dot(query_one, key_one.T, preferred_element_type=jnp.float32) * score_scale
        scores = jnp.where(causal, scores, -1e30)
        row_max = jnp.max(scores, axis=-1, keepdims=True)
        weights = jnp.exp(scores - row_max)
        probabilities = (weights / jnp.sum(weights, axis=-1, keepdims=True)).astype(jnp.bfloat16)
        return jnp.dot(probabilities, value_one, preferred_element_type=jnp.float32)

    local_out = lax.map(
        one_head,
        (
            jnp.moveaxis(query_heads, 1, 0),
            jnp.moveaxis(key_heads, 1, 0),
            jnp.moveaxis(value_heads, 1, 0),
        ),
    )
    local_out = jnp.moveaxis(local_out, 0, 1)
    query_feat = feature(query_heads.astype(jnp.float32))
    numerator = jnp.einsum("qhd,hde->qhe", query_feat, mem_m, precision=highest)
    denominator = jnp.einsum("qhd,hd->qh", query_feat, mem_z, precision=highest)
    recalled = numerator / jnp.maximum(denominator, 1.0)[..., None]
    gate_value = jax.nn.sigmoid(mem_gate)[None, :, None]
    combined = (
        (gate_value * recalled + (1.0 - gate_value) * local_out)
        .astype(jnp.bfloat16)
        .reshape(seg_rows, feat_width)
    )
    result_width = combined.shape[1]
    outgoing = combined[jnp.minimum(where_to, seg_rows - 1)]
    incoming = lax.all_to_all(outgoing, "ctx", split_axis=0, concat_axis=0, tiled=True)
    summed = jnp.dot(
        lax.all_gather(
            incoming.reshape(ctx_count * capacity, result_width)[send_slot],
            "head",
            axis=1,
            tiled=True,
        ),
        out_weight,
        preferred_element_type=jnp.float32,
    )
    return summed.astype(jnp.bfloat16)


def solution(mesh):
    return jax.shard_map(
        per_device,
        mesh=mesh,
        in_specs=(
            P("ctx", "head"),
            P("ctx", "head"),
            P("ctx", "head"),
            P(),
            P(),
            P("head"),
            P(None, "head"),
        ),
        out_specs=P("ctx", "head"),
        check_vma=False,
    )
```

profile of v0, /device:TPU:1, one launch (start us, length us, event | category | flops | bytes accessed | tf_op | source)
XLA Modules:
  0.0 706.0 jit_solution(6407079576093628454)
XLA Ops:
  7.5 9.0 %reduce-window.16 = s32[32,8,128]{2,1,0:T(8,128)S(1)} reduce-window(s32[32,8,128]{2,1,0:T(8,128)S(1)} %fusion.65, s32[]{:T(128)} %constant.132.clone.1), window={size=1x1x128 pad=0_0x0_0x127_0}, to_apply=%region_3.4 | reduce-window | flops 4161536 | bytes 262148 | tf_op jit(solution)/shard_map/reduce-window.2
  17.1 8.1 %scatter_custom_fusion = bf16[1536,1024]{1,0:T(8,128)(2,1)} fusion(s32[1024]{0:T(1024)S(1)} %bitcast.161, bf16[1024,1024]{1,0:T(8,128)(2,1)} %param.12, bf16[]{:T(256)} %constant.136.clone.1), kind=kCustom, calls=%fused_computation.64 | custom fusion | bytes 3146240 | tf_op jit(solution)/shard_map/scatter | solution.py:52
  25.2 8.6 %all-to-all-start = ((bf16[32,48,1024]{2,1,0:T(8,128)(2,1)}), bf16[32,48,1024]{2,1,0:T(8,128)(2,1)S(1)}, u32[]{:S(2)}, u32[]{:S(2)}) async-start(bf16[32,48,1024]{2,1,0:T(8,128)(2,1)} %bitcast.16), calls=%async_computation | async-start | bytes 6291456 | tf_op jit(solution)/shard_map/all_to_all | solution.py:58
  33.8 8.1 %scatter_custom_fusion.2 = bf16[1536,1024]{1,0:T(8,128)(2,1)} fusion(s32[1024]{0:T(1024)S(1)} %bitcast.162, bf16[1024,1024]{1,0:T(8,128)(2,1)} %param.13, bf16[]{:T(256)} %constant.136.clone.1), kind=kCustom, calls=%fused_computation.62 | custom fusion | bytes 3146240 | tf_op jit(solution)/shard_map/scatter | solution.py:52
  41.9 31.7 %all-to-all-done = bf16[32,48,1024]{2,1,0:T(8,128)(2,1)S(1)} async-done(((bf16[32,48,1024]{2,1,0:T(8,128)(2,1)}), bf16[32,48,1024]{2,1,0:T(8,128)(2,1)S(1)}, u32[]{:S(2)}, u32[]{:S(2)}) %all-to-all-start) | async-done | bytes 3145760 | tf_op jit(solution)/shard_map/all_to_all | solution.py:58
  75.3 5.0 all-to-all-start.1
  80.5 9.0 %reduce-window.14 = s32[32,8,128]{2,1,0:T(8,128)S(1)} reduce-window(s32[32,8,128]{2,1,0:T(8,128)S(1)} %fusion.67, s32[]{:T(128)} %constant.132.clone.1), window={size=1x1x128 pad=0_0x0_0x127_0}, to_apply=%region_0.1 | reduce-window | flops 4161536 | bytes 262148 | tf_op jit(solution)/shard_map/reduce-window
  90.5 120.2 %scatter_custom_fusion.6 = s32[1536]{0:T(1024)S(1)} fusion(s32[32768]{0:T(1024)S(1)} %bitcast.154, s32[32768]{0:T(1024)S(1)} %bitcast.155, s32[]{:T(128)} %constant.137.clone.1), kind=kCustom, calls=%fused_computation.134 | custom fusion | bytes 6148
  210.8 8.8 %scatter_custom_fusion.1 = bf16[1024,1024]{1,0:T(8,128)(2,1)S(1)} fusion(s32[1536]{0:T(1024)S(1)} %fusion.69, bf16[1536,1024]{1,0:T(8,128)(2,1)} %bitcast.143, bf16[]{:T(256)} %constant.136.clone.1), kind=kCustom, calls=%fused_computation.70 | custom fusion | bytes 2097664 | tf_op jit(solution)/shard_map/scatter | solution.py:75
  219.6 2.6 copy.46
  222.2 10.1 %scatter_custom_fusion.3 = bf16[1024,1024]{1,0:T(8,128)(2,1)} fusion(s32[1536]{0:T(1024)S(1)} %fusion.69, bf16[1536,1024]{1,0:T(8,128)(2,1)} %bitcast.20, bf16[]{:T(256)} %constant.136.clone.1), kind=kCustom, calls=%fused_computation.68 | custom fusion | bytes 2097664 | tf_op jit(solution)/shard_map/scatter | solution.py:75
  232.3 3.9 copy.47
  236.2 6.8 fusion.20
  243.0 8.1 %scatter_custom_fusion.4 = bf16[1536,1024]{1,0:T(8,128)(2,1)} fusion(s32[1024]{0:T(1024)S(1)} %bitcast.163, bf16[1024,1024]{1,0:T(8,128)(2,1)} %param.11, bf16[]{:T(256)} %constant.136.clone.1), kind=kCustom, calls=%fused_computation.60 | custom fusion | bytes 3146240 | tf_op jit(solution)/shard_map/scatter | solution.py:52
  251.1 7.6 %all-to-all-start.2 = ((bf16[32,48,1024]{2,1,0:T(8,128)(2,1)}), bf16[32,48,1024]{2,1,0:T(8,128)(2,1)}, u32[]{:S(2)}, u32[]{:S(2)}) async-start(bf16[32,48,1024]{2,1,0:T(8,128)(2,1)} %bitcast.142), calls=%async_computation.2 | async-start | bytes 6291456 | tf_op jit(solution)/shard_map/all_to_all | solution.py:57
  262.2 95.4 %all-reduce = f32[32]{0:T(128)S(1)} all-reduce(f32[32]{0:T(128)S(1)} %dynamic-update-slice), channel_id=1, replica_groups=mesh['ctx'=32,'head'=4] {'ctx'}, use_global_device_ids=true, to_apply=%add | all-reduce | flops 32 | bytes 256
  357.6 9.9 %scatter_custom_fusion.5 = bf16[1024,1024]{1,0:T(8,128)(2,1)} fusion(s32[1536]{0:T(1024)S(1)} %fusion.69, bf16[1536,1024]{1,0:T(8,128)(2,1)} %bitcast.25, bf16[]{:T(256)} %constant.136.clone.1), kind=kCustom, calls=%fused_computation.66 | custom fusion | bytes 2097664 | tf_op jit(solution)/shard_map/scatter | solution.py:75
  367.5 4.0 copy.49
  371.5 1.9 fusion.24
  373.4 20.8 %all_gather.22 = f32[32,8,128]{2,1,0:T(8,128)S(1)} all-gather(f32[1,8,128]{2,1,0:T(8,128)S(1)} %bitcast.158), channel_id=1, replica_groups=mesh['ctx'=32,'head'=4] {'ctx'}, dimensions={0}, use_global_device_ids=true | all-gather | bytes 135168 | tf_op jit(solution)/shard_map/all_gather | solution.py:9
  394.2 38.4 %while.26 = (s32[]{:T(128)}, f32[8,1024,128]{1,2,0:T(8,128)}, bf16[8,1024,128]{1,2,0:T(8,128)(2,1)}, bf16[8,1024,128]{1,2,0:T(8,128)(2,1)}, bf16[8,1024,128]{1,2,0:T(8,128)(2,1)}, /*index=5*/s32[]{:T(128)}) while((s32[]{:T(128)}, f32[8,1024,128]{1,2,0:T(8,128)}, bf16[8,1024,128]{1,2,0:T(8,128)(2,1)}, ...), condition=%wide.region_18.19_spmd.clone, body=%wide.region_15.18_spmd.clone.sunk | while | flops 552597504 | bytes 13916229 | solution.py:114
  394.2 1.8 fusion.95
  396.5 2.5 fusion.97
  399.0 1.8 fusion.95
  401.3 2.5 fusion.97
  403.8 1.8 fusion.95
  406.1 2.5 fusion.97
  408.6 1.8 fusion.95
  410.9 2.5 fusion.97
  413.4 1.8 fusion.95
  415.7 2.5 fusion.97
  418.2 1.8 fusion.95
  420.5 2.5 fusion.97
  423.0 1.8 fusion.95
  425.3 2.5 fusion.97
  427.8 1.8 fusion.95
  430.1 2.5 fusion.97
  432.6 3.2 while.25
  433.3 1.9 add_select_fusion.9
  435.8 3.8 fusion.29
  439.6 8.4 %fusion.27 = bf16[1024,8,128]{0,2,1:T(8,128)(2,1)} fusion(f32[8,1024,128]{1,2,0:T(8,128)} %get-tuple-element.98, f32[8]{0:T(128)S(1)} %get-tuple-element.150, f32[1024,8]{0,1:T(8,128)S(1)} %fusion.68, f32[8]{0:T(128)S(1)} %get-tuple-element.151, bf16[1024,8,128]{0,2,1:T(8,128)(2,1)S(1)} %bitcast.148, f32[8,128,128]{2,1,0:T(8,128)S(1)} %get-tuple-element.96, ...), kind=kOutput, calls=%fused_computation.48 | convolution fusion | flops 1621229568 | bytes 8945732 | tf_op jit(solution)/shard_map/qhd,hde->qhe/dot_general | solution.py:124
  448.1 2.9 copy.56
  450.9 5.8 gather_fusion
  456.7 100.2 %all-to-all-start.3 = ((bf16[32,48,1024]{2,1,0:T(8,128)(2,1)}), bf16[32,48,1024]{2,1,0:T(8,128)(2,1)S(1)}, u32[]{:S(2)}, u32[]{:S(2)}) async-start(bf16[32,48,1024]{2,1,0:T(8,128)(2,1)} %bitcast.141), calls=%async_computation.3 | async-start | bytes 6291456 | tf_op jit(solution)/shard_map/all_to_all | solution.py:135
  557.0 39.7 %all-to-all-done.3 = bf16[32,48,1024]{2,1,0:T(8,128)(2,1)S(1)} async-done(((bf16[32,48,1024]{2,1,0:T(8,128)(2,1)}), bf16[32,48,1024]{2,1,0:T(8,128)(2,1)S(1)}, u32[]{:S(2)}, u32[]{:S(2)}) %all-to-all-start.3) | async-done | bytes 3145760 | tf_op jit(solution)/shard_map/all_to_all | solution.py:135
  596.8 5.3 gather_fusion.1
  602.1 82.3 %all-gather.7.cloned.1.call-done = bf16[1024,4096]{1,0:T(8,128)(2,1)} async-done(((bf16[1024,1024]{1,0:T(8,128)(2,1)}), bf16[1024,4096]{1,0:T(8,128)(2,1)}) %all-gather.7.cloned.1.call-update) | async-done | bytes 8388624 | tf_op jit(solution)/shard_map/all_gather | solution.py:137
  684.4 14.6 %convolution_convert_fusion = bf16[1024,1024]{1,0:T(8,128)(2,1)} fusion(bf16[1024,4096]{1,0:T(8,128)(2,1)} %all-gather.7.cloned.1.call-done, bf16[4096,1024]{1,0:T(8,128)(2,1)} %param.17), kind=kOutput, calls=%fused_computation.59 | convolution fusion | flops 8590983168 | bytes 18874368 | tf_op jit(solution)/shard_map/dot_general | solution.py:136
  (81 shorter events, 12.0 us)
Async XLA Ops:
  25.2 48.4 %all-to-all-start = ((bf16[32,48,1024]{2,1,0:T(8,128)(2,1)}), bf16[32,48,1024]{2,1,0:T(8,128)(2,1)S(1)}, u32[]{:S(2)}, u32[]{:S(2)}) async-start(bf16[32,48,1024]{2,1,0:T(8,128)(2,1)} %bitcast.16), calls=%async_computation | async-start | bytes 6291456 | tf_op jit(solution)/shard_map/all_to_all | solution.py:58
  73.6 1.7 copy-start
  73.6 6.8 copy-start.2
  73.6 16.6 %copy-start.5 = (s32[2]{0:T(128)S(1)}, s32[2]{0:T(128)}, u32[]{:S(2)}) copy-start(s32[2]{0:T(128)} %constant.143) | copy-start | bytes 28
  73.6 16.7 %copy-start.4 = (s32[2]{0:T(128)S(1)}, s32[2]{0:T(128)}, u32[]{:S(2)}) copy-start(s32[2]{0:T(128)} %constant.146) | copy-start | bytes 28
  75.3 146.9 %all-to-all-start.1 = ((bf16[32,48,1024]{2,1,0:T(8,128)(2,1)}), bf16[32,48,1024]{2,1,0:T(8,128)(2,1)}, u32[]{:S(2)}, u32[]{:S(2)}) async-start(bf16[32,48,1024]{2,1,0:T(8,128)(2,1)} %bitcast.19), calls=%async_computation.1 | async-start | bytes 6291456 | tf_op jit(solution)/shard_map/all_to_all | solution.py:59
  80.3 352.3 %all-gather.5.cloned.1.call-start = ((), (), s32[]{:S(2)}) async-start(), calls=%async_computation.4 | async-start | bytes 17301504 | tf_op jit(solution)/shard_map/all_gather | solution.py:9
  251.1 7.6 %copy-start.3 = (s32[32]{0:T(128)S(1)}, s32[32]{0:T(128)}, u32[]{:S(2)}) copy-start(s32[32]{0:T(128)} %param.15) | copy-start | bytes 388
  251.1 9.7 %copy-start.7 = (u32[128]{0:T(128)S(1)}, u32[128]{0:T(128)}, u32[]{:S(2)}) copy-start(u32[128]{0:T(128)} %constant.153) | copy-start | bytes 1540
  251.1 106.5 %copy-start.6 = (f32[8]{0:T(128)S(1)}, f32[8]{0:T(128)}, u32[]{:S(2)}) copy-start(f32[8]{0:T(128)} %param.16) | copy-start | bytes 100
  251.1 106.5 %all-to-all-start.2 = ((bf16[32,48,1024]{2,1,0:T(8,128)(2,1)}), bf16[32,48,1024]{2,1,0:T(8,128)(2,1)}, u32[]{:S(2)}, u32[]{:S(2)}) async-start(bf16[32,48,1024]{2,1,0:T(8,128)(2,1)} %bitcast.142), calls=%async_computation.2 | async-start | bytes 6291456 | tf_op jit(solution)/shard_map/all_to_all | solution.py:57
  432.6 3.2 copy-start.1
  456.7 140.0 %all-to-all-start.3 = ((bf16[32,48,1024]{2,1,0:T(8,128)(2,1)}), bf16[32,48,1024]{2,1,0:T(8,128)(2,1)S(1)}, u32[]{:S(2)}, u32[]{:S(2)}) async-start(bf16[32,48,1024]{2,1,0:T(8,128)(2,1)} %bitcast.141), calls=%async_computation.3 | async-start | bytes 6291456 | tf_op jit(solution)/shard_map/all_to_all | solution.py:135
  557.0 127.4 %all-gather.7.cloned.1.call-start = ((), (), s32[]{:S(2)}) async-start(), calls=%async_computation.5 | async-start | bytes 10485760 | tf_op jit(solution)/shard_map/all_gather | solution.py:137
Sparse Core Ops, SparseCore 0:
  243.1 105.8 all-gather.4
  602.2 82.0 all-gather.6
where the time goes:
time: 717 us; the launch traced here: 706 us
  local copies, waits for them, and re-layouts  203 us (28%)
  waiting for transfers between devices  154 us (21%)
  starting transfers between devices  121 us (17%)
  blocking collectives  116 us (16%)
  matrix products  67.8 us (9%)
  other arithmetic  28.2 us (4%)
  between operations  15.3 us (2%)
    unnamed x22, local copies, waits for them, and re-layouts  123 us
    all_to_all x1, starting transfers between devices, per_device(): lax.all_to_all(outgoing, 'ctx', split_axis=0, concat_axis=0, tiled=True)  100 us
    unnamed x1, blocking collectives  95.4 us
    all_gather x1, waiting for transfers between devices, per_device(): lax.all_gather(incoming.reshape(ctx_count * capacity, result_width)[send_...  82.3 us
    all_to_all x1, waiting for transfers between devices, per_device(): lax.all_to_all(outgoing, 'ctx', split_axis=0, concat_axis=0, tiled=True)  39.7 us
    scatter x6, local copies, waits for them, and re-layouts, place_rows(): return jnp.zeros((seg_rows, feat_width), received.dtype).at[positions].se...  39.3 us
    all_to_all x1, waiting for transfers between devices, per_device(): lax.all_to_all(scatter_rows(keys), 'ctx', split_axis=0, concat_axis=0, ti...  31.7 us
    scatter x3, local copies, waits for them, and re-layouts, scatter_rows(): jnp.zeros((ctx_count * capacity, feat_width), source.dtype).at[send_slot]  24.3 us
  transfers between devices with their start and end apart: 6, of which 3 were waited for; matrix products, arithmetic and copies ran while one was open for 30% of the time, Pallas kernels for 0%

commit v1 on v0

v1 whole, which is shorter than its diff:
```python
import jax
import jax.numpy as jnp
from jax import lax
from jax.sharding import PartitionSpec as P


def feature(inputs):
    return jax.nn.elu(inputs) + 1.0


def per_device(queries, keys, values, row_target, seg_doc, mem_gate, out_weight):
    highest = lax.Precision.HIGHEST
    f32, bf16 = jnp.float32, jnp.bfloat16
    n = lax.axis_size("ctx")
    me = lax.axis_index("ctx")
    seg, width = queries.shape
    heads = mem_gate.shape[0]
    dh = width // heads
    cap = seg // n + (seg // n) // 2
    slots = n * cap

    targets = row_target.reshape(n, seg)
    r_idx = jnp.arange(seg, dtype=jnp.int32)
    o_idx = jnp.arange(n, dtype=jnp.int32)
    s_idx = jnp.arange(slots, dtype=jnp.int32)
    w_idx = jnp.arange(cap, dtype=jnp.int32)
    lower = (r_idx[None, :] < r_idx[:, None]).astype(bf16)

    mine = lax.dynamic_index_in_dim(targets, me, 0, keepdims=False)
    owner = mine // seg
    match = (owner[:, None] == o_idx[None, :]).astype(bf16)
    before = jnp.dot(lower, match, preferred_element_type=f32)
    within = jnp.sum(jnp.where(match > 0, before, 0.0), axis=1).astype(jnp.int32)
    send_slot = owner * cap + within
    slot_row = jnp.sum(
        jnp.where(send_slot[None, :] == s_idx[:, None], r_idx[None, :], 0), axis=1
    )

    arrived = (targets // seg) == me
    rank = jnp.dot(arrived.astype(bf16), lower.T, preferred_element_type=f32).astype(jnp.int32)
    hit = arrived[:, None, :] & (rank[:, None, :] == w_idx[None, :, None])
    pslot = jnp.sum(jnp.where(hit, (targets % seg)[:, None, :], 0), axis=2).reshape(slots)
    count = jnp.sum(arrived.astype(jnp.int32), axis=1)
    valid = (w_idx[None, :] < count[:, None]).reshape(slots)
    tok_slot = jnp.sum(
        jnp.where((pslot[None, :] == r_idx[:, None]) & valid[None, :], s_idx[None, :], 0),
        axis=1,
    )

    def dispatch(source):
        buffer = jnp.take(source, slot_row, axis=0, mode="clip").reshape(n, cap, width)
        got = lax.all_to_all(buffer, "ctx", 0, 0, tiled=True).reshape(slots, width)
        return jnp.take(got, tok_slot, axis=0, mode="clip").reshape(seg, heads, dh)

    key_heads = dispatch(keys)
    value_heads = dispatch(values)
    query_heads = dispatch(queries)

    key_feat = feature(key_heads.astype(f32))
    delta_m = jnp.einsum(
        "khd,khe->hde", key_feat, value_heads.astype(f32), precision=highest
    )
    delta_z = jnp.sum(key_feat, axis=0)
    delta = jnp.concatenate([delta_m, delta_z[:, None, :]], axis=1)
    doc = seg_doc[me]
    start = jnp.min(jnp.where(seg_doc == doc, o_idx, n))
    total = delta
    step = 1
    while step < n:
        perm = [(j, j + step) for j in range(n - step)]
        got = lax.ppermute(total, "ctx", perm)
        total = total + jnp.where(me - step >= start, got, jnp.zeros_like(got))
        step *= 2
    memory = total - delta
    mem_m = memory[:, :dh, :]
    mem_z = memory[:, dh, :]

    score_scale = dh ** (-0.5)
    scores = jnp.einsum(
        "qhd,khd->hqk", query_heads, key_heads, preferred_element_type=f32
    ) * score_scale
    causal = r_idx[:, None] >= r_idx[None, :]
    scores = jnp.where(causal[None], scores, -1e30)
    row_max = jnp.max(scores, axis=-1, keepdims=True)
    weights = jnp.exp(scores - row_max)
    probabilities = (weights / jnp.sum(weights, axis=-1, keepdims=True)).astype(bf16)
    local_out = jnp.einsum(
        "hqk,khd->qhd", probabilities, value_heads, preferred_element_type=f32
    )

    query_feat = feature(query_heads.astype(f32))
    numerator = jnp.einsum("qhd,hde->qhe", query_feat, mem_m, precision=highest)
    denominator = jnp.einsum("qhd,hd->qh", query_feat, mem_z, precision=highest)
    recalled = numerator / jnp.maximum(denominator, 1.0)[..., None]
    gate_value = jax.nn.sigmoid(mem_gate)[None, :, None]
    combined = (
        (gate_value * recalled + (1.0 - gate_value) * local_out)
        .astype(bf16)
        .reshape(seg, width)
    )

    outgoing = jnp.take(combined, pslot, axis=0, mode="clip").reshape(n, cap, width)
    incoming = lax.all_to_all(outgoing, "ctx", 0, 0, tiled=True).reshape(slots, width)
    rows = jnp.take(incoming, send_slot, axis=0, mode="clip")
    gathered = lax.all_gather(rows, "head", axis=1, tiled=True)
    summed = jnp.dot(gathered, out_weight, preferred_element_type=f32)
    return summed.astype(bf16)


def solution(mesh):
    return jax.shard_map(
        per_device,
        mesh=mesh,
        in_specs=(
            P("ctx", "head"),
            P("ctx", "head"),
            P("ctx", "head"),
            P(),
            P(),
            P("head"),
            P(None, "head"),
        ),
        out_specs=P("ctx", "head"),
        check_vma=False,
    )
```

time: 717 us -> 437 us (0.61)
  local copies, waits for them, and re-layouts: 203 us -> 63.9 us
  blocking collectives: 116 us -> 0 us
  starting transfers between devices: 121 us -> 54.1 us
  waiting for transfers between devices: 154 us -> 210 us
  other arithmetic: 28.2 us -> 15.3 us
    unnamed x22 -> x29, local copies, waits for them, and re-layouts: 123 us -> 2.42 us
    unnamed x1 -> x0, blocking collectives: 95.4 us -> none
    all_to_all x4, starting transfers between devices: 121 us -> 30.5 us  [the longest x3 19.2 us: dispatch(): got = lax.all_to_all(buffer, 'ctx', 0, 0, tiled=True).reshape(slots, width)]
    scatter x9 -> x0, local copies, waits for them, and re-layouts: 63.5 us -> none  [the longest x6 39.3 us: place_rows(): return jnp.zeros((seg_rows, feat_width), received.dtype).at[positions].se...]
    gather x2 -> x8, local copies, waits for them, and re-layouts: 11.2 us -> 49.7 us  [the longest x3 20.9 us: dispatch(): return jnp.take(got, tok_slot, axis=0, mode='clip').reshape(seg, heads, dh)]
    ppermute x0 -> x5, waiting for transfers between devices: none -> 33.1 us  [per_device(): got = lax.ppermute(total, 'ctx', perm)]
    ppermute x0 -> x5, starting transfers between devices: none -> 23.5 us  [per_device(): got = lax.ppermute(total, 'ctx', perm)]
    all_to_all x4, waiting for transfers between devices: 71.4 us -> 93.8 us  [the longest x3 54.1 us: dispatch(): got = lax.all_to_all(buffer, 'ctx', 0, 0, tiled=True).reshape(slots, width)]
  transfers between devices with their start and end apart: 6 -> 10, of which waited for: 3 -> 7; matrix products, arithmetic and copies ran while one was open for 30% -> 21% of each run, Pallas kernels for 0% -> 0%
where the time goes in v1:
time: 437 us; the launch traced here: 428 us
  waiting for transfers between devices  210 us (48%)
  matrix products  67.9 us (16%)
  local copies, waits for them, and re-layouts  63.9 us (15%)
  starting transfers between devices  54.1 us (12%)
  between operations  17.2 us (4%)
  other arithmetic  15.3 us (4%)
    all_gather x1, waiting for transfers between devices, per_device(): gathered = lax.all_gather(rows, 'head', axis=1, tiled=True)  83.1 us
    all_to_all x3, waiting for transfers between devices, dispatch(): got = lax.all_to_all(buffer, 'ctx', 0, 0, tiled=True).reshape(slots, width)  54.1 us
    all_to_all x1, waiting for transfers between devices, per_device(): lax.all_to_all(outgoing, 'ctx', 0, 0, tiled=True).reshape(slots, width)  39.7 us
    ppermute x5, waiting for transfers between devices, per_device(): got = lax.ppermute(total, 'ctx', perm)  33.1 us
    ppermute x5, starting transfers between devices, per_device(): got = lax.ppermute(total, 'ctx', perm)  23.5 us
    gather x3, local copies, waits for them, and re-layouts, dispatch(): return jnp.take(got, tok_slot, axis=0, mode='clip').reshape(seg, heads, dh)  20.9 us
    dot_general x1, matrix products, per_device(): jnp.einsum('hqk,khd->qhd', probabilities, value_heads, preferred_element_...  19.4 us
    all_to_all x3, starting transfers between devices, dispatch(): got = lax.all_to_all(buffer, 'ctx', 0, 0, tiled=True).reshape(slots, width)  19.2 us
  transfers between devices with their start and end apart: 10, of which 7 were waited for; matrix products, arithmetic and copies ran while one was open for 21% of the time, Pallas kernels for 0%

profile of v1, /device:TPU:1, one launch (start us, length us, event | category | flops | bytes accessed | tf_op | source)
XLA Modules:
  0.0 428.3 jit_solution(12497643664026182384)
XLA Ops:
  6.5 1.1 reshape.229
  9.0 5.8 %gather_fusion.2 = bf16[1536,1024]{1,0:T(8,128)(2,1)} fusion(bf16[1024,1024]{1,0:T(8,128)(2,1)S(1)} %copy-done, s32[2048]{0:T(1024)S(1)} %pad_clamp_fusion.1), kind=kCustom, calls=%fused_computation.2 | custom fusion | bytes 6297600 | tf_op jit(solution)/shard_map/jit(_take)/gather | solution.py:51
  14.8 8.8 %all-to-all-start.1 = ((bf16[32,48,1024]{2,1,0:T(8,128)(2,1)}), bf16[32,48,1024]{2,1,0:T(8,128)(2,1)}, u32[]{:S(2)}, u32[]{:S(2)}) async-start(bf16[32,48,1024]{2,1,0:T(8,128)(2,1)} %bitcast.148), calls=%async_computation.1 | async-start | bytes 6291456 | tf_op jit(solution)/shard_map/all_to_all | solution.py:52
  23.6 5.8 %gather_fusion = bf16[1536,1024]{1,0:T(8,128)(2,1)} fusion(bf16[1024,1024]{1,0:T(8,128)(2,1)S(1)} %copy-done.2, s32[2048]{0:T(1024)S(1)} %pad_clamp_fusion.1), kind=kCustom, calls=%fused_computation | custom fusion | bytes 6297600 | tf_op jit(solution)/shard_map/jit(_take)/gather | solution.py:51
  29.4 34.0 %all-to-all-done.1 = bf16[32,48,1024]{2,1,0:T(8,128)(2,1)} async-done(((bf16[32,48,1024]{2,1,0:T(8,128)(2,1)}), bf16[32,48,1024]{2,1,0:T(8,128)(2,1)}, u32[]{:S(2)}, u32[]{:S(2)}) %all-to-all-start.1) | async-done | bytes 3145760 | tf_op jit(solution)/shard_map/all_to_all | solution.py:52
  63.4 5.2 %all-to-all-start = ((bf16[32,48,1024]{2,1,0:T(8,128)(2,1)}), bf16[32,48,1024]{2,1,0:T(8,128)(2,1)}, u32[]{:S(2)}, u32[]{:S(2)}) async-start(bf16[32,48,1024]{2,1,0:T(8,128)(2,1)} %bitcast.146), calls=%async_computation | async-start | bytes 6291456 | tf_op jit(solution)/shard_map/all_to_all | solution.py:52
  69.4 1.7 select_reduce_fusion.1
  71.3 5.8 %gather_fusion.4 = bf16[1536,1024]{1,0:T(8,128)(2,1)} fusion(bf16[1024,1024]{1,0:T(8,128)(2,1)S(1)} %copy-done.3, s32[2048]{0:T(1024)S(1)} %pad_clamp_fusion.1), kind=kCustom, calls=%fused_computation.4 | custom fusion | bytes 6297600 | tf_op jit(solution)/shard_map/jit(_take)/gather | solution.py:51
  77.1 1.3 select_reduce_fusion
  78.4 7.3 %gather_fusion.3 = bf16[1024,1024]{1,0:T(8,128)(2,1)S(1)} fusion(bf16[1536,1024]{1,0:T(8,128)(2,1)} %bitcast.6, s32[1024]{0:T(1024)S(1)} %broadcast_clamp_fusion.1), kind=kCustom, calls=%fused_computation.3 | custom fusion | bytes 4198400 | tf_op jit(solution)/shard_map/jit(_take)/gather | solution.py:53
  85.7 2.6 copy.73
  88.3 20.1 %all-to-all-done = bf16[32,48,1024]{2,1,0:T(8,128)(2,1)} async-done(((bf16[32,48,1024]{2,1,0:T(8,128)(2,1)}), bf16[32,48,1024]{2,1,0:T(8,128)(2,1)}, u32[]{:S(2)}, u32[]{:S(2)}) %all-to-all-start) | async-done | bytes 3145760 | tf_op jit(solution)/shard_map/all_to_all | solution.py:52
  108.4 5.3 %all-to-all-start.2 = ((bf16[32,48,1024]{2,1,0:T(8,128)(2,1)}), bf16[32,48,1024]{2,1,0:T(8,128)(2,1)S(1)}, u32[]{:S(2)}, u32[]{:S(2)}) async-start(bf16[32,48,1024]{2,1,0:T(8,128)(2,1)} %bitcast.145), calls=%async_computation.2 | async-start | bytes 6291456 | tf_op jit(solution)/shard_map/all_to_all | solution.py:52
  113.7 8.4 %gather_fusion.1 = bf16[1024,1024]{1,0:T(8,128)(2,1)} fusion(bf16[1536,1024]{1,0:T(8,128)(2,1)} %bitcast.4, s32[1024]{0:T(1024)S(1)} %broadcast_clamp_fusion.1), kind=kCustom, calls=%fused_computation.1 | custom fusion | bytes 4198400 | tf_op jit(solution)/shard_map/jit(_take)/gather | solution.py:53
  122.1 7.2 %fusion.10 = f32[8,128,128]{2,1,0:T(8,128)S(1)} fusion(bf16[1024,8,128]{0,2,1:T(8,128)(2,1)} %bitcast.149, bf16[1024,1024]{1,0:T(8,128)(2,1)} %gather_fusion.1), kind=kOutput, calls=%fused_computation.33 | convolution fusion | flops 1615855616 | bytes 4718592 | tf_op jit(solution)/shard_map/khd,khe->hde/dot_general | solution.py:60
  129.3 1.9 fusion.14
  131.3 0.9 copy.51
  132.2 3.5 collective-permute-start
  136.3 1.3 fusion.98
  138.3 16.2 %collective-permute-done = f32[8,129,128]{2,0,1:T(8,128)} collective-permute-done((f32[8,129,128]{2,0,1:T(8,128)}, f32[8,129,128]{2,0,1:T(8,128)}, u32[]{:S(2)}, u32[]{:S(2)}) %collective-permute-start) | collective-permute-done | bytes 528416 | tf_op jit(solution)/shard_map/ppermute | solution.py:71
  154.5 1.3 fusion.88
  156.6 0.9 copy.53
  157.5 3.3 collective-permute-start.1
  161.5 8.1 %collective-permute-done.1 = f32[8,129,128]{2,0,1:T(8,128)} collective-permute-done((f32[8,129,128]{2,0,1:T(8,128)}, f32[8,129,128]{2,0,1:T(8,128)}, u32[]{:S(2)}, u32[]{:S(2)}) %collective-permute-start.1) | collective-permute-done | bytes 528416 | tf_op jit(solution)/shard_map/ppermute | solution.py:71
  169.6 1.3 fusion.87
  171.7 0.9 copy.55
  172.6 8.8 %collective-permute-start.2 = (f32[8,129,128]{2,0,1:T(8,128)}, f32[8,129,128]{2,0,1:T(8,128)}, u32[]{:S(2)}, u32[]{:S(2)}) collective-permute-start(f32[8,129,128]{2,0,1:T(8,128)} %copy.55), channel_id=1, source_target_pairs={{0,16},{4,20},{8,24},{12,28},{16,32},{20,36},{24,40},{28,44},{32,4... | collective-permute-start | bytes 1585160 | tf_op jit(solution)/shard_map/ppermute | solution.py:71
  182.1 8.8 %collective-permute-done.2 = f32[8,129,128]{2,0,1:T(8,128)} collective-permute-done((f32[8,129,128]{2,0,1:T(8,128)}, f32[8,129,128]{2,0,1:T(8,128)}, u32[]{:S(2)}, u32[]{:S(2)}) %collective-permute-start.2) | collective-permute-done | bytes 528416 | tf_op jit(solution)/shard_map/ppermute | solution.py:71
  190.8 1.3 fusion.86
  193.0 0.9 copy.57
  193.9 2.5 collective-permute-start.3
  197.7 1.3 iota_compare_fusion.3
  199.0 5.3 %gather_fusion.5 = bf16[1024,1024]{1,0:T(8,128)(2,1)} fusion(bf16[1536,1024]{1,0:T(8,128)(2,1)S(1)} %bitcast.143, s32[1024]{0:T(1024)S(1)} %broadcast_clamp_fusion.1), kind=kCustom, calls=%fused_computation.5 | custom fusion | bytes 4198400 | tf_op jit(solution)/shard_map/jit(_take)/gather | solution.py:53
  204.3 1.3 fusion.85
  205.7 0.9 copy.59
  206.6 5.4 %collective-permute-start.4 = (f32[8,129,128]{2,0,1:T(8,128)}, f32[8,129,128]{2,0,1:T(8,128)}, u32[]{:S(2)}, u32[]{:S(2)}) collective-permute-start(f32[8,129,128]{2,0,1:T(8,128)} %copy.59), channel_id=1, source_target_pairs={{0,64},{4,68},{8,72},{12,76},{16,80},{20,84},{24,88},{28,92},{32,9... | collective-permute-start | bytes 1585160 | tf_op jit(solution)/shard_map/ppermute | solution.py:71
  212.0 13.4 %fusion.113 = f32[8,1024]{1,0:T(8,128)S(1)} fusion(pred[1024,1024]{0,1:T(8,128)(4,1)} %iota_compare_fusion.3, bf16[1024,1024]{1,0:T(8,128)(2,1)} %gather_fusion.5, bf16[1024,1024]{1,0:T(8,128)(2,1)} %gather_fusion.1), kind=kOutput, calls=%fused_computation.147 | convolution fusion | flops 2181039104 | bytes 5275648 | tf_op jit(solution)/shard_map/sub | solution.py:85
  225.4 19.4 %fusion.5 = f32[8,128,1024]{2,1,0:T(8,128)} fusion(bf16[1024,8,128]{0,2,1:T(8,128)(2,1)} %bitcast.150, f32[8,1024]{1,0:T(8,128)S(1)} %fusion.113, pred[1024,1024]{0,1:T(8,128)(4,1)} %iota_compare_fusion.3, bf16[1024,1024]{1,0:T(8,128)(2,1)S(1)} %copy-done.10, bf16[1024,1024]{1,0:T(8,128)(2,1)} %gather_fusion.1), kind=kOutput, calls=%fused_computation.16 | convolution fusion | flops 4336919552 | bytes 11567104 | tf_op jit(solution)/shard_map/hqk,khd->qhd/dot_general | solution.py:87
  244.8 1.2 fusion.84
  246.0 4.9 %fusion.21 = f32[8,1,1024]{2,1,0:T(1,128)S(1)} fusion(f32[8,129,128]{2,1,0:T(8,128)S(1)} %fusion.84, bf16[1024,1024]{1,0:T(8,128)(2,1)S(1)} %copy-done.10), kind=kOutput, calls=%fused_computation.47 | convolution fusion | flops 17825792 | bytes 2134016 | tf_op jit(solution)/shard_map/qhd,hd->qh/dot_general | solution.py:93
  251.0 7.1 %fusion.17 = bf16[1024,8,128]{0,2,1:T(8,128)(2,1)} fusion(f32[8,128,1024]{2,1,0:T(8,128)S(1)} %copy-done.13, f32[8]{0:T(128)S(1)} %get-tuple-element.5, f32[1024,8]{0,1:T(8,128)S(1)} %fusion.95, f32[8]{0:T(128)S(1)} %get-tuple-element.6, f32[8,129,128]{2,1,0:T(8,128)S(1)} %fusion.84, bf16[1024,1024]{1,0:T(8,128)(2,1)S(1)} %copy-done.10), kind=kOutput, calls=%fused_computation.40 | convolution fusion | flops 1621098496 | bytes 8946688 | tf_op jit(solution)/shard_map/qhd,hde->qhe/dot_general | solution.py:92
  258.1 2.9 copy.67
  261.0 5.8 %gather_fusion.6 = bf16[1536,1024]{1,0:T(8,128)(2,1)} fusion(bf16[1024,1024]{1,0:T(8,128)(2,1)S(1)} %copy.67, s32[2048]{0:T(1024)S(1)} %pad_clamp_fusion), kind=kCustom, calls=%fused_computation.6 | custom fusion | bytes 6297600 | tf_op jit(solution)/shard_map/jit(_take)/gather | solution.py:102
  266.8 11.3 %all-to-all-start.3 = ((bf16[32,48,1024]{2,1,0:T(8,128)(2,1)}), bf16[32,48,1024]{2,1,0:T(8,128)(2,1)S(1)}, u32[]{:S(2)}, u32[]{:S(2)}) async-start(bf16[32,48,1024]{2,1,0:T(8,128)(2,1)} %bitcast.147), calls=%async_computation.3 | async-start | bytes 6291456 | tf_op jit(solution)/shard_map/all_to_all | solution.py:103
  278.2 39.7 %all-to-all-done.3 = bf16[32,48,1024]{2,1,0:T(8,128)(2,1)S(1)} async-done(((bf16[32,48,1024]{2,1,0:T(8,128)(2,1)}), bf16[32,48,1024]{2,1,0:T(8,128)(2,1)S(1)}, u32[]{:S(2)}, u32[]{:S(2)}) %all-to-all-start.3) | async-done | bytes 3145760 | tf_op jit(solution)/shard_map/all_to_all | solution.py:103
  317.9 5.5 %gather_fusion.7 = bf16[1024,1024]{1,0:T(8,128)(2,1)} fusion(bf16[1536,1024]{1,0:T(8,128)(2,1)S(1)} %bitcast.144, s32[1024]{0:T(1024)S(1)} %broadcast_clamp_fusion), kind=kCustom, calls=%fused_computation.7 | custom fusion | bytes 4198400 | tf_op jit(solution)/shard_map/jit(_take)/gather | solution.py:104
  323.4 83.1 %all-gather.3.cloned.1.call-done = bf16[1024,4096]{1,0:T(8,128)(2,1)} async-done(((bf16[1024,1024]{1,0:T(8,128)(2,1)}), bf16[1024,4096]{1,0:T(8,128)(2,1)}) %all-gather.3.cloned.1.call-update) | async-done | bytes 8388624 | tf_op jit(solution)/shard_map/all_gather | solution.py:105
  406.5 14.8 %convolution_convert_fusion = bf16[1024,1024]{1,0:T(8,128)(2,1)} fusion(bf16[1024,4096]{1,0:T(8,128)(2,1)} %all-gather.3.cloned.1.call-done, bf16[4096,1024]{1,0:T(8,128)(2,1)} %param.13), kind=kOutput, calls=%fused_computation.66 | convolution fusion | flops 8590983168 | bytes 18874368 | tf_op jit(solution)/shard_map/dot_general | solution.py:106
  (54 shorter events, 5.5 us)
Async XLA Ops:
  6.5 2.5 copy-start
  14.8 8.8 %copy-start.2 = (bf16[1024,1024]{1,0:T(8,128)(2,1)S(1)}, bf16[1024,1024]{1,0:T(8,128)(2,1)}, u32[]{:S(2)}) copy-start(bf16[1024,1024]{1,0:T(8,128)(2,1)} %param.8) | copy-start | bytes 6291460
  14.8 48.6 %all-to-all-start.1 = ((bf16[32,48,1024]{2,1,0:T(8,128)(2,1)}), bf16[32,48,1024]{2,1,0:T(8,128)(2,1)}, u32[]{:S(2)}, u32[]{:S(2)}) async-start(bf16[32,48,1024]{2,1,0:T(8,128)(2,1)} %bitcast.148), calls=%async_computation.1 | async-start | bytes 6291456 | tf_op jit(solution)/shard_map/all_to_all | solution.py:52
  63.4 7.9 %copy-start.3 = (bf16[1024,1024]{1,0:T(8,128)(2,1)S(1)}, bf16[1024,1024]{1,0:T(8,128)(2,1)}, u32[]{:S(2)}) copy-start(bf16[1024,1024]{1,0:T(8,128)(2,1)} %param.7) | copy-start | bytes 6291460
  63.4 45.0 %all-to-all-start = ((bf16[32,48,1024]{2,1,0:T(8,128)(2,1)}), bf16[32,48,1024]{2,1,0:T(8,128)(2,1)}, u32[]{:S(2)}, u32[]{:S(2)}) async-start(bf16[32,48,1024]{2,1,0:T(8,128)(2,1)} %bitcast.146), calls=%async_computation | async-start | bytes 6291456 | tf_op jit(solution)/shard_map/all_to_all | solution.py:52
  108.4 90.6 %all-to-all-start.2 = ((bf16[32,48,1024]{2,1,0:T(8,128)(2,1)}), bf16[32,48,1024]{2,1,0:T(8,128)(2,1)S(1)}, u32[]{:S(2)}, u32[]{:S(2)}) async-start(bf16[32,48,1024]{2,1,0:T(8,128)(2,1)} %bitcast.145), calls=%async_computation.2 | async-start | bytes 6291456 | tf_op jit(solution)/shard_map/all_to_all | solution.py:52
  122.1 7.2 %copy-start.4 = (bf16[1024,1024]{1,0:T(8,128)(2,1)S(1)}, bf16[1024,1024]{1,0:T(8,128)(2,1)}, u32[]{:S(2)}) copy-start(bf16[1024,1024]{1,0:T(8,128)(2,1)} %gather_fusion.1) | copy-start | bytes 6291460
  129.3 1.9 copy-start.8
  129.3 6.4 %copy-start.11 = (s32[32]{0:T(128)S(1)}, s32[32]{0:T(128)}, u32[]{:S(2)}) copy-start(s32[32]{0:T(128)} %param.11) | copy-start | bytes 388
  132.2 22.3 %collective-permute-start = (f32[8,129,128]{2,0,1:T(8,128)}, f32[8,129,128]{2,0,1:T(8,128)}, u32[]{:S(2)}, u32[]{:S(2)}) collective-permute-start(f32[8,129,128]{2,0,1:T(8,128)} %copy.51), channel_id=1, source_target_pairs={{0,4},{4,8},{8,12},{12,16},{16,20},{20,24},{24,28},{28,32},{32,36}... | collective-permute-start | bytes 1585160 | tf_op jit(solution)/shard_map/ppermute | solution.py:71
  155.8 0.8 copy-start.7
  157.5 12.0 %collective-permute-start.1 = (f32[8,129,128]{2,0,1:T(8,128)}, f32[8,129,128]{2,0,1:T(8,128)}, u32[]{:S(2)}, u32[]{:S(2)}) collective-permute-start(f32[8,129,128]{2,0,1:T(8,128)} %copy.53), channel_id=1, source_target_pairs={{0,8},{4,12},{8,16},{12,20},{16,24},{20,28},{24,32},{28,36},{32,40... | collective-permute-start | bytes 1585160 | tf_op jit(solution)/shard_map/ppermute | solution.py:71
  161.4 37.5 %copy-start.12 = (f32[8]{0:T(128)S(1)}, f32[8]{0:T(128)}, u32[]{:S(2)}) copy-start(f32[8]{0:T(128)} %param.12) | copy-start | bytes 100
  170.9 0.8 copy-start.6
  172.6 18.2 %collective-permute-start.2 = (f32[8,129,128]{2,0,1:T(8,128)}, f32[8,129,128]{2,0,1:T(8,128)}, u32[]{:S(2)}, u32[]{:S(2)}) collective-permute-start(f32[8,129,128]{2,0,1:T(8,128)} %copy.55), channel_id=1, source_target_pairs={{0,16},{4,20},{8,24},{12,28},{16,32},{20,36},{24,40},{28,44},{32,4... | collective-permute-start | bytes 1585160 | tf_op jit(solution)/shard_map/ppermute | solution.py:71
  192.2 0.8 copy-start.5
  193.9 10.4 %collective-permute-start.3 = (f32[8,129,128]{2,0,1:T(8,128)}, f32[8,129,128]{2,0,1:T(8,128)}, u32[]{:S(2)}, u32[]{:S(2)}) collective-permute-start(f32[8,129,128]{2,0,1:T(8,128)} %copy.57), channel_id=1, source_target_pairs={{0,32},{4,36},{8,40},{12,44},{16,48},{20,52},{24,56},{28,60},{32,6... | collective-permute-start | bytes 1585160 | tf_op jit(solution)/shard_map/ppermute | solution.py:71
  206.6 18.8 %copy-start.10 = (bf16[1024,1024]{1,0:T(8,128)(2,1)S(1)}, bf16[1024,1024]{1,0:T(8,128)(2,1)}, u32[]{:S(2)}) copy-start(bf16[1024,1024]{1,0:T(8,128)(2,1)} %gather_fusion.5) | copy-start | bytes 6291460
  206.6 38.2 %collective-permute-start.4 = (f32[8,129,128]{2,0,1:T(8,128)}, f32[8,129,128]{2,0,1:T(8,128)}, u32[]{:S(2)}, u32[]{:S(2)}) collective-permute-start(f32[8,129,128]{2,0,1:T(8,128)} %copy.59), channel_id=1, source_target_pairs={{0,64},{4,68},{8,72},{12,76},{16,80},{20,84},{24,88},{28,92},{32,9... | collective-permute-start | bytes 1585160 | tf_op jit(solution)/shard_map/ppermute | solution.py:71
  225.4 19.4 %copy-start.9 = (f32[8,128,128]{2,1,0:T(8,128)S(1)}, f32[8,128,128]{2,1,0:T(8,128)}, u32[]{:S(2)}) copy-start(f32[8,128,128]{2,1,0:T(8,128)} %copy-done.8) | copy-start | bytes 1572868
  246.0 5.0 %copy-start.13 = (f32[8,128,1024]{2,1,0:T(8,128)S(1)}, f32[8,128,1024]{2,1,0:T(8,128)}, u32[]{:S(2)}) copy-start(f32[8,128,1024]{2,1,0:T(8,128)} %fusion.5) | copy-start | bytes 12582916
  266.8 51.1 %all-to-all-start.3 = ((bf16[32,48,1024]{2,1,0:T(8,128)(2,1)}), bf16[32,48,1024]{2,1,0:T(8,128)(2,1)S(1)}, u32[]{:S(2)}, u32[]{:S(2)}) async-start(bf16[32,48,1024]{2,1,0:T(8,128)(2,1)} %bitcast.147), calls=%async_computation.3 | async-start | bytes 6291456 | tf_op jit(solution)/shard_map/all_to_all | solution.py:103
  278.1 128.4 %all-gather.3.cloned.1.call-start = ((), (), s32[]{:S(2)}) async-start(), calls=%async_computation.4 | async-start | bytes 10485760 | tf_op jit(solution)/shard_map/all_gather | solution.py:105
  406.5 14.8 %copy-start.1 = (bf16[1024,1024]{1,0:T(8,128)(2,1)S(1)}, bf16[1024,1024]{1,0:T(8,128)(2,1)}, u32[]{:S(2)}) copy-start(bf16[1024,1024]{1,0:T(8,128)(2,1)} %param.9) | copy-start | bytes 6291460
Sparse Core Ops, SparseCore 0:
  323.5 82.9 all-gather.2

commit v2 on v1

--- a/solution.py
+++ b/solution.py
@@ -64,29 +64,44 @@
     delta = jnp.concatenate([delta_m, delta_z[:, None, :]], axis=1)
     doc = seg_doc[me]
     start = jnp.min(jnp.where(seg_doc == doc, o_idx, n))
-    total = delta
+    score_scale = dh ** (-0.5)
+    causal = r_idx[:, None] >= r_idx[None, :]
+
+    def local_attention(query_part, key_part, value_part):
+        scores = jnp.einsum(
+            "qhd,khd->hqk", query_part, key_part, preferred_element_type=f32
+        ) * score_scale
+        scores = jnp.where(causal[None], scores, -1e30)
+        row_max = jnp.max(scores, axis=-1, keepdims=True)
+        weights = jnp.exp(scores - row_max)
+        probabilities = (weights / jnp.sum(weights, axis=-1, keepdims=True)).astype(bf16)
+        return jnp.einsum(
+            "hqk,khd->qhd", probabilities, value_part, preferred_element_type=f32
+        )
+
+    shifts = []
     step = 1
     while step < n:
+        shifts.append(step)
+        step *= 2
+    cuts = [round(heads * i / len(shifts)) for i in range(len(shifts) + 1)]
+    pieces = []
+    total = delta
+    for k, step in enumerate(shifts):
+        lo, hi = cuts[k], cuts[k + 1]
+        total, operands = lax.optimization_barrier(
+            (total, (query_heads[:, lo:hi], key_heads[:, lo:hi], value_heads[:, lo:hi]))
+        )
         perm = [(j, j + step) for j in range(n - step)]
         got = lax.ppermute(total, "ctx", perm)
+        piece = local_attention(*operands)
+        got, piece = lax.optimization_barrier((got, piece))
+        pieces.append(piece)
         total = total + jnp.where(me - step >= start, got, jnp.zeros_like(got))
-        step *= 2
+    local_out = jnp.concatenate(pieces, axis=1)
     memory = total - delta
     mem_m = memory[:, :dh, :]
     mem_z = memory[:, dh, :]
-
-    score_scale = dh ** (-0.5)
-    scores = jnp.einsum(
-        "qhd,khd->hqk", query_heads, key_heads, preferred_element_type=f32
-    ) * score_scale
-    causal = r_idx[:, None] >= r_idx[None, :]
-    scores = jnp.where(causal[None], scores, -1e30)
-    row_max = jnp.max(scores, axis=-1, keepdims=True)
-    weights = jnp.exp(scores - row_max)
-    probabilities = (weights / jnp.sum(weights, axis=-1, keepdims=True)).astype(bf16)
-    local_out = jnp.einsum(
-        "hqk,khd->qhd", probabilities, value_heads, preferred_element_type=f32
-    )
 
     query_feat = feature(query_heads.astype(f32))
     numerator = jnp.einsum("qhd,hde->qhe", query_feat, mem_m, precision=highest)
@@ -99,11 +114,25 @@
         .reshape(seg, width)
     )
 
-    outgoing = jnp.take(combined, pslot, axis=0, mode="clip").reshape(n, cap, width)
-    incoming = lax.all_to_all(outgoing, "ctx", 0, 0, tiled=True).reshape(slots, width)
-    rows = jnp.take(incoming, send_slot, axis=0, mode="clip")
-    gathered = lax.all_gather(rows, "head", axis=1, tiled=True)
-    summed = jnp.dot(gathered, out_weight, preferred_element_type=f32)
+    head_count = lax.axis_size("head")
+    out_cols = out_weight.shape[1]
+    halves = 2
+    half = width // halves
+    weight_parts = out_weight.reshape(head_count, halves, half, out_cols)
+    summed = None
+    for p in range(halves):
+        outgoing = jnp.take(
+            combined[:, p * half:(p + 1) * half], pslot, axis=0, mode="clip"
+        ).reshape(n, cap, half)
+        incoming = lax.all_to_all(outgoing, "ctx", 0, 0, tiled=True).reshape(slots, half)
+        rows = jnp.take(incoming, send_slot, axis=0, mode="clip")
+        gathered = lax.all_gather(rows, "head", axis=1, tiled=True)
+        part = jnp.dot(
+            gathered,
+            weight_parts[:, p].reshape(head_count * half, out_cols),
+            preferred_element_type=f32,
+        )
+        summed = part if summed is None else summed + part
     return summed.astype(bf16)
 
 

time: 437 us -> 443 us (1.014)
  waiting for transfers between devices: 210 us -> 150 us
  local copies, waits for them, and re-layouts: 63.9 us -> 99.5 us
  blocking collectives: 0 us -> 26.7 us
  matrix products: 67.9 us -> 80.3 us
  starting transfers between devices: 54.1 us -> 48 us
    all_gather x1 -> x2, waiting for transfers between devices: 83.1 us -> 44.3 us  [per_device(): gathered = lax.all_gather(rows, 'head', axis=1, tiled=True)]
    all_to_all x0 -> x1, blocking collectives: none -> 26.7 us  [per_device(): lax.all_to_all(outgoing, 'ctx', 0, 0, tiled=True).reshape(slots, half)]
    ppermute x5, waiting for transfers between devices: 33.1 us -> 13.4 us  [per_device(): got = lax.ppermute(total, 'ctx', perm)]
    all_to_all x1, waiting for transfers between devices: 39.7 us -> 22.7 us  [per_device(): lax.all_to_all(outgoing, 'ctx', 0, 0, tiled=True).reshape(slots, half)]
    slice x0 -> x8, local copies, waits for them, and re-layouts: none -> 15.9 us  [the longest x1 5.96 us: per_device(): weight_parts[:, p].reshape(head_count * half, out_cols)]
    all_to_all x3, waiting for transfers between devices: 54.1 us -> 69.9 us  [dispatch(): got = lax.all_to_all(buffer, 'ctx', 0, 0, tiled=True).reshape(slots, width)]
    sub x1 -> x3, matrix products: 13.4 us -> 23.2 us  [local_attention(): weights = jnp.exp(scores - row_max)]
    optimization_barrier x0 -> x8, local copies, waits for them, and re-layouts: none -> 7.28 us  [per_device(): lax.optimization_barrier((total, (query_heads[:, lo:hi], key_heads[:, lo:...]
  transfers between devices with their start and end apart: 10 -> 11, of which waited for: 7 -> 8; matrix products, arithmetic and copies ran while one was open for 21% -> 29% of each run, Pallas kernels for 0% -> 0%
where the time goes in v2:
time: 443 us; the launch traced here: 436 us
  waiting for transfers between devices  150 us (34%)
  local copies, waits for them, and re-layouts  99.5 us (22%)
  matrix products  80.3 us (18%)
  starting transfers between devices  48 us (11%)
  blocking collectives  26.7 us (6%)
  between operations  17.6 us (4%)
  other arithmetic  13.6 us (3%)
    all_to_all x3, waiting for transfers between devices, dispatch(): got = lax.all_to_all(buffer, 'ctx', 0, 0, tiled=True).reshape(slots, width)  69.9 us
    all_gather x2, waiting for transfers between devices, per_device(): gathered = lax.all_gather(rows, 'head', axis=1, tiled=True)  44.3 us
    all_to_all x1, blocking collectives, per_device(): lax.all_to_all(outgoing, 'ctx', 0, 0, tiled=True).reshape(slots, half)  26.7 us
    sub x3, matrix products, local_attention(): weights = jnp.exp(scores - row_max)  23.2 us
    ppermute x5, starting transfers between devices, per_device(): got = lax.ppermute(total, 'ctx', perm)  22.8 us
    all_to_all x1, waiting for transfers between devices, per_device(): lax.all_to_all(outgoing, 'ctx', 0, 0, tiled=True).reshape(slots, half)  22.7 us
    gather x3, local copies, waits for them, and re-layouts, dispatch(): return jnp.take(got, tok_slot, axis=0, mode='clip').reshape(seg, heads, dh)  22.2 us
    dot_general x2, matrix products, per_device(): jnp.dot(gathered, weight_parts[:, p].reshape(head_count * half, out_cols)...  20.5 us
  transfers between devices with their start and end apart: 11, of which 8 were waited for; matrix products, arithmetic and copies ran while one was open for 29% of the time, Pallas kernels for 0%

profile of v2, /device:TPU:1, one launch (start us, length us, event | category | flops | bytes accessed | tf_op | source)
XLA Modules:
  0.0 436.1 jit_solution(7300121392805873844)
XLA Ops:
  11.6 5.8 %gather_fusion.2 = bf16[1536,1024]{1,0:T(8,128)(2,1)} fusion(bf16[1024,1024]{1,0:T(8,128)(2,1)S(1)} %copy-done, s32[2048]{0:T(1024)S(1)} %get-tuple-element.100), kind=kCustom, calls=%fused_computation.2 | custom fusion | bytes 6297600 | tf_op jit(solution)/shard_map/jit(_take)/gather | solution.py:51
  17.4 8.8 %all-to-all-start.1 = ((bf16[32,48,1024]{2,1,0:T(8,128)(2,1)}), bf16[32,48,1024]{2,1,0:T(8,128)(2,1)}, u32[]{:S(2)}, u32[]{:S(2)}) async-start(bf16[32,48,1024]{2,1,0:T(8,128)(2,1)} %bitcast.156), calls=%async_computation.1 | async-start | bytes 6291456 | tf_op jit(solution)/shard_map/all_to_all | solution.py:52
  26.2 5.8 %gather_fusion = bf16[1536,1024]{1,0:T(8,128)(2,1)} fusion(bf16[1024,1024]{1,0:T(8,128)(2,1)S(1)} %copy-done.2, s32[2048]{0:T(1024)S(1)} %get-tuple-element.100), kind=kCustom, calls=%fused_computation | custom fusion | bytes 6297600 | tf_op jit(solution)/shard_map/jit(_take)/gather | solution.py:51
  32.0 34.0 %all-to-all-done.1 = bf16[32,48,1024]{2,1,0:T(8,128)(2,1)} async-done(((bf16[32,48,1024]{2,1,0:T(8,128)(2,1)}), bf16[32,48,1024]{2,1,0:T(8,128)(2,1)}, u32[]{:S(2)}, u32[]{:S(2)}) %all-to-all-start.1) | async-done | bytes 3145760 | tf_op jit(solution)/shard_map/all_to_all | solution.py:52
  66.0 5.0 %all-to-all-start = ((bf16[32,48,1024]{2,1,0:T(8,128)(2,1)}), bf16[32,48,1024]{2,1,0:T(8,128)(2,1)}, u32[]{:S(2)}, u32[]{:S(2)}) async-start(bf16[32,48,1024]{2,1,0:T(8,128)(2,1)} %bitcast.155), calls=%async_computation | async-start | bytes 6291456 | tf_op jit(solution)/shard_map/all_to_all | solution.py:52
  71.0 5.8 %gather_fusion.4 = bf16[1536,1024]{1,0:T(8,128)(2,1)} fusion(bf16[1024,1024]{1,0:T(8,128)(2,1)S(1)} %copy-done.3, s32[2048]{0:T(1024)S(1)} %get-tuple-element.100), kind=kCustom, calls=%fused_computation.4 | custom fusion | bytes 6297600 | tf_op jit(solution)/shard_map/jit(_take)/gather | solution.py:51
  76.8 34.0 %all-to-all-done = bf16[32,48,1024]{2,1,0:T(8,128)(2,1)} async-done(((bf16[32,48,1024]{2,1,0:T(8,128)(2,1)}), bf16[32,48,1024]{2,1,0:T(8,128)(2,1)}, u32[]{:S(2)}, u32[]{:S(2)}) %all-to-all-start) | async-done | bytes 3145760 | tf_op jit(solution)/shard_map/all_to_all | solution.py:52
  110.8 5.3 %all-to-all-start.2 = ((bf16[32,48,1024]{2,1,0:T(8,128)(2,1)}), bf16[32,48,1024]{2,1,0:T(8,128)(2,1)S(1)}, u32[]{:S(2)}, u32[]{:S(2)}) async-start(bf16[32,48,1024]{2,1,0:T(8,128)(2,1)} %bitcast.154), calls=%async_computation.2 | async-start | bytes 6291456 | tf_op jit(solution)/shard_map/all_to_all | solution.py:52
  124.3 8.3 %gather_fusion.3 = bf16[1024,1024]{1,0:T(8,128)(2,1)} fusion(bf16[1536,1024]{1,0:T(8,128)(2,1)} %bitcast.6, s32[1024]{0:T(1024)S(1)} %broadcast_clamp_fusion.1), kind=kCustom, calls=%fused_computation.3 | custom fusion | bytes 4198400 | tf_op jit(solution)/shard_map/jit(_take)/gather | solution.py:53
  132.6 8.3 %gather_fusion.1 = bf16[1024,1024]{1,0:T(8,128)(2,1)} fusion(bf16[1536,1024]{1,0:T(8,128)(2,1)} %bitcast.4, s32[1024]{0:T(1024)S(1)} %broadcast_clamp_fusion.1), kind=kCustom, calls=%fused_computation.1 | custom fusion | bytes 4198400 | tf_op jit(solution)/shard_map/jit(_take)/gather | solution.py:53
  141.0 3.5 copy_bitcast_fusion.2
  146.2 1.9 fusion.14
  148.1 5.8 %fusion.10 = f32[8,128,128]{2,1,0:T(8,128)} fusion(bf16[1024,1024]{1,0:T(8,128)(2,1)S(1)} %copy-done.4, bf16[1024,1024]{1,0:T(8,128)(2,1)S(1)} %copy-done.6), kind=kOutput, calls=%fused_computation.41 | convolution fusion | flops 1615855616 | bytes 4718592 | tf_op jit(solution)/shard_map/khd,khe->hde/dot_general | solution.py:60
  153.8 1.9 all-to-all-done.2
  155.7 5.5 %gather_fusion.5 = bf16[1024,1024]{1,0:T(8,128)(2,1)} fusion(bf16[1536,1024]{1,0:T(8,128)(2,1)S(1)} %bitcast.150, s32[1024]{0:T(1024)S(1)} %broadcast_clamp_fusion.1), kind=kCustom, calls=%fused_computation.5 | custom fusion | bytes 4198400 | tf_op jit(solution)/shard_map/jit(_take)/gather | solution.py:53
  161.3 2.1 copy_bitcast_fusion
  167.2 2.1 fusion.109
  171.4 3.2 collective-permute-start
  174.6 8.0 %fusion.115 = (f32[2,1024]{1,0:T(2,128)S(1)}, f32[2,1024,1024]{1,2,0:T(8,128)}) fusion(pred[1024,1024]{0,1:T(8,128)(4,1)} %iota_compare_fusion.3, bf16[1024,2,128]{2,0,1:T(8,128)(2,1)} %get-tuple-element.37, bf16[1024,2,128]{2,0,1:T(8,128)(2,1)} %get-tuple-element.38), kind=kOutput, calls=%fused_computation.196 | convolution fusion | flops 545260544 | bytes 10493952 | tf_op jit(solution)/shard_map/sub | solution.py:76
  182.6 5.3 %fusion.52 = f32[1024,2,128]{0,2,1:T(8,128)} fusion(bf16[1024,2,128]{0,2,1:T(8,128)(2,1)} %copy.129, f32[2,1024,1024]{1,2,0:T(8,128)} %get-tuple-element.90, f32[2,1024]{1,0:T(2,128)S(1)} %get-tuple-element.89), kind=kOutput, calls=%fused_computation.93 | convolution fusion | flops 541065216 | bytes 9969664 | tf_op jit(solution)/shard_map/hqk,khd->qhd/dot_general | solution.py:78
  187.8 1.9 fusion.114
  189.7 2.0 copy.130
  191.7 2.0 copy.131
  194.5 1.8 fusion.112
  197.5 1.9 collective-permute-start.1
  203.4 7.2 %collective-permute-done.1 = f32[8,129,128]{2,0,1:T(8,128)S(1)} collective-permute-done((f32[8,129,128]{2,0,1:T(8,128)S(1)}, f32[8,129,128]{2,0,1:T(8,128)S(1)}, u32[]{:S(2)}, u32[]{:S(2)}) %collective-permute-start.1) | collective-permute-done | bytes 528416 | tf_op jit(solution)/shard_map/ppermute | solution.py:96
  211.6 6.6 %collective-permute-start.2 = (f32[8,129,128]{2,0,1:T(8,128)}, f32[8,129,128]{2,0,1:T(8,128)}, u32[]{:S(2)}, u32[]{:S(2)}) collective-permute-start(f32[8,129,128]{2,0,1:T(8,128)} %copy.104), channel_id=1, source_target_pairs={{0,16},{4,20},{8,24},{12,28},{16,32},{20,36},{24,40},{28,44},{32,4... | collective-permute-start | bytes 1585160 | tf_op jit(solution)/shard_map/ppermute | solution.py:96
  218.3 7.6 %fusion.116 = (f32[2,1024]{1,0:T(2,128)S(1)}, f32[2,1024,1024]{1,2,0:T(8,128)}) fusion(pred[1024,1024]{0,1:T(8,128)(4,1)S(1)} %copy-done.11, bf16[1024,2,128]{2,0,1:T(8,128)(2,1)} %get-tuple-element.47, bf16[1024,2,128]{2,0,1:T(8,128)(2,1)} %get-tuple-element.48), kind=kOutput, calls=%fused_computation.197 | convolution fusion | flops 545260544 | bytes 10493952 | tf_op jit(solution)/shard_map/sub | solution.py:76
  225.9 4.4 fusion.51
  232.4 4.2 collective-permute-start.3
  240.5 6.2 %collective-permute-done.3 = f32[8,129,128]{2,0,1:T(8,128)S(1)} collective-permute-done((f32[8,129,128]{2,0,1:T(8,128)S(1)}, f32[8,129,128]{2,0,1:T(8,128)S(1)}, u32[]{:S(2)}, u32[]{:S(2)}) %collective-permute-start.3) | collective-permute-done | bytes 528416 | tf_op jit(solution)/shard_map/ppermute | solution.py:96
  247.0 7.0 %collective-permute-start.4 = (f32[8,129,128]{2,0,1:T(8,128)S(1)}, f32[8,129,128]{2,0,1:T(8,128)}, u32[]{:S(2)}, u32[]{:S(2)}) collective-permute-start(f32[8,129,128]{2,0,1:T(8,128)S(1)} %copy.115), channel_id=1, source_target_pairs={{0,64},{4,68},{8,72},{12,76},{16,80},{20,84},{24,88},{28,92},{32,9... | collective-permute-start | bytes 1585160 | tf_op jit(solution)/shard_map/ppermute | solution.py:96
  253.9 7.6 %fusion.117 = (f32[2,1024]{1,0:T(2,128)S(1)}, f32[2,1024,1024]{1,2,0:T(8,128)}) fusion(pred[1024,1024]{0,1:T(8,128)(4,1)S(1)} %copy-done.11, bf16[1024,2,128]{2,0,1:T(8,128)(2,1)} %get-tuple-element.57, bf16[1024,2,128]{2,0,1:T(8,128)(2,1)} %get-tuple-element.58), kind=kOutput, calls=%fused_computation.198 | convolution fusion | flops 545260544 | bytes 10493952 | tf_op jit(solution)/shard_map/sub | solution.py:76
  261.6 4.4 %fusion.50 = f32[1024,2,128]{0,2,1:T(8,128)S(1)} fusion(bf16[1024,2,128]{0,2,1:T(8,128)(2,1)} %copy.131, f32[2,1024,1024]{1,2,0:T(8,128)} %get-tuple-element.98, f32[2,1024]{1,0:T(2,128)S(1)} %get-tuple-element.97), kind=kOutput, calls=%fused_computation.91 | convolution fusion | flops 541065216 | bytes 9969664 | tf_op jit(solution)/shard_map/hqk,khd->qhd/dot_general | solution.py:78
  267.7 4.9 %fusion.34 = f32[8,1,1024]{2,1,0:T(1,128)S(1)} fusion(f32[8,129,128]{2,1,0:T(8,128)S(1)} %fusion.67, bf16[1024,1024]{1,0:T(8,128)(2,1)S(1)} %copy-done.7), kind=kOutput, calls=%fused_computation.74 | convolution fusion | flops 17825792 | bytes 2134016 | tf_op jit(solution)/shard_map/qhd,hd->qh/dot_general | solution.py:108
  272.8 6.3 %fusion.19 = bf16[1024,8,128]{0,2,1:T(8,128)(2,1)S(1)} fusion(f32[1024,8,128]{0,2,1:T(8,128)S(1)} %constant_dynamic-update-slice_fusion, f32[8]{0:T(128)S(1)} %get-tuple-element.65, f32[1024,8]{0,1:T(8,128)S(1)} %fusion.86, f32[8]{0:T(128)S(1)} %get-tuple-element.66, f32[8,129,128]{2,1,0:T(8,128)S(1)} %fusion.67, bf16[1024,1024]{1,0:T(8,128)(2,1)S(1)} %copy-done.7), kind=kOutput, calls=%fused_computation.50 | convolution fusion | flops 1621098496 | bytes 8946688 | tf_op jit(solution)/shard_map/qhd,hde->qhe/dot_general | solution.py:107
  281.7 5.4 %gather_fusion.6 = bf16[1536,512]{1,0:T(8,128)(2,1)} fusion(bf16[1024,512]{1,0:T(8,128)(2,1)S(1)} %copy.132, s32[2048]{0:T(1024)S(1)} %get-tuple-element.99), kind=kCustom, calls=%fused_computation.6 | custom fusion | bytes 3151872 | tf_op jit(solution)/shard_map/jit(_take)/gather | solution.py:124
  287.1 6.0 %all-to-all-start.3 = ((bf16[32,48,512]{2,1,0:T(8,128)(2,1)}), bf16[32,48,512]{2,1,0:T(8,128)(2,1)S(1)}, u32[]{:S(2)}, u32[]{:S(2)}) async-start(bf16[32,48,512]{2,1,0:T(8,128)(2,1)} %bitcast.31), calls=%async_computation.3 | async-start | bytes 3145728 | tf_op jit(solution)/shard_map/all_to_all | solution.py:127
  293.2 22.7 %all-to-all-done.3 = bf16[32,48,512]{2,1,0:T(8,128)(2,1)S(1)} async-done(((bf16[32,48,512]{2,1,0:T(8,128)(2,1)}), bf16[32,48,512]{2,1,0:T(8,128)(2,1)S(1)}, u32[]{:S(2)}, u32[]{:S(2)}) %all-to-all-start.3) | async-done | bytes 1572896 | tf_op jit(solution)/shard_map/all_to_all | solution.py:127
  315.9 5.1 %gather_fusion.7 = bf16[1024,512]{1,0:T(8,128)(2,1)} fusion(bf16[1536,512]{1,0:T(8,128)(2,1)S(1)} %bitcast.151, s32[1024]{0:T(1024)S(1)} %broadcast_clamp_fusion), kind=kCustom, calls=%fused_computation.7 | custom fusion | bytes 2101248 | tf_op jit(solution)/shard_map/jit(_take)/gather | solution.py:128
  321.6 4.8 %gather_fusion.8 = bf16[1536,512]{1,0:T(8,128)(2,1)S(1)} fusion(bf16[1024,512]{1,0:T(8,128)(2,1)S(1)} %copy.133, s32[2048]{0:T(1024)S(1)} %get-tuple-element.99), kind=kCustom, calls=%fused_computation.8 | custom fusion | bytes 3151872 | tf_op jit(solution)/shard_map/jit(_take)/gather | solution.py:124
  326.4 26.7 %all_to_all.25 = bf16[32,48,512]{2,1,0:T(8,128)(2,1)S(1)} all-to-all(bf16[32,48,512]{2,1,0:T(8,128)(2,1)S(1)} %bitcast.159), channel_id=1, replica_groups=mesh['ctx'=32,'head'=4] {'ctx'}, dimensions={0} | all-to-all | bytes 3145728 | tf_op jit(solution)/shard_map/all_to_all | solution.py:127
  353.2 5.1 %gather_fusion.9 = bf16[1024,512]{1,0:T(8,128)(2,1)} fusion(bf16[1536,512]{1,0:T(8,128)(2,1)S(1)} %bitcast.152, s32[1024]{0:T(1024)S(1)} %broadcast_clamp_fusion), kind=kCustom, calls=%fused_computation.9 | custom fusion | bytes 2101248 | tf_op jit(solution)/shard_map/jit(_take)/gather | solution.py:128
  358.3 6.0 %fusion.107 = (bf16[4,1,512,1024]{3,2,1,0:T(8,128)(2,1)}, bf16[4,1,512,1024]{3,2,1,0:T(8,128)(2,1)}) fusion(bf16[4,2,512,1024]{3,2,1,0:T(8,128)(2,1)} %bitcast.157), kind=kLoop, calls=%fused_computation.188 | loop fusion | bytes 16777216 | tf_op jit(solution)/shard_map/slice | solution.py:132
  364.2 3.8 all-gather.5.cloned.1.call-done
  368.1 9.9 %fusion.118 = f32[1024,1024]{1,0:T(8,128)} fusion(bf16[1024,2048]{1,0:T(8,128)(2,1)} %all-gather.5.cloned.1.call-done, bf16[2048,1024]{1,0:T(8,128)(2,1)} %bitcast.161), kind=kOutput, calls=%fused_computation.199 | convolution fusion | flops 4294967296 | bytes 12582912 | tf_op jit(solution)/shard_map/dot_general | solution.py:130
  377.9 40.5 %all-gather.7.cloned.1.call-done = bf16[1024,2048]{1,0:T(8,128)(2,1)} async-done(((bf16[1024,512]{1,0:T(8,128)(2,1)}), bf16[1024,2048]{1,0:T(8,128)(2,1)}) %all-gather.7.cloned.1.call-update) | async-done | bytes 4194320 | tf_op jit(solution)/shard_map/all_gather | solution.py:129
  418.4 10.6 %add_convert_fusion = bf16[1024,1024]{1,0:T(8,128)(2,1)} fusion(f32[1024,1024]{1,0:T(8,128)} %fusion.118, bf16[1024,2048]{1,0:T(8,128)(2,1)} %all-gather.7.cloned.1.call-done, bf16[2048,1024]{1,0:T(8,128)(2,1)} %bitcast.160), kind=kOutput, calls=%fused_computation.51 | convolution fusion | flops 4297064448 | bytes 14680064 | tf_op jit(solution)/shard_map/dot_general | solution.py:130
  (106 shorter events, 35.7 us)
Async XLA Ops:
  6.5 5.0 %copy-start = (bf16[1024,1024]{1,0:T(8,128)(2,1)S(1)}, bf16[1024,1024]{1,0:T(8,128)(2,1)}, u32[]{:S(2)}) copy-start(bf16[1024,1024]{1,0:T(8,128)(2,1)} %param.9) | copy-start | bytes 6291460
  17.4 8.8 %copy-start.2 = (bf16[1024,1024]{1,0:T(8,128)(2,1)S(1)}, bf16[1024,1024]{1,0:T(8,128)(2,1)}, u32[]{:S(2)}) copy-start(bf16[1024,1024]{1,0:T(8,128)(2,1)} %param.8) | copy-start | bytes 6291460
  17.4 48.6 %all-to-all-start.1 = ((bf16[32,48,1024]{2,1,0:T(8,128)(2,1)}), bf16[32,48,1024]{2,1,0:T(8,128)(2,1)}, u32[]{:S(2)}, u32[]{:S(2)}) async-start(bf16[32,48,1024]{2,1,0:T(8,128)(2,1)} %bitcast.156), calls=%async_computation.1 | async-start | bytes 6291456 | tf_op jit(solution)/shard_map/all_to_all | solution.py:52
  32.0 39.0 %copy-start.3 = (bf16[1024,1024]{1,0:T(8,128)(2,1)S(1)}, bf16[1024,1024]{1,0:T(8,128)(2,1)}, u32[]{:S(2)}) copy-start(bf16[1024,1024]{1,0:T(8,128)(2,1)} %param.7) | copy-start | bytes 6291460
  66.0 44.9 %all-to-all-start = ((bf16[32,48,1024]{2,1,0:T(8,128)(2,1)}), bf16[32,48,1024]{2,1,0:T(8,128)(2,1)}, u32[]{:S(2)}, u32[]{:S(2)}) async-start(bf16[32,48,1024]{2,1,0:T(8,128)(2,1)} %bitcast.155), calls=%async_computation | async-start | bytes 6291456 | tf_op jit(solution)/shard_map/all_to_all | solution.py:52
  76.8 39.4 %copy-start.20 = (s32[32]{0:T(128)S(1)}, s32[32]{0:T(128)}, u32[]{:S(2)}) copy-start(s32[32]{0:T(128)} %param.11) | copy-start | bytes 388
  76.8 46.2 %copy-start.21 = (f32[8]{0:T(128)S(1)}, f32[8]{0:T(128)}, u32[]{:S(2)}) copy-start(f32[8]{0:T(128)} %param.12) | copy-start | bytes 100
  110.8 44.9 %all-to-all-start.2 = ((bf16[32,48,1024]{2,1,0:T(8,128)(2,1)}), bf16[32,48,1024]{2,1,0:T(8,128)(2,1)S(1)}, u32[]{:S(2)}, u32[]{:S(2)}) async-start(bf16[32,48,1024]{2,1,0:T(8,128)(2,1)} %bitcast.154), calls=%async_computation.2 | async-start | bytes 6291456 | tf_op jit(solution)/shard_map/all_to_all | solution.py:52
  141.0 3.5 copy-start.4
  141.0 5.2 %copy-start.6 = (bf16[1024,1024]{1,0:T(8,128)(2,1)S(1)}, bf16[1024,1024]{1,0:T(8,128)(2,1)}, u32[]{:S(2)}) copy-start(bf16[1024,1024]{1,0:T(8,128)(2,1)} %gather_fusion.1) | copy-start | bytes 6291460
  161.3 3.3 copy-start.8
  163.4 3.8 copy-start.9
  163.4 3.2 copy-start.5
  166.6 3.9 copy-start.10
  171.4 24.9 %collective-permute-start = (f32[8,129,128]{2,0,1:T(8,128)}, f32[8,129,128]{2,0,1:T(8,128)}, u32[]{:S(2)}, u32[]{:S(2)}) collective-permute-start(f32[8,129,128]{2,0,1:T(8,128)} %copy.93), channel_id=1, source_target_pairs={{0,4},{4,8},{8,12},{12,16},{16,20},{20,24},{24,28},{28,32},{32,36}... | collective-permute-start | bytes 1585160 | tf_op jit(solution)/shard_map/ppermute | solution.py:96
  193.7 5.7 %copy-start.12 = (f32[1024,2,128]{0,2,1:T(8,128)S(1)}, f32[1024,2,128]{0,2,1:T(8,128)}, u32[]{:S(2)}) copy-start(f32[1024,2,128]{0,2,1:T(8,128)} %fusion.52) | copy-start | bytes 3145732
  193.7 6.9 %copy-start.19 = (bf16[1024,1,128]{2,0,1:T(8,128)(2,1)S(1)}, bf16[1024,1,128]{2,0,1:T(8,128)(2,1)}, u32[]{:S(2)}) copy-start(bf16[1024,1,128]{2,0,1:T(8,128)(2,1)} %get-tuple-element.42) | copy-start | bytes 786436
  197.5 13.1 %collective-permute-start.1 = (f32[8,129,128]{2,0,1:T(8,128)S(1)}, f32[8,129,128]{2,0,1:T(8,128)S(1)}, u32[]{:S(2)}, u32[]{:S(2)}) collective-permute-start(f32[8,129,128]{2,0,1:T(8,128)S(1)} %copy.99), channel_id=1, source_target_pairs={{0,8},{4,12},{8,16},{12,20},{16,24},{20,28},{24,32},{28,36},{32,40... | collective-permute-start | bytes 1585160 | tf_op jit(solution)/shard_map/ppermute | solution.py:96
  201.9 16.4 %copy-start.11 = (pred[1024,1024]{0,1:T(8,128)(4,1)S(1)}, pred[1024,1024]{0,1:T(8,128)(4,1)}, u32[]{:S(2)}) copy-start(pred[1024,1024]{0,1:T(8,128)(4,1)} %iota_compare_fusion.3) | copy-start | bytes 3145732
  211.6 19.5 %collective-permute-start.2 = (f32[8,129,128]{2,0,1:T(8,128)}, f32[8,129,128]{2,0,1:T(8,128)}, u32[]{:S(2)}, u32[]{:S(2)}) collective-permute-start(f32[8,129,128]{2,0,1:T(8,128)} %copy.104), channel_id=1, source_target_pairs={{0,16},{4,20},{8,24},{12,28},{16,32},{20,36},{24,40},{28,44},{32,4... | collective-permute-start | bytes 1585160 | tf_op jit(solution)/shard_map/ppermute | solution.py:96
  225.9 4.4 %copy-start.14 = (f32[1024,1,128]{0,2,1:T(8,128)S(1)}, f32[1024,1,128]{0,2,1:T(8,128)}, u32[]{:S(2)}) copy-start(f32[1024,1,128]{0,2,1:T(8,128)} %fusion.54) | copy-start | bytes 1572868
  225.9 10.7 %copy-start.16 = (bf16[1024,1,128]{2,0,1:T(8,128)(2,1)S(1)}, bf16[1024,1,128]{2,0,1:T(8,128)(2,1)}, u32[]{:S(2)}) copy-start(bf16[1024,1,128]{2,0,1:T(8,128)(2,1)} %get-tuple-element.52) | copy-start | bytes 786436
  225.9 10.7 %copy-start.18 = (bf16[1024,1,128]{2,0,1:T(8,128)(2,1)S(1)}, bf16[1024,1,128]{2,0,1:T(8,128)(2,1)}, u32[]{:S(2)}) copy-start(bf16[1024,1,128]{2,0,1:T(8,128)(2,1)} %get-tuple-element.53) | copy-start | bytes 786436
  232.4 14.3 %collective-permute-start.3 = (f32[8,129,128]{2,0,1:T(8,128)S(1)}, f32[8,129,128]{2,0,1:T(8,128)S(1)}, u32[]{:S(2)}, u32[]{:S(2)}) collective-permute-start(f32[8,129,128]{2,0,1:T(8,128)S(1)} %copy.110), channel_id=1, source_target_pairs={{0,32},{4,36},{8,40},{12,44},{16,48},{20,52},{24,56},{28,60},{32,6... | collective-permute-start | bytes 1585160 | tf_op jit(solution)/shard_map/ppermute | solution.py:96
  237.3 1.6 copy-start.17
  247.0 19.6 %collective-permute-start.4 = (f32[8,129,128]{2,0,1:T(8,128)S(1)}, f32[8,129,128]{2,0,1:T(8,128)}, u32[]{:S(2)}, u32[]{:S(2)}) collective-permute-start(f32[8,129,128]{2,0,1:T(8,128)S(1)} %copy.115), channel_id=1, source_target_pairs={{0,64},{4,68},{8,72},{12,76},{16,80},{20,84},{24,88},{28,92},{32,9... | collective-permute-start | bytes 1585160 | tf_op jit(solution)/shard_map/ppermute | solution.py:96
  261.6 4.4 %copy-start.13 = (f32[1024,1,128]{0,2,1:T(8,128)S(1)}, f32[1024,1,128]{0,2,1:T(8,128)}, u32[]{:S(2)}) copy-start(f32[1024,1,128]{0,2,1:T(8,128)} %fusion.53) | copy-start | bytes 1572868
  261.6 4.9 %copy-start.15 = (f32[1024,8,128]{0,2,1:T(8,128)S(1)}, f32[1024,8,128]{0,2,1:T(8,128)}, u32[]{:S(2)}) copy-start(f32[1024,8,128]{0,2,1:T(8,128)} %constant_dynamic-update-slice_fusion.2) | copy-start | bytes 12582916
  261.6 6.2 %copy-start.7 = (bf16[1024,1024]{1,0:T(8,128)(2,1)S(1)}, bf16[1024,1024]{1,0:T(8,128)(2,1)}, u32[]{:S(2)}) copy-start(bf16[1024,1024]{1,0:T(8,128)(2,1)} %gather_fusion.5) | copy-start | bytes 6291460
  287.1 28.8 %all-to-all-start.3 = ((bf16[32,48,512]{2,1,0:T(8,128)(2,1)}), bf16[32,48,512]{2,1,0:T(8,128)(2,1)S(1)}, u32[]{:S(2)}, u32[]{:S(2)}) async-start(bf16[32,48,512]{2,1,0:T(8,128)(2,1)} %bitcast.31), calls=%async_computation.3 | async-start | bytes 3145728 | tf_op jit(solution)/shard_map/all_to_all | solution.py:127
  293.1 74.9 %all-gather.5.cloned.1.call-start = ((), (), s32[]{:S(2)}) async-start(), calls=%async_computation.5 | async-start | bytes 5242880 | tf_op jit(solution)/shard_map/all_gather | solution.py:129
  321.0 97.4 %all-gather.7.cloned.1.call-start = ((), (), s32[]{:S(2)}) async-start(), calls=%async_computation.6 | async-start | bytes 5242880 | tf_op jit(solution)/shard_map/all_gather | solution.py:129
  418.4 10.6 %copy-start.1 = (bf16[1024,1024]{1,0:T(8,128)(2,1)S(1)}, bf16[1024,1024]{1,0:T(8,128)(2,1)}, u32[]{:S(2)}) copy-start(bf16[1024,1024]{1,0:T(8,128)(2,1)} %param.9) | copy-start | bytes 6291460
Sparse Core Ops, SparseCore 0:
  321.1 46.8 all-gather.4
  369.7 48.6 all-gather.6

commit v3 on v2

v3 whole, which is shorter than its diff:
```python
import jax
import jax.numpy as jnp
from jax import lax
from jax.sharding import PartitionSpec as P


def feature(inputs):
    return jax.nn.elu(inputs) + 1.0


def per_device(queries, keys, values, row_target, seg_doc, mem_gate, out_weight):
    highest = lax.Precision.HIGHEST
    f32, bf16 = jnp.float32, jnp.bfloat16
    n = lax.axis_size("ctx")
    me = lax.axis_index("ctx")
    seg, width = queries.shape
    heads = mem_gate.shape[0]
    dh = width // heads
    cap = seg // n + (seg // n) // 2
    slots = n * cap

    targets = row_target.reshape(n, seg)
    r_idx = jnp.arange(seg, dtype=jnp.int32)
    o_idx = jnp.arange(n, dtype=jnp.int32)
    s_idx = jnp.arange(slots, dtype=jnp.int32)
    w_idx = jnp.arange(cap, dtype=jnp.int32)
    lower = (r_idx[None, :] < r_idx[:, None]).astype(bf16)

    mine = lax.dynamic_index_in_dim(targets, me, 0, keepdims=False)
    owner = mine // seg
    match = (owner[:, None] == o_idx[None, :]).astype(bf16)
    before = jnp.dot(lower, match, preferred_element_type=f32)
    within = jnp.sum(jnp.where(match > 0, before, 0.0), axis=1).astype(jnp.int32)
    send_slot = owner * cap + within
    slot_row = jnp.sum(
        jnp.where(send_slot[None, :] == s_idx[:, None], r_idx[None, :], 0), axis=1
    )

    arrived = (targets // seg) == me
    rank = jnp.dot(arrived.astype(bf16), lower.T, preferred_element_type=f32).astype(jnp.int32)
    hit = arrived[:, None, :] & (rank[:, None, :] == w_idx[None, :, None])
    pslot = jnp.sum(jnp.where(hit, (targets % seg)[:, None, :], 0), axis=2).reshape(slots)
    count = jnp.sum(arrived.astype(jnp.int32), axis=1)
    valid = (w_idx[None, :] < count[:, None]).reshape(slots)
    tok_slot = jnp.sum(
        jnp.where((pslot[None, :] == r_idx[:, None]) & valid[None, :], s_idx[None, :], 0),
        axis=1,
    )

    doc = seg_doc[me]
    start = jnp.min(jnp.where(seg_doc == doc, o_idx, n))
    score_scale = dh ** (-0.5)
    causal = r_idx[:, None] >= r_idx[None, :]
    head_count = lax.axis_size("head")
    out_cols = out_weight.shape[1]
    groups = 2
    group_heads = heads // groups
    group_width = width // groups
    weight_parts = out_weight.reshape(head_count, groups, group_width, out_cols)
    gate_all = jax.nn.sigmoid(mem_gate)
    shifts = []
    step = 1
    while step < n:
        shifts.append(step)
        step *= 2
    cuts = [round(group_heads * i / len(shifts)) for i in range(len(shifts) + 1)]

    def dispatch(source, g):
        columns = source[:, g * group_width:(g + 1) * group_width]
        buffer = jnp.take(columns, slot_row, axis=0, mode="clip").reshape(n, cap, group_width)
        got = lax.all_to_all(buffer, "ctx", 0, 0, tiled=True).reshape(slots, group_width)
        return jnp.take(got, tok_slot, axis=0, mode="clip").reshape(seg, group_heads, dh)

    def local_attention(query_part, key_part, value_part):
        scores = jnp.einsum(
            "qhd,khd->hqk", query_part, key_part, preferred_element_type=f32
        ) * score_scale
        scores = jnp.where(causal[None], scores, -1e30)
        row_max = jnp.max(scores, axis=-1, keepdims=True)
        weights = jnp.exp(scores - row_max)
        probabilities = (weights / jnp.sum(weights, axis=-1, keepdims=True)).astype(bf16)
        return jnp.einsum(
            "hqk,khd->qhd", probabilities, value_part, preferred_element_type=f32
        )

    def one_group(g):
        key_heads = dispatch(keys, g)
        value_heads = dispatch(values, g)
        query_heads = dispatch(queries, g)

        key_feat = feature(key_heads.astype(f32))
        delta_m = jnp.einsum(
            "khd,khe->hde", key_feat, value_heads.astype(f32), precision=highest
        )
        delta_z = jnp.sum(key_feat, axis=0)
        delta = jnp.concatenate([delta_m, delta_z[:, None, :]], axis=1)

        pieces = []
        total = delta
        for k, step in enumerate(shifts):
            lo, hi = cuts[k], cuts[k + 1]
            total, operands = lax.optimization_barrier(
                (total, (query_heads[:, lo:hi], key_heads[:, lo:hi], value_heads[:, lo:hi]))
            )
            perm = [(j, j + step) for j in range(n - step)]
            got = lax.ppermute(total, "ctx", perm)
            if hi > lo:
                piece = local_attention(*operands)
                got, piece = lax.optimization_barrier((got, piece))
                pieces.append(piece)
            total = total + jnp.where(me - step >= start, got, jnp.zeros_like(got))
        local_out = jnp.concatenate(pieces, axis=1)
        memory = total - delta
        mem_m = memory[:, :dh, :]
        mem_z = memory[:, dh, :]

        query_feat = feature(query_heads.astype(f32))
        numerator = jnp.einsum("qhd,hde->qhe", query_feat, mem_m, precision=highest)
        denominator = jnp.einsum("qhd,hd->qh", query_feat, mem_z, precision=highest)
        recalled = numerator / jnp.maximum(denominator, 1.0)[..., None]
        gate_value = gate_all[g * group_heads:(g + 1) * group_heads][None, :, None]
        combined = (
            (gate_value * recalled + (1.0 - gate_value) * local_out)
            .astype(bf16)
            .reshape(seg, group_width)
        )

        outgoing = jnp.take(combined, pslot, axis=0, mode="clip").reshape(n, cap, group_width)
        incoming = lax.all_to_all(outgoing, "ctx", 0, 0, tiled=True).reshape(slots, group_width)
        rows = jnp.take(incoming, send_slot, axis=0, mode="clip")
        gathered = lax.all_gather(rows, "head", axis=1, tiled=True)
        return jnp.dot(
            gathered,
            weight_parts[:, g].reshape(head_count * group_width, out_cols),
            preferred_element_type=f32,
        )

    summed = one_group(0)
    for g in range(1, groups):
        summed = summed + one_group(g)
    return summed.astype(bf16)


def solution(mesh):
    return jax.shard_map(
        per_device,
        mesh=mesh,
        in_specs=(
            P("ctx", "head"),
            P("ctx", "head"),
            P("ctx", "head"),
            P(),
            P(),
            P("head"),
            P(None, "head"),
        ),
        out_specs=P("ctx", "head"),
        check_vma=False,
    )
```

time: 443 us -> 446 us (level)
  waiting for transfers between devices: 150 us -> 102 us
  starting transfers between devices: 48 us -> 92 us
  matrix products: 80.3 us -> 55.3 us
  local copies, waits for them, and re-layouts: 99.5 us -> 120 us
  other arithmetic: 13.6 us -> 20.1 us
  blocking collectives: 26.7 us -> 31.2 us
    all_to_all x4 -> x7, waiting for transfers between devices: 92.5 us -> 58.2 us  [the longest x6 45.5 us: dispatch(): lax.all_to_all(buffer, 'ctx', 0, 0, tiled=True).reshape(slots, group_width)]
    gather x10 -> x16, local copies, waits for them, and re-layouts: 60 us -> 89.7 us  [the longest x6 35.4 us: dispatch(): jnp.take(got, tok_slot, axis=0, mode='clip').reshape(seg, group_heads, dh)]
    all_to_all x4 -> x7, starting transfers between devices: 25.1 us -> 51.3 us  [the longest x6 39.3 us: dispatch(): lax.all_to_all(buffer, 'ctx', 0, 0, tiled=True).reshape(slots, group_width)]
    sub x3 -> x0, matrix products: 23.2 us -> none  [local_attention(): weights = jnp.exp(scores - row_max)]
    ppermute x5 -> x10, starting transfers between devices: 22.8 us -> 40.6 us  [one_group(): got = lax.ppermute(total, 'ctx', perm)]
    all_gather x2, waiting for transfers between devices: 44.3 us -> 30.3 us  [one_group(): gathered = lax.all_gather(rows, 'head', axis=1, tiled=True)]
    dot_general x5 -> x8, matrix products: 17.2 us -> 7.64 us  [local_attention(): jnp.einsum('hqk,khd->qhd', probabilities, value_part, preferred_element_t...]
    optimization_barrier x8 -> x0, local copies, waits for them, and re-layouts: 7.28 us -> none  [per_device(): lax.optimization_barrier((total, (query_heads[:, lo:hi], key_heads[:, lo:...]
  transfers between devices with their start and end apart: 11 -> 19, of which waited for: 8 -> 11; matrix products, arithmetic and copies ran while one was open for 29% -> 40% of each run, Pallas kernels for 0% -> 0%
where the time goes in v3:
time: 446 us; the launch traced here: 438 us
  local copies, waits for them, and re-layouts  120 us (27%)
  waiting for transfers between devices  102 us (23%)
  starting transfers between devices  92 us (21%)
  matrix products  55.3 us (12%)
  blocking collectives  31.2 us (7%)
  other arithmetic  20.1 us (5%)
  between operations  17.8 us (4%)
    all_to_all x6, waiting for transfers between devices, dispatch(): lax.all_to_all(buffer, 'ctx', 0, 0, tiled=True).reshape(slots, group_width)  45.5 us
    ppermute x10, starting transfers between devices, one_group(): got = lax.ppermute(total, 'ctx', perm)  40.6 us
    all_to_all x6, starting transfers between devices, dispatch(): lax.all_to_all(buffer, 'ctx', 0, 0, tiled=True).reshape(slots, group_width)  39.3 us
    gather x6, local copies, waits for them, and re-layouts, dispatch(): jnp.take(got, tok_slot, axis=0, mode='clip').reshape(seg, group_heads, dh)  35.4 us
    gather x6, local copies, waits for them, and re-layouts, dispatch(): jnp.take(columns, slot_row, axis=0, mode='clip')  33.9 us
    all_to_all x1, blocking collectives, one_group(): lax.all_to_all(outgoing, 'ctx', 0, 0, tiled=True)  31.2 us
    all_gather x2, waiting for transfers between devices, one_group(): gathered = lax.all_gather(rows, 'head', axis=1, tiled=True)  30.3 us
    dot_general x2, matrix products, one_group(): jnp.dot(gathered, weight_parts[:, g].reshape(head_count * group_width, ou...  21.1 us
  transfers between devices with their start and end apart: 19, of which 11 were waited for; matrix products, arithmetic and copies ran while one was open for 40% of the time, Pallas kernels for 0%

profile of v3, /device:TPU:1, one launch (start us, length us, event | category | flops | bytes accessed | tf_op | source)
XLA Modules:
  0.0 438.4 jit_solution(8863361947327172703)
XLA Ops:
  9.7 5.4 %gather_fusion = bf16[1536,512]{1,0:T(8,128)(2,1)} fusion(bf16[1024,512]{1,0:T(8,128)(2,1)S(1)} %get-tuple-element.114, s32[2048]{0:T(1024)S(1)} %pad_clamp_fusion.1), kind=kCustom, calls=%fused_computation | custom fusion | bytes 3151872 | tf_op jit(solution)/shard_map/jit(_take)/gather | solution.py:70
  15.1 8.6 %all-to-all-start = ((bf16[32,48,512]{2,1,0:T(8,128)(2,1)}), bf16[32,48,512]{2,1,0:T(8,128)(2,1)}, u32[]{:S(2)}, u32[]{:S(2)}) async-start(bf16[32,48,512]{2,1,0:T(8,128)(2,1)} %bitcast.300), calls=%async_computation | async-start | bytes 3145728 | tf_op jit(solution)/shard_map/all_to_all | solution.py:71
  25.4 5.4 %gather_fusion.2 = bf16[1536,512]{1,0:T(8,128)(2,1)} fusion(bf16[1024,512]{1,0:T(8,128)(2,1)S(1)} %get-tuple-element.112, s32[2048]{0:T(1024)S(1)} %pad_clamp_fusion.1), kind=kCustom, calls=%fused_computation.2 | custom fusion | bytes 3151872 | tf_op jit(solution)/shard_map/jit(_take)/gather | solution.py:70
  30.8 15.6 %all-to-all-done = bf16[32,48,512]{2,1,0:T(8,128)(2,1)} async-done(((bf16[32,48,512]{2,1,0:T(8,128)(2,1)}), bf16[32,48,512]{2,1,0:T(8,128)(2,1)}, u32[]{:S(2)}, u32[]{:S(2)}) %all-to-all-start) | async-done | bytes 1572896 | tf_op jit(solution)/shard_map/all_to_all | solution.py:71
  46.5 5.0 %all-to-all-start.1 = ((bf16[32,48,512]{2,1,0:T(8,128)(2,1)}), bf16[32,48,512]{2,1,0:T(8,128)(2,1)}, u32[]{:S(2)}, u32[]{:S(2)}) async-start(bf16[32,48,512]{2,1,0:T(8,128)(2,1)} %bitcast.299), calls=%async_computation.1 | async-start | bytes 3145728 | tf_op jit(solution)/shard_map/all_to_all | solution.py:71
  54.1 6.8 %gather_fusion.4 = bf16[1536,512]{1,0:T(8,128)(2,1)} fusion(bf16[1024,512]{1,0:T(8,128)(2,1)} %get-tuple-element.110, s32[2048]{0:T(1024)S(1)} %pad_clamp_fusion.1), kind=kCustom, calls=%fused_computation.4 | custom fusion | bytes 3151872 | tf_op jit(solution)/shard_map/jit(_take)/gather | solution.py:70
  60.9 13.3 %all-to-all-done.1 = bf16[32,48,512]{2,1,0:T(8,128)(2,1)} async-done(((bf16[32,48,512]{2,1,0:T(8,128)(2,1)}), bf16[32,48,512]{2,1,0:T(8,128)(2,1)}, u32[]{:S(2)}, u32[]{:S(2)}) %all-to-all-start.1) | async-done | bytes 1572896 | tf_op jit(solution)/shard_map/all_to_all | solution.py:71
  74.3 5.0 %all-to-all-start.2 = ((bf16[32,48,512]{2,1,0:T(8,128)(2,1)}), bf16[32,48,512]{2,1,0:T(8,128)(2,1)}, u32[]{:S(2)}, u32[]{:S(2)}) async-start(bf16[32,48,512]{2,1,0:T(8,128)(2,1)} %bitcast.298), calls=%async_computation.2 | async-start | bytes 3145728 | tf_op jit(solution)/shard_map/all_to_all | solution.py:71
  79.5 5.5 %gather_fusion.8 = bf16[1536,512]{1,0:T(8,128)(2,1)} fusion(bf16[1024,512]{1,0:T(8,128)(2,1)S(1)} %get-tuple-element.113, s32[2048]{0:T(1024)S(1)} %pad_clamp_fusion.1), kind=kCustom, calls=%fused_computation.8 | custom fusion | bytes 3151872 | tf_op jit(solution)/shard_map/jit(_take)/gather | solution.py:70
  85.5 16.6 %all-to-all-done.2 = bf16[32,48,512]{2,1,0:T(8,128)(2,1)} async-done(((bf16[32,48,512]{2,1,0:T(8,128)(2,1)}), bf16[32,48,512]{2,1,0:T(8,128)(2,1)}, u32[]{:S(2)}, u32[]{:S(2)}) %all-to-all-start.2) | async-done | bytes 1572896 | tf_op jit(solution)/shard_map/all_to_all | solution.py:71
  102.1 5.3 %all-to-all-start.4 = ((bf16[32,48,512]{2,1,0:T(8,128)(2,1)}), bf16[32,48,512]{2,1,0:T(8,128)(2,1)}, u32[]{:S(2)}, u32[]{:S(2)}) async-start(bf16[32,48,512]{2,1,0:T(8,128)(2,1)} %bitcast.296), calls=%async_computation.4 | async-start | bytes 3145728 | tf_op jit(solution)/shard_map/all_to_all | solution.py:71
  114.4 5.4 %gather_fusion.10 = bf16[1536,512]{1,0:T(8,128)(2,1)} fusion(bf16[1024,512]{1,0:T(8,128)(2,1)S(1)} %get-tuple-element.111, s32[2048]{0:T(1024)S(1)} %pad_clamp_fusion.1), kind=kCustom, calls=%fused_computation.10 | custom fusion | bytes 3151872 | tf_op jit(solution)/shard_map/jit(_take)/gather | solution.py:70
  119.8 5.4 %gather_fusion.12 = bf16[1536,512]{1,0:T(8,128)(2,1)} fusion(bf16[1024,512]{1,0:T(8,128)(2,1)S(1)} %get-tuple-element.109, s32[2048]{0:T(1024)S(1)} %pad_clamp_fusion.1), kind=kCustom, calls=%fused_computation.12 | custom fusion | bytes 3151872 | tf_op jit(solution)/shard_map/jit(_take)/gather | solution.py:70
  127.8 5.6 %gather_fusion.1 = bf16[1024,512]{1,0:T(8,128)(2,1)S(1)} fusion(bf16[1536,512]{1,0:T(8,128)(2,1)} %bitcast.4, s32[1024]{0:T(1024)S(1)} %broadcast_clamp_fusion.1), kind=kCustom, calls=%fused_computation.1 | custom fusion | bytes 2101248 | tf_op jit(solution)/shard_map/jit(_take)/gather | solution.py:72
  133.4 7.5 %all-to-all-start.5 = ((bf16[32,48,512]{2,1,0:T(8,128)(2,1)}), bf16[32,48,512]{2,1,0:T(8,128)(2,1)S(1)}, u32[]{:S(2)}, u32[]{:S(2)}) async-start(bf16[32,48,512]{2,1,0:T(8,128)(2,1)} %bitcast.297), calls=%async_computation.5 | async-start | bytes 3145728 | tf_op jit(solution)/shard_map/all_to_all | solution.py:71
  142.5 6.7 %gather_fusion.3 = bf16[1024,512]{1,0:T(8,128)(2,1)} fusion(bf16[1536,512]{1,0:T(8,128)(2,1)} %bitcast.6, s32[1024]{0:T(1024)S(1)} %broadcast_clamp_fusion.1), kind=kCustom, calls=%fused_computation.3 | custom fusion | bytes 2101248 | tf_op jit(solution)/shard_map/jit(_take)/gather | solution.py:72
  149.2 6.8 %gather_fusion.5 = bf16[1024,512]{1,0:T(8,128)(2,1)} fusion(bf16[1536,512]{1,0:T(8,128)(2,1)} %bitcast.9, s32[1024]{0:T(1024)S(1)} %broadcast_clamp_fusion.1), kind=kCustom, calls=%fused_computation.5 | custom fusion | bytes 2101248 | tf_op jit(solution)/shard_map/jit(_take)/gather | solution.py:72
  160.8 3.2 fusion.22
  164.0 7.9 %all-to-all-start.6 = ((bf16[32,48,512]{2,1,0:T(8,128)(2,1)}), bf16[32,48,512]{2,1,0:T(8,128)(2,1)S(1)}, u32[]{:S(2)}, u32[]{:S(2)}) async-start(bf16[32,48,512]{2,1,0:T(8,128)(2,1)} %bitcast.295), calls=%async_computation.6 | async-start | bytes 3145728 | tf_op jit(solution)/shard_map/all_to_all | solution.py:71
  172.9 2.9 fusion.167
  175.8 3.5 collective-permute-start
  179.4 7.0 %gather_fusion.9 = bf16[1024,512]{1,0:T(8,128)(2,1)} fusion(bf16[1536,512]{1,0:T(8,128)(2,1)} %bitcast.46, s32[1024]{0:T(1024)} %copy-done.31), kind=kCustom, calls=%fused_computation.9 | custom fusion | bytes 2101248 | tf_op jit(solution)/shard_map/jit(_take)/gather | solution.py:72
  186.3 5.3 %gather_fusion.11 = bf16[1024,512]{1,0:T(8,128)(2,1)} fusion(bf16[1536,512]{1,0:T(8,128)(2,1)S(1)} %bitcast.290, s32[1024]{0:T(1024)} %copy-done.31), kind=kCustom, calls=%fused_computation.11 | custom fusion | bytes 2101248 | tf_op jit(solution)/shard_map/jit(_take)/gather | solution.py:72
  191.7 2.9 fusion.35
  199.4 3.3 fusion.31
  202.7 4.0 gather_fusion.13
  218.0 3.1 collective-permute-start.1
  226.8 4.3 collective-permute-start.2
  233.7 4.0 collective-permute-done.2
  237.8 6.1 %collective-permute-start.3 = (f32[4,129,128]{2,1,0:T(8,128)S(1)}, f32[4,129,128]{2,1,0:T(8,128)S(1)}, u32[]{:S(2)}, u32[]{:S(2)}) collective-permute-start(f32[4,129,128]{2,1,0:T(8,128)S(1)} %select_add_fusion.5), channel_id=1, source_target_pairs={{0,32},{4,36},{8,40},{12,44},{16,48},{20,52},{24,56},{28,60},{32,6... | collective-permute-start | bytes 792584 | tf_op jit(solution)/shard_map/ppermute | solution.py:106
  247.4 5.6 %collective-permute-start.4 = (f32[4,129,128]{2,1,0:T(8,128)S(1)}, f32[4,129,128]{2,1,0:T(8,128)S(1)}, u32[]{:S(2)}, u32[]{:S(2)}) collective-permute-start(f32[4,129,128]{2,1,0:T(8,128)S(1)} %select_add_fusion.4), channel_id=1, source_target_pairs={{0,64},{4,68},{8,72},{12,76},{16,80},{20,84},{24,88},{28,92},{32,9... | collective-permute-start | bytes 792584 | tf_op jit(solution)/shard_map/ppermute | solution.py:106
  259.0 3.2 fusion.39
  262.7 5.4 %gather_fusion.6 = bf16[1536,512]{1,0:T(8,128)(2,1)} fusion(bf16[1024,512]{1,0:T(8,128)(2,1)S(1)} %copy.73, s32[2048]{0:T(1024)S(1)} %copy-done.34), kind=kCustom, calls=%fused_computation.6 | custom fusion | bytes 3151872 | tf_op jit(solution)/shard_map/jit(_take)/gather | solution.py:128
  268.1 12.0 %all-to-all-start.3 = ((bf16[32,48,512]{2,1,0:T(8,128)(2,1)}), bf16[32,48,512]{2,1,0:T(8,128)(2,1)S(1)}, u32[]{:S(2)}, u32[]{:S(2)}) async-start(bf16[32,48,512]{2,1,0:T(8,128)(2,1)} %bitcast.38), calls=%async_computation.3 | async-start | bytes 3145728 | tf_op jit(solution)/shard_map/all_to_all | solution.py:129
  280.2 2.9 fusion.9
  285.2 4.8 %collective-permute-start.7 = (f32[4,129,128]{2,1,0:T(8,128)S(1)}, f32[4,129,128]{2,1,0:T(8,128)S(1)}, u32[]{:S(2)}, u32[]{:S(2)}) collective-permute-start(f32[4,129,128]{2,1,0:T(8,128)S(1)} %select_add_fusion.2), channel_id=1, source_target_pairs={{0,16},{4,20},{8,24},{12,28},{16,32},{20,36},{24,40},{28,44},{32,4... | collective-permute-start | bytes 792584 | tf_op jit(solution)/shard_map/ppermute | solution.py:106
  290.1 12.7 %all-to-all-done.3 = bf16[32,48,512]{2,1,0:T(8,128)(2,1)S(1)} async-done(((bf16[32,48,512]{2,1,0:T(8,128)(2,1)}), bf16[32,48,512]{2,1,0:T(8,128)(2,1)S(1)}, u32[]{:S(2)}, u32[]{:S(2)}) %all-to-all-start.3) | async-done | bytes 1572896 | tf_op jit(solution)/shard_map/all_to_all | solution.py:129
  302.8 5.1 %gather_fusion.7 = bf16[1024,512]{1,0:T(8,128)(2,1)} fusion(bf16[1536,512]{1,0:T(8,128)(2,1)S(1)} %bitcast.292, s32[1024]{0:T(1024)S(1)} %broadcast_clamp_fusion), kind=kCustom, calls=%fused_computation.7 | custom fusion | bytes 2101248 | tf_op jit(solution)/shard_map/jit(_take)/gather | solution.py:130
  312.3 2.7 collective-permute-done.8
  315.0 6.7 %collective-permute-start.9 = (f32[4,129,128]{2,1,0:T(8,128)S(1)}, f32[4,129,128]{2,1,0:T(8,128)S(1)}, u32[]{:S(2)}, u32[]{:S(2)}) collective-permute-start(f32[4,129,128]{2,1,0:T(8,128)S(1)} %select_add_fusion), channel_id=1, source_target_pairs={{0,64},{4,68},{8,72},{12,76},{16,80},{20,84},{24,88},{28,92},{32,9... | collective-permute-start | bytes 792584 | tf_op jit(solution)/shard_map/ppermute | solution.py:106
  329.1 3.2 fusion.41
  332.8 4.8 %gather_fusion.14 = bf16[1536,512]{1,0:T(8,128)(2,1)S(1)} fusion(bf16[1024,512]{1,0:T(8,128)(2,1)S(1)} %copy.91, s32[2048]{0:T(1024)S(1)} %copy-done.34), kind=kCustom, calls=%fused_computation.14 | custom fusion | bytes 3151872 | tf_op jit(solution)/shard_map/jit(_take)/gather | solution.py:128
  337.6 31.2 %all_to_all.40 = bf16[32,48,512]{2,1,0:T(8,128)(2,1)S(1)} all-to-all(bf16[32,48,512]{2,1,0:T(8,128)(2,1)S(1)} %bitcast.301), channel_id=1, replica_groups=mesh['ctx'=32,'head'=4] {'ctx'}, dimensions={0} | all-to-all | bytes 3145728 | tf_op jit(solution)/shard_map/all_to_all | solution.py:129
  368.8 5.1 %gather_fusion.15 = bf16[1024,512]{1,0:T(8,128)(2,1)} fusion(bf16[1536,512]{1,0:T(8,128)(2,1)S(1)} %bitcast.293, s32[1024]{0:T(1024)S(1)} %broadcast_clamp_fusion), kind=kCustom, calls=%fused_computation.15 | custom fusion | bytes 2101248 | tf_op jit(solution)/shard_map/jit(_take)/gather | solution.py:130
  374.0 6.0 %fusion.160 = (bf16[4,1,512,1024]{3,2,1,0:T(8,128)(2,1)}, bf16[4,1,512,1024]{3,2,1,0:T(8,128)(2,1)}) fusion(bf16[4,2,512,1024]{3,2,1,0:T(8,128)(2,1)} %bitcast.294), kind=kLoop, calls=%fused_computation.270 | loop fusion | bytes 16777216 | tf_op jit(solution)/shard_map/slice | solution.py:134
  379.9 10.6 %fusion.171 = f32[1024,1024]{1,0:T(8,128)} fusion(bf16[1024,2048]{1,0:T(8,128)(2,1)} %all-gather.5.cloned.1.call-done, bf16[2048,1024]{1,0:T(8,128)(2,1)} %bitcast.303), kind=kOutput, calls=%fused_computation.281 | convolution fusion | flops 4294967296 | bytes 12582912 | tf_op jit(solution)/shard_map/dot_general | solution.py:132
  390.5 30.3 %all-gather.7.cloned.1.call-done = bf16[1024,2048]{1,0:T(8,128)(2,1)} async-done(((bf16[1024,512]{1,0:T(8,128)(2,1)}), bf16[1024,2048]{1,0:T(8,128)(2,1)}) %all-gather.7.cloned.1.call-update) | async-done | bytes 4194320 | tf_op jit(solution)/shard_map/all_gather | solution.py:131
  420.8 10.5 %add_convert_fusion = bf16[1024,1024]{1,0:T(8,128)(2,1)} fusion(f32[1024,1024]{1,0:T(8,128)} %fusion.171, bf16[1024,2048]{1,0:T(8,128)(2,1)} %all-gather.7.cloned.1.call-done, bf16[2048,1024]{1,0:T(8,128)(2,1)} %bitcast.302), kind=kOutput, calls=%fused_computation.36 | convolution fusion | flops 4297064448 | bytes 14680064 | tf_op jit(solution)/shard_map/dot_general | solution.py:132
  (193 shorter events, 70.3 us)
Async XLA Ops:
  8.9 6.2 %copy-start.35 = (s32[1024]{0:T(1024)}, s32[1024]{0:T(1024)S(1)}, u32[]{:S(2)}) copy-start(s32[1024]{0:T(1024)S(1)} %convert_element_type.96) | copy-start | bytes 12292
  15.1 31.4 %all-to-all-start = ((bf16[32,48,512]{2,1,0:T(8,128)(2,1)}), bf16[32,48,512]{2,1,0:T(8,128)(2,1)}, u32[]{:S(2)}, u32[]{:S(2)}) async-start(bf16[32,48,512]{2,1,0:T(8,128)(2,1)} %bitcast.300), calls=%async_computation | async-start | bytes 3145728 | tf_op jit(solution)/shard_map/all_to_all | solution.py:71
  46.5 27.8 %all-to-all-start.1 = ((bf16[32,48,512]{2,1,0:T(8,128)(2,1)}), bf16[32,48,512]{2,1,0:T(8,128)(2,1)}, u32[]{:S(2)}, u32[]{:S(2)}) async-start(bf16[32,48,512]{2,1,0:T(8,128)(2,1)} %bitcast.299), calls=%async_computation.1 | async-start | bytes 3145728 | tf_op jit(solution)/shard_map/all_to_all | solution.py:71
  74.3 27.8 %all-to-all-start.2 = ((bf16[32,48,512]{2,1,0:T(8,128)(2,1)}), bf16[32,48,512]{2,1,0:T(8,128)(2,1)}, u32[]{:S(2)}, u32[]{:S(2)}) async-start(bf16[32,48,512]{2,1,0:T(8,128)(2,1)} %bitcast.298), calls=%async_computation.2 | async-start | bytes 3145728 | tf_op jit(solution)/shard_map/all_to_all | solution.py:71
  85.0 24.4 %copy-start.44 = (s32[32]{0:T(128)S(1)}, s32[32]{0:T(128)}, u32[]{:S(2)}) copy-start(s32[32]{0:T(128)} %param.11) | copy-start | bytes 388
  102.1 31.3 %all-to-all-start.4 = ((bf16[32,48,512]{2,1,0:T(8,128)(2,1)}), bf16[32,48,512]{2,1,0:T(8,128)(2,1)}, u32[]{:S(2)}, u32[]{:S(2)}) async-start(bf16[32,48,512]{2,1,0:T(8,128)(2,1)} %bitcast.296), calls=%async_computation.4 | async-start | bytes 3145728 | tf_op jit(solution)/shard_map/all_to_all | solution.py:71
  119.8 6.0 %copy-start.45 = (f32[8]{0:T(128)S(1)}, f32[8]{0:T(128)}, u32[]{:S(2)}) copy-start(f32[8]{0:T(128)} %param.12) | copy-start | bytes 100
  127.8 21.4 %copy-start.31 = (s32[1024]{0:T(1024)}, s32[1024]{0:T(1024)S(1)}, u32[]{:S(2)}) copy-start(s32[1024]{0:T(1024)S(1)} %broadcast_clamp_fusion.1) | copy-start | bytes 12292
  133.4 30.6 %all-to-all-start.5 = ((bf16[32,48,512]{2,1,0:T(8,128)(2,1)}), bf16[32,48,512]{2,1,0:T(8,128)(2,1)S(1)}, u32[]{:S(2)}, u32[]{:S(2)}) async-start(bf16[32,48,512]{2,1,0:T(8,128)(2,1)} %bitcast.297), calls=%async_computation.5 | async-start | bytes 3145728 | tf_op jit(solution)/shard_map/all_to_all | solution.py:71
  164.0 38.6 %all-to-all-start.6 = ((bf16[32,48,512]{2,1,0:T(8,128)(2,1)}), bf16[32,48,512]{2,1,0:T(8,128)(2,1)S(1)}, u32[]{:S(2)}, u32[]{:S(2)}) async-start(bf16[32,48,512]{2,1,0:T(8,128)(2,1)} %bitcast.295), calls=%async_computation.6 | async-start | bytes 3145728 | tf_op jit(solution)/shard_map/all_to_all | solution.py:71
  175.8 41.2 %collective-permute-start = (f32[4,129,128]{2,1,0:T(8,128)S(1)}, f32[4,129,128]{2,1,0:T(8,128)}, u32[]{:S(2)}, u32[]{:S(2)}) collective-permute-start(f32[4,129,128]{2,1,0:T(8,128)S(1)} %pad_maximum_fusion), channel_id=1, source_target_pairs={{0,4},{4,8},{8,12},{12,16},{16,20},{20,24},{24,28},{28,32},{32,36}... | collective-permute-start | bytes 792584 | tf_op jit(solution)/shard_map/ppermute | solution.py:106
  191.7 7.7 %copy-start = (bf16[1024,512]{1,0:T(8,128)(2,1)S(1)}, bf16[1024,512]{1,0:T(8,128)(2,1)}, u32[]{:S(2)}) copy-start(bf16[1024,512]{1,0:T(8,128)(2,1)} %gather_fusion.9) | copy-start | bytes 3145732
  191.7 7.7 %copy-start.5 = (bf16[1024,512]{1,0:T(8,128)(2,1)S(1)}, bf16[1024,512]{1,0:T(8,128)(2,1)}, u32[]{:S(2)}) copy-start(bf16[1024,512]{1,0:T(8,128)(2,1)} %gather_fusion.11) | copy-start | bytes 3145732
  197.0 5.7 %copy-start.32 = (s32[1024]{0:T(1024)S(1)}, s32[1024]{0:T(1024)}, u32[]{:S(2)}) copy-start(s32[1024]{0:T(1024)} %copy-done.31) | copy-start | bytes 12292
  206.7 5.4 %copy-start.24 = (bf16[1024,1,128]{2,0,1:T(8,128)(2,1)S(1)}, bf16[1024,1,128]{2,0,1:T(8,128)(2,1)}, u32[]{:S(2)}) copy-start(bf16[1024,1,128]{2,0,1:T(8,128)(2,1)} %get-tuple-element.58) | copy-start | bytes 786436
  206.7 5.4 %copy-start.30 = (bf16[1024,1,128]{2,0,1:T(8,128)(2,1)S(1)}, bf16[1024,1,128]{2,0,1:T(8,128)(2,1)}, u32[]{:S(2)}) copy-start(bf16[1024,1,128]{2,0,1:T(8,128)(2,1)} %get-tuple-element.57) | copy-start | bytes 786436
  209.9 11.2 %collective-permute-start.5 = (f32[4,129,128]{2,1,0:T(8,128)S(1)}, f32[4,129,128]{2,1,0:T(8,128)S(1)}, u32[]{:S(2)}, u32[]{:S(2)}) collective-permute-start(f32[4,129,128]{2,1,0:T(8,128)S(1)} %pad_maximum_fusion.1), channel_id=1, source_target_pairs={{0,4},{4,8},{8,12},{12,16},{16,20},{20,24},{24,28},{28,32},{32,36}... | collective-permute-start | bytes 792584 | tf_op jit(solution)/shard_map/ppermute | solution.py:106
  215.4 7.8 %copy-start.22 = (bf16[1024,1,128]{2,0,1:T(8,128)(2,1)S(1)}, bf16[1024,1,128]{2,0,1:T(8,128)(2,1)}, u32[]{:S(2)}) copy-start(bf16[1024,1,128]{2,0,1:T(8,128)(2,1)} %get-tuple-element.63) | copy-start | bytes 786436
  215.4 7.8 %copy-start.29 = (bf16[1024,1,128]{2,0,1:T(8,128)(2,1)S(1)}, bf16[1024,1,128]{2,0,1:T(8,128)(2,1)}, u32[]{:S(2)}) copy-start(bf16[1024,1,128]{2,0,1:T(8,128)(2,1)} %get-tuple-element.62) | copy-start | bytes 786436
  218.0 8.8 %collective-permute-start.1 = (f32[4,129,128]{2,1,0:T(8,128)S(1)}, f32[4,129,128]{2,1,0:T(8,128)S(1)}, u32[]{:S(2)}, u32[]{:S(2)}) collective-permute-start(f32[4,129,128]{2,1,0:T(8,128)S(1)} %select_add_fusion.7), channel_id=1, source_target_pairs={{0,8},{4,12},{8,16},{12,20},{16,24},{20,28},{24,32},{28,36},{32,40... | collective-permute-start | bytes 792584 | tf_op jit(solution)/shard_map/ppermute | solution.py:106
  221.1 64.0 %collective-permute-start.6 = (f32[4,129,128]{2,1,0:T(8,128)S(1)}, f32[4,129,128]{2,1,0:T(8,128)S(1)}, u32[]{:S(2)}, u32[]{:S(2)}) collective-permute-start(f32[4,129,128]{2,1,0:T(8,128)S(1)} %select_add_fusion.3), channel_id=1, source_target_pairs={{0,8},{4,12},{8,16},{12,20},{16,24},{20,28},{24,32},{28,36},{32,40... | collective-permute-start | bytes 792584 | tf_op jit(solution)/shard_map/ppermute | solution.py:106
  225.2 18.7 %copy-start.20 = (bf16[1024,1,128]{2,0,1:T(8,128)(2,1)S(1)}, bf16[1024,1,128]{2,0,1:T(8,128)(2,1)}, u32[]{:S(2)}) copy-start(bf16[1024,1,128]{2,0,1:T(8,128)(2,1)} %get-tuple-element.69) | copy-start | bytes 786436
  225.2 18.7 %copy-start.28 = (bf16[1024,1,128]{2,0,1:T(8,128)(2,1)S(1)}, bf16[1024,1,128]{2,0,1:T(8,128)(2,1)}, u32[]{:S(2)}) copy-start(bf16[1024,1,128]{2,0,1:T(8,128)(2,1)} %get-tuple-element.68) | copy-start | bytes 786436
  226.8 11.0 %collective-permute-start.2 = (f32[4,129,128]{2,1,0:T(8,128)S(1)}, f32[4,129,128]{2,1,0:T(8,128)S(1)}, u32[]{:S(2)}, u32[]{:S(2)}) collective-permute-start(f32[4,129,128]{2,1,0:T(8,128)S(1)} %select_add_fusion.6), channel_id=1, source_target_pairs={{0,16},{4,20},{8,24},{12,28},{16,32},{20,36},{24,40},{28,44},{32,4... | collective-permute-start | bytes 792584 | tf_op jit(solution)/shard_map/ppermute | solution.py:106
  237.8 7.3 %copy-start.19 = (bf16[1024,1,128]{2,0,1:T(8,128)(2,1)S(1)}, bf16[1024,1,128]{2,0,1:T(8,128)(2,1)}, u32[]{:S(2)}) copy-start(bf16[1024,1,128]{2,0,1:T(8,128)(2,1)} %get-tuple-element.67) | copy-start | bytes 786436
  237.8 9.5 %collective-permute-start.3 = (f32[4,129,128]{2,1,0:T(8,128)S(1)}, f32[4,129,128]{2,1,0:T(8,128)S(1)}, u32[]{:S(2)}, u32[]{:S(2)}) collective-permute-start(f32[4,129,128]{2,1,0:T(8,128)S(1)} %select_add_fusion.5), channel_id=1, source_target_pairs={{0,32},{4,36},{8,40},{12,44},{16,48},{20,52},{24,56},{28,60},{32,6... | collective-permute-start | bytes 792584 | tf_op jit(solution)/shard_map/ppermute | solution.py:106
  245.2 7.9 %copy-start.18 = (bf16[1024,1,128]{2,0,1:T(8,128)(2,1)S(1)}, bf16[1024,1,128]{2,0,1:T(8,128)(2,1)}, u32[]{:S(2)}) copy-start(bf16[1024,1,128]{2,0,1:T(8,128)(2,1)} %get-tuple-element.74) | copy-start | bytes 786436
  245.2 7.9 %copy-start.27 = (bf16[1024,1,128]{2,0,1:T(8,128)(2,1)S(1)}, bf16[1024,1,128]{2,0,1:T(8,128)(2,1)}, u32[]{:S(2)}) copy-start(bf16[1024,1,128]{2,0,1:T(8,128)(2,1)} %get-tuple-element.73) | copy-start | bytes 786436
  247.4 6.9 %copy-start.17 = (bf16[1024,1,128]{2,0,1:T(8,128)(2,1)S(1)}, bf16[1024,1,128]{2,0,1:T(8,128)(2,1)}, u32[]{:S(2)}) copy-start(bf16[1024,1,128]{2,0,1:T(8,128)(2,1)} %get-tuple-element.72) | copy-start | bytes 786436
  247.4 8.9 %collective-permute-start.4 = (f32[4,129,128]{2,1,0:T(8,128)S(1)}, f32[4,129,128]{2,1,0:T(8,128)S(1)}, u32[]{:S(2)}, u32[]{:S(2)}) collective-permute-start(f32[4,129,128]{2,1,0:T(8,128)S(1)} %select_add_fusion.4), channel_id=1, source_target_pairs={{0,64},{4,68},{8,72},{12,76},{16,80},{20,84},{24,88},{28,92},{32,9... | collective-permute-start | bytes 792584 | tf_op jit(solution)/shard_map/ppermute | solution.py:106
  255.1 3.8 copy-start.42
  268.1 14.9 %copy-start.16 = (bf16[1024,1,128]{2,0,1:T(8,128)(2,1)S(1)}, bf16[1024,1,128]{2,0,1:T(8,128)(2,1)}, u32[]{:S(2)}) copy-start(bf16[1024,1,128]{2,0,1:T(8,128)(2,1)} %get-tuple-element.86) | copy-start | bytes 786436
  268.1 34.7 %all-to-all-start.3 = ((bf16[32,48,512]{2,1,0:T(8,128)(2,1)}), bf16[32,48,512]{2,1,0:T(8,128)(2,1)S(1)}, u32[]{:S(2)}, u32[]{:S(2)}) async-start(bf16[32,48,512]{2,1,0:T(8,128)(2,1)} %bitcast.38), calls=%async_computation.3 | async-start | bytes 3145728 | tf_op jit(solution)/shard_map/all_to_all | solution.py:129
  280.1 99.8 %all-gather.5.cloned.1.call-start = ((), (), s32[]{:S(2)}) async-start(), calls=%async_computation.8 | async-start | bytes 5242880 | tf_op jit(solution)/shard_map/all_gather | solution.py:131
  283.6 6.4 %copy-start.36 = (s32[1024]{0:T(1024)S(1)}, s32[1024]{0:T(1024)}, u32[]{:S(2)}) copy-start(s32[1024]{0:T(1024)} %copy-done.35) | copy-start | bytes 12292
  285.2 22.7 %collective-permute-start.7 = (f32[4,129,128]{2,1,0:T(8,128)S(1)}, f32[4,129,128]{2,1,0:T(8,128)S(1)}, u32[]{:S(2)}, u32[]{:S(2)}) collective-permute-start(f32[4,129,128]{2,1,0:T(8,128)S(1)} %select_add_fusion.2), channel_id=1, source_target_pairs={{0,16},{4,20},{8,24},{12,28},{16,32},{20,36},{24,40},{28,44},{32,4... | collective-permute-start | bytes 792584 | tf_op jit(solution)/shard_map/ppermute | solution.py:106
  302.8 7.4 %copy-start.15 = (bf16[1024,1,128]{2,0,1:T(8,128)(2,1)S(1)}, bf16[1024,1,128]{2,0,1:T(8,128)(2,1)}, u32[]{:S(2)}) copy-start(bf16[1024,1,128]{2,0,1:T(8,128)(2,1)} %get-tuple-element.94) | copy-start | bytes 786436
  302.8 7.4 %copy-start.26 = (bf16[1024,1,128]{2,0,1:T(8,128)(2,1)S(1)}, bf16[1024,1,128]{2,0,1:T(8,128)(2,1)}, u32[]{:S(2)}) copy-start(bf16[1024,1,128]{2,0,1:T(8,128)(2,1)} %get-tuple-element.93) | copy-start | bytes 786436
  307.9 112.9 %all-gather.7.cloned.1.call-start = ((), (), s32[]{:S(2)}) async-start(), calls=%async_computation.9 | async-start | bytes 5242880 | tf_op jit(solution)/shard_map/all_gather | solution.py:131
  308.0 7.0 %collective-permute-start.8 = (f32[4,129,128]{2,1,0:T(8,128)S(1)}, f32[4,129,128]{2,1,0:T(8,128)S(1)}, u32[]{:S(2)}, u32[]{:S(2)}) collective-permute-start(f32[4,129,128]{2,1,0:T(8,128)S(1)} %select_add_fusion.1), channel_id=1, source_target_pairs={{0,32},{4,36},{8,40},{12,44},{16,48},{20,52},{24,56},{28,60},{32,6... | collective-permute-start | bytes 792584 | tf_op jit(solution)/shard_map/ppermute | solution.py:106
  311.5 10.3 %copy-start.13 = (bf16[1024,1,128]{2,0,1:T(8,128)(2,1)S(1)}, bf16[1024,1,128]{2,0,1:T(8,128)(2,1)}, u32[]{:S(2)}) copy-start(bf16[1024,1,128]{2,0,1:T(8,128)(2,1)} %get-tuple-element.99) | copy-start | bytes 786436
  311.5 10.3 %copy-start.25 = (bf16[1024,1,128]{2,0,1:T(8,128)(2,1)S(1)}, bf16[1024,1,128]{2,0,1:T(8,128)(2,1)}, u32[]{:S(2)}) copy-start(bf16[1024,1,128]{2,0,1:T(8,128)(2,1)} %get-tuple-element.98) | copy-start | bytes 786436
  315.0 8.0 %copy-start.12 = (bf16[1024,1,128]{2,0,1:T(8,128)(2,1)S(1)}, bf16[1024,1,128]{2,0,1:T(8,128)(2,1)}, u32[]{:S(2)}) copy-start(bf16[1024,1,128]{2,0,1:T(8,128)(2,1)} %get-tuple-element.97) | copy-start | bytes 786436
  315.0 11.4 %collective-permute-start.9 = (f32[4,129,128]{2,1,0:T(8,128)S(1)}, f32[4,129,128]{2,1,0:T(8,128)S(1)}, u32[]{:S(2)}, u32[]{:S(2)}) collective-permute-start(f32[4,129,128]{2,1,0:T(8,128)S(1)} %select_add_fusion), channel_id=1, source_target_pairs={{0,64},{4,68},{8,72},{12,76},{16,80},{20,84},{24,88},{28,92},{32,9... | collective-permute-start | bytes 792584 | tf_op jit(solution)/shard_map/ppermute | solution.py:106
  323.8 5.2 %copy-start.40 = (f32[4]{0:T(128)S(1)}, f32[4]{0:T(128)}, u32[]{:S(2)}) copy-start(f32[4]{0:T(128)} %get-tuple-element.140) | copy-start | bytes 52
  323.9 5.2 %copy-start.41 = (f32[4]{0:T(128)S(1)}, f32[4]{0:T(128)}, u32[]{:S(2)}) copy-start(f32[4]{0:T(128)} %get-tuple-element.142) | copy-start | bytes 52
  323.9 5.2 %copy-start.46 = (f32[1024,1,128]{0,2,1:T(8,128)S(1)}, f32[1024,1,128]{0,2,1:T(8,128)}, u32[]{:S(2)}) copy-start(f32[1024,1,128]{0,2,1:T(8,128)} %fusion.63) | copy-start | bytes 1572868
  323.9 5.2 %copy-start.47 = (f32[1024,1,128]{0,2,1:T(8,128)S(1)}, f32[1024,1,128]{0,2,1:T(8,128)}, u32[]{:S(2)}) copy-start(f32[1024,1,128]{0,2,1:T(8,128)} %fusion.62) | copy-start | bytes 1572868
  (19 other events, 52.5 us)
Sparse Core Ops, SparseCore 0:
  308.0 51.0 all-gather.4
  374.1 46.6 all-gather.6

commit v4 on v3

--- a/solution.py
+++ b/solution.py
@@ -53,23 +53,19 @@
     causal = r_idx[:, None] >= r_idx[None, :]
     head_count = lax.axis_size("head")
     out_cols = out_weight.shape[1]
-    groups = 2
-    group_heads = heads // groups
-    group_width = width // groups
-    weight_parts = out_weight.reshape(head_count, groups, group_width, out_cols)
+    bounds = [0, heads - heads // 4, heads]
+    weight_rows = out_weight.reshape(head_count, heads, dh, out_cols)
     gate_all = jax.nn.sigmoid(mem_gate)
     shifts = []
     step = 1
     while step < n:
         shifts.append(step)
         step *= 2
-    cuts = [round(group_heads * i / len(shifts)) for i in range(len(shifts) + 1)]
 
-    def dispatch(source, g):
-        columns = source[:, g * group_width:(g + 1) * group_width]
-        buffer = jnp.take(columns, slot_row, axis=0, mode="clip").reshape(n, cap, group_width)
-        got = lax.all_to_all(buffer, "ctx", 0, 0, tiled=True).reshape(slots, group_width)
-        return jnp.take(got, tok_slot, axis=0, mode="clip").reshape(seg, group_heads, dh)
+    joined = jnp.concatenate([keys, values, queries], axis=1)
+    buffer = jnp.take(joined, slot_row, axis=0, mode="clip").reshape(n, cap, 3 * width)
+    got = lax.all_to_all(buffer, "ctx", 0, 0, tiled=True).reshape(slots, 3 * width)
+    arrived_rows = jnp.take(got, tok_slot, axis=0, mode="clip").reshape(seg, 3, heads, dh)
 
     def local_attention(query_part, key_part, value_part):
         scores = jnp.einsum(
@@ -83,10 +79,15 @@
             "hqk,khd->qhd", probabilities, value_part, preferred_element_type=f32
         )
 
-    def one_group(g):
-        key_heads = dispatch(keys, g)
-        value_heads = dispatch(values, g)
-        query_heads = dispatch(queries, g)
+    def one_group(g, hold):
+        first, last = bounds[g], bounds[g + 1]
+        group_heads = last - first
+        group_width = group_heads * dh
+        cuts = [first + round(group_heads * i / len(shifts)) for i in range(len(shifts) + 1)]
+        cuts = [c - first for c in cuts]
+        key_heads = arrived_rows[:, 0, first:last]
+        value_heads = arrived_rows[:, 1, first:last]
+        query_heads = arrived_rows[:, 2, first:last]
 
         key_feat = feature(key_heads.astype(f32))
         delta_m = jnp.einsum(
@@ -94,6 +95,8 @@
         )
         delta_z = jnp.sum(key_feat, axis=0)
         delta = jnp.concatenate([delta_m, delta_z[:, None, :]], axis=1)
+        if hold is not None:
+            delta, _ = lax.optimization_barrier((delta, hold))
 
         pieces = []
         total = delta
@@ -118,7 +121,7 @@
         numerator = jnp.einsum("qhd,hde->qhe", query_feat, mem_m, precision=highest)
         denominator = jnp.einsum("qhd,hd->qh", query_feat, mem_z, precision=highest)
         recalled = numerator / jnp.maximum(denominator, 1.0)[..., None]
-        gate_value = gate_all[g * group_heads:(g + 1) * group_heads][None, :, None]
+        gate_value = gate_all[first:last][None, :, None]
         combined = (
             (gate_value * recalled + (1.0 - gate_value) * local_out)
             .astype(bf16)
@@ -129,15 +132,17 @@
         incoming = lax.all_to_all(outgoing, "ctx", 0, 0, tiled=True).reshape(slots, group_width)
         rows = jnp.take(incoming, send_slot, axis=0, mode="clip")
         gathered = lax.all_gather(rows, "head", axis=1, tiled=True)
-        return jnp.dot(
+        part = jnp.dot(
             gathered,
-            weight_parts[:, g].reshape(head_count * group_width, out_cols),
+            weight_rows[:, first:last].reshape(head_count * group_width, out_cols),
             preferred_element_type=f32,
         )
+        return part, combined
 
-    summed = one_group(0)
-    for g in range(1, groups):
-        summed = summed + one_group(g)
+    summed, hold = one_group(0, None)
+    for g in range(1, len(bounds) - 1):
+        part, hold = one_group(g, hold)
+        summed = summed + part
     return summed.astype(bf16)
 
 

time: 446 us -> 489 us (1.096)
  waiting for transfers between devices: 102 us -> 177 us
  local copies, waits for them, and re-layouts: 120 us -> 93.4 us
  starting transfers between devices: 92 us -> 85.8 us
    all_to_all x6 -> x1, waiting for transfers between devices: 45.5 us -> 117 us  [per_device(): lax.all_to_all(buffer, 'ctx', 0, 0, tiled=True).reshape(slots, 3 * width)]
    all_to_all x6 -> x1, starting transfers between devices: 39.3 us -> 9.47 us  [per_device(): lax.all_to_all(buffer, 'ctx', 0, 0, tiled=True).reshape(slots, 3 * width)]
    ppermute x10, starting transfers between devices: 40.6 us -> 66.6 us  [one_group(): got = lax.ppermute(total, 'ctx', perm)]
    gather x12 -> x3, local copies, waits for them, and re-layouts: 69.3 us -> 47.1 us  [the longest x2 25.7 us: per_device(): jnp.take(got, tok_slot, axis=0, mode='clip').reshape(seg, 3, heads, dh)]
    all_gather x2, waiting for transfers between devices: 30.3 us -> 11.8 us  [one_group(): gathered = lax.all_gather(rows, 'head', axis=1, tiled=True)]
    all_to_all x1, waiting for transfers between devices: 12.7 us -> 30.3 us  [one_group(): lax.all_to_all(outgoing, 'ctx', 0, 0, tiled=True)]
    reshape x6 -> x0, local copies, waits for them, and re-layouts: 8.77 us -> none  [dispatch(): jnp.take(got, tok_slot, axis=0, mode='clip').reshape(seg, group_heads, dh)]
    concatenate x0 -> x1, other arithmetic: none -> 5.41 us  [per_device(): joined = jnp.concatenate([keys, values, queries], axis=1)]
  transfers between devices with their start and end apart: 19 -> 14, of which waited for: 11 -> 10; matrix products, arithmetic and copies ran while one was open for 40% -> 15% of each run, Pallas kernels for 0% -> 0%
where the time goes in v4:
time: 489 us; the launch traced here: 482 us
  waiting for transfers between devices  177 us (36%)
  local copies, waits for them, and re-layouts  93.4 us (19%)
  starting transfers between devices  85.8 us (18%)
  matrix products  58.4 us (12%)
  blocking collectives  29.2 us (6%)
  other arithmetic  20.3 us (4%)
  between operations  17.7 us (4%)
    all_to_all x1, waiting for transfers between devices, per_device(): lax.all_to_all(buffer, 'ctx', 0, 0, tiled=True).reshape(slots, 3 * width)  117 us
    ppermute x10, starting transfers between devices, one_group(): got = lax.ppermute(total, 'ctx', perm)  66.6 us
    all_to_all x1, waiting for transfers between devices, one_group(): lax.all_to_all(outgoing, 'ctx', 0, 0, tiled=True)  30.3 us
    all_to_all x1, blocking collectives, one_group(): lax.all_to_all(outgoing, 'ctx', 0, 0, tiled=True)  29.2 us
    gather x2, local copies, waits for them, and re-layouts, per_device(): jnp.take(got, tok_slot, axis=0, mode='clip').reshape(seg, 3, heads, dh)  25.7 us
    gather x1, local copies, waits for them, and re-layouts, per_device(): jnp.take(joined, slot_row, axis=0, mode='clip').reshape(n, cap, 3 * width)  21.4 us
    ppermute x10, waiting for transfers between devices, one_group(): got = lax.ppermute(total, 'ctx', perm)  18.6 us
    dot_general x2, matrix products, one_group(): jnp.dot(gathered, weight_rows[:, first:last].reshape(head_count * group_w...  18.6 us
  transfers between devices with their start and end apart: 14, of which 10 were waited for; matrix products, arithmetic and copies ran while one was open for 15% of the time, Pallas kernels for 0%

profile of v4, /device:TPU:1, one launch (start us, length us, event | category | flops | bytes accessed | tf_op | source)
XLA Modules:
  0.0 482.1 jit_solution(695160722528141395)
XLA Ops:
  9.8 1.7 select_reduce_fusion.1
  11.6 5.4 %pad_maximum_fusion = bf16[1024,3072]{1,0:T(8,128)(2,1)} fusion(bf16[1024,1024]{1,0:T(8,128)(2,1)S(1)} %copy-done.1, bf16[1024,1024]{1,0:T(8,128)(2,1)} %param.9, bf16[1024,1024]{1,0:T(8,128)(2,1)} %param.8), kind=kLoop, calls=%fused_computation.15 | loop fusion | flops 18874368 | bytes 12582912 | tf_op jit(solution)/shard_map/concatenate | solution.py:65
  17.0 21.4 %gather_fusion = bf16[1536,3072]{1,0:T(8,128)(2,1)} fusion(bf16[1024,3072]{1,0:T(8,128)(2,1)} %pad_maximum_fusion, s32[2048]{0:T(1024)S(1)} %get-tuple-element.143), kind=kCustom, calls=%fused_computation | custom fusion | bytes 18880512 | tf_op jit(solution)/shard_map/jit(_take)/gather | solution.py:66
  38.4 9.5 %all-to-all-start = ((bf16[32,48,3072]{2,1,0:T(8,128)(2,1)}), bf16[32,48,3072]{2,1,0:T(8,128)(2,1)}, u32[]{:S(2)}, u32[]{:S(2)}) async-start(bf16[32,48,3072]{2,1,0:T(8,128)(2,1)} %bitcast.221), calls=%async_computation | async-start | bytes 18874368 | tf_op jit(solution)/shard_map/all_to_all | solution.py:67
  56.8 116.6 %all-to-all-done = bf16[32,48,3072]{2,1,0:T(8,128)(2,1)} async-done(((bf16[32,48,3072]{2,1,0:T(8,128)(2,1)}), bf16[32,48,3072]{2,1,0:T(8,128)(2,1)}, u32[]{:S(2)}, u32[]{:S(2)}) %all-to-all-start) | async-done | bytes 9437216 | tf_op jit(solution)/shard_map/all_to_all | solution.py:67
  173.3 17.1 %gather_fusion.1 = bf16[1024,3072]{1,0:T(8,128)(2,1)} fusion(bf16[1536,3072]{1,0:T(8,128)(2,1)} %bitcast.4, s32[1024]{0:T(1024)S(1)} %broadcast_clamp_fusion.1), kind=kCustom, calls=%fused_computation.1 | custom fusion | bytes 12587008 | tf_op jit(solution)/shard_map/jit(_take)/gather | solution.py:68
  190.4 8.6 %copy.29 = bf16[1024,3072]{0,1:T(8,128)(2,1)} copy(bf16[1024,3072]{1,0:T(8,128)(2,1)} %gather_fusion.1) | data formatting | bytes 12582912 | tf_op jit(solution)/shard_map/jit(_take)/gather | solution.py:68
  199.0 4.9 %fusion.28 = f32[6,128,128]{2,1,0:T(8,128)S(1)} fusion(bf16[1024,3,8,128]{0,3,2,1:T(8,128)(2,1)} %bitcast.222), kind=kOutput, calls=%fused_computation.72 | convolution fusion | flops 1211891712 | bytes 3538944 | tf_op jit(solution)/shard_map/khd,khe->hde/dot_general | solution.py:93
  205.4 1.7 fusion.150
  207.1 2.6 copy.54
  209.7 2.1 fusion.151
  211.7 1.9 slice.163
  216.3 22.1 %collective-permute-start = (f32[6,129,128]{2,1,0:T(8,128)S(1)}, f32[6,129,128]{2,1,0:T(8,128)S(1)}, u32[]{:S(2)}, u32[]{:S(2)}) collective-permute-start(f32[6,129,128]{2,1,0:T(8,128)S(1)} %pad_maximum_fusion.1), channel_id=1, source_target_pairs={{0,4},{4,8},{8,12},{12,16},{16,20},{20,24},{24,28},{28,32},{32,36}... | collective-permute-start | bytes 1188872 | tf_op jit(solution)/shard_map/ppermute | solution.py:109
  240.5 2.7 collective-permute-done
  246.0 1.5 fusion.58
  248.4 2.0 collective-permute-done.1
  250.4 5.3 %collective-permute-start.2 = (f32[6,129,128]{2,1,0:T(8,128)S(1)}, f32[6,129,128]{2,1,0:T(8,128)}, u32[]{:S(2)}, u32[]{:S(2)}) collective-permute-start(f32[6,129,128]{2,1,0:T(8,128)S(1)} %select_add_fusion.2), channel_id=1, source_target_pairs={{0,16},{4,20},{8,24},{12,28},{16,32},{20,36},{24,40},{28,44},{32,4... | collective-permute-start | bytes 1188872 | tf_op jit(solution)/shard_map/ppermute | solution.py:109
  255.8 5.3 %fusion.159 = (f32[2,1024]{1,0:T(2,128)S(1)}, f32[2,1024,1024]{1,2,0:T(8,128)}) fusion(pred[1024,1024]{0,1:T(8,128)(4,1)S(1)} %copy-done.2, bf16[1024,2,128]{0,2,1:T(8,128)(2,1)S(1)} %copy-done.5, bf16[1024,2,128]{0,2,1:T(8,128)(2,1)S(1)} %slice.162), kind=kOutput, calls=%fused_computation.256 | convolution fusion | flops 545260544 | bytes 10493952 | tf_op jit(solution)/shard_map/sub | solution.py:76
  261.1 4.3 fusion.49
  269.3 2.8 collective-permute-done.3
  272.1 15.5 %collective-permute-start.4 = (f32[6,129,128]{2,1,0:T(8,128)S(1)}, f32[6,129,128]{2,1,0:T(8,128)S(1)}, u32[]{:S(2)}, u32[]{:S(2)}) collective-permute-start(f32[6,129,128]{2,1,0:T(8,128)S(1)} %select_add_fusion), channel_id=1, source_target_pairs={{0,64},{4,68},{8,72},{12,76},{16,80},{20,84},{24,88},{28,92},{32,9... | collective-permute-start | bytes 1188872 | tf_op jit(solution)/shard_map/ppermute | solution.py:109
  289.8 3.8 collective-permute-done.4
  293.7 2.9 fusion.23
  296.7 4.6 fusion.22
  302.0 5.7 %gather_fusion.2 = bf16[1536,768]{1,0:T(8,128)(2,1)} fusion(bf16[1024,768]{1,0:T(8,128)(2,1)S(1)} %copy.37, s32[2048]{0:T(1024)S(1)} %get-tuple-element.142), kind=kCustom, calls=%fused_computation.2 | custom fusion | bytes 4724736 | tf_op jit(solution)/shard_map/jit(_take)/gather | solution.py:131
  307.7 9.4 %all-to-all-start.1 = ((bf16[32,48,768]{2,1,0:T(8,128)(2,1)}), bf16[32,48,768]{2,1,0:T(8,128)(2,1)S(1)}, u32[]{:S(2)}, u32[]{:S(2)}) async-start(bf16[32,48,768]{2,1,0:T(8,128)(2,1)} %bitcast.235), calls=%async_computation.1 | async-start | bytes 4718592 | tf_op jit(solution)/shard_map/all_to_all | solution.py:132
  318.0 30.3 %all-to-all-done.1 = bf16[32,48,768]{2,1,0:T(8,128)(2,1)S(1)} async-done(((bf16[32,48,768]{2,1,0:T(8,128)(2,1)}), bf16[32,48,768]{2,1,0:T(8,128)(2,1)S(1)}, u32[]{:S(2)}, u32[]{:S(2)}) %all-to-all-start.1) | async-done | bytes 2359328 | tf_op jit(solution)/shard_map/all_to_all | solution.py:132
  348.2 5.2 %gather_fusion.3 = bf16[1024,768]{1,0:T(8,128)(2,1)} fusion(bf16[1536,768]{1,0:T(8,128)(2,1)S(1)} %bitcast.220, s32[1024]{0:T(1024)S(1)} %broadcast_clamp_fusion), kind=kCustom, calls=%fused_computation.3 | custom fusion | bytes 3149824 | tf_op jit(solution)/shard_map/jit(_take)/gather | solution.py:133
  355.5 1.6 fusion.72
  357.1 2.3 fusion.73
  359.5 2.4 collective-permute-start.5
  362.0 2.0 collective-permute-done.5
  364.0 2.4 collective-permute-start.6
  368.5 5.5 %collective-permute-start.7 = (f32[2,129,128]{2,1,0:T(8,128)S(1)}, f32[2,129,128]{2,1,0:T(8,128)S(1)}, u32[]{:S(2)}, u32[]{:S(2)}) collective-permute-start(f32[2,129,128]{2,1,0:T(8,128)S(1)} %select_add_fusion.6), channel_id=1, source_target_pairs={{0,16},{4,20},{8,24},{12,28},{16,32},{20,36},{24,40},{28,44},{32,4... | collective-permute-start | bytes 396296 | tf_op jit(solution)/shard_map/ppermute | solution.py:109
  374.0 2.0 collective-permute-done.7
  376.0 5.7 %collective-permute-start.8 = (f32[2,129,128]{2,1,0:T(8,128)S(1)}, f32[2,129,128]{2,1,0:T(8,128)S(1)}, u32[]{:S(2)}, u32[]{:S(2)}) collective-permute-start(f32[2,129,128]{2,1,0:T(8,128)S(1)} %select_add_fusion.5), channel_id=1, source_target_pairs={{0,32},{4,36},{8,40},{12,44},{16,48},{20,52},{24,56},{28,60},{32,6... | collective-permute-start | bytes 396296 | tf_op jit(solution)/shard_map/ppermute | solution.py:109
  383.8 4.8 collective-permute-start.9
  388.7 3.3 collective-permute-done.9
  392.1 2.1 fusion.69
  394.1 2.6 fusion.53
  396.9 4.8 gather_fusion.4
  401.7 29.2 %all_to_all.15 = bf16[32,48,256]{2,1,0:T(8,128)(2,1)S(1)} all-to-all(bf16[32,48,256]{2,1,0:T(8,128)(2,1)S(1)} %bitcast.241), channel_id=1, replica_groups=mesh['ctx'=32,'head'=4] {'ctx'}, dimensions={0} | all-to-all | bytes 1572864 | tf_op jit(solution)/shard_map/all_to_all | solution.py:132
  430.9 4.9 %gather_fusion.5 = bf16[1024,256]{1,0:T(8,128)(2,1)} fusion(bf16[1536,256]{1,0:T(8,128)(2,1)S(1)} %bitcast.234, s32[1024]{0:T(1024)S(1)} %broadcast_clamp_fusion), kind=kCustom, calls=%fused_computation.5 | custom fusion | bytes 1052672 | tf_op jit(solution)/shard_map/jit(_take)/gather | solution.py:133
  435.9 6.5 %slice.172 = bf16[4,6,128,1024]{3,2,1,0:T(8,128)(2,1)} slice(bf16[4,8,128,1024]{3,2,1,0:T(8,128)(2,1)} %bitcast.236), slice={[0:4], [0:6], [0:128], [0:1024]} | slice | bytes 12582912 | tf_op jit(solution)/shard_map/slice | solution.py:137
  442.4 2.0 slice.184
  444.4 12.1 %fusion.160 = f32[1024,1024]{1,0:T(8,128)} fusion(bf16[1024,3072]{1,0:T(8,128)(2,1)} %all-gather.5.cloned.1.call-done, bf16[3072,1024]{1,0:T(8,128)(2,1)} %bitcast.238), kind=kOutput, calls=%fused_computation.257 | convolution fusion | flops 6442450944 | bytes 16777216 | tf_op jit(solution)/shard_map/dot_general | solution.py:135
  456.5 11.8 %all-gather.7.cloned.1.call-done = bf16[1024,1024]{1,0:T(8,128)(2,1)} async-done(((bf16[1024,256]{1,0:T(8,128)(2,1)}), bf16[1024,1024]{1,0:T(8,128)(2,1)}) %all-gather.7.cloned.1.call-update) | async-done | bytes 2097168 | tf_op jit(solution)/shard_map/all_gather | solution.py:134
  468.3 6.5 %add_convert_fusion = bf16[1024,1024]{1,0:T(8,128)(2,1)} fusion(f32[1024,1024]{1,0:T(8,128)} %fusion.160, bf16[1024,1024]{1,0:T(8,128)(2,1)} %all-gather.7.cloned.1.call-done, bf16[1024,1024]{1,0:T(8,128)(2,1)S(1)} %bitcast.242), kind=kOutput, calls=%fused_computation.24 | convolution fusion | flops 2149580800 | bytes 10485760 | tf_op jit(solution)/shard_map/dot_general | solution.py:135
  (128 shorter events, 33.2 us)
Async XLA Ops:
  6.5 5.0 %copy-start.1 = (bf16[1024,1024]{1,0:T(8,128)(2,1)S(1)}, bf16[1024,1024]{1,0:T(8,128)(2,1)}, u32[]{:S(2)}) copy-start(bf16[1024,1024]{1,0:T(8,128)(2,1)} %param.7) | copy-start | bytes 6291460
  7.6 9.4 %copy-start.3 = (s32[32,1024]{1,0:T(8,128)}, s32[32,1024]{1,0:T(8,128)S(1)}, u32[]{:S(2)}) copy-start(s32[32,1024]{1,0:T(8,128)S(1)} %reshape.405) | copy-start | bytes 393220
  38.4 9.6 %copy-start.14 = (s32[32]{0:T(128)S(1)}, s32[32]{0:T(128)}, u32[]{:S(2)}) copy-start(s32[32]{0:T(128)} %param.11) | copy-start | bytes 388
  38.4 15.9 %copy-start.15 = (f32[8]{0:T(128)S(1)}, f32[8]{0:T(128)}, u32[]{:S(2)}) copy-start(f32[8]{0:T(128)} %param.12) | copy-start | bytes 100
  38.4 135.0 %all-to-all-start = ((bf16[32,48,3072]{2,1,0:T(8,128)(2,1)}), bf16[32,48,3072]{2,1,0:T(8,128)(2,1)}, u32[]{:S(2)}, u32[]{:S(2)}) async-start(bf16[32,48,3072]{2,1,0:T(8,128)(2,1)} %bitcast.221), calls=%async_computation | async-start | bytes 18874368 | tf_op jit(solution)/shard_map/all_to_all | solution.py:67
  54.3 0.6 copy-start.16
  199.0 4.9 %copy-start = (bf16[1024,3072]{0,1:T(8,128)(2,1)S(1)}, bf16[1024,3072]{0,1:T(8,128)(2,1)}, u32[]{:S(2)}) copy-start(bf16[1024,3072]{0,1:T(8,128)(2,1)} %copy.29) | copy-start | bytes 18874372
  216.3 26.9 %collective-permute-start = (f32[6,129,128]{2,1,0:T(8,128)S(1)}, f32[6,129,128]{2,1,0:T(8,128)S(1)}, u32[]{:S(2)}, u32[]{:S(2)}) collective-permute-start(f32[6,129,128]{2,1,0:T(8,128)S(1)} %pad_maximum_fusion.1), channel_id=1, source_target_pairs={{0,4},{4,8},{8,12},{12,16},{16,20},{20,24},{24,28},{28,32},{32,36}... | collective-permute-start | bytes 1188872 | tf_op jit(solution)/shard_map/ppermute | solution.py:109
  243.3 7.0 %collective-permute-start.1 = (f32[6,129,128]{2,1,0:T(8,128)S(1)}, f32[6,129,128]{2,1,0:T(8,128)S(1)}, u32[]{:S(2)}, u32[]{:S(2)}) collective-permute-start(f32[6,129,128]{2,1,0:T(8,128)S(1)} %select_add_fusion.3), channel_id=1, source_target_pairs={{0,8},{4,12},{8,16},{12,20},{16,24},{20,28},{24,32},{28,36},{32,40... | collective-permute-start | bytes 1188872 | tf_op jit(solution)/shard_map/ppermute | solution.py:109
  245.9 9.8 %copy-start.2 = (pred[1024,1024]{0,1:T(8,128)(4,1)S(1)}, pred[1024,1024]{0,1:T(8,128)(4,1)}, u32[]{:S(2)}) copy-start(pred[1024,1024]{0,1:T(8,128)(4,1)} %iota_compare_fusion.3) | copy-start | bytes 3145732
  245.9 9.8 %copy-start.5 = (bf16[1024,2,128]{0,2,1:T(8,128)(2,1)S(1)}, bf16[1024,2,128]{0,2,1:T(8,128)(2,1)}, u32[]{:S(2)}) copy-start(bf16[1024,2,128]{0,2,1:T(8,128)(2,1)} %slice.161) | copy-start | bytes 1572868
  250.4 10.7 %copy-start.4 = (bf16[1024,2,128]{2,0,1:T(8,128)(2,1)S(1)}, bf16[1024,2,128]{2,0,1:T(8,128)(2,1)}, u32[]{:S(2)}) copy-start(bf16[1024,2,128]{2,0,1:T(8,128)(2,1)} %slice.163) | copy-start | bytes 1572868
  250.4 15.2 %collective-permute-start.2 = (f32[6,129,128]{2,1,0:T(8,128)S(1)}, f32[6,129,128]{2,1,0:T(8,128)}, u32[]{:S(2)}, u32[]{:S(2)}) collective-permute-start(f32[6,129,128]{2,1,0:T(8,128)S(1)} %select_add_fusion.2), channel_id=1, source_target_pairs={{0,16},{4,20},{8,24},{12,28},{16,32},{20,36},{24,40},{28,44},{32,4... | collective-permute-start | bytes 1188872 | tf_op jit(solution)/shard_map/ppermute | solution.py:109
  261.1 4.4 copy-start.6
  261.1 4.4 copy-start.13
  261.1 6.0 %copy-start.11 = (bf16[1024,1,128]{0,2,1:T(8,128)(2,1)S(1)}, bf16[1024,1,128]{0,2,1:T(8,128)(2,1)}, u32[]{:S(2)}) copy-start(bf16[1024,1,128]{0,2,1:T(8,128)(2,1)} %get-tuple-element.68) | copy-start | bytes 786436
  261.1 6.0 %copy-start.12 = (bf16[1024,1,128]{0,2,1:T(8,128)(2,1)S(1)}, bf16[1024,1,128]{0,2,1:T(8,128)(2,1)}, u32[]{:S(2)}) copy-start(bf16[1024,1,128]{0,2,1:T(8,128)(2,1)} %get-tuple-element.69) | copy-start | bytes 786436
  265.6 2.8 copy-start.10
  265.7 6.4 %collective-permute-start.3 = (f32[6,129,128]{2,1,0:T(8,128)S(1)}, f32[6,129,128]{2,1,0:T(8,128)S(1)}, u32[]{:S(2)}, u32[]{:S(2)}) collective-permute-start(f32[6,129,128]{2,1,0:T(8,128)S(1)} %select_add_fusion.1), channel_id=1, source_target_pairs={{0,32},{4,36},{8,40},{12,44},{16,48},{20,52},{24,56},{28,60},{32,6... | collective-permute-start | bytes 1188872 | tf_op jit(solution)/shard_map/ppermute | solution.py:109
  268.4 19.2 %copy-start.8 = (bf16[1024,1,128]{0,2,1:T(8,128)(2,1)S(1)}, bf16[1024,1,128]{0,2,1:T(8,128)(2,1)}, u32[]{:S(2)}) copy-start(bf16[1024,1,128]{0,2,1:T(8,128)(2,1)} %get-tuple-element.73) | copy-start | bytes 786436
  268.4 19.2 %copy-start.9 = (bf16[1024,1,128]{0,2,1:T(8,128)(2,1)S(1)}, bf16[1024,1,128]{0,2,1:T(8,128)(2,1)}, u32[]{:S(2)}) copy-start(bf16[1024,1,128]{0,2,1:T(8,128)(2,1)} %get-tuple-element.74) | copy-start | bytes 786436
  272.1 16.8 %copy-start.7 = (bf16[1024,1,128]{2,0,1:T(8,128)(2,1)S(1)}, bf16[1024,1,128]{2,0,1:T(8,128)(2,1)}, u32[]{:S(2)}) copy-start(bf16[1024,1,128]{2,0,1:T(8,128)(2,1)} %get-tuple-element.72) | copy-start | bytes 786436
  272.1 21.5 %collective-permute-start.4 = (f32[6,129,128]{2,1,0:T(8,128)S(1)}, f32[6,129,128]{2,1,0:T(8,128)S(1)}, u32[]{:S(2)}, u32[]{:S(2)}) collective-permute-start(f32[6,129,128]{2,1,0:T(8,128)S(1)} %select_add_fusion), channel_id=1, source_target_pairs={{0,64},{4,68},{8,72},{12,76},{16,80},{20,84},{24,88},{28,92},{32,9... | collective-permute-start | bytes 1188872 | tf_op jit(solution)/shard_map/ppermute | solution.py:109
  288.4 5.3 %slice-start = ((s8[6291456]{0:T(1024)(128)(4,1)}), s8[4194304]{0:T(1024)(128)(4,1)S(1)}, s32[]{:S(2)}) async-start(s8[6291456]{0:T(1024)(128)(4,1)} %bitcast.230), calls=%async_computation.5 | async-start | bytes 8388608
  288.9 4.8 slice-start.1
  293.7 2.9 copy-start.18
  293.7 2.9 copy-start.19
  307.7 40.6 %all-to-all-start.1 = ((bf16[32,48,768]{2,1,0:T(8,128)(2,1)}), bf16[32,48,768]{2,1,0:T(8,128)(2,1)S(1)}, u32[]{:S(2)}, u32[]{:S(2)}) async-start(bf16[32,48,768]{2,1,0:T(8,128)(2,1)} %bitcast.235), calls=%async_computation.1 | async-start | bytes 4718592 | tf_op jit(solution)/shard_map/all_to_all | solution.py:132
  317.1 127.3 %all-gather.5.cloned.1.call-start = ((), (), s32[]{:S(2)}) async-start(), calls=%async_computation.3 | async-start | bytes 7864320 | tf_op jit(solution)/shard_map/all_gather | solution.py:134
  353.5 114.8 %all-gather.7.cloned.1.call-start = ((), (), s32[]{:S(2)}) async-start(), calls=%async_computation.4 | async-start | bytes 2621440 | tf_op jit(solution)/shard_map/all_gather | solution.py:134
  359.5 4.4 collective-permute-start.5
  364.0 4.5 collective-permute-start.6
  368.5 7.5 %collective-permute-start.7 = (f32[2,129,128]{2,1,0:T(8,128)S(1)}, f32[2,129,128]{2,1,0:T(8,128)S(1)}, u32[]{:S(2)}, u32[]{:S(2)}) collective-permute-start(f32[2,129,128]{2,1,0:T(8,128)S(1)} %select_add_fusion.6), channel_id=1, source_target_pairs={{0,16},{4,20},{8,24},{12,28},{16,32},{20,36},{24,40},{28,44},{32,4... | collective-permute-start | bytes 396296 | tf_op jit(solution)/shard_map/ppermute | solution.py:109
  376.0 7.8 %collective-permute-start.8 = (f32[2,129,128]{2,1,0:T(8,128)S(1)}, f32[2,129,128]{2,1,0:T(8,128)S(1)}, u32[]{:S(2)}, u32[]{:S(2)}) collective-permute-start(f32[2,129,128]{2,1,0:T(8,128)S(1)} %select_add_fusion.5), channel_id=1, source_target_pairs={{0,32},{4,36},{8,40},{12,44},{16,48},{20,52},{24,56},{28,60},{32,6... | collective-permute-start | bytes 396296 | tf_op jit(solution)/shard_map/ppermute | solution.py:109
  383.0 5.6 %copy-start.17 = (f32[8]{0:T(128)S(1)}, f32[8]{0:T(128)}, u32[]{:S(2)}) copy-start(f32[8]{0:T(128)} %copy-done.16) | copy-start | bytes 100
  383.8 8.2 %collective-permute-start.9 = (f32[2,129,128]{2,1,0:T(8,128)S(1)}, f32[2,129,128]{2,1,0:T(8,128)S(1)}, u32[]{:S(2)}, u32[]{:S(2)}) collective-permute-start(f32[2,129,128]{2,1,0:T(8,128)S(1)} %select_add_fusion.4), channel_id=1, source_target_pairs={{0,64},{4,68},{8,72},{12,76},{16,80},{20,84},{24,88},{28,92},{32,9... | collective-permute-start | bytes 396296 | tf_op jit(solution)/shard_map/ppermute | solution.py:109
Sparse Core Ops, SparseCore 0:
  353.6 64.3 all-gather.4
  436.0 32.2 all-gather.6

commit v5 on v4

--- a/solution.py
+++ b/solution.py
@@ -53,7 +53,7 @@
     causal = r_idx[:, None] >= r_idx[None, :]
     head_count = lax.axis_size("head")
     out_cols = out_weight.shape[1]
-    bounds = [0, heads - heads // 4, heads]
+    bounds = [0, heads // 2, heads]
     weight_rows = out_weight.reshape(head_count, heads, dh, out_cols)
     gate_all = jax.nn.sigmoid(mem_gate)
     shifts = []
@@ -62,10 +62,14 @@
         shifts.append(step)
         step *= 2
 
-    joined = jnp.concatenate([keys, values, queries], axis=1)
-    buffer = jnp.take(joined, slot_row, axis=0, mode="clip").reshape(n, cap, 3 * width)
-    got = lax.all_to_all(buffer, "ctx", 0, 0, tiled=True).reshape(slots, 3 * width)
-    arrived_rows = jnp.take(got, tok_slot, axis=0, mode="clip").reshape(seg, 3, heads, dh)
+    def dispatch(source):
+        buffer = jnp.take(source, slot_row, axis=0, mode="clip").reshape(n, cap, width)
+        got = lax.all_to_all(buffer, "ctx", 0, 0, tiled=True).reshape(slots, width)
+        return jnp.take(got, tok_slot, axis=0, mode="clip").reshape(seg, heads, dh)
+
+    key_all = dispatch(keys)
+    value_all = dispatch(values)
+    query_all = dispatch(queries)
 
     def local_attention(query_part, key_part, value_part):
         scores = jnp.einsum(
@@ -85,9 +89,9 @@
         group_width = group_heads * dh
         cuts = [first + round(group_heads * i / len(shifts)) for i in range(len(shifts) + 1)]
         cuts = [c - first for c in cuts]
-        key_heads = arrived_rows[:, 0, first:last]
-        value_heads = arrived_rows[:, 1, first:last]
-        query_heads = arrived_rows[:, 2, first:last]
+        key_heads = key_all[:, first:last]
+        value_heads = value_all[:, first:last]
+        query_heads = query_all[:, first:last]
 
         key_feat = feature(key_heads.astype(f32))
         delta_m = jnp.einsum(

time: 489 us -> 419 us (0.86)
  waiting for transfers between devices: 177 us -> 119 us
  starting transfers between devices: 85.8 us -> 77.7 us
  other arithmetic: 20.3 us -> 12.7 us
    all_to_all x1 -> x3, waiting for transfers between devices: 117 us -> 64.5 us  [dispatch(): got = lax.all_to_all(buffer, 'ctx', 0, 0, tiled=True).reshape(slots, width)]
    all_to_all x1, waiting for transfers between devices: 30.3 us -> 0.01 us  [one_group(): lax.all_to_all(outgoing, 'ctx', 0, 0, tiled=True)]
    all_gather x2, waiting for transfers between devices: 11.8 us -> 30.1 us  [one_group(): gathered = lax.all_gather(rows, 'head', axis=1, tiled=True)]
    ppermute x10, starting transfers between devices: 66.6 us -> 50 us  [one_group(): got = lax.ppermute(total, 'ctx', perm)]
    all_to_all x1 -> x3, starting transfers between devices: 9.47 us -> 19.1 us  [dispatch(): got = lax.all_to_all(buffer, 'ctx', 0, 0, tiled=True).reshape(slots, width)]
    concatenate x1 -> x0, other arithmetic: 5.41 us -> none  [per_device(): joined = jnp.concatenate([keys, values, queries], axis=1)]
    ppermute x10, waiting for transfers between devices: 18.6 us -> 24 us  [one_group(): got = lax.ppermute(total, 'ctx', perm)]
    sub x1 -> x0, matrix products: 5.32 us -> none  [local_attention(): weights = jnp.exp(scores - row_max)]
  transfers between devices with their start and end apart: 14 -> 16, of which waited for: 10 -> 11; matrix products, arithmetic and copies ran while one was open for 15% -> 31% of each run, Pallas kernels for 0% -> 0%
where the time goes in v5:
time: 419 us; the launch traced here: 412 us
  waiting for transfers between devices  119 us (28%)
  local copies, waits for them, and re-layouts  95.5 us (23%)
  starting transfers between devices  77.7 us (19%)
  matrix products  57.4 us (14%)
  blocking collectives  31.7 us (8%)
  between operations  18.3 us (4%)
  other arithmetic  12.7 us (3%)
    all_to_all x3, waiting for transfers between devices, dispatch(): got = lax.all_to_all(buffer, 'ctx', 0, 0, tiled=True).reshape(slots, width)  64.5 us
    ppermute x10, starting transfers between devices, one_group(): got = lax.ppermute(total, 'ctx', perm)  50 us
    all_to_all x1, blocking collectives, one_group(): lax.all_to_all(outgoing, 'ctx', 0, 0, tiled=True)  31.7 us
    all_gather x2, waiting for transfers between devices, one_group(): gathered = lax.all_gather(rows, 'head', axis=1, tiled=True)  30.1 us
    gather x4, local copies, waits for them, and re-layouts, dispatch(): return jnp.take(got, tok_slot, axis=0, mode='clip').reshape(seg, heads, dh)  25.3 us
    ppermute x10, waiting for transfers between devices, one_group(): got = lax.ppermute(total, 'ctx', perm)  24 us
    dot_general x2, matrix products, one_group(): jnp.dot(gathered, weight_rows[:, first:last].reshape(head_count * group_w...  21.2 us
    all_to_all x3, starting transfers between devices, dispatch(): got = lax.all_to_all(buffer, 'ctx', 0, 0, tiled=True).reshape(slots, width)  19.1 us
  transfers between devices with their start and end apart: 16, of which 11 were waited for; matrix products, arithmetic and copies ran while one was open for 31% of the time, Pallas kernels for 0%

profile of v5, /device:TPU:1, one launch (start us, length us, event | category | flops | bytes accessed | tf_op | source)
XLA Modules:
  0.0 412.0 jit_solution(13050558006056642406)
XLA Ops:
  9.0 5.8 %gather_fusion.4 = bf16[1536,1024]{1,0:T(8,128)(2,1)} fusion(bf16[1024,1024]{1,0:T(8,128)(2,1)S(1)} %copy-done, s32[2048]{0:T(1024)S(1)} %pad_clamp_fusion.1), kind=kCustom, calls=%fused_computation.4 | custom fusion | bytes 6297600 | tf_op jit(solution)/shard_map/jit(_take)/gather | solution.py:66
  14.8 8.8 %all-to-all-start.2 = ((bf16[32,48,1024]{2,1,0:T(8,128)(2,1)}), bf16[32,48,1024]{2,1,0:T(8,128)(2,1)}, u32[]{:S(2)}, u32[]{:S(2)}) async-start(bf16[32,48,1024]{2,1,0:T(8,128)(2,1)} %bitcast.224), calls=%async_computation.2 | async-start | bytes 6291456 | tf_op jit(solution)/shard_map/all_to_all | solution.py:67
  23.6 5.8 %gather_fusion = bf16[1536,1024]{1,0:T(8,128)(2,1)} fusion(bf16[1024,1024]{1,0:T(8,128)(2,1)S(1)} %copy-done.2, s32[2048]{0:T(1024)S(1)} %pad_clamp_fusion.1), kind=kCustom, calls=%fused_computation | custom fusion | bytes 6297600 | tf_op jit(solution)/shard_map/jit(_take)/gather | solution.py:66
  29.4 34.0 %all-to-all-done.2 = bf16[32,48,1024]{2,1,0:T(8,128)(2,1)} async-done(((bf16[32,48,1024]{2,1,0:T(8,128)(2,1)}), bf16[32,48,1024]{2,1,0:T(8,128)(2,1)}, u32[]{:S(2)}, u32[]{:S(2)}) %all-to-all-start.2) | async-done | bytes 3145760 | tf_op jit(solution)/shard_map/all_to_all | solution.py:67
  63.4 5.0 %all-to-all-start = ((bf16[32,48,1024]{2,1,0:T(8,128)(2,1)}), bf16[32,48,1024]{2,1,0:T(8,128)(2,1)}, u32[]{:S(2)}, u32[]{:S(2)}) async-start(bf16[32,48,1024]{2,1,0:T(8,128)(2,1)} %bitcast.222), calls=%async_computation | async-start | bytes 6291456 | tf_op jit(solution)/shard_map/all_to_all | solution.py:67
  76.6 5.8 %gather_fusion.2 = bf16[1536,1024]{1,0:T(8,128)(2,1)} fusion(bf16[1024,1024]{1,0:T(8,128)(2,1)S(1)} %copy-done.3, s32[2048]{0:T(1024)S(1)} %pad_clamp_fusion.1), kind=kCustom, calls=%fused_computation.2 | custom fusion | bytes 6297600 | tf_op jit(solution)/shard_map/jit(_take)/gather | solution.py:66
  84.3 24.0 %all-to-all-done = bf16[32,48,1024]{2,1,0:T(8,128)(2,1)} async-done(((bf16[32,48,1024]{2,1,0:T(8,128)(2,1)}), bf16[32,48,1024]{2,1,0:T(8,128)(2,1)}, u32[]{:S(2)}, u32[]{:S(2)}) %all-to-all-start) | async-done | bytes 3145760 | tf_op jit(solution)/shard_map/all_to_all | solution.py:67
  108.3 5.3 %all-to-all-start.1 = ((bf16[32,48,1024]{2,1,0:T(8,128)(2,1)}), bf16[32,48,1024]{2,1,0:T(8,128)(2,1)S(1)}, u32[]{:S(2)}, u32[]{:S(2)}) async-start(bf16[32,48,1024]{2,1,0:T(8,128)(2,1)} %bitcast.223), calls=%async_computation.1 | async-start | bytes 6291456 | tf_op jit(solution)/shard_map/all_to_all | solution.py:67
  113.6 8.3 %gather_fusion.5 = bf16[1024,1024]{1,0:T(8,128)(2,1)} fusion(bf16[1536,1024]{1,0:T(8,128)(2,1)} %bitcast.10, s32[1024]{0:T(1024)S(1)} %broadcast_clamp_fusion.1), kind=kCustom, calls=%fused_computation.5 | custom fusion | bytes 4198400 | tf_op jit(solution)/shard_map/jit(_take)/gather | solution.py:68
  121.9 2.2 copy.107
  124.1 4.6 %fusion.168 = (bf16[1024,1,128]{2,1,0:T(2,128)(2,1)}, bf16[1024,1,128]{2,1,0:T(2,128)(2,1)}, bf16[1024,1,128]{2,1,0:T(2,128)(2,1)}, bf16[1024,1,128]{2,1,0:T(2,1...) fusion(bf16[1024,8,128]{2,1,0:T(8,128)(2,1)S(1)} %bitcast.218), kind=kLoop, calls=%fused_computation.262 | loop fusion | bytes 4194304 | tf_op jit(solution)/shard_map/slice | solution.py:110
  129.5 8.3 %gather_fusion.1 = bf16[1024,1024]{1,0:T(8,128)(2,1)} fusion(bf16[1536,1024]{1,0:T(8,128)(2,1)} %bitcast.4, s32[1024]{0:T(1024)S(1)} %broadcast_clamp_fusion.1), kind=kCustom, calls=%fused_computation.1 | custom fusion | bytes 4198400 | tf_op jit(solution)/shard_map/jit(_take)/gather | solution.py:68
  137.8 2.2 copy.106
  140.0 2.0 fusion.169
  142.0 4.7 %fusion.167 = (bf16[1024,1,128]{2,1,0:T(2,128)(2,1)}, bf16[1024,1,128]{2,1,0:T(2,128)(2,1)}, bf16[1024,1,128]{2,1,0:T(2,128)(2,1)}, bf16[1024,1,128]{2,1,0:T(2,1...) fusion(bf16[1024,8,128]{2,1,0:T(8,128)(2,1)S(1)} %bitcast.221), kind=kLoop, calls=%fused_computation.261 | loop fusion | bytes 4194304 | tf_op jit(solution)/shard_map/slice | solution.py:110
  146.7 6.5 %all-to-all-done.1 = bf16[32,48,1024]{2,1,0:T(8,128)(2,1)S(1)} async-done(((bf16[32,48,1024]{2,1,0:T(8,128)(2,1)}), bf16[32,48,1024]{2,1,0:T(8,128)(2,1)S(1)}, u32[]{:S(2)}, u32[]{:S(2)}) %all-to-all-start.1) | async-done | bytes 3145760 | tf_op jit(solution)/shard_map/all_to_all | solution.py:67
  153.2 5.3 %gather_fusion.3 = bf16[1024,1024]{1,0:T(8,128)(2,1)} fusion(bf16[1536,1024]{1,0:T(8,128)(2,1)S(1)} %bitcast.215, s32[1024]{0:T(1024)S(1)} %broadcast_clamp_fusion.1), kind=kCustom, calls=%fused_computation.3 | custom fusion | bytes 4198400 | tf_op jit(solution)/shard_map/jit(_take)/gather | solution.py:68
  158.6 3.3 copy.48
  162.9 2.5 fusion.54
  165.5 1.9 fusion.46
  167.5 3.2 collective-permute-start
  173.5 2.5 fusion.47
  184.1 3.1 collective-permute-done.1
  187.3 5.6 %collective-permute-start.2 = (f32[4,129,128]{2,1,0:T(8,128)S(1)}, f32[4,129,128]{2,1,0:T(8,128)S(1)}, u32[]{:S(2)}, u32[]{:S(2)}) collective-permute-start(f32[4,129,128]{2,1,0:T(8,128)S(1)} %select_add_fusion.6), channel_id=1, source_target_pairs={{0,16},{4,20},{8,24},{12,28},{16,32},{20,36},{24,40},{28,44},{32,4... | collective-permute-start | bytes 792584 | tf_op jit(solution)/shard_map/ppermute | solution.py:113
  194.5 3.8 collective-permute-done.2
  198.3 6.5 %collective-permute-start.3 = (f32[4,129,128]{2,1,0:T(8,128)S(1)}, f32[4,129,128]{2,1,0:T(8,128)S(1)}, u32[]{:S(2)}, u32[]{:S(2)}) collective-permute-start(f32[4,129,128]{2,1,0:T(8,128)S(1)} %select_add_fusion.5), channel_id=1, source_target_pairs={{0,32},{4,36},{8,40},{12,44},{16,48},{20,52},{24,56},{28,60},{32,6... | collective-permute-start | bytes 792584 | tf_op jit(solution)/shard_map/ppermute | solution.py:113
  207.6 1.9 collective-permute-done.3
  209.6 4.2 %collective-permute-start.4 = (f32[4,129,128]{2,1,0:T(8,128)S(1)}, f32[4,129,128]{2,1,0:T(8,128)S(1)}, u32[]{:S(2)}, u32[]{:S(2)}) collective-permute-start(f32[4,129,128]{2,1,0:T(8,128)S(1)} %select_add_fusion.4), channel_id=1, source_target_pairs={{0,64},{4,68},{8,72},{12,76},{16,80},{20,84},{24,88},{28,92},{32,9... | collective-permute-start | bytes 792584 | tf_op jit(solution)/shard_map/ppermute | solution.py:113
  217.4 2.5 fusion.49
  219.9 3.1 fusion.29
  223.6 6.1 %collective-permute-start.5 = (f32[4,129,128]{2,1,0:T(8,128)S(1)}, f32[4,129,128]{2,1,0:T(8,128)S(1)}, u32[]{:S(2)}, u32[]{:S(2)}) collective-permute-start(f32[4,129,128]{2,1,0:T(8,128)S(1)} %pad_maximum_fusion.1), channel_id=1, source_target_pairs={{0,4},{4,8},{8,12},{12,16},{16,20},{20,24},{24,28},{28,32},{32,36}... | collective-permute-start | bytes 792584 | tf_op jit(solution)/shard_map/ppermute | solution.py:113
  229.8 5.4 %gather_fusion.6 = bf16[1536,512]{1,0:T(8,128)(2,1)} fusion(bf16[1024,512]{1,0:T(8,128)(2,1)S(1)} %copy.61, s32[2048]{0:T(1024)S(1)} %pad_clamp_fusion), kind=kCustom, calls=%fused_computation.6 | custom fusion | bytes 3151872 | tf_op jit(solution)/shard_map/jit(_take)/gather | solution.py:135
  235.2 8.2 %all-to-all-start.3 = ((bf16[32,48,512]{2,1,0:T(8,128)(2,1)}), bf16[32,48,512]{2,1,0:T(8,128)(2,1)S(1)}, u32[]{:S(2)}, u32[]{:S(2)}) async-start(bf16[32,48,512]{2,1,0:T(8,128)(2,1)} %bitcast.39), calls=%async_computation.3 | async-start | bytes 3145728 | tf_op jit(solution)/shard_map/all_to_all | solution.py:136
  246.6 3.4 collective-permute-start.6
  252.9 13.7 %collective-permute-done.6 = f32[4,129,128]{2,1,0:T(8,128)S(1)} collective-permute-done((f32[4,129,128]{2,1,0:T(8,128)S(1)}, f32[4,129,128]{2,1,0:T(8,128)S(1)}, u32[]{:S(2)}, u32[]{:S(2)}) %collective-permute-start.6) | collective-permute-done | bytes 264224 | tf_op jit(solution)/shard_map/ppermute | solution.py:113
  266.6 5.8 %collective-permute-start.7 = (f32[4,129,128]{2,1,0:T(8,128)S(1)}, f32[4,129,128]{2,1,0:T(8,128)S(1)}, u32[]{:S(2)}, u32[]{:S(2)}) collective-permute-start(f32[4,129,128]{2,1,0:T(8,128)S(1)} %select_add_fusion.2), channel_id=1, source_target_pairs={{0,16},{4,20},{8,24},{12,28},{16,32},{20,36},{24,40},{28,44},{32,4... | collective-permute-start | bytes 792584 | tf_op jit(solution)/shard_map/ppermute | solution.py:113
  273.4 5.1 %gather_fusion.7 = bf16[1024,512]{1,0:T(8,128)(2,1)} fusion(bf16[1536,512]{1,0:T(8,128)(2,1)S(1)} %bitcast.216, s32[1024]{0:T(1024)S(1)} %broadcast_clamp_fusion), kind=kCustom, calls=%fused_computation.7 | custom fusion | bytes 2101248 | tf_op jit(solution)/shard_map/jit(_take)/gather | solution.py:137
  278.6 6.1 %collective-permute-start.8 = (f32[4,129,128]{2,1,0:T(8,128)S(1)}, f32[4,129,128]{2,1,0:T(8,128)S(1)}, u32[]{:S(2)}, u32[]{:S(2)}) collective-permute-start(f32[4,129,128]{2,1,0:T(8,128)S(1)} %select_add_fusion.1), channel_id=1, source_target_pairs={{0,32},{4,36},{8,40},{12,44},{16,48},{20,52},{24,56},{28,60},{32,6... | collective-permute-start | bytes 792584 | tf_op jit(solution)/shard_map/ppermute | solution.py:113
  288.8 7.2 %collective-permute-start.9 = (f32[4,129,128]{2,1,0:T(8,128)S(1)}, f32[4,129,128]{2,1,0:T(8,128)S(1)}, u32[]{:S(2)}, u32[]{:S(2)}) collective-permute-start(f32[4,129,128]{2,1,0:T(8,128)S(1)} %select_add_fusion), channel_id=1, source_target_pairs={{0,64},{4,68},{8,72},{12,76},{16,80},{20,84},{24,88},{28,92},{32,9... | collective-permute-start | bytes 792584 | tf_op jit(solution)/shard_map/ppermute | solution.py:113
  299.3 2.5 fusion.42
  301.8 3.2 fusion.31
  305.5 4.8 %gather_fusion.8 = bf16[1536,512]{1,0:T(8,128)(2,1)S(1)} fusion(bf16[1024,512]{1,0:T(8,128)(2,1)S(1)} %copy.75, s32[2048]{0:T(1024)S(1)} %pad_clamp_fusion), kind=kCustom, calls=%fused_computation.8 | custom fusion | bytes 3151872 | tf_op jit(solution)/shard_map/jit(_take)/gather | solution.py:135
  310.4 31.7 %all_to_all.25 = bf16[32,48,512]{2,1,0:T(8,128)(2,1)S(1)} all-to-all(bf16[32,48,512]{2,1,0:T(8,128)(2,1)S(1)} %bitcast.231), channel_id=1, replica_groups=mesh['ctx'=32,'head'=4] {'ctx'}, dimensions={0} | all-to-all | bytes 3145728 | tf_op jit(solution)/shard_map/all_to_all | solution.py:136
  342.1 5.1 %gather_fusion.9 = bf16[1024,512]{1,0:T(8,128)(2,1)} fusion(bf16[1536,512]{1,0:T(8,128)(2,1)S(1)} %bitcast.217, s32[1024]{0:T(1024)S(1)} %broadcast_clamp_fusion), kind=kCustom, calls=%fused_computation.9 | custom fusion | bytes 2101248 | tf_op jit(solution)/shard_map/jit(_take)/gather | solution.py:137
  347.2 6.1 %fusion.164 = (bf16[4,4,128,1024]{3,2,1,0:T(8,128)(2,1)}, bf16[4,4,128,1024]{3,2,1,0:T(8,128)(2,1)}) fusion(bf16[4,8,128,1024]{3,2,1,0:T(8,128)(2,1)} %bitcast.227), kind=kLoop, calls=%fused_computation.258 | loop fusion | bytes 16777216 | tf_op jit(solution)/shard_map/slice | solution.py:141
  353.3 10.6 %fusion.171 = f32[1024,1024]{1,0:T(8,128)} fusion(bf16[1024,2048]{1,0:T(8,128)(2,1)} %all-gather.5.cloned.1.call-done, bf16[2048,1024]{1,0:T(8,128)(2,1)} %bitcast.233), kind=kOutput, calls=%fused_computation.265 | convolution fusion | flops 4294967296 | bytes 12582912 | tf_op jit(solution)/shard_map/dot_general | solution.py:139
  363.9 30.1 %all-gather.7.cloned.1.call-done = bf16[1024,2048]{1,0:T(8,128)(2,1)} async-done(((bf16[1024,512]{1,0:T(8,128)(2,1)}), bf16[1024,2048]{1,0:T(8,128)(2,1)}) %all-gather.7.cloned.1.call-update) | async-done | bytes 4194320 | tf_op jit(solution)/shard_map/all_gather | solution.py:138
  394.1 10.6 %add_convert_fusion = bf16[1024,1024]{1,0:T(8,128)(2,1)} fusion(f32[1024,1024]{1,0:T(8,128)} %fusion.171, bf16[1024,2048]{1,0:T(8,128)(2,1)} %all-gather.7.cloned.1.call-done, bf16[2048,1024]{1,0:T(8,128)(2,1)} %bitcast.232), kind=kOutput, calls=%fused_computation.26 | convolution fusion | flops 4297064448 | bytes 14680064 | tf_op jit(solution)/shard_map/dot_general | solution.py:139
  (173 shorter events, 44.9 us)
Async XLA Ops:
  14.8 8.8 %copy-start.2 = (bf16[1024,1024]{1,0:T(8,128)(2,1)S(1)}, bf16[1024,1024]{1,0:T(8,128)(2,1)}, u32[]{:S(2)}) copy-start(bf16[1024,1024]{1,0:T(8,128)(2,1)} %param.8) | copy-start | bytes 6291460
  14.8 48.6 %all-to-all-start.2 = ((bf16[32,48,1024]{2,1,0:T(8,128)(2,1)}), bf16[32,48,1024]{2,1,0:T(8,128)(2,1)}, u32[]{:S(2)}, u32[]{:S(2)}) async-start(bf16[32,48,1024]{2,1,0:T(8,128)(2,1)} %bitcast.224), calls=%async_computation.2 | async-start | bytes 6291456 | tf_op jit(solution)/shard_map/all_to_all | solution.py:67
  29.4 39.0 %copy-start.35 = (s32[32]{0:T(128)S(1)}, s32[32]{0:T(128)}, u32[]{:S(2)}) copy-start(s32[32]{0:T(128)} %param.11) | copy-start | bytes 388
  29.4 47.1 %copy-start.3 = (bf16[1024,1024]{1,0:T(8,128)(2,1)S(1)}, bf16[1024,1024]{1,0:T(8,128)(2,1)}, u32[]{:S(2)}) copy-start(bf16[1024,1024]{1,0:T(8,128)(2,1)} %param.9) | copy-start | bytes 6291460
  63.4 44.9 %all-to-all-start = ((bf16[32,48,1024]{2,1,0:T(8,128)(2,1)}), bf16[32,48,1024]{2,1,0:T(8,128)(2,1)}, u32[]{:S(2)}, u32[]{:S(2)}) async-start(bf16[32,48,1024]{2,1,0:T(8,128)(2,1)} %bitcast.222), calls=%async_computation | async-start | bytes 6291456 | tf_op jit(solution)/shard_map/all_to_all | solution.py:67
  76.5 5.8 %copy-start.36 = (f32[8]{0:T(128)S(1)}, f32[8]{0:T(128)}, u32[]{:S(2)}) copy-start(f32[8]{0:T(128)} %param.12) | copy-start | bytes 100
  108.3 45.0 %all-to-all-start.1 = ((bf16[32,48,1024]{2,1,0:T(8,128)(2,1)}), bf16[32,48,1024]{2,1,0:T(8,128)(2,1)S(1)}, u32[]{:S(2)}, u32[]{:S(2)}) async-start(bf16[32,48,1024]{2,1,0:T(8,128)(2,1)} %bitcast.223), calls=%async_computation.1 | async-start | bytes 6291456 | tf_op jit(solution)/shard_map/all_to_all | solution.py:67
  124.1 4.6 %copy-start.4 = (bf16[128,8,8,128]{3,2,1,0:T(8,128)(2,1)}, bf16[128,8,8,128]{3,2,1,0:T(8,128)(2,1)S(1)}, u32[]{:S(2)}) copy-start(bf16[128,8,8,128]{3,2,1,0:T(8,128)(2,1)S(1)} %copy.107) | copy-start | bytes 6291460
  158.6 4.4 %copy-start.7 = (bf16[1024,4,128]{2,1,0:T(4,128)(2,1)S(1)}, bf16[1024,4,128]{2,1,0:T(4,128)(2,1)}, u32[]{:S(2)}) copy-start(bf16[1024,4,128]{2,1,0:T(4,128)(2,1)} %get-tuple-element.138) | copy-start | bytes 3145732
  161.9 3.6 copy-start.6
  162.9 4.5 %copy-start.22 = (bf16[1024,1,128]{2,1,0:T(2,128)(2,1)S(1)}, bf16[1024,1,128]{2,1,0:T(2,128)(2,1)}, u32[]{:S(2)}) copy-start(bf16[1024,1,128]{2,1,0:T(2,128)(2,1)} %get-tuple-element.128) | copy-start | bytes 786436
  162.9 7.8 %copy-start.31 = (bf16[1024,1,128]{2,0,1:T(8,128)(2,1)S(1)}, bf16[1024,1,128]{2,0,1:T(8,128)(2,1)}, u32[]{:S(2)}) copy-start(bf16[1024,1,128]{2,0,1:T(8,128)(2,1)} %copy.86) | copy-start | bytes 786436
  167.5 12.0 %collective-permute-start = (f32[4,129,128]{2,1,0:T(8,128)S(1)}, f32[4,129,128]{2,1,0:T(8,128)S(1)}, u32[]{:S(2)}, u32[]{:S(2)}) collective-permute-start(f32[4,129,128]{2,1,0:T(8,128)S(1)} %pad_maximum_fusion), channel_id=1, source_target_pairs={{0,4},{4,8},{8,12},{12,16},{16,20},{20,24},{24,28},{28,32},{32,36}... | collective-permute-start | bytes 792584 | tf_op jit(solution)/shard_map/ppermute | solution.py:113
  173.5 3.4 copy-start.15
  173.5 4.1 %copy-start.14 = (bf16[1024,1,128]{2,1,0:T(2,128)(2,1)S(1)}, bf16[1024,1,128]{2,1,0:T(2,128)(2,1)}, u32[]{:S(2)}) copy-start(bf16[1024,1,128]{2,1,0:T(2,128)(2,1)} %get-tuple-element.133) | copy-start | bytes 786436
  173.5 4.2 %copy-start.13 = (bf16[1024,1,128]{2,1,0:T(2,128)(2,1)S(1)}, bf16[1024,1,128]{2,1,0:T(2,128)(2,1)}, u32[]{:S(2)}) copy-start(bf16[1024,1,128]{2,1,0:T(2,128)(2,1)} %get-tuple-element.134) | copy-start | bytes 786436
  173.5 4.2 %copy-start.12 = (bf16[1024,1,128]{2,1,0:T(2,128)(2,1)S(1)}, bf16[1024,1,128]{2,1,0:T(2,128)(2,1)}, u32[]{:S(2)}) copy-start(bf16[1024,1,128]{2,1,0:T(2,128)(2,1)} %get-tuple-element.135) | copy-start | bytes 786436
  173.5 4.2 %copy-start.21 = (bf16[1024,1,128]{2,1,0:T(2,128)(2,1)S(1)}, bf16[1024,1,128]{2,1,0:T(2,128)(2,1)}, u32[]{:S(2)}) copy-start(bf16[1024,1,128]{2,1,0:T(2,128)(2,1)} %get-tuple-element.123) | copy-start | bytes 786436
  173.5 5.0 %copy-start.20 = (bf16[1024,1,128]{2,1,0:T(2,128)(2,1)S(1)}, bf16[1024,1,128]{2,1,0:T(2,128)(2,1)}, u32[]{:S(2)}) copy-start(bf16[1024,1,128]{2,1,0:T(2,128)(2,1)} %get-tuple-element.124) | copy-start | bytes 786436
  176.1 3.2 copy-start.19
  176.1 3.2 copy-start.18
  176.1 3.2 copy-start.17
  179.5 7.7 %collective-permute-start.1 = (f32[4,129,128]{2,1,0:T(8,128)S(1)}, f32[4,129,128]{2,1,0:T(8,128)S(1)}, u32[]{:S(2)}, u32[]{:S(2)}) collective-permute-start(f32[4,129,128]{2,1,0:T(8,128)S(1)} %select_add_fusion.7), channel_id=1, source_target_pairs={{0,8},{4,12},{8,16},{12,20},{16,24},{20,28},{24,32},{28,36},{32,40... | collective-permute-start | bytes 792584 | tf_op jit(solution)/shard_map/ppermute | solution.py:113
  182.6 10.2 %copy-start.5 = (bf16[128,8,8,128]{3,2,1,0:T(8,128)(2,1)S(1)}, bf16[128,8,8,128]{3,2,1,0:T(8,128)(2,1)}, u32[]{:S(2)}) copy-start(bf16[128,8,8,128]{3,2,1,0:T(8,128)(2,1)} %copy-done.4) | copy-start | bytes 6291460
  187.3 11.0 %collective-permute-start.2 = (f32[4,129,128]{2,1,0:T(8,128)S(1)}, f32[4,129,128]{2,1,0:T(8,128)S(1)}, u32[]{:S(2)}, u32[]{:S(2)}) collective-permute-start(f32[4,129,128]{2,1,0:T(8,128)S(1)} %select_add_fusion.6), channel_id=1, source_target_pairs={{0,16},{4,20},{8,24},{12,28},{16,32},{20,36},{24,40},{28,44},{32,4... | collective-permute-start | bytes 792584 | tf_op jit(solution)/shard_map/ppermute | solution.py:113
  198.3 11.2 %collective-permute-start.3 = (f32[4,129,128]{2,1,0:T(8,128)S(1)}, f32[4,129,128]{2,1,0:T(8,128)S(1)}, u32[]{:S(2)}, u32[]{:S(2)}) collective-permute-start(f32[4,129,128]{2,1,0:T(8,128)S(1)} %select_add_fusion.5), channel_id=1, source_target_pairs={{0,32},{4,36},{8,40},{12,44},{16,48},{20,52},{24,56},{28,60},{32,6... | collective-permute-start | bytes 792584 | tf_op jit(solution)/shard_map/ppermute | solution.py:113
  209.6 7.7 %collective-permute-start.4 = (f32[4,129,128]{2,1,0:T(8,128)S(1)}, f32[4,129,128]{2,1,0:T(8,128)S(1)}, u32[]{:S(2)}, u32[]{:S(2)}) collective-permute-start(f32[4,129,128]{2,1,0:T(8,128)S(1)} %select_add_fusion.4), channel_id=1, source_target_pairs={{0,64},{4,68},{8,72},{12,76},{16,80},{20,84},{24,88},{28,92},{32,9... | collective-permute-start | bytes 792584 | tf_op jit(solution)/shard_map/ppermute | solution.py:113
  216.6 3.3 copy-start.33
  216.6 3.3 copy-start.34
  223.6 20.1 %copy-start.29 = (bf16[1024,1,128]{2,0,1:T(8,128)(2,1)S(1)}, bf16[1024,1,128]{2,0,1:T(8,128)(2,1)}, u32[]{:S(2)}) copy-start(bf16[1024,1,128]{2,0,1:T(8,128)(2,1)} %copy.97) | copy-start | bytes 786436
  223.6 20.1 %copy-start.30 = (bf16[1024,1,128]{2,0,1:T(8,128)(2,1)S(1)}, bf16[1024,1,128]{2,0,1:T(8,128)(2,1)}, u32[]{:S(2)}) copy-start(bf16[1024,1,128]{2,0,1:T(8,128)(2,1)} %copy.98) | copy-start | bytes 786436
  223.6 22.9 %collective-permute-start.5 = (f32[4,129,128]{2,1,0:T(8,128)S(1)}, f32[4,129,128]{2,1,0:T(8,128)S(1)}, u32[]{:S(2)}, u32[]{:S(2)}) collective-permute-start(f32[4,129,128]{2,1,0:T(8,128)S(1)} %pad_maximum_fusion.1), channel_id=1, source_target_pairs={{0,4},{4,8},{8,12},{12,16},{16,20},{20,24},{24,28},{28,32},{32,36}... | collective-permute-start | bytes 792584 | tf_op jit(solution)/shard_map/ppermute | solution.py:113
  235.2 38.2 %all-to-all-start.3 = ((bf16[32,48,512]{2,1,0:T(8,128)(2,1)}), bf16[32,48,512]{2,1,0:T(8,128)(2,1)S(1)}, u32[]{:S(2)}, u32[]{:S(2)}) async-start(bf16[32,48,512]{2,1,0:T(8,128)(2,1)} %bitcast.39), calls=%async_computation.3 | async-start | bytes 3145728 | tf_op jit(solution)/shard_map/all_to_all | solution.py:136
  243.4 109.9 %all-gather.5.cloned.1.call-start = ((), (), s32[]{:S(2)}) async-start(), calls=%async_computation.5 | async-start | bytes 5242880 | tf_op jit(solution)/shard_map/all_gather | solution.py:138
  244.9 5.1 %copy-start.27 = (bf16[1024,1,128]{2,0,1:T(8,128)(2,1)S(1)}, bf16[1024,1,128]{2,0,1:T(8,128)(2,1)}, u32[]{:S(2)}) copy-start(bf16[1024,1,128]{2,0,1:T(8,128)(2,1)} %copy.99) | copy-start | bytes 786436
  245.0 5.1 %copy-start.28 = (bf16[1024,1,128]{2,0,1:T(8,128)(2,1)S(1)}, bf16[1024,1,128]{2,0,1:T(8,128)(2,1)}, u32[]{:S(2)}) copy-start(bf16[1024,1,128]{2,0,1:T(8,128)(2,1)} %copy.100) | copy-start | bytes 786436
  246.6 4.7 %copy-start.25 = (bf16[1024,1,128]{0,2,1:T(8,128)(2,1)S(1)}, bf16[1024,1,128]{0,2,1:T(8,128)(2,1)}, u32[]{:S(2)}) copy-start(bf16[1024,1,128]{0,2,1:T(8,128)(2,1)} %get-tuple-element.88) | copy-start | bytes 786436
  246.6 20.0 %collective-permute-start.6 = (f32[4,129,128]{2,1,0:T(8,128)S(1)}, f32[4,129,128]{2,1,0:T(8,128)S(1)}, u32[]{:S(2)}, u32[]{:S(2)}) collective-permute-start(f32[4,129,128]{2,1,0:T(8,128)S(1)} %select_add_fusion.3), channel_id=1, source_target_pairs={{0,8},{4,12},{8,16},{12,20},{16,24},{20,28},{24,32},{28,36},{32,40... | collective-permute-start | bytes 792584 | tf_op jit(solution)/shard_map/ppermute | solution.py:113
  251.3 21.2 %copy-start.9 = (bf16[1024,1,128]{2,1,0:T(2,128)(2,1)S(1)}, bf16[1024,1,128]{2,1,0:T(2,128)(2,1)}, u32[]{:S(2)}) copy-start(bf16[1024,1,128]{2,1,0:T(2,128)(2,1)} %get-tuple-element.129) | copy-start | bytes 786436
  251.3 21.2 %copy-start.8 = (bf16[1024,1,128]{2,1,0:T(2,128)(2,1)S(1)}, bf16[1024,1,128]{2,1,0:T(2,128)(2,1)}, u32[]{:S(2)}) copy-start(bf16[1024,1,128]{2,1,0:T(2,128)(2,1)} %get-tuple-element.130) | copy-start | bytes 786436
  251.3 21.3 %copy-start.11 = (bf16[1024,1,128]{2,1,0:T(2,128)(2,1)S(1)}, bf16[1024,1,128]{2,1,0:T(2,128)(2,1)}, u32[]{:S(2)}) copy-start(bf16[1024,1,128]{2,1,0:T(2,128)(2,1)} %get-tuple-element.121) | copy-start | bytes 786436
  251.3 21.3 %copy-start.10 = (bf16[1024,1,128]{2,1,0:T(2,128)(2,1)S(1)}, bf16[1024,1,128]{2,1,0:T(2,128)(2,1)}, u32[]{:S(2)}) copy-start(bf16[1024,1,128]{2,1,0:T(2,128)(2,1)} %get-tuple-element.122) | copy-start | bytes 786436
  266.6 11.9 %collective-permute-start.7 = (f32[4,129,128]{2,1,0:T(8,128)S(1)}, f32[4,129,128]{2,1,0:T(8,128)S(1)}, u32[]{:S(2)}, u32[]{:S(2)}) collective-permute-start(f32[4,129,128]{2,1,0:T(8,128)S(1)} %select_add_fusion.2), channel_id=1, source_target_pairs={{0,16},{4,20},{8,24},{12,28},{16,32},{20,36},{24,40},{28,44},{32,4... | collective-permute-start | bytes 792584 | tf_op jit(solution)/shard_map/ppermute | solution.py:113
  278.5 115.6 %all-gather.7.cloned.1.call-start = ((), (), s32[]{:S(2)}) async-start(), calls=%async_computation.6 | async-start | bytes 5242880 | tf_op jit(solution)/shard_map/all_gather | solution.py:138
  278.6 8.3 %copy-start.24 = (bf16[1024,1,128]{0,2,1:T(8,128)(2,1)S(1)}, bf16[1024,1,128]{0,2,1:T(8,128)(2,1)}, u32[]{:S(2)}) copy-start(bf16[1024,1,128]{0,2,1:T(8,128)(2,1)} %get-tuple-element.94) | copy-start | bytes 786436
  278.6 10.2 %collective-permute-start.8 = (f32[4,129,128]{2,1,0:T(8,128)S(1)}, f32[4,129,128]{2,1,0:T(8,128)S(1)}, u32[]{:S(2)}, u32[]{:S(2)}) collective-permute-start(f32[4,129,128]{2,1,0:T(8,128)S(1)} %select_add_fusion.1), channel_id=1, source_target_pairs={{0,32},{4,36},{8,40},{12,44},{16,48},{20,52},{24,56},{28,60},{32,6... | collective-permute-start | bytes 792584 | tf_op jit(solution)/shard_map/ppermute | solution.py:113
  288.8 10.4 %collective-permute-start.9 = (f32[4,129,128]{2,1,0:T(8,128)S(1)}, f32[4,129,128]{2,1,0:T(8,128)S(1)}, u32[]{:S(2)}, u32[]{:S(2)}) collective-permute-start(f32[4,129,128]{2,1,0:T(8,128)S(1)} %select_add_fusion), channel_id=1, source_target_pairs={{0,64},{4,68},{8,72},{12,76},{16,80},{20,84},{24,88},{28,92},{32,9... | collective-permute-start | bytes 792584 | tf_op jit(solution)/shard_map/ppermute | solution.py:113
  394.1 10.6 %copy-start.1 = (bf16[1024,1024]{1,0:T(8,128)(2,1)S(1)}, bf16[1024,1024]{1,0:T(8,128)(2,1)}, u32[]{:S(2)}) copy-start(bf16[1024,1024]{1,0:T(8,128)(2,1)} %param.7) | copy-start | bytes 6291460
  (7 other events, 17.9 us)
Sparse Core Ops, SparseCore 0:
  278.6 51.5 all-gather.4
  347.3 46.6 all-gather.6

commit v6 on v5

--- a/solution.py
+++ b/solution.py
@@ -54,7 +54,7 @@
     head_count = lax.axis_size("head")
     out_cols = out_weight.shape[1]
     bounds = [0, heads // 2, heads]
-    weight_rows = out_weight.reshape(head_count, heads, dh, out_cols)
+    weight_blocks = out_weight.reshape(head_count, width, out_cols)
     gate_all = jax.nn.sigmoid(mem_gate)
     shifts = []
     step = 1
@@ -135,12 +135,19 @@
         outgoing = jnp.take(combined, pslot, axis=0, mode="clip").reshape(n, cap, group_width)
         incoming = lax.all_to_all(outgoing, "ctx", 0, 0, tiled=True).reshape(slots, group_width)
         rows = jnp.take(incoming, send_slot, axis=0, mode="clip")
-        gathered = lax.all_gather(rows, "head", axis=1, tiled=True)
-        part = jnp.dot(
-            gathered,
-            weight_rows[:, first:last].reshape(head_count * group_width, out_cols),
-            preferred_element_type=f32,
-        )
+        head_index = lax.axis_index("head")
+
+        def project(block, source):
+            weight = lax.dynamic_index_in_dim(weight_blocks, source, 0, keepdims=False)
+            return jnp.dot(
+                block, weight[first * dh:last * dh], preferred_element_type=f32
+            )
+
+        part = project(rows, head_index)
+        for shift in range(1, head_count):
+            perm = [(j, (j + shift) % head_count) for j in range(head_count)]
+            arrived = lax.ppermute(rows, "head", perm)
+            part = part + project(arrived, (head_index + head_count - shift) % head_count)
         return part, combined
 
     summed, hold = one_group(0, None)

time: 419 us -> 451 us (1.076)
  waiting for transfers between devices: 119 us -> 164 us
  blocking collectives: 31.7 us -> 0 us
  starting transfers between devices: 77.7 us -> 98 us
  matrix products: 57.4 us -> 73.8 us
  between operations: 18.3 us -> 4.38 us
  local copies, waits for them, and re-layouts: 95.5 us -> 89.8 us
    ppermute x0 -> x6, waiting for transfers between devices: none -> 71.2 us  [one_group(): arrived = lax.ppermute(rows, 'head', perm)]
    all_to_all x1 -> x0, blocking collectives: 31.7 us -> none  [one_group(): lax.all_to_all(outgoing, 'ctx', 0, 0, tiled=True)]
    all_gather x2 -> x0, waiting for transfers between devices: 30.1 us -> none  [one_group(): gathered = lax.all_gather(rows, 'head', axis=1, tiled=True)]
    dot_general x2 -> x8, matrix products: 21.2 us -> 36.7 us  [project(): jnp.dot(block, weight[first * dh:last * dh], preferred_element_type=f32)]
    all_to_all x1 -> x2, starting transfers between devices: 8.23 us -> 20.8 us  [one_group(): lax.all_to_all(outgoing, 'ctx', 0, 0, tiled=True)]
    ppermute x0 -> x6, starting transfers between devices: none -> 9.79 us  [one_group(): arrived = lax.ppermute(rows, 'head', perm)]
    slice x1 -> x0, local copies, waits for them, and re-layouts: 6.1 us -> none  [one_group(): weight_rows[:, first:last].reshape(head_count * group_width, out_cols)]
  transfers between devices with their start and end apart: 16 -> 21, of which waited for: 11 -> 15; matrix products, arithmetic and copies ran while one was open for 31% -> 31% of each run, Pallas kernels for 0% -> 0%
where the time goes in v6:
time: 451 us; the launch traced here: 443 us
  waiting for transfers between devices  164 us (36%)
  starting transfers between devices  98 us (22%)
  local copies, waits for them, and re-layouts  89.8 us (20%)
  matrix products  73.8 us (16%)
  other arithmetic  13.2 us (3%)
    ppermute x6, waiting for transfers between devices, one_group(): arrived = lax.ppermute(rows, 'head', perm)  71.2 us
    all_to_all x3, waiting for transfers between devices, dispatch(): got = lax.all_to_all(buffer, 'ctx', 0, 0, tiled=True).reshape(slots, width)  64.9 us
    ppermute x10, starting transfers between devices, one_group(): got = lax.ppermute(total, 'ctx', perm)  48.3 us
    dot_general x8, matrix products, project(): jnp.dot(block, weight[first * dh:last * dh], preferred_element_type=f32)  36.7 us
    ppermute x10, waiting for transfers between devices, one_group(): got = lax.ppermute(total, 'ctx', perm)  27.9 us
    gather x4, local copies, waits for them, and re-layouts, dispatch(): return jnp.take(got, tok_slot, axis=0, mode='clip').reshape(seg, heads, dh)  25.1 us
    all_to_all x2, starting transfers between devices, one_group(): lax.all_to_all(outgoing, 'ctx', 0, 0, tiled=True)  20.8 us
    all_to_all x3, starting transfers between devices, dispatch(): got = lax.all_to_all(buffer, 'ctx', 0, 0, tiled=True).reshape(slots, width)  19.1 us
  transfers between devices with their start and end apart: 21, of which 15 were waited for; matrix products, arithmetic and copies ran while one was open for 31% of the time, Pallas kernels for 0%

profile of v6, /device:TPU:1, one launch (start us, length us, event | category | flops | bytes accessed | tf_op | source)
XLA Modules:
  0.0 443.3 jit_solution(10984195118910749621)
XLA Ops:
  2.5 5.8 %gather_fusion.4 = bf16[1536,1024]{1,0:T(8,128)(2,1)} fusion(bf16[1024,1024]{1,0:T(8,128)(2,1)S(1)} %copy-done, s32[2048]{0:T(1024)S(1)} %pad_clamp_fusion.1), kind=kCustom, calls=%fused_computation.4 | custom fusion | bytes 6297600 | tf_op jit(solution)/shard_map/jit(_take)/gather | solution.py:66
  8.3 8.8 %all-to-all-start.2 = ((bf16[32,48,1024]{2,1,0:T(8,128)(2,1)}), bf16[32,48,1024]{2,1,0:T(8,128)(2,1)}, u32[]{:S(2)}, u32[]{:S(2)}) async-start(bf16[32,48,1024]{2,1,0:T(8,128)(2,1)} %bitcast.252), calls=%async_computation.2 | async-start | bytes 6291456 | tf_op jit(solution)/shard_map/all_to_all | solution.py:67
  17.1 5.8 %gather_fusion = bf16[1536,1024]{1,0:T(8,128)(2,1)} fusion(bf16[1024,1024]{1,0:T(8,128)(2,1)S(1)} %copy-done.2, s32[2048]{0:T(1024)S(1)} %pad_clamp_fusion.1), kind=kCustom, calls=%fused_computation | custom fusion | bytes 6297600 | tf_op jit(solution)/shard_map/jit(_take)/gather | solution.py:66
  22.9 34.0 %all-to-all-done.2 = bf16[32,48,1024]{2,1,0:T(8,128)(2,1)} async-done(((bf16[32,48,1024]{2,1,0:T(8,128)(2,1)}), bf16[32,48,1024]{2,1,0:T(8,128)(2,1)}, u32[]{:S(2)}, u32[]{:S(2)}) %all-to-all-start.2) | async-done | bytes 3145760 | tf_op jit(solution)/shard_map/all_to_all | solution.py:67
  56.9 5.0 %all-to-all-start = ((bf16[32,48,1024]{2,1,0:T(8,128)(2,1)}), bf16[32,48,1024]{2,1,0:T(8,128)(2,1)}, u32[]{:S(2)}, u32[]{:S(2)}) async-start(bf16[32,48,1024]{2,1,0:T(8,128)(2,1)} %bitcast.251), calls=%async_computation | async-start | bytes 6291456 | tf_op jit(solution)/shard_map/all_to_all | solution.py:67
  65.3 5.8 %gather_fusion.2 = bf16[1536,1024]{1,0:T(8,128)(2,1)} fusion(bf16[1024,1024]{1,0:T(8,128)(2,1)S(1)} %copy-done.3, s32[2048]{0:T(1024)S(1)} %pad_clamp_fusion.1), kind=kCustom, calls=%fused_computation.2 | custom fusion | bytes 6297600 | tf_op jit(solution)/shard_map/jit(_take)/gather | solution.py:66
  73.1 28.7 %all-to-all-done = bf16[32,48,1024]{2,1,0:T(8,128)(2,1)} async-done(((bf16[32,48,1024]{2,1,0:T(8,128)(2,1)}), bf16[32,48,1024]{2,1,0:T(8,128)(2,1)}, u32[]{:S(2)}, u32[]{:S(2)}) %all-to-all-start) | async-done | bytes 3145760 | tf_op jit(solution)/shard_map/all_to_all | solution.py:67
  101.8 5.3 %all-to-all-start.1 = ((bf16[32,48,1024]{2,1,0:T(8,128)(2,1)}), bf16[32,48,1024]{2,1,0:T(8,128)(2,1)S(1)}, u32[]{:S(2)}, u32[]{:S(2)}) async-start(bf16[32,48,1024]{2,1,0:T(8,128)(2,1)} %bitcast.250), calls=%async_computation.1 | async-start | bytes 6291456 | tf_op jit(solution)/shard_map/all_to_all | solution.py:67
  111.5 8.3 %gather_fusion.5 = bf16[1024,1024]{1,0:T(8,128)(2,1)} fusion(bf16[1536,1024]{1,0:T(8,128)(2,1)} %bitcast.10, s32[1024]{0:T(1024)S(1)} %broadcast_clamp_fusion.1), kind=kCustom, calls=%fused_computation.5 | custom fusion | bytes 4198400 | tf_op jit(solution)/shard_map/jit(_take)/gather | solution.py:68
  122.0 4.6 %fusion.183 = (bf16[1024,1,128]{2,1,0:T(2,128)(2,1)}, bf16[1024,1,128]{2,1,0:T(2,128)(2,1)}, bf16[1024,1,128]{2,1,0:T(2,128)(2,1)}, bf16[1024,1,128]{2,1,0:T(2,1...) fusion(bf16[1024,8,128]{2,1,0:T(8,128)(2,1)S(1)} %bitcast.246), kind=kLoop, calls=%fused_computation.285 | loop fusion | bytes 4194304 | tf_op jit(solution)/shard_map/slice | solution.py:110
  127.3 8.3 %gather_fusion.1 = bf16[1024,1024]{1,0:T(8,128)(2,1)} fusion(bf16[1536,1024]{1,0:T(8,128)(2,1)} %bitcast.4, s32[1024]{0:T(1024)S(1)} %broadcast_clamp_fusion.1), kind=kCustom, calls=%fused_computation.1 | custom fusion | bytes 4198400 | tf_op jit(solution)/shard_map/jit(_take)/gather | solution.py:68
  139.9 4.6 %fusion.182 = (bf16[1024,1,128]{2,1,0:T(2,128)(2,1)}, bf16[1024,1,128]{2,1,0:T(2,128)(2,1)}, bf16[1024,1,128]{2,1,0:T(2,128)(2,1)}, bf16[1024,1,128]{2,1,0:T(2,1...) fusion(bf16[1024,8,128]{2,1,0:T(8,128)(2,1)S(1)} %bitcast.249), kind=kLoop, calls=%fused_computation.284 | loop fusion | bytes 4194304 | tf_op jit(solution)/shard_map/slice | solution.py:110
  146.7 5.3 %gather_fusion.3 = bf16[1024,1024]{1,0:T(8,128)(2,1)} fusion(bf16[1536,1024]{1,0:T(8,128)(2,1)S(1)} %bitcast.243, s32[1024]{0:T(1024)S(1)} %broadcast_clamp_fusion.1), kind=kCustom, calls=%fused_computation.3 | custom fusion | bytes 4198400 | tf_op jit(solution)/shard_map/jit(_take)/gather | solution.py:68
  152.0 3.2 copy.48
  156.3 2.5 fusion.54
  160.8 3.2 collective-permute-start
  166.9 2.5 fusion.47
  175.6 3.1 collective-permute-done.1
  178.7 5.9 %collective-permute-start.2 = (f32[4,129,128]{2,1,0:T(8,128)S(1)}, f32[4,129,128]{2,1,0:T(8,128)S(1)}, u32[]{:S(2)}, u32[]{:S(2)}) collective-permute-start(f32[4,129,128]{2,1,0:T(8,128)S(1)} %select_add_fusion.6), channel_id=1, source_target_pairs={{0,16},{4,20},{8,24},{12,28},{16,32},{20,36},{24,40},{28,44},{32,4... | collective-permute-start | bytes 792584 | tf_op jit(solution)/shard_map/ppermute | solution.py:113
  186.2 3.5 collective-permute-done.2
  189.8 6.0 %collective-permute-start.3 = (f32[4,129,128]{2,1,0:T(8,128)S(1)}, f32[4,129,128]{2,1,0:T(8,128)S(1)}, u32[]{:S(2)}, u32[]{:S(2)}) collective-permute-start(f32[4,129,128]{2,1,0:T(8,128)S(1)} %select_add_fusion.5), channel_id=1, source_target_pairs={{0,32},{4,36},{8,40},{12,44},{16,48},{20,52},{24,56},{28,60},{32,6... | collective-permute-start | bytes 792584 | tf_op jit(solution)/shard_map/ppermute | solution.py:113
  199.9 5.6 %collective-permute-start.4 = (f32[4,129,128]{2,1,0:T(8,128)S(1)}, f32[4,129,128]{2,1,0:T(8,128)S(1)}, u32[]{:S(2)}, u32[]{:S(2)}) collective-permute-start(f32[4,129,128]{2,1,0:T(8,128)S(1)} %select_add_fusion.4), channel_id=1, source_target_pairs={{0,64},{4,68},{8,72},{12,76},{16,80},{20,84},{24,88},{28,92},{32,9... | collective-permute-start | bytes 792584 | tf_op jit(solution)/shard_map/ppermute | solution.py:113
  209.0 2.5 fusion.49
  211.6 3.1 fusion.29
  214.6 5.6 %collective-permute-start.8 = (f32[4,129,128]{2,1,0:T(8,128)S(1)}, f32[4,129,128]{2,1,0:T(8,128)S(1)}, u32[]{:S(2)}, u32[]{:S(2)}) collective-permute-start(f32[4,129,128]{2,1,0:T(8,128)S(1)} %pad_maximum_fusion.1), channel_id=1, source_target_pairs={{0,4},{4,8},{8,12},{12,16},{16,20},{20,24},{24,28},{28,32},{32,36}... | collective-permute-start | bytes 792584 | tf_op jit(solution)/shard_map/ppermute | solution.py:113
  229.4 8.7 %collective-permute-start.10 = (f32[4,129,128]{2,1,0:T(8,128)S(1)}, f32[4,129,128]{2,1,0:T(8,128)}, u32[]{:S(2)}, u32[]{:S(2)}) collective-permute-start(f32[4,129,128]{2,1,0:T(8,128)S(1)} %select_add_fusion.2), channel_id=1, source_target_pairs={{0,16},{4,20},{8,24},{12,28},{16,32},{20,36},{24,40},{28,44},{32,4... | collective-permute-start | bytes 792584 | tf_op jit(solution)/shard_map/ppermute | solution.py:113
  242.3 5.4 %gather_fusion.6 = bf16[1536,512]{1,0:T(8,128)(2,1)} fusion(bf16[1024,512]{1,0:T(8,128)(2,1)S(1)} %copy.61, s32[2048]{0:T(1024)S(1)} %pad_clamp_fusion), kind=kCustom, calls=%fused_computation.6 | custom fusion | bytes 3151872 | tf_op jit(solution)/shard_map/jit(_take)/gather | solution.py:135
  247.7 10.8 %all-to-all-start.3 = ((bf16[32,48,512]{2,1,0:T(8,128)(2,1)}), bf16[32,48,512]{2,1,0:T(8,128)(2,1)S(1)}, u32[]{:S(2)}, u32[]{:S(2)}) async-start(bf16[32,48,512]{2,1,0:T(8,128)(2,1)} %bitcast.267), calls=%async_computation.3 | async-start | bytes 3145728 | tf_op jit(solution)/shard_map/all_to_all | solution.py:136
  258.6 3.4 collective-permute-start.11
  265.8 15.9 %collective-permute-done.11 = f32[4,129,128]{2,1,0:T(8,128)S(1)} collective-permute-done((f32[4,129,128]{2,1,0:T(8,128)S(1)}, f32[4,129,128]{2,1,0:T(8,128)S(1)}, u32[]{:S(2)}, u32[]{:S(2)}) %collective-permute-start.11) | collective-permute-done | bytes 264224 | tf_op jit(solution)/shard_map/ppermute | solution.py:113
  281.8 5.6 %collective-permute-start.12 = (f32[4,129,128]{2,1,0:T(8,128)S(1)}, f32[4,129,128]{2,1,0:T(8,128)S(1)}, u32[]{:S(2)}, u32[]{:S(2)}) collective-permute-start(f32[4,129,128]{2,1,0:T(8,128)S(1)} %select_add_fusion), channel_id=1, source_target_pairs={{0,64},{4,68},{8,72},{12,76},{16,80},{20,84},{24,88},{28,92},{32,9... | collective-permute-start | bytes 792584 | tf_op jit(solution)/shard_map/ppermute | solution.py:113
  292.6 2.5 fusion.42
  295.2 4.1 fusion.31
  300.8 5.4 %gather_fusion.8 = bf16[1536,512]{1,0:T(8,128)(2,1)} fusion(bf16[1024,512]{1,0:T(8,128)(2,1)S(1)} %copy.75, s32[2048]{0:T(1024)S(1)} %pad_clamp_fusion), kind=kCustom, calls=%fused_computation.8 | custom fusion | bytes 3151872 | tf_op jit(solution)/shard_map/jit(_take)/gather | solution.py:135
  306.3 10.0 %all-to-all-start.4 = ((bf16[32,48,512]{2,1,0:T(8,128)(2,1)}), bf16[32,48,512]{2,1,0:T(8,128)(2,1)S(1)}, u32[]{:S(2)}, u32[]{:S(2)}) async-start(bf16[32,48,512]{2,1,0:T(8,128)(2,1)} %bitcast.266), calls=%async_computation.4 | async-start | bytes 3145728 | tf_op jit(solution)/shard_map/all_to_all | solution.py:136
  316.3 5.1 %gather_fusion.7 = bf16[1024,512]{1,0:T(8,128)(2,1)} fusion(bf16[1536,512]{1,0:T(8,128)(2,1)S(1)} %bitcast.245, s32[1024]{0:T(1024)S(1)} %broadcast_clamp_fusion), kind=kCustom, calls=%fused_computation.7 | custom fusion | bytes 2101248 | tf_op jit(solution)/shard_map/jit(_take)/gather | solution.py:137
  321.4 3.8 collective-permute-start.7
  326.6 4.8 %fusion.79 = f32[1024,1024]{1,0:T(8,128)} fusion(bf16[1024,512]{1,0:T(8,128)(2,1)} %gather_fusion.7, bf16[4,1024,1024]{2,1,0:T(8,128)(2,1)} %bitcast.255, s32[]{:T(128)S(6)} %select_n.244), kind=kOutput, calls=%fused_computation.132 | convolution fusion | flops 1073741824 | bytes 6291460 | tf_op jit(solution)/shard_map/dot_general | solution.py:142
  331.4 38.9 %collective-permute-done.7 = bf16[1024,512]{1,0:T(8,128)(2,1)S(1)} collective-permute-done((bf16[1024,512]{1,0:T(8,128)(2,1)}, bf16[1024,512]{1,0:T(8,128)(2,1)S(1)}, u32[]{:S(2)}, u32[]{:S(2)}) %collective-permute-start.7) | collective-permute-done | bytes 1048608 | tf_op jit(solution)/shard_map/ppermute | solution.py:149
  370.3 4.4 fusion.76
  374.7 4.0 gather_fusion.9
  378.8 4.8 %fusion.78 = f32[1024,1024]{1,0:T(8,128)} fusion(bf16[1024,512]{1,0:T(8,128)(2,1)} %collective-permute-done.5, bf16[4,1024,1024]{2,1,0:T(8,128)(2,1)} %bitcast.257, s32[]{:T(128)S(6)} %select_n.246), kind=kOutput, calls=%fused_computation.130 | convolution fusion | flops 1073741824 | bytes 6291460 | tf_op jit(solution)/shard_map/dot_general | solution.py:142
  383.5 4.5 %collective-permute-start.14 = (bf16[1024,512]{1,0:T(8,128)(2,1)S(1)}, bf16[1024,512]{1,0:T(8,128)(2,1)S(1)}, u32[]{:S(2)}, u32[]{:S(2)}) collective-permute-start(bf16[1024,512]{1,0:T(8,128)(2,1)S(1)} %gather_fusion.9), channel_id=1, source_target_pairs={{0,2},{1,3},{2,0},{3,1},{4,6},{5,7},{6,4},{7,5},{8,10},{9,11},{10,... | collective-permute-start | bytes 3145736 | tf_op jit(solution)/shard_map/ppermute | solution.py:149
  388.0 4.7 %fusion.77 = f32[1024,1024]{1,0:T(8,128)} fusion(bf16[1024,512]{1,0:T(8,128)(2,1)} %collective-permute-done.6, bf16[4,1024,1024]{2,1,0:T(8,128)(2,1)} %bitcast.258, s32[]{:T(128)S(6)} %select_n.248), kind=kOutput, calls=%fused_computation.128 | convolution fusion | flops 1073741824 | bytes 6291460 | tf_op jit(solution)/shard_map/dot_general | solution.py:142
  395.2 9.3 %collective-permute-done.13 = bf16[1024,512]{1,0:T(8,128)(2,1)S(1)} collective-permute-done((bf16[1024,512]{1,0:T(8,128)(2,1)S(1)}, bf16[1024,512]{1,0:T(8,128)(2,1)S(1)}, u32[]{:S(2)}, u32[]{:S(2)}) %collective-permute-start.13) | collective-permute-done | bytes 1048608 | tf_op jit(solution)/shard_map/ppermute | solution.py:149
  407.0 20.8 %collective-permute-done.14 = bf16[1024,512]{1,0:T(8,128)(2,1)S(1)} collective-permute-done((bf16[1024,512]{1,0:T(8,128)(2,1)S(1)}, bf16[1024,512]{1,0:T(8,128)(2,1)S(1)}, u32[]{:S(2)}, u32[]{:S(2)}) %collective-permute-start.14) | collective-permute-done | bytes 1048608 | tf_op jit(solution)/shard_map/ppermute | solution.py:149
  427.8 2.5 fusion.72
  432.5 10.6 %add_convert_fusion = bf16[1024,1024]{1,0:T(8,128)(2,1)} fusion(f32[1024,1024]{1,0:T(8,128)S(1)} %fusion.72, f32[1024,1024]{1,0:T(8,128)S(1)} %fusion.74, f32[1024,1024]{1,0:T(8,128)S(1)} %fusion.73, f32[1024,1024]{1,0:T(8,128)} %fusion.76, f32[1024,1024]{1,0:T(8,128)} %fusion.77, f32[1024,1024]{1,0:T(8,128)} %fusion.79, f32[1024,1024]{1,0:T(8,128)} %fusion.78, ...), kind=kOutput, calls=%fused_computation.26 | convolution fusion | flops 1082130432 | bytes 33554440 | tf_op jit(solution)/shard_map/dot_general | solution.py:142
  (191 shorter events, 71.7 us)
Async XLA Ops:
  1.7 6.6 %copy-start.29 = (s32[1024]{0:T(1024)}, s32[1024]{0:T(1024)S(1)}, u32[]{:S(2)}) copy-start(s32[1024]{0:T(1024)S(1)} %convert_element_type.90) | copy-start | bytes 12292
  8.3 8.8 %copy-start.2 = (bf16[1024,1024]{1,0:T(8,128)(2,1)S(1)}, bf16[1024,1024]{1,0:T(8,128)(2,1)}, u32[]{:S(2)}) copy-start(bf16[1024,1024]{1,0:T(8,128)(2,1)} %param.8) | copy-start | bytes 6291460
  8.3 48.6 %all-to-all-start.2 = ((bf16[32,48,1024]{2,1,0:T(8,128)(2,1)}), bf16[32,48,1024]{2,1,0:T(8,128)(2,1)}, u32[]{:S(2)}, u32[]{:S(2)}) async-start(bf16[32,48,1024]{2,1,0:T(8,128)(2,1)} %bitcast.252), calls=%async_computation.2 | async-start | bytes 6291456 | tf_op jit(solution)/shard_map/all_to_all | solution.py:67
  22.9 39.0 %copy-start.39 = (s32[32]{0:T(128)S(1)}, s32[32]{0:T(128)}, u32[]{:S(2)}) copy-start(s32[32]{0:T(128)} %param.11) | copy-start | bytes 388
  22.9 42.4 %copy-start.3 = (bf16[1024,1024]{1,0:T(8,128)(2,1)S(1)}, bf16[1024,1024]{1,0:T(8,128)(2,1)}, u32[]{:S(2)}) copy-start(bf16[1024,1024]{1,0:T(8,128)(2,1)} %param.9) | copy-start | bytes 6291460
  56.9 44.9 %all-to-all-start = ((bf16[32,48,1024]{2,1,0:T(8,128)(2,1)}), bf16[32,48,1024]{2,1,0:T(8,128)(2,1)}, u32[]{:S(2)}, u32[]{:S(2)}) async-start(bf16[32,48,1024]{2,1,0:T(8,128)(2,1)} %bitcast.251), calls=%async_computation | async-start | bytes 6291456 | tf_op jit(solution)/shard_map/all_to_all | solution.py:67
  65.3 6.5 %copy-start.31 = (s32[1536]{0:T(1024)}, s32[1536]{0:T(1024)S(1)}, u32[]{:S(2)}) copy-start(s32[1536]{0:T(1024)S(1)} %eq.93) | copy-start | bytes 18436
  65.3 5.8 %copy-start.38 = (f32[8]{0:T(128)S(1)}, f32[8]{0:T(128)}, u32[]{:S(2)}) copy-start(f32[8]{0:T(128)} %param.12) | copy-start | bytes 100
  101.8 44.9 %all-to-all-start.1 = ((bf16[32,48,1024]{2,1,0:T(8,128)(2,1)}), bf16[32,48,1024]{2,1,0:T(8,128)(2,1)S(1)}, u32[]{:S(2)}, u32[]{:S(2)}) async-start(bf16[32,48,1024]{2,1,0:T(8,128)(2,1)} %bitcast.250), calls=%async_computation.1 | async-start | bytes 6291456 | tf_op jit(solution)/shard_map/all_to_all | solution.py:67
  122.0 4.6 %copy-start.4 = (bf16[128,8,8,128]{3,2,1,0:T(8,128)(2,1)}, bf16[128,8,8,128]{3,2,1,0:T(8,128)(2,1)S(1)}, u32[]{:S(2)}) copy-start(bf16[128,8,8,128]{3,2,1,0:T(8,128)(2,1)S(1)} %copy.107) | copy-start | bytes 6291460
  152.0 4.3 copy-start.7
  156.3 4.5 %copy-start.22 = (bf16[1024,1,128]{2,1,0:T(2,128)(2,1)S(1)}, bf16[1024,1,128]{2,1,0:T(2,128)(2,1)}, u32[]{:S(2)}) copy-start(bf16[1024,1,128]{2,1,0:T(2,128)(2,1)} %get-tuple-element.126) | copy-start | bytes 786436
  156.3 7.8 %copy-start.27 = (bf16[1024,1,128]{2,0,1:T(8,128)(2,1)S(1)}, bf16[1024,1,128]{2,0,1:T(8,128)(2,1)}, u32[]{:S(2)}) copy-start(bf16[1024,1,128]{2,0,1:T(8,128)(2,1)} %copy.86) | copy-start | bytes 786436
  160.8 10.0 %collective-permute-start = (f32[4,129,128]{2,1,0:T(8,128)S(1)}, f32[4,129,128]{2,1,0:T(8,128)S(1)}, u32[]{:S(2)}, u32[]{:S(2)}) collective-permute-start(f32[4,129,128]{2,1,0:T(8,128)S(1)} %pad_maximum_fusion), channel_id=1, source_target_pairs={{0,4},{4,8},{8,12},{12,16},{16,20},{20,24},{24,28},{28,32},{32,36}... | collective-permute-start | bytes 792584 | tf_op jit(solution)/shard_map/ppermute | solution.py:113
  170.9 7.7 %collective-permute-start.1 = (f32[4,129,128]{2,1,0:T(8,128)S(1)}, f32[4,129,128]{2,1,0:T(8,128)S(1)}, u32[]{:S(2)}, u32[]{:S(2)}) collective-permute-start(f32[4,129,128]{2,1,0:T(8,128)S(1)} %select_add_fusion.7), channel_id=1, source_target_pairs={{0,8},{4,12},{8,16},{12,20},{16,24},{20,28},{24,32},{28,36},{32,40... | collective-permute-start | bytes 792584 | tf_op jit(solution)/shard_map/ppermute | solution.py:113
  174.1 10.5 %copy-start.5 = (bf16[128,8,8,128]{3,2,1,0:T(8,128)(2,1)S(1)}, bf16[128,8,8,128]{3,2,1,0:T(8,128)(2,1)}, u32[]{:S(2)}) copy-start(bf16[128,8,8,128]{3,2,1,0:T(8,128)(2,1)} %copy-done.4) | copy-start | bytes 6291460
  178.7 11.0 %collective-permute-start.2 = (f32[4,129,128]{2,1,0:T(8,128)S(1)}, f32[4,129,128]{2,1,0:T(8,128)S(1)}, u32[]{:S(2)}, u32[]{:S(2)}) collective-permute-start(f32[4,129,128]{2,1,0:T(8,128)S(1)} %select_add_fusion.6), channel_id=1, source_target_pairs={{0,16},{4,20},{8,24},{12,28},{16,32},{20,36},{24,40},{28,44},{32,4... | collective-permute-start | bytes 792584 | tf_op jit(solution)/shard_map/ppermute | solution.py:113
  189.8 10.1 %collective-permute-start.3 = (f32[4,129,128]{2,1,0:T(8,128)S(1)}, f32[4,129,128]{2,1,0:T(8,128)S(1)}, u32[]{:S(2)}, u32[]{:S(2)}) collective-permute-start(f32[4,129,128]{2,1,0:T(8,128)S(1)} %select_add_fusion.5), channel_id=1, source_target_pairs={{0,32},{4,36},{8,40},{12,44},{16,48},{20,52},{24,56},{28,60},{32,6... | collective-permute-start | bytes 792584 | tf_op jit(solution)/shard_map/ppermute | solution.py:113
  199.9 9.0 %collective-permute-start.4 = (f32[4,129,128]{2,1,0:T(8,128)S(1)}, f32[4,129,128]{2,1,0:T(8,128)S(1)}, u32[]{:S(2)}, u32[]{:S(2)}) collective-permute-start(f32[4,129,128]{2,1,0:T(8,128)S(1)} %select_add_fusion.4), channel_id=1, source_target_pairs={{0,64},{4,68},{8,72},{12,76},{16,80},{20,84},{24,88},{28,92},{32,9... | collective-permute-start | bytes 792584 | tf_op jit(solution)/shard_map/ppermute | solution.py:113
  214.6 9.1 %collective-permute-start.8 = (f32[4,129,128]{2,1,0:T(8,128)S(1)}, f32[4,129,128]{2,1,0:T(8,128)S(1)}, u32[]{:S(2)}, u32[]{:S(2)}) collective-permute-start(f32[4,129,128]{2,1,0:T(8,128)S(1)} %pad_maximum_fusion.1), channel_id=1, source_target_pairs={{0,4},{4,8},{8,12},{12,16},{16,20},{20,24},{24,28},{28,32},{32,36}... | collective-permute-start | bytes 792584 | tf_op jit(solution)/shard_map/ppermute | solution.py:113
  223.8 5.6 %collective-permute-start.9 = (f32[4,129,128]{2,1,0:T(8,128)S(1)}, f32[4,129,128]{2,1,0:T(8,128)S(1)}, u32[]{:S(2)}, u32[]{:S(2)}) collective-permute-start(f32[4,129,128]{2,1,0:T(8,128)S(1)} %select_add_fusion.3), channel_id=1, source_target_pairs={{0,8},{4,12},{8,16},{12,20},{16,24},{20,28},{24,32},{28,36},{32,40... | collective-permute-start | bytes 792584 | tf_op jit(solution)/shard_map/ppermute | solution.py:113
  227.3 10.8 %copy-start.32 = (s32[1536]{0:T(1024)S(1)}, s32[1536]{0:T(1024)}, u32[]{:S(2)}) copy-start(s32[1536]{0:T(1024)} %copy-done.31) | copy-start | bytes 18436
  227.3 10.8 %copy-start.30 = (s32[1024]{0:T(1024)S(1)}, s32[1024]{0:T(1024)}, u32[]{:S(2)}) copy-start(s32[1024]{0:T(1024)} %copy-done.29) | copy-start | bytes 12292
  227.3 11.4 %copy-start.9 = (bf16[1024,1,128]{2,1,0:T(2,128)(2,1)S(1)}, bf16[1024,1,128]{2,1,0:T(2,128)(2,1)}, u32[]{:S(2)}) copy-start(bf16[1024,1,128]{2,1,0:T(2,128)(2,1)} %get-tuple-element.127) | copy-start | bytes 786436
  227.3 12.2 %copy-start.8 = (bf16[1024,1,128]{2,1,0:T(2,128)(2,1)S(1)}, bf16[1024,1,128]{2,1,0:T(2,128)(2,1)}, u32[]{:S(2)}) copy-start(bf16[1024,1,128]{2,1,0:T(2,128)(2,1)} %get-tuple-element.128) | copy-start | bytes 786436
  227.4 12.9 %copy-start.11 = (bf16[1024,1,128]{2,1,0:T(2,128)(2,1)S(1)}, bf16[1024,1,128]{2,1,0:T(2,128)(2,1)}, u32[]{:S(2)}) copy-start(bf16[1024,1,128]{2,1,0:T(2,128)(2,1)} %get-tuple-element.119) | copy-start | bytes 786436
  227.4 13.6 %copy-start.10 = (bf16[1024,1,128]{2,1,0:T(2,128)(2,1)S(1)}, bf16[1024,1,128]{2,1,0:T(2,128)(2,1)}, u32[]{:S(2)}) copy-start(bf16[1024,1,128]{2,1,0:T(2,128)(2,1)} %get-tuple-element.120) | copy-start | bytes 786436
  229.4 29.1 %collective-permute-start.10 = (f32[4,129,128]{2,1,0:T(8,128)S(1)}, f32[4,129,128]{2,1,0:T(8,128)}, u32[]{:S(2)}, u32[]{:S(2)}) collective-permute-start(f32[4,129,128]{2,1,0:T(8,128)S(1)} %select_add_fusion.2), channel_id=1, source_target_pairs={{0,16},{4,20},{8,24},{12,28},{16,32},{20,36},{24,40},{28,44},{32,4... | collective-permute-start | bytes 792584 | tf_op jit(solution)/shard_map/ppermute | solution.py:113
  247.7 58.6 %all-to-all-start.3 = ((bf16[32,48,512]{2,1,0:T(8,128)(2,1)}), bf16[32,48,512]{2,1,0:T(8,128)(2,1)S(1)}, u32[]{:S(2)}, u32[]{:S(2)}) async-start(bf16[32,48,512]{2,1,0:T(8,128)(2,1)} %bitcast.267), calls=%async_computation.3 | async-start | bytes 3145728 | tf_op jit(solution)/shard_map/all_to_all | solution.py:136
  258.6 5.7 %copy-start.25 = (bf16[1024,1,128]{0,2,1:T(8,128)(2,1)S(1)}, bf16[1024,1,128]{0,2,1:T(8,128)(2,1)}, u32[]{:S(2)}) copy-start(bf16[1024,1,128]{0,2,1:T(8,128)(2,1)} %get-tuple-element.94) | copy-start | bytes 786436
  258.6 23.2 %collective-permute-start.11 = (f32[4,129,128]{2,1,0:T(8,128)S(1)}, f32[4,129,128]{2,1,0:T(8,128)S(1)}, u32[]{:S(2)}, u32[]{:S(2)}) collective-permute-start(f32[4,129,128]{2,1,0:T(8,128)S(1)} %select_add_fusion.1), channel_id=1, source_target_pairs={{0,32},{4,36},{8,40},{12,44},{16,48},{20,52},{24,56},{28,60},{32,6... | collective-permute-start | bytes 792584 | tf_op jit(solution)/shard_map/ppermute | solution.py:113
  264.3 23.2 %copy-start.26 = (bf16[1024,1,128]{2,0,1:T(8,128)(2,1)S(1)}, bf16[1024,1,128]{2,0,1:T(8,128)(2,1)}, u32[]{:S(2)}) copy-start(bf16[1024,1,128]{2,0,1:T(8,128)(2,1)} %copy.103) | copy-start | bytes 786436
  264.3 23.2 %copy-start.28 = (bf16[1024,1,128]{2,0,1:T(8,128)(2,1)S(1)}, bf16[1024,1,128]{2,0,1:T(8,128)(2,1)}, u32[]{:S(2)}) copy-start(bf16[1024,1,128]{2,0,1:T(8,128)(2,1)} %copy.104) | copy-start | bytes 786436
  281.8 6.9 %copy-start.24 = (bf16[1024,1,128]{0,2,1:T(8,128)(2,1)S(1)}, bf16[1024,1,128]{0,2,1:T(8,128)(2,1)}, u32[]{:S(2)}) copy-start(bf16[1024,1,128]{0,2,1:T(8,128)(2,1)} %get-tuple-element.99) | copy-start | bytes 786436
  281.8 10.7 %collective-permute-start.12 = (f32[4,129,128]{2,1,0:T(8,128)S(1)}, f32[4,129,128]{2,1,0:T(8,128)S(1)}, u32[]{:S(2)}, u32[]{:S(2)}) collective-permute-start(f32[4,129,128]{2,1,0:T(8,128)S(1)} %select_add_fusion), channel_id=1, source_target_pairs={{0,64},{4,68},{8,72},{12,76},{16,80},{20,84},{24,88},{28,92},{32,9... | collective-permute-start | bytes 792584 | tf_op jit(solution)/shard_map/ppermute | solution.py:113
  290.3 4.9 %copy-start.34 = (f32[4]{0:T(128)S(1)}, f32[4]{0:T(128)}, u32[]{:S(2)}) copy-start(f32[4]{0:T(128)} %get-tuple-element.138) | copy-start | bytes 52
  290.3 4.9 %copy-start.35 = (f32[4]{0:T(128)S(1)}, f32[4]{0:T(128)}, u32[]{:S(2)}) copy-start(f32[4]{0:T(128)} %get-tuple-element.140) | copy-start | bytes 52
  290.3 4.9 %copy-start.40 = (f32[1024,1,128]{0,2,1:T(8,128)S(1)}, f32[1024,1,128]{0,2,1:T(8,128)}, u32[]{:S(2)}) copy-start(f32[1024,1,128]{0,2,1:T(8,128)} %fusion.59) | copy-start | bytes 1572868
  290.3 4.9 %copy-start.41 = (f32[1024,1,128]{0,2,1:T(8,128)S(1)}, f32[1024,1,128]{0,2,1:T(8,128)}, u32[]{:S(2)}) copy-start(f32[1024,1,128]{0,2,1:T(8,128)} %fusion.58) | copy-start | bytes 1572868
  300.8 15.4 %copy-start.33 = (s32[1024,1]{0,1:T(1,128)S(1)}, s32[1024,1]{0,1:T(1,128)}, u32[]{:S(2)}) copy-start(s32[1024,1]{0,1:T(1,128)} %multiply_add_fusion) | copy-start | bytes 12292
  306.3 68.4 %all-to-all-start.4 = ((bf16[32,48,512]{2,1,0:T(8,128)(2,1)}), bf16[32,48,512]{2,1,0:T(8,128)(2,1)S(1)}, u32[]{:S(2)}, u32[]{:S(2)}) async-start(bf16[32,48,512]{2,1,0:T(8,128)(2,1)} %bitcast.266), calls=%async_computation.4 | async-start | bytes 3145728 | tf_op jit(solution)/shard_map/all_to_all | solution.py:136
  321.4 48.9 %collective-permute-start.7 = (bf16[1024,512]{1,0:T(8,128)(2,1)}, bf16[1024,512]{1,0:T(8,128)(2,1)S(1)}, u32[]{:S(2)}, u32[]{:S(2)}) collective-permute-start(bf16[1024,512]{1,0:T(8,128)(2,1)} %gather_fusion.7), channel_id=1, source_target_pairs={{0,3},{1,0},{2,1},{3,2},{4,7},{5,4},{6,5},{7,6},{8,11},{9,8},{10,9... | collective-permute-start | bytes 3145736 | tf_op jit(solution)/shard_map/ppermute | solution.py:149
  325.1 53.6 %collective-permute-start.5 = (bf16[1024,512]{1,0:T(8,128)(2,1)}, bf16[1024,512]{1,0:T(8,128)(2,1)}, u32[]{:S(2)}, u32[]{:S(2)}) collective-permute-start(bf16[1024,512]{1,0:T(8,128)(2,1)} %gather_fusion.7), channel_id=1, source_target_pairs={{0,1},{1,2},{2,3},{3,0},{4,5},{5,6},{6,7},{7,4},{8,9},{9,10},{10,1... | collective-permute-start | bytes 3145736 | tf_op jit(solution)/shard_map/ppermute | solution.py:149
  325.2 62.8 %collective-permute-start.6 = (bf16[1024,512]{1,0:T(8,128)(2,1)}, bf16[1024,512]{1,0:T(8,128)(2,1)}, u32[]{:S(2)}, u32[]{:S(2)}) collective-permute-start(bf16[1024,512]{1,0:T(8,128)(2,1)} %gather_fusion.7), channel_id=1, source_target_pairs={{0,2},{1,3},{2,0},{3,1},{4,6},{5,7},{6,4},{7,5},{8,10},{9,11},{10,... | collective-permute-start | bytes 3145736 | tf_op jit(solution)/shard_map/ppermute | solution.py:149
  378.7 25.8 %collective-permute-start.13 = (bf16[1024,512]{1,0:T(8,128)(2,1)S(1)}, bf16[1024,512]{1,0:T(8,128)(2,1)S(1)}, u32[]{:S(2)}, u32[]{:S(2)}) collective-permute-start(bf16[1024,512]{1,0:T(8,128)(2,1)S(1)} %gather_fusion.9), channel_id=1, source_target_pairs={{0,1},{1,2},{2,3},{3,0},{4,5},{5,6},{6,7},{7,4},{8,9},{9,10},{10,1... | collective-permute-start | bytes 3145736 | tf_op jit(solution)/shard_map/ppermute | solution.py:149
  383.5 44.3 %collective-permute-start.14 = (bf16[1024,512]{1,0:T(8,128)(2,1)S(1)}, bf16[1024,512]{1,0:T(8,128)(2,1)S(1)}, u32[]{:S(2)}, u32[]{:S(2)}) collective-permute-start(bf16[1024,512]{1,0:T(8,128)(2,1)S(1)} %gather_fusion.9), channel_id=1, source_target_pairs={{0,2},{1,3},{2,0},{3,1},{4,6},{5,7},{6,4},{7,5},{8,10},{9,11},{10,... | collective-permute-start | bytes 3145736 | tf_op jit(solution)/shard_map/ppermute | solution.py:149
  392.7 39.8 %collective-permute-start.15 = (bf16[1024,512]{1,0:T(8,128)(2,1)S(1)}, bf16[1024,512]{1,0:T(8,128)(2,1)}, u32[]{:S(2)}, u32[]{:S(2)}) collective-permute-start(bf16[1024,512]{1,0:T(8,128)(2,1)S(1)} %gather_fusion.9), channel_id=1, source_target_pairs={{0,3},{1,0},{2,1},{3,2},{4,7},{5,4},{6,5},{7,6},{8,11},{9,8},{10,9... | collective-permute-start | bytes 3145736 | tf_op jit(solution)/shard_map/ppermute | solution.py:149
  432.5 10.6 %copy-start.1 = (bf16[1024,1024]{1,0:T(8,128)(2,1)S(1)}, bf16[1024,1024]{1,0:T(8,128)(2,1)}, u32[]{:S(2)}) copy-start(bf16[1024,1024]{1,0:T(8,128)(2,1)} %param.7) | copy-start | bytes 6291460
  (15 other events, 39.7 us)

commit v7 on v5

--- a/solution.py
+++ b/solution.py
@@ -56,11 +56,11 @@
     bounds = [0, heads // 2, heads]
     weight_rows = out_weight.reshape(head_count, heads, dh, out_cols)
     gate_all = jax.nn.sigmoid(mem_gate)
-    shifts = []
-    step = 1
-    while step < n:
-        shifts.append(step)
-        step *= 2
+    rounds = []
+    base = 1
+    while base < n:
+        rounds.append([k * base for k in range(1, 4) if k * base < n])
+        base *= 4
 
     def dispatch(source):
         buffer = jnp.take(source, slot_row, axis=0, mode="clip").reshape(n, cap, width)
@@ -68,6 +68,11 @@
         return jnp.take(got, tok_slot, axis=0, mode="clip").reshape(seg, heads, dh)
 
     key_all = dispatch(keys)
+    weight_parts = [
+        weight_rows[:, bounds[g]:bounds[g + 1]].reshape(head_count * (bounds[g + 1] - bounds[g]) * dh, out_cols)
+        for g in range(len(bounds) - 1)
+    ]
+    key_all, weight_parts = lax.optimization_barrier((key_all, weight_parts))
     value_all = dispatch(values)
     query_all = dispatch(queries)
 
@@ -87,7 +92,7 @@
         first, last = bounds[g], bounds[g + 1]
         group_heads = last - first
         group_width = group_heads * dh
-        cuts = [first + round(group_heads * i / len(shifts)) for i in range(len(shifts) + 1)]
+        cuts = [first + round(group_heads * i / len(rounds)) for i in range(len(rounds) + 1)]
         cuts = [c - first for c in cuts]
         key_heads = key_all[:, first:last]
         value_heads = value_all[:, first:last]
@@ -104,18 +109,21 @@
 
         pieces = []
         total = delta
-        for k, step in enumerate(shifts):
+        for k, shifts in enumerate(rounds):
             lo, hi = cuts[k], cuts[k + 1]
             total, operands = lax.optimization_barrier(
                 (total, (query_heads[:, lo:hi], key_heads[:, lo:hi], value_heads[:, lo:hi]))
             )
-            perm = [(j, j + step) for j in range(n - step)]
-            got = lax.ppermute(total, "ctx", perm)
+            arrivals = [
+                lax.ppermute(total, "ctx", [(j, j + shift) for j in range(n - shift)])
+                for shift in shifts
+            ]
             if hi > lo:
                 piece = local_attention(*operands)
-                got, piece = lax.optimization_barrier((got, piece))
+                arrivals, piece = lax.optimization_barrier((arrivals, piece))
                 pieces.append(piece)
-            total = total + jnp.where(me - step >= start, got, jnp.zeros_like(got))
+            for shift, got in zip(shifts, arrivals):
+                total = total + jnp.where(me - shift >= start, got, jnp.zeros_like(got))
         local_out = jnp.concatenate(pieces, axis=1)
         memory = total - delta
         mem_m = memory[:, :dh, :]
@@ -138,7 +146,7 @@
         gathered = lax.all_gather(rows, "head", axis=1, tiled=True)
         part = jnp.dot(
             gathered,
-            weight_rows[:, first:last].reshape(head_count * group_width, out_cols),
+            weight_parts[g],
             preferred_element_type=f32,
         )
         return part, combined

time: 419 us -> 445 us (1.062)
  starting transfers between devices: 77.7 us -> 92.4 us
  matrix products: 57.4 us -> 69.8 us
    sub x0 -> x2, matrix products: none -> 12.9 us  [local_attention(): weights = jnp.exp(scores - row_max)]
    ppermute x10 -> x14, starting transfers between devices: 50 us -> 62.6 us  [one_group(): lax.ppermute(total, 'ctx', [(j, j + shift) for j in range(n - shift)])]
    all_gather x2, waiting for transfers between devices: 30.1 us -> 36.9 us  [one_group(): gathered = lax.all_gather(rows, 'head', axis=1, tiled=True)]
    all_to_all x3, waiting for transfers between devices: 64.5 us -> 58 us  [dispatch(): got = lax.all_to_all(buffer, 'ctx', 0, 0, tiled=True).reshape(slots, width)]
    dot_general x8 -> x6, matrix products: 12.1 us -> 14.5 us  [local_attention(): jnp.einsum('hqk,khd->qhd', probabilities, value_part, preferred_element_t...]
    ppermute x10 -> x14, waiting for transfers between devices: 24 us -> 23.4 us  [one_group(): lax.ppermute(total, 'ctx', [(j, j + shift) for j in range(n - shift)])]
  transfers between devices with their start and end apart: 16 -> 20, of which waited for: 11 -> 10; matrix products, arithmetic and copies ran while one was open for 31% -> 29% of each run, Pallas kernels for 0% -> 0%
where the time goes in v7:
time: 445 us; the launch traced here: 438 us
  waiting for transfers between devices  118 us (27%)
  local copies, waits for them, and re-layouts  95.5 us (21%)
  starting transfers between devices  92.4 us (21%)
  matrix products  69.8 us (16%)
  blocking collectives  30.6 us (7%)
  between operations  18.5 us (4%)
  other arithmetic  13.2 us (3%)
    ppermute x14, starting transfers between devices, one_group(): lax.ppermute(total, 'ctx', [(j, j + shift) for j in range(n - shift)])  62.6 us
    all_to_all x3, waiting for transfers between devices, dispatch(): got = lax.all_to_all(buffer, 'ctx', 0, 0, tiled=True).reshape(slots, width)  58 us
    all_gather x2, waiting for transfers between devices, one_group(): gathered = lax.all_gather(rows, 'head', axis=1, tiled=True)  36.9 us
    all_to_all x1, blocking collectives, one_group(): lax.all_to_all(outgoing, 'ctx', 0, 0, tiled=True)  30.6 us
    gather x4, local copies, waits for them, and re-layouts, dispatch(): return jnp.take(got, tok_slot, axis=0, mode='clip').reshape(seg, heads, dh)  26.3 us
    ppermute x14, waiting for transfers between devices, one_group(): lax.ppermute(total, 'ctx', [(j, j + shift) for j in range(n - shift)])  23.4 us
    dot_general x2, matrix products, one_group(): part = jnp.dot(gathered, weight_parts[g], preferred_element_type=f32)  20.5 us
    all_to_all x3, starting transfers between devices, dispatch(): got = lax.all_to_all(buffer, 'ctx', 0, 0, tiled=True).reshape(slots, width)  19.1 us
  transfers between devices with their start and end apart: 20, of which 10 were waited for; matrix products, arithmetic and copies ran while one was open for 29% of the time, Pallas kernels for 0%

profile of v7, /device:TPU:1, one launch (start us, length us, event | category | flops | bytes accessed | tf_op | source)
XLA Modules:
  0.0 438.4 jit_solution(17403683778569290854)
XLA Ops:
  9.0 5.8 %gather_fusion.4 = bf16[1536,1024]{1,0:T(8,128)(2,1)} fusion(bf16[1024,1024]{1,0:T(8,128)(2,1)S(1)} %copy-done, s32[2048]{0:T(1024)S(1)} %pad_clamp_fusion.1), kind=kCustom, calls=%fused_computation.4 | custom fusion | bytes 6297600 | tf_op jit(solution)/shard_map/jit(_take)/gather | solution.py:66
  14.8 8.8 %all-to-all-start.2 = ((bf16[32,48,1024]{2,1,0:T(8,128)(2,1)}), bf16[32,48,1024]{2,1,0:T(8,128)(2,1)}, u32[]{:S(2)}, u32[]{:S(2)}) async-start(bf16[32,48,1024]{2,1,0:T(8,128)(2,1)} %bitcast.169), calls=%async_computation.2 | async-start | bytes 6291456 | tf_op jit(solution)/shard_map/all_to_all | solution.py:67
  23.6 5.9 %gather_fusion.2 = bf16[1536,1024]{1,0:T(8,128)(2,1)} fusion(bf16[1024,1024]{1,0:T(8,128)(2,1)S(1)} %copy-done.2, s32[2048]{0:T(1024)S(1)} %pad_clamp_fusion.1), kind=kCustom, calls=%fused_computation.2 | custom fusion | bytes 6297600 | tf_op jit(solution)/shard_map/jit(_take)/gather | solution.py:66
  29.5 33.9 %all-to-all-done.2 = bf16[32,48,1024]{2,1,0:T(8,128)(2,1)} async-done(((bf16[32,48,1024]{2,1,0:T(8,128)(2,1)}), bf16[32,48,1024]{2,1,0:T(8,128)(2,1)}, u32[]{:S(2)}, u32[]{:S(2)}) %all-to-all-start.2) | async-done | bytes 3145760 | tf_op jit(solution)/shard_map/all_to_all | solution.py:67
  63.4 5.0 %all-to-all-start.1 = ((bf16[32,48,1024]{2,1,0:T(8,128)(2,1)}), bf16[32,48,1024]{2,1,0:T(8,128)(2,1)}, u32[]{:S(2)}, u32[]{:S(2)}) async-start(bf16[32,48,1024]{2,1,0:T(8,128)(2,1)} %bitcast.167), calls=%async_computation.1 | async-start | bytes 6291456 | tf_op jit(solution)/shard_map/all_to_all | solution.py:67
  76.9 5.8 %gather_fusion = bf16[1536,1024]{1,0:T(8,128)(2,1)} fusion(bf16[1024,1024]{1,0:T(8,128)(2,1)S(1)} %copy-done.3, s32[2048]{0:T(1024)S(1)} %pad_clamp_fusion.1), kind=kCustom, calls=%fused_computation | custom fusion | bytes 6297600 | tf_op jit(solution)/shard_map/jit(_take)/gather | solution.py:66
  84.2 24.1 %all-to-all-done.1 = bf16[32,48,1024]{2,1,0:T(8,128)(2,1)} async-done(((bf16[32,48,1024]{2,1,0:T(8,128)(2,1)}), bf16[32,48,1024]{2,1,0:T(8,128)(2,1)}, u32[]{:S(2)}, u32[]{:S(2)}) %all-to-all-start.1) | async-done | bytes 3145760 | tf_op jit(solution)/shard_map/all_to_all | solution.py:67
  108.3 5.3 %all-to-all-start = ((bf16[32,48,1024]{2,1,0:T(8,128)(2,1)}), bf16[32,48,1024]{2,1,0:T(8,128)(2,1)S(1)}, u32[]{:S(2)}, u32[]{:S(2)}) async-start(bf16[32,48,1024]{2,1,0:T(8,128)(2,1)} %bitcast.168), calls=%async_computation | async-start | bytes 6291456 | tf_op jit(solution)/shard_map/all_to_all | solution.py:67
  114.9 6.1 %fusion.146 = (bf16[4,4,128,1024]{3,2,1,0:T(8,128)(2,1)}, bf16[4,4,128,1024]{3,2,1,0:T(8,128)(2,1)}) fusion(bf16[4,8,128,1024]{3,2,1,0:T(8,128)(2,1)} %bitcast.172), kind=kLoop, calls=%fused_computation.228 | loop fusion | bytes 16777216 | tf_op jit(solution)/shard_map/slice | solution.py:72
  121.0 8.3 %gather_fusion.5 = bf16[1024,1024]{1,0:T(8,128)(2,1)} fusion(bf16[1536,1024]{1,0:T(8,128)(2,1)} %bitcast.13, s32[1024]{0:T(1024)S(1)} %broadcast_clamp_fusion.1), kind=kCustom, calls=%fused_computation.5 | custom fusion | bytes 4198400 | tf_op jit(solution)/shard_map/jit(_take)/gather | solution.py:68
  129.3 3.6 copy.101
  132.9 8.3 %gather_fusion.3 = bf16[1024,1024]{1,0:T(8,128)(2,1)} fusion(bf16[1536,1024]{1,0:T(8,128)(2,1)} %bitcast.9, s32[1024]{0:T(1024)S(1)} %broadcast_clamp_fusion.1), kind=kCustom, calls=%fused_computation.3 | custom fusion | bytes 4198400 | tf_op jit(solution)/shard_map/jit(_take)/gather | solution.py:68
  141.2 4.0 copy.54
  153.7 2.6 fusion.150
  156.3 5.7 %gather_fusion.1 = bf16[1024,1024]{1,0:T(8,128)(2,1)} fusion(bf16[1536,1024]{1,0:T(8,128)(2,1)S(1)} %bitcast.161, s32[1024]{0:T(1024)S(1)} %broadcast_clamp_fusion.1), kind=kCustom, calls=%fused_computation.1 | custom fusion | bytes 4198400 | tf_op jit(solution)/shard_map/jit(_take)/gather | solution.py:68
  166.4 2.5 fusion.54
  169.0 3.3 fusion.47
  173.3 5.1 %collective-permute-start.2 = (f32[4,129,128]{2,1,0:T(8,128)S(1)}, f32[4,129,128]{2,1,0:T(8,128)S(1)}, u32[]{:S(2)}, u32[]{:S(2)}) collective-permute-start(f32[4,129,128]{2,1,0:T(8,128)S(1)} %pad_maximum_fusion), channel_id=1, source_target_pairs={{0,12},{4,16},{8,20},{12,24},{16,28},{20,32},{24,36},{28,40},{32,4... | collective-permute-start | bytes 792584 | tf_op jit(solution)/shard_map/ppermute | solution.py:118
  189.9 3.0 collective-permute-done
  193.0 5.4 %collective-permute-start.5 = (f32[4,129,128]{2,1,0:T(8,128)S(1)}, f32[4,129,128]{2,1,0:T(8,128)S(1)}, u32[]{:S(2)}, u32[]{:S(2)}) collective-permute-start(f32[4,129,128]{2,1,0:T(8,128)S(1)} %select_add_fusion.3), channel_id=1, source_target_pairs={{0,48},{4,52},{8,56},{12,60},{16,64},{20,68},{24,72},{28,76},{32,8... | collective-permute-start | bytes 792584 | tf_op jit(solution)/shard_map/ppermute | solution.py:118
  198.3 3.6 collective-permute-start.4
  201.9 4.1 collective-permute-start.3
  206.0 5.4 %fusion.155 = (f32[2,1024]{1,0:T(2,128)S(1)}, f32[2,1024,1024]{1,2,0:T(8,128)}) fusion(pred[1024,1024]{0,1:T(8,128)(4,1)S(1)} %copy-done.12, bf16[1024,2,128]{2,0,1:T(8,128)(2,1)S(1)} %copy.92, bf16[1024,2,128]{2,0,1:T(8,128)(2,1)S(1)} %get-tuple-element.64), kind=kOutput, calls=%fused_computation.237 | convolution fusion | flops 545260544 | bytes 10493952 | tf_op jit(solution)/shard_map/sub | solution.py:85
  211.3 4.2 fusion.57
  215.6 8.2 %collective-permute-start.6 = (f32[4,129,128]{2,1,0:T(8,128)S(1)}, f32[4,129,128]{2,1,0:T(8,128)S(1)}, u32[]{:S(2)}, u32[]{:S(2)}) collective-permute-start(f32[4,129,128]{2,1,0:T(8,128)S(1)} %select_add_fusion.2), channel_id=1, source_target_pairs={{0,64},{4,68},{8,72},{12,76},{16,80},{20,84},{24,88},{28,92},{32,9... | collective-permute-start | bytes 792584 | tf_op jit(solution)/shard_map/ppermute | solution.py:118
  230.4 3.1 fusion.33
  234.1 5.4 %gather_fusion.6 = bf16[1536,512]{1,0:T(8,128)(2,1)} fusion(bf16[1024,512]{1,0:T(8,128)(2,1)S(1)} %copy.66, s32[2048]{0:T(1024)S(1)} %pad_clamp_fusion), kind=kCustom, calls=%fused_computation.6 | custom fusion | bytes 3151872 | tf_op jit(solution)/shard_map/jit(_take)/gather | solution.py:143
  239.5 10.6 %all-to-all-start.3 = ((bf16[32,48,512]{2,1,0:T(8,128)(2,1)}), bf16[32,48,512]{2,1,0:T(8,128)(2,1)S(1)}, u32[]{:S(2)}, u32[]{:S(2)}) async-start(bf16[32,48,512]{2,1,0:T(8,128)(2,1)} %bitcast.33), calls=%async_computation.3 | async-start | bytes 3145728 | tf_op jit(solution)/shard_map/all_to_all | solution.py:144
  252.8 5.2 %collective-permute-start.9 = (f32[4,129,128]{2,1,0:T(8,128)S(1)}, f32[4,129,128]{2,1,0:T(8,128)S(1)}, u32[]{:S(2)}, u32[]{:S(2)}) collective-permute-start(f32[4,129,128]{2,1,0:T(8,128)S(1)} %pad_maximum_fusion.1), channel_id=1, source_target_pairs={{0,12},{4,16},{8,20},{12,24},{16,28},{20,32},{24,36},{28,40},{32,4... | collective-permute-start | bytes 792584 | tf_op jit(solution)/shard_map/ppermute | solution.py:118
  260.2 2.7 collective-permute-start.7
  266.6 6.7 %collective-permute-done.9 = f32[4,129,128]{2,1,0:T(8,128)S(1)} collective-permute-done((f32[4,129,128]{2,1,0:T(8,128)S(1)}, f32[4,129,128]{2,1,0:T(8,128)S(1)}, u32[]{:S(2)}, u32[]{:S(2)}) %collective-permute-start.9) | collective-permute-done | bytes 264224 | tf_op jit(solution)/shard_map/ppermute | solution.py:118
  273.3 6.0 %collective-permute-done.8 = f32[4,129,128]{2,1,0:T(8,128)S(1)} collective-permute-done((f32[4,129,128]{2,1,0:T(8,128)S(1)}, f32[4,129,128]{2,1,0:T(8,128)S(1)}, u32[]{:S(2)}, u32[]{:S(2)}) %collective-permute-start.8) | collective-permute-done | bytes 264224 | tf_op jit(solution)/shard_map/ppermute | solution.py:118
  280.0 2.5 collective-permute-done.7
  282.6 5.1 %gather_fusion.7 = bf16[1024,512]{1,0:T(8,128)(2,1)} fusion(bf16[1536,512]{1,0:T(8,128)(2,1)S(1)} %bitcast.162, s32[1024]{0:T(1024)S(1)} %broadcast_clamp_fusion), kind=kCustom, calls=%fused_computation.7 | custom fusion | bytes 2101248 | tf_op jit(solution)/shard_map/jit(_take)/gather | solution.py:145
  288.8 5.6 %collective-permute-start.12 = (f32[4,129,128]{2,1,0:T(8,128)S(1)}, f32[4,129,128]{2,1,0:T(8,128)S(1)}, u32[]{:S(2)}, u32[]{:S(2)}) collective-permute-start(f32[4,129,128]{2,1,0:T(8,128)S(1)} %select_add_fusion.1), channel_id=1, source_target_pairs={{0,48},{4,52},{8,56},{12,60},{16,64},{20,68},{24,72},{28,76},{32,8... | collective-permute-start | bytes 792584 | tf_op jit(solution)/shard_map/ppermute | solution.py:118
  294.4 3.4 collective-permute-start.11
  297.7 4.3 collective-permute-start.10
  302.1 7.5 %fusion.156 = (f32[2,1024]{1,0:T(2,128)S(1)}, f32[2,1024,1024]{1,2,0:T(8,128)}) fusion(pred[1024,1024]{0,1:T(8,128)(4,1)S(1)} %copy-done.13, bf16[1024,2,128]{2,0,1:T(8,128)(2,1)S(1)} %copy-done.16, bf16[1024,2,128]{2,0,1:T(8,128)(2,1)} %get-tuple-element.88), kind=kOutput, calls=%fused_computation.238 | convolution fusion | flops 545260544 | bytes 10493952 | tf_op jit(solution)/shard_map/sub | solution.py:85
  309.6 4.2 fusion.56
  314.0 8.1 %collective-permute-start.13 = (f32[4,129,128]{2,1,0:T(8,128)S(1)}, f32[4,129,128]{2,1,0:T(8,128)S(1)}, u32[]{:S(2)}, u32[]{:S(2)}) collective-permute-start(f32[4,129,128]{2,1,0:T(8,128)S(1)} %select_add_fusion), channel_id=1, source_target_pairs={{0,64},{4,68},{8,72},{12,76},{16,80},{20,84},{24,88},{28,92},{32,9... | collective-permute-start | bytes 792584 | tf_op jit(solution)/shard_map/ppermute | solution.py:118
  326.9 2.5 fusion.42
  329.4 3.1 fusion.35
  333.1 4.8 %gather_fusion.8 = bf16[1536,512]{1,0:T(8,128)(2,1)S(1)} fusion(bf16[1024,512]{1,0:T(8,128)(2,1)S(1)} %copy.79, s32[2048]{0:T(1024)S(1)} %pad_clamp_fusion), kind=kCustom, calls=%fused_computation.8 | custom fusion | bytes 3151872 | tf_op jit(solution)/shard_map/jit(_take)/gather | solution.py:143
  337.9 30.6 %all_to_all.25 = bf16[32,48,512]{2,1,0:T(8,128)(2,1)S(1)} all-to-all(bf16[32,48,512]{2,1,0:T(8,128)(2,1)S(1)} %bitcast.178), channel_id=1, replica_groups=mesh['ctx'=32,'head'=4] {'ctx'}, dimensions={0} | all-to-all | bytes 3145728 | tf_op jit(solution)/shard_map/all_to_all | solution.py:144
  368.5 5.1 %gather_fusion.9 = bf16[1024,512]{1,0:T(8,128)(2,1)} fusion(bf16[1536,512]{1,0:T(8,128)(2,1)S(1)} %bitcast.163, s32[1024]{0:T(1024)S(1)} %broadcast_clamp_fusion), kind=kCustom, calls=%fused_computation.9 | custom fusion | bytes 2101248 | tf_op jit(solution)/shard_map/jit(_take)/gather | solution.py:145
  373.6 9.9 %fusion.157 = f32[1024,1024]{1,0:T(8,128)} fusion(bf16[1024,2048]{1,0:T(8,128)(2,1)} %all-gather.5.cloned.1.call-done, bf16[2048,1024]{1,0:T(8,128)(2,1)} %bitcast.180), kind=kOutput, calls=%fused_computation.239 | convolution fusion | flops 4294967296 | bytes 12582912 | tf_op jit(solution)/shard_map/dot_general | solution.py:147
  383.6 36.9 %all-gather.7.cloned.1.call-done = bf16[1024,2048]{1,0:T(8,128)(2,1)} async-done(((bf16[1024,512]{1,0:T(8,128)(2,1)}), bf16[1024,2048]{1,0:T(8,128)(2,1)}) %all-gather.7.cloned.1.call-update) | async-done | bytes 4194320 | tf_op jit(solution)/shard_map/all_gather | solution.py:146
  420.5 10.6 %add_convert_fusion = bf16[1024,1024]{1,0:T(8,128)(2,1)} fusion(f32[1024,1024]{1,0:T(8,128)} %fusion.157, bf16[1024,2048]{1,0:T(8,128)(2,1)} %all-gather.7.cloned.1.call-done, bf16[2048,1024]{1,0:T(8,128)(2,1)} %bitcast.179), kind=kOutput, calls=%fused_computation.36 | convolution fusion | flops 4297064448 | bytes 14680064 | tf_op jit(solution)/shard_map/dot_general | solution.py:147
  (149 shorter events, 58.2 us)
Async XLA Ops:
  14.8 8.8 %copy-start.2 = (bf16[1024,1024]{1,0:T(8,128)(2,1)S(1)}, bf16[1024,1024]{1,0:T(8,128)(2,1)}, u32[]{:S(2)}) copy-start(bf16[1024,1024]{1,0:T(8,128)(2,1)} %param.9) | copy-start | bytes 6291460
  14.8 48.6 %all-to-all-start.2 = ((bf16[32,48,1024]{2,1,0:T(8,128)(2,1)}), bf16[32,48,1024]{2,1,0:T(8,128)(2,1)}, u32[]{:S(2)}, u32[]{:S(2)}) async-start(bf16[32,48,1024]{2,1,0:T(8,128)(2,1)} %bitcast.169), calls=%async_computation.2 | async-start | bytes 6291456 | tf_op jit(solution)/shard_map/all_to_all | solution.py:67
  29.5 39.0 %copy-start.28 = (s32[32]{0:T(128)S(1)}, s32[32]{0:T(128)}, u32[]{:S(2)}) copy-start(s32[32]{0:T(128)} %param.11) | copy-start | bytes 388
  29.5 47.4 %copy-start.3 = (bf16[1024,1024]{1,0:T(8,128)(2,1)S(1)}, bf16[1024,1024]{1,0:T(8,128)(2,1)}, u32[]{:S(2)}) copy-start(bf16[1024,1024]{1,0:T(8,128)(2,1)} %param.8) | copy-start | bytes 6291460
  63.4 44.9 %all-to-all-start.1 = ((bf16[32,48,1024]{2,1,0:T(8,128)(2,1)}), bf16[32,48,1024]{2,1,0:T(8,128)(2,1)}, u32[]{:S(2)}, u32[]{:S(2)}) async-start(bf16[32,48,1024]{2,1,0:T(8,128)(2,1)} %bitcast.167), calls=%async_computation.1 | async-start | bytes 6291456 | tf_op jit(solution)/shard_map/all_to_all | solution.py:67
  76.9 7.1 %copy-start.29 = (f32[8]{0:T(128)S(1)}, f32[8]{0:T(128)}, u32[]{:S(2)}) copy-start(f32[8]{0:T(128)} %param.12) | copy-start | bytes 100
  108.3 48.0 %all-to-all-start = ((bf16[32,48,1024]{2,1,0:T(8,128)(2,1)}), bf16[32,48,1024]{2,1,0:T(8,128)(2,1)S(1)}, u32[]{:S(2)}, u32[]{:S(2)}) async-start(bf16[32,48,1024]{2,1,0:T(8,128)(2,1)} %bitcast.168), calls=%async_computation | async-start | bytes 6291456 | tf_op jit(solution)/shard_map/all_to_all | solution.py:67
  145.2 4.6 %copy-start.4 = (bf16[128,8,8,128]{3,2,1,0:T(8,128)(2,1)S(1)}, bf16[128,8,8,128]{3,2,1,0:T(8,128)(2,1)}, u32[]{:S(2)}) copy-start(bf16[128,8,8,128]{3,2,1,0:T(8,128)(2,1)} %copy.101) | copy-start | bytes 6291460
  169.0 4.2 copy-start.11
  173.3 14.4 %collective-permute-start.2 = (f32[4,129,128]{2,1,0:T(8,128)S(1)}, f32[4,129,128]{2,1,0:T(8,128)S(1)}, u32[]{:S(2)}, u32[]{:S(2)}) collective-permute-start(f32[4,129,128]{2,1,0:T(8,128)S(1)} %pad_maximum_fusion), channel_id=1, source_target_pairs={{0,12},{4,16},{8,20},{12,24},{16,28},{20,32},{24,36},{28,40},{32,4... | collective-permute-start | bytes 792584 | tf_op jit(solution)/shard_map/ppermute | solution.py:118
  179.6 6.4 %copy-start.7 = (bf16[1024,2,128]{2,1,0:T(2,128)(2,1)S(1)}, bf16[1024,2,128]{2,1,0:T(2,128)(2,1)}, u32[]{:S(2)}) copy-start(bf16[1024,2,128]{2,1,0:T(2,128)(2,1)} %get-tuple-element.126) | copy-start | bytes 1572868
  179.6 6.5 %copy-start.10 = (bf16[1024,1,128]{2,1,0:T(2,128)(2,1)S(1)}, bf16[1024,1,128]{2,1,0:T(2,128)(2,1)}, u32[]{:S(2)}) copy-start(bf16[1024,1,128]{2,1,0:T(2,128)(2,1)} %get-tuple-element.119) | copy-start | bytes 786436
  181.1 24.9 %copy-start.12 = (pred[1024,1024]{0,1:T(8,128)(4,1)S(1)}, pred[1024,1024]{0,1:T(8,128)(4,1)}, u32[]{:S(2)}) copy-start(pred[1024,1024]{0,1:T(8,128)(4,1)} %iota_compare_fusion.3) | copy-start | bytes 3145732
  181.1 8.8 %collective-permute-start.1 = (f32[4,129,128]{2,1,0:T(8,128)S(1)}, f32[4,129,128]{2,1,0:T(8,128)S(1)}, u32[]{:S(2)}, u32[]{:S(2)}) collective-permute-start(f32[4,129,128]{2,1,0:T(8,128)S(1)} %pad_maximum_fusion), channel_id=1, source_target_pairs={{0,8},{4,12},{8,16},{12,20},{16,24},{20,28},{24,32},{28,36},{32,40... | collective-permute-start | bytes 792584 | tf_op jit(solution)/shard_map/ppermute | solution.py:118
  183.4 9.4 %collective-permute-start = (f32[4,129,128]{2,1,0:T(8,128)S(1)}, f32[4,129,128]{2,1,0:T(8,128)S(1)}, u32[]{:S(2)}, u32[]{:S(2)}) collective-permute-start(f32[4,129,128]{2,1,0:T(8,128)S(1)} %pad_maximum_fusion), channel_id=1, source_target_pairs={{0,4},{4,8},{8,12},{12,16},{16,20},{20,24},{24,28},{28,32},{32,36}... | collective-permute-start | bytes 792584 | tf_op jit(solution)/shard_map/ppermute | solution.py:118
  192.9 18.4 %copy-start.18 = (bf16[1024,2,128]{0,2,1:T(8,128)(2,1)S(1)}, bf16[1024,2,128]{0,2,1:T(8,128)(2,1)}, u32[]{:S(2)}) copy-start(bf16[1024,2,128]{0,2,1:T(8,128)(2,1)} %get-tuple-element.62) | copy-start | bytes 1572868
  193.0 22.6 %collective-permute-start.5 = (f32[4,129,128]{2,1,0:T(8,128)S(1)}, f32[4,129,128]{2,1,0:T(8,128)S(1)}, u32[]{:S(2)}, u32[]{:S(2)}) collective-permute-start(f32[4,129,128]{2,1,0:T(8,128)S(1)} %select_add_fusion.3), channel_id=1, source_target_pairs={{0,48},{4,52},{8,56},{12,60},{16,64},{20,68},{24,72},{28,76},{32,8... | collective-permute-start | bytes 792584 | tf_op jit(solution)/shard_map/ppermute | solution.py:118
  198.3 17.2 %collective-permute-start.4 = (f32[4,129,128]{2,1,0:T(8,128)S(1)}, f32[4,129,128]{2,1,0:T(8,128)}, u32[]{:S(2)}, u32[]{:S(2)}) collective-permute-start(f32[4,129,128]{2,1,0:T(8,128)S(1)} %select_add_fusion.3), channel_id=1, source_target_pairs={{0,32},{4,36},{8,40},{12,44},{16,48},{20,52},{24,56},{28,60},{32,6... | collective-permute-start | bytes 792584 | tf_op jit(solution)/shard_map/ppermute | solution.py:118
  201.9 13.6 %collective-permute-start.3 = (f32[4,129,128]{2,1,0:T(8,128)S(1)}, f32[4,129,128]{2,1,0:T(8,128)}, u32[]{:S(2)}, u32[]{:S(2)}) collective-permute-start(f32[4,129,128]{2,1,0:T(8,128)S(1)} %select_add_fusion.3), channel_id=1, source_target_pairs={{0,16},{4,20},{8,24},{12,28},{16,32},{20,36},{24,40},{28,44},{32,4... | collective-permute-start | bytes 792584 | tf_op jit(solution)/shard_map/ppermute | solution.py:118
  211.3 12.5 %copy-start.22 = (bf16[1024,1,128]{2,0,1:T(8,128)(2,1)S(1)}, bf16[1024,1,128]{2,0,1:T(8,128)(2,1)}, u32[]{:S(2)}) copy-start(bf16[1024,1,128]{2,0,1:T(8,128)(2,1)} %copy.93) | copy-start | bytes 786436
  211.3 12.5 %copy-start.27 = (bf16[1024,1,128]{2,0,1:T(8,128)(2,1)S(1)}, bf16[1024,1,128]{2,0,1:T(8,128)(2,1)}, u32[]{:S(2)}) copy-start(bf16[1024,1,128]{2,0,1:T(8,128)(2,1)} %get-tuple-element.71) | copy-start | bytes 786436
  215.6 9.5 %copy-start.26 = (bf16[1024,1,128]{0,2,1:T(8,128)(2,1)S(1)}, bf16[1024,1,128]{0,2,1:T(8,128)(2,1)}, u32[]{:S(2)}) copy-start(bf16[1024,1,128]{0,2,1:T(8,128)(2,1)} %get-tuple-element.69) | copy-start | bytes 786436
  215.6 12.1 %collective-permute-start.6 = (f32[4,129,128]{2,1,0:T(8,128)S(1)}, f32[4,129,128]{2,1,0:T(8,128)S(1)}, u32[]{:S(2)}, u32[]{:S(2)}) collective-permute-start(f32[4,129,128]{2,1,0:T(8,128)S(1)} %select_add_fusion.2), channel_id=1, source_target_pairs={{0,64},{4,68},{8,72},{12,76},{16,80},{20,84},{24,88},{28,92},{32,9... | collective-permute-start | bytes 792584 | tf_op jit(solution)/shard_map/ppermute | solution.py:118
  226.6 3.7 copy-start.31
  234.1 17.1 %copy-start.6 = (bf16[1024,2,128]{2,1,0:T(2,128)(2,1)S(1)}, bf16[1024,2,128]{2,1,0:T(2,128)(2,1)}, u32[]{:S(2)}) copy-start(bf16[1024,2,128]{2,1,0:T(2,128)(2,1)} %get-tuple-element.125) | copy-start | bytes 1572868
  239.5 12.5 %copy-start.9 = (bf16[1024,1,128]{2,1,0:T(2,128)(2,1)S(1)}, bf16[1024,1,128]{2,1,0:T(2,128)(2,1)}, u32[]{:S(2)}) copy-start(bf16[1024,1,128]{2,1,0:T(2,128)(2,1)} %get-tuple-element.117) | copy-start | bytes 786436
  239.5 13.3 %copy-start.8 = (bf16[1024,1,128]{2,1,0:T(2,128)(2,1)S(1)}, bf16[1024,1,128]{2,1,0:T(2,128)(2,1)}, u32[]{:S(2)}) copy-start(bf16[1024,1,128]{2,1,0:T(2,128)(2,1)} %get-tuple-element.118) | copy-start | bytes 786436
  239.5 43.1 %all-to-all-start.3 = ((bf16[32,48,512]{2,1,0:T(8,128)(2,1)}), bf16[32,48,512]{2,1,0:T(8,128)(2,1)S(1)}, u32[]{:S(2)}, u32[]{:S(2)}) async-start(bf16[32,48,512]{2,1,0:T(8,128)(2,1)} %bitcast.33), calls=%async_computation.3 | async-start | bytes 3145728 | tf_op jit(solution)/shard_map/all_to_all | solution.py:144
  250.1 123.5 %all-gather.5.cloned.1.call-start = ((), (), s32[]{:S(2)}) async-start(), calls=%async_computation.5 | async-start | bytes 5242880 | tf_op jit(solution)/shard_map/all_gather | solution.py:146
  252.8 12.3 %copy-start.25 = (bf16[1024,1,128]{0,2,1:T(8,128)(2,1)S(1)}, bf16[1024,1,128]{0,2,1:T(8,128)(2,1)}, u32[]{:S(2)}) copy-start(bf16[1024,1,128]{0,2,1:T(8,128)(2,1)} %get-tuple-element.79) | copy-start | bytes 786436
  252.8 20.5 %collective-permute-start.9 = (f32[4,129,128]{2,1,0:T(8,128)S(1)}, f32[4,129,128]{2,1,0:T(8,128)S(1)}, u32[]{:S(2)}, u32[]{:S(2)}) collective-permute-start(f32[4,129,128]{2,1,0:T(8,128)S(1)} %pad_maximum_fusion.1), channel_id=1, source_target_pairs={{0,12},{4,16},{8,20},{12,24},{16,28},{20,32},{24,36},{28,40},{32,4... | collective-permute-start | bytes 792584 | tf_op jit(solution)/shard_map/ppermute | solution.py:118
  258.0 21.3 %collective-permute-start.8 = (f32[4,129,128]{2,1,0:T(8,128)S(1)}, f32[4,129,128]{2,1,0:T(8,128)S(1)}, u32[]{:S(2)}, u32[]{:S(2)}) collective-permute-start(f32[4,129,128]{2,1,0:T(8,128)S(1)} %pad_maximum_fusion.1), channel_id=1, source_target_pairs={{0,8},{4,12},{8,16},{12,20},{16,24},{20,28},{24,32},{28,36},{32,40... | collective-permute-start | bytes 792584 | tf_op jit(solution)/shard_map/ppermute | solution.py:118
  260.2 22.4 %collective-permute-start.7 = (f32[4,129,128]{2,1,0:T(8,128)S(1)}, f32[4,129,128]{2,1,0:T(8,128)}, u32[]{:S(2)}, u32[]{:S(2)}) collective-permute-start(f32[4,129,128]{2,1,0:T(8,128)S(1)} %pad_maximum_fusion.1), channel_id=1, source_target_pairs={{0,4},{4,8},{8,12},{12,16},{16,20},{20,24},{24,28},{28,32},{32,36}... | collective-permute-start | bytes 792584 | tf_op jit(solution)/shard_map/ppermute | solution.py:118
  273.3 6.0 %copy-start.19 = (f32[4,129,128]{2,1,0:T(8,128)}, f32[4,129,128]{2,1,0:T(8,128)S(1)}, u32[]{:S(2)}) copy-start(f32[4,129,128]{2,1,0:T(8,128)S(1)} %collective-permute-done.9) | copy-start | bytes 792580
  282.6 19.5 %copy-start.13 = (pred[1024,1024]{0,1:T(8,128)(4,1)S(1)}, pred[1024,1024]{0,1:T(8,128)(4,1)}, u32[]{:S(2)}) copy-start(pred[1024,1024]{0,1:T(8,128)(4,1)} %iota_compare_fusion.3) | copy-start | bytes 3145732
  282.6 19.5 %copy-start.16 = (bf16[1024,2,128]{2,0,1:T(8,128)(2,1)S(1)}, bf16[1024,2,128]{2,0,1:T(8,128)(2,1)}, u32[]{:S(2)}) copy-start(bf16[1024,2,128]{2,0,1:T(8,128)(2,1)} %copy.97) | copy-start | bytes 1572868
  287.7 132.8 %all-gather.7.cloned.1.call-start = ((), (), s32[]{:S(2)}) async-start(), calls=%async_computation.6 | async-start | bytes 5242880 | tf_op jit(solution)/shard_map/all_gather | solution.py:146
  288.8 20.8 %copy-start.17 = (bf16[1024,2,128]{0,2,1:T(8,128)(2,1)S(1)}, bf16[1024,2,128]{0,2,1:T(8,128)(2,1)}, u32[]{:S(2)}) copy-start(bf16[1024,2,128]{0,2,1:T(8,128)(2,1)} %get-tuple-element.86) | copy-start | bytes 1572868
  288.8 25.1 %collective-permute-start.12 = (f32[4,129,128]{2,1,0:T(8,128)S(1)}, f32[4,129,128]{2,1,0:T(8,128)S(1)}, u32[]{:S(2)}, u32[]{:S(2)}) collective-permute-start(f32[4,129,128]{2,1,0:T(8,128)S(1)} %select_add_fusion.1), channel_id=1, source_target_pairs={{0,48},{4,52},{8,56},{12,60},{16,64},{20,68},{24,72},{28,76},{32,8... | collective-permute-start | bytes 792584 | tf_op jit(solution)/shard_map/ppermute | solution.py:118
  294.4 19.5 %collective-permute-start.11 = (f32[4,129,128]{2,1,0:T(8,128)S(1)}, f32[4,129,128]{2,1,0:T(8,128)S(1)}, u32[]{:S(2)}, u32[]{:S(2)}) collective-permute-start(f32[4,129,128]{2,1,0:T(8,128)S(1)} %select_add_fusion.1), channel_id=1, source_target_pairs={{0,32},{4,36},{8,40},{12,44},{16,48},{20,52},{24,56},{28,60},{32,6... | collective-permute-start | bytes 792584 | tf_op jit(solution)/shard_map/ppermute | solution.py:118
  297.7 16.1 %collective-permute-start.10 = (f32[4,129,128]{2,1,0:T(8,128)S(1)}, f32[4,129,128]{2,1,0:T(8,128)}, u32[]{:S(2)}, u32[]{:S(2)}) collective-permute-start(f32[4,129,128]{2,1,0:T(8,128)S(1)} %select_add_fusion.1), channel_id=1, source_target_pairs={{0,16},{4,20},{8,24},{12,28},{16,32},{20,36},{24,40},{28,44},{32,4... | collective-permute-start | bytes 792584 | tf_op jit(solution)/shard_map/ppermute | solution.py:118
  309.6 12.5 %copy-start.21 = (bf16[1024,1,128]{2,0,1:T(8,128)(2,1)S(1)}, bf16[1024,1,128]{2,0,1:T(8,128)(2,1)}, u32[]{:S(2)}) copy-start(bf16[1024,1,128]{2,0,1:T(8,128)(2,1)} %copy.98) | copy-start | bytes 786436
  309.6 12.5 %copy-start.24 = (bf16[1024,1,128]{2,0,1:T(8,128)(2,1)S(1)}, bf16[1024,1,128]{2,0,1:T(8,128)(2,1)}, u32[]{:S(2)}) copy-start(bf16[1024,1,128]{2,0,1:T(8,128)(2,1)} %get-tuple-element.95) | copy-start | bytes 786436
  313.9 9.4 %copy-start.23 = (bf16[1024,1,128]{0,2,1:T(8,128)(2,1)S(1)}, bf16[1024,1,128]{0,2,1:T(8,128)(2,1)}, u32[]{:S(2)}) copy-start(bf16[1024,1,128]{0,2,1:T(8,128)(2,1)} %get-tuple-element.93) | copy-start | bytes 786436
  314.0 12.9 %collective-permute-start.13 = (f32[4,129,128]{2,1,0:T(8,128)S(1)}, f32[4,129,128]{2,1,0:T(8,128)S(1)}, u32[]{:S(2)}, u32[]{:S(2)}) collective-permute-start(f32[4,129,128]{2,1,0:T(8,128)S(1)} %select_add_fusion), channel_id=1, source_target_pairs={{0,64},{4,68},{8,72},{12,76},{16,80},{20,84},{24,88},{28,92},{32,9... | collective-permute-start | bytes 792584 | tf_op jit(solution)/shard_map/ppermute | solution.py:118
  323.4 3.5 copy-start.14
  324.9 4.5 %copy-start.30 = (f32[1024,1,128]{0,2,1:T(8,128)S(1)}, f32[1024,1,128]{0,2,1:T(8,128)}, u32[]{:S(2)}) copy-start(f32[1024,1,128]{0,2,1:T(8,128)} %fusion.59) | copy-start | bytes 1572868
  420.5 10.6 %copy-start.1 = (bf16[1024,1024]{1,0:T(8,128)(2,1)S(1)}, bf16[1024,1024]{1,0:T(8,128)(2,1)}, u32[]{:S(2)}) copy-start(bf16[1024,1024]{1,0:T(8,128)(2,1)} %param.7) | copy-start | bytes 6291460
  (4 other events, 8.1 us)
Sparse Core Ops, SparseCore 0:
  287.8 52.1 all-gather.4
  373.7 46.6 all-gather.6

commit v8 on v5

--- a/solution.py
+++ b/solution.py
@@ -53,7 +53,7 @@
     causal = r_idx[:, None] >= r_idx[None, :]
     head_count = lax.axis_size("head")
     out_cols = out_weight.shape[1]
-    bounds = [0, heads // 2, heads]
+    bounds = [0, heads - (3 * heads) // 8, heads]
     weight_rows = out_weight.reshape(head_count, heads, dh, out_cols)
     gate_all = jax.nn.sigmoid(mem_gate)
     shifts = []
@@ -68,6 +68,12 @@
         return jnp.take(got, tok_slot, axis=0, mode="clip").reshape(seg, heads, dh)
 
     key_all = dispatch(keys)
+    weight_parts = [
+        weight_rows[:, bounds[g]:bounds[g + 1]].reshape(
+            head_count * (bounds[g + 1] - bounds[g]) * dh, out_cols
+        )
+        for g in range(len(bounds) - 1)
+    ]
     value_all = dispatch(values)
     query_all = dispatch(queries)
 
@@ -83,7 +89,7 @@
             "hqk,khd->qhd", probabilities, value_part, preferred_element_type=f32
         )
 
-    def one_group(g, hold):
+    def one_group(g, hold, weights):
         first, last = bounds[g], bounds[g + 1]
         group_heads = last - first
         group_width = group_heads * dh
@@ -100,7 +106,7 @@
         delta_z = jnp.sum(key_feat, axis=0)
         delta = jnp.concatenate([delta_m, delta_z[:, None, :]], axis=1)
         if hold is not None:
-            delta, _ = lax.optimization_barrier((delta, hold))
+            delta, _ = lax.optimization_barrier((delta, hold[0]))
 
         pieces = []
         total = delta
@@ -109,6 +115,8 @@
             total, operands = lax.optimization_barrier(
                 (total, (query_heads[:, lo:hi], key_heads[:, lo:hi], value_heads[:, lo:hi]))
             )
+            if hold is not None and k == 1:
+                total, _ = lax.optimization_barrier((total, hold[1]))
             perm = [(j, j + step) for j in range(n - step)]
             got = lax.ppermute(total, "ctx", perm)
             if hi > lo:
@@ -138,14 +146,14 @@
         gathered = lax.all_gather(rows, "head", axis=1, tiled=True)
         part = jnp.dot(
             gathered,
-            weight_rows[:, first:last].reshape(head_count * group_width, out_cols),
+            weights[g],
             preferred_element_type=f32,
         )
-        return part, combined
+        return part, (combined, rows), weights
 
-    summed, hold = one_group(0, None)
+    summed, hold, weight_parts = one_group(0, None, weight_parts)
     for g in range(1, len(bounds) - 1):
-        part, hold = one_group(g, hold)
+        part, hold, weight_parts = one_group(g, hold, weight_parts)
         summed = summed + part
     return summed.astype(bf16)
 

time: 419 us -> 419 us (level)
  starting transfers between devices: 77.7 us -> 84.7 us
  waiting for transfers between devices: 119 us -> 114 us
  blocking collectives: 31.7 us -> 26.8 us
    all_to_all x1, waiting for transfers between devices: 0.01 us -> 14.7 us  [one_group(): lax.all_to_all(outgoing, 'ctx', 0, 0, tiled=True)]
    all_gather x2, waiting for transfers between devices: 30.1 us -> 18.4 us  [one_group(): gathered = lax.all_gather(rows, 'head', axis=1, tiled=True)]
    ppermute x10, waiting for transfers between devices: 24 us -> 13 us  [one_group(): got = lax.ppermute(total, 'ctx', perm)]
    all_to_all x1, starting transfers between devices: 8.23 us -> 15.7 us  [one_group(): lax.all_to_all(outgoing, 'ctx', 0, 0, tiled=True)]
    all_to_all x1, blocking collectives: 31.7 us -> 26.8 us  [one_group(): lax.all_to_all(outgoing, 'ctx', 0, 0, tiled=True)]
    slice x1 -> x2, local copies, waits for them, and re-layouts: 6.1 us -> 9.46 us  [per_device(): weight_rows[:, bounds[g]:bounds[g + 1]]]
  transfers between devices with their start and end apart: 16 -> 16, of which waited for: 11 -> 12; matrix products, arithmetic and copies ran while one was open for 31% -> 29% of each run, Pallas kernels for 0% -> 0%
where the time goes in v8:
time: 419 us; the launch traced here: 413 us
  waiting for transfers between devices  114 us (27%)
  local copies, waits for them, and re-layouts  97.5 us (23%)
  starting transfers between devices  84.7 us (20%)
  matrix products  58 us (14%)
  blocking collectives  26.8 us (6%)
  between operations  17.9 us (4%)
  other arithmetic  13.9 us (3%)
    all_to_all x3, waiting for transfers between devices, dispatch(): got = lax.all_to_all(buffer, 'ctx', 0, 0, tiled=True).reshape(slots, width)  67.7 us
    ppermute x10, starting transfers between devices, one_group(): got = lax.ppermute(total, 'ctx', perm)  49.7 us
    all_to_all x1, blocking collectives, one_group(): lax.all_to_all(outgoing, 'ctx', 0, 0, tiled=True)  26.8 us
    gather x4, local copies, waits for them, and re-layouts, dispatch(): return jnp.take(got, tok_slot, axis=0, mode='clip').reshape(seg, heads, dh)  25.9 us
    dot_general x2, matrix products, one_group(): part = jnp.dot(gathered, weights[g], preferred_element_type=f32)  19.5 us
    all_to_all x3, starting transfers between devices, dispatch(): got = lax.all_to_all(buffer, 'ctx', 0, 0, tiled=True).reshape(slots, width)  19.1 us
    all_gather x2, waiting for transfers between devices, one_group(): gathered = lax.all_gather(rows, 'head', axis=1, tiled=True)  18.4 us
    gather x3, local copies, waits for them, and re-layouts, dispatch(): jnp.take(source, slot_row, axis=0, mode='clip').reshape(n, cap, width)  17.5 us
  transfers between devices with their start and end apart: 16, of which 12 were waited for; matrix products, arithmetic and copies ran while one was open for 29% of the time, Pallas kernels for 0%

profile of v8, /device:TPU:1, one launch (start us, length us, event | category | flops | bytes accessed | tf_op | source)
XLA Modules:
  0.0 412.7 jit_solution(5850490624442742968)
XLA Ops:
  11.6 5.8 %gather_fusion.2 = bf16[1536,1024]{1,0:T(8,128)(2,1)} fusion(bf16[1024,1024]{1,0:T(8,128)(2,1)S(1)} %copy-done, s32[2048]{0:T(1024)S(1)} %get-tuple-element.157), kind=kCustom, calls=%fused_computation.2 | custom fusion | bytes 6297600 | tf_op jit(solution)/shard_map/jit(_take)/gather | solution.py:66
  17.4 8.8 %all-to-all-start.1 = ((bf16[32,48,1024]{2,1,0:T(8,128)(2,1)}), bf16[32,48,1024]{2,1,0:T(8,128)(2,1)}, u32[]{:S(2)}, u32[]{:S(2)}) async-start(bf16[32,48,1024]{2,1,0:T(8,128)(2,1)} %bitcast.224), calls=%async_computation.1 | async-start | bytes 6291456 | tf_op jit(solution)/shard_map/all_to_all | solution.py:67
  26.2 5.8 %gather_fusion = bf16[1536,1024]{1,0:T(8,128)(2,1)} fusion(bf16[1024,1024]{1,0:T(8,128)(2,1)S(1)} %copy-done.2, s32[2048]{0:T(1024)S(1)} %get-tuple-element.157), kind=kCustom, calls=%fused_computation | custom fusion | bytes 6297600 | tf_op jit(solution)/shard_map/jit(_take)/gather | solution.py:66
  32.0 34.0 %all-to-all-done.1 = bf16[32,48,1024]{2,1,0:T(8,128)(2,1)} async-done(((bf16[32,48,1024]{2,1,0:T(8,128)(2,1)}), bf16[32,48,1024]{2,1,0:T(8,128)(2,1)}, u32[]{:S(2)}, u32[]{:S(2)}) %all-to-all-start.1) | async-done | bytes 3145760 | tf_op jit(solution)/shard_map/all_to_all | solution.py:67
  66.0 5.0 %all-to-all-start = ((bf16[32,48,1024]{2,1,0:T(8,128)(2,1)}), bf16[32,48,1024]{2,1,0:T(8,128)(2,1)}, u32[]{:S(2)}, u32[]{:S(2)}) async-start(bf16[32,48,1024]{2,1,0:T(8,128)(2,1)} %bitcast.223), calls=%async_computation | async-start | bytes 6291456 | tf_op jit(solution)/shard_map/all_to_all | solution.py:67
  76.1 5.8 %gather_fusion.4 = bf16[1536,1024]{1,0:T(8,128)(2,1)} fusion(bf16[1024,1024]{1,0:T(8,128)(2,1)S(1)} %copy-done.3, s32[2048]{0:T(1024)S(1)} %get-tuple-element.157), kind=kCustom, calls=%fused_computation.4 | custom fusion | bytes 6297600 | tf_op jit(solution)/shard_map/jit(_take)/gather | solution.py:66
  82.0 28.9 %all-to-all-done = bf16[32,48,1024]{2,1,0:T(8,128)(2,1)} async-done(((bf16[32,48,1024]{2,1,0:T(8,128)(2,1)}), bf16[32,48,1024]{2,1,0:T(8,128)(2,1)}, u32[]{:S(2)}, u32[]{:S(2)}) %all-to-all-start) | async-done | bytes 3145760 | tf_op jit(solution)/shard_map/all_to_all | solution.py:67
  110.9 5.3 %all-to-all-start.2 = ((bf16[32,48,1024]{2,1,0:T(8,128)(2,1)}), bf16[32,48,1024]{2,1,0:T(8,128)(2,1)S(1)}, u32[]{:S(2)}, u32[]{:S(2)}) async-start(bf16[32,48,1024]{2,1,0:T(8,128)(2,1)} %bitcast.222), calls=%async_computation.2 | async-start | bytes 6291456 | tf_op jit(solution)/shard_map/all_to_all | solution.py:67
  117.5 8.3 %gather_fusion.3 = bf16[1024,1024]{1,0:T(8,128)(2,1)} fusion(bf16[1536,1024]{1,0:T(8,128)(2,1)} %bitcast.6, s32[1024]{0:T(1024)S(1)} %broadcast_clamp_fusion.1), kind=kCustom, calls=%fused_computation.3 | custom fusion | bytes 4198400 | tf_op jit(solution)/shard_map/jit(_take)/gather | solution.py:68
  125.8 4.0 copy.48
  129.8 8.3 %gather_fusion.1 = bf16[1024,1024]{1,0:T(8,128)(2,1)} fusion(bf16[1536,1024]{1,0:T(8,128)(2,1)} %bitcast.4, s32[1024]{0:T(1024)S(1)} %broadcast_clamp_fusion.1), kind=kCustom, calls=%fused_computation.1 | custom fusion | bytes 4198400 | tf_op jit(solution)/shard_map/jit(_take)/gather | solution.py:68
  138.1 2.4 copy.106
  143.2 3.1 fusion.32
  146.3 4.7 %fusion.162 = (bf16[1024,1,128]{2,1,0:T(2,128)(2,1)}, bf16[1024,1,128]{2,1,0:T(2,128)(2,1)}, bf16[1024,1,128]{2,1,0:T(2,128)(2,1)}, bf16[1024,1,128]{2,1,0:T(2,1...) fusion(bf16[1024,8,128]{2,1,0:T(8,128)(2,1)S(1)} %bitcast.216), kind=kLoop, calls=%fused_computation.262 | loop fusion | bytes 4194304 | tf_op jit(solution)/shard_map/slice | solution.py:116
  151.0 4.9 %all-to-all-done.2 = bf16[32,48,1024]{2,1,0:T(8,128)(2,1)S(1)} async-done(((bf16[32,48,1024]{2,1,0:T(8,128)(2,1)}), bf16[32,48,1024]{2,1,0:T(8,128)(2,1)S(1)}, u32[]{:S(2)}, u32[]{:S(2)}) %all-to-all-start.2) | async-done | bytes 3145760 | tf_op jit(solution)/shard_map/all_to_all | solution.py:67
  155.8 5.3 %gather_fusion.5 = bf16[1024,1024]{1,0:T(8,128)(2,1)} fusion(bf16[1536,1024]{1,0:T(8,128)(2,1)S(1)} %bitcast.211, s32[1024]{0:T(1024)S(1)} %broadcast_clamp_fusion.1), kind=kCustom, calls=%fused_computation.5 | custom fusion | bytes 4198400 | tf_op jit(solution)/shard_map/jit(_take)/gather | solution.py:68
  161.2 2.3 copy.107
  163.5 4.6 %fusion.163 = (bf16[1024,1,128]{2,1,0:T(2,128)(2,1)S(1)}, bf16[1024,1,128]{2,1,0:T(2,128)(2,1)S(1)}, bf16[1024,1,128]{2,1,0:T(2,128)(2,1)}, bf16[1024,1,128]{2,1...) fusion(bf16[1024,8,128]{2,1,0:T(8,128)(2,1)S(1)} %bitcast.218), kind=kLoop, calls=%fused_computation.263 | loop fusion | bytes 4194304 | tf_op jit(solution)/shard_map/slice | solution.py:116
  168.2 3.4 collective-permute-start
  175.8 2.0 collective-permute-start.1
  180.6 2.0 collective-permute-done.1
  182.6 6.2 %collective-permute-start.2 = (f32[5,129,128]{2,1,0:T(8,128)S(1)}, f32[5,129,128]{2,1,0:T(8,128)S(1)}, u32[]{:S(2)}, u32[]{:S(2)}) collective-permute-start(f32[5,129,128]{2,1,0:T(8,128)S(1)} %select_add_fusion.2), channel_id=1, source_target_pairs={{0,16},{4,20},{8,24},{12,28},{16,32},{20,36},{24,40},{28,44},{32,4... | collective-permute-start | bytes 990728 | tf_op jit(solution)/shard_map/ppermute | solution.py:121
  193.5 5.4 %collective-permute-start.3 = (f32[5,129,128]{2,1,0:T(8,128)S(1)}, f32[5,129,128]{2,1,0:T(8,128)S(1)}, u32[]{:S(2)}, u32[]{:S(2)}) collective-permute-start(f32[5,129,128]{2,1,0:T(8,128)S(1)} %select_add_fusion.1), channel_id=1, source_target_pairs={{0,32},{4,36},{8,40},{12,44},{16,48},{20,52},{24,56},{28,60},{32,6... | collective-permute-start | bytes 990728 | tf_op jit(solution)/shard_map/ppermute | solution.py:121
  203.2 5.9 %collective-permute-start.4 = (f32[5,129,128]{2,1,0:T(8,128)S(1)}, f32[5,129,128]{2,1,0:T(8,128)S(1)}, u32[]{:S(2)}, u32[]{:S(2)}) collective-permute-start(f32[5,129,128]{2,1,0:T(8,128)S(1)} %select_add_fusion), channel_id=1, source_target_pairs={{0,64},{4,68},{8,72},{12,76},{16,80},{20,84},{24,88},{28,92},{32,9... | collective-permute-start | bytes 990728 | tf_op jit(solution)/shard_map/ppermute | solution.py:121
  213.4 3.1 fusion.27
  216.6 5.0 %fusion.26 = bf16[1024,5,128]{0,2,1:T(8,128)(2,1)} fusion(f32[1024,5,128]{0,2,1:T(8,128)S(1)} %constant_dynamic-update-slice_fusion, f32[5]{0:T(128)S(1)} %get-tuple-element.139, f32[1024,5]{0,1:T(8,128)S(1)} %fusion.127, f32[5]{0:T(128)S(1)} %get-tuple-element.138, bf16[1024,5,128]{2,1,0:T(8,128)(2,1)S(1)} %bitcast.220, ...), kind=kOutput, calls=%fused_computation.78 | convolution fusion | flops 1013186560 | bytes 6390784 | tf_op jit(solution)/shard_map/qhd,hde->qhe/dot_general | solution.py:133
  223.3 5.6 %gather_fusion.6 = bf16[1536,640]{1,0:T(8,128)(2,1)} fusion(bf16[1024,640]{1,0:T(8,128)(2,1)S(1)} %copy.63, s32[2048]{0:T(1024)S(1)} %get-tuple-element.156), kind=kCustom, calls=%fused_computation.6 | custom fusion | bytes 3938304 | tf_op jit(solution)/shard_map/jit(_take)/gather | solution.py:143
  228.8 15.7 %all-to-all-start.3 = ((bf16[32,48,640]{2,1,0:T(8,128)(2,1)}), bf16[32,48,640]{2,1,0:T(8,128)(2,1)S(1)}, u32[]{:S(2)}, u32[]{:S(2)}) async-start(bf16[32,48,640]{2,1,0:T(8,128)(2,1)} %bitcast.232), calls=%async_computation.3 | async-start | bytes 3932160 | tf_op jit(solution)/shard_map/all_to_all | solution.py:144
  245.6 2.1 slice.217
  250.0 3.1 fusion.53
  253.1 3.5 collective-permute-start.5
  256.7 14.7 %all-to-all-done.3 = bf16[32,48,640]{2,1,0:T(8,128)(2,1)S(1)} async-done(((bf16[32,48,640]{2,1,0:T(8,128)(2,1)}), bf16[32,48,640]{2,1,0:T(8,128)(2,1)S(1)}, u32[]{:S(2)}, u32[]{:S(2)}) %all-to-all-start.3) | async-done | bytes 1966112 | tf_op jit(solution)/shard_map/all_to_all | solution.py:144
  271.4 5.2 %gather_fusion.7 = bf16[1024,640]{1,0:T(8,128)(2,1)} fusion(bf16[1536,640]{1,0:T(8,128)(2,1)S(1)} %bitcast.212, s32[1024]{0:T(1024)S(1)} %broadcast_clamp_fusion), kind=kCustom, calls=%fused_computation.7 | custom fusion | bytes 2625536 | tf_op jit(solution)/shard_map/jit(_take)/gather | solution.py:145
  282.8 3.5 collective-permute-done.6
  286.4 5.4 %collective-permute-start.7 = (f32[3,129,128]{2,1,0:T(8,128)S(1)}, f32[3,129,128]{2,1,0:T(8,128)S(1)}, u32[]{:S(2)}, u32[]{:S(2)}) collective-permute-start(f32[3,129,128]{2,1,0:T(8,128)S(1)} %select_add_fusion.6), channel_id=1, source_target_pairs={{0,16},{4,20},{8,24},{12,28},{16,32},{20,36},{24,40},{28,44},{32,4... | collective-permute-start | bytes 594440 | tf_op jit(solution)/shard_map/ppermute | solution.py:121
  294.6 9.5 %collective-permute-start.8 = (f32[3,129,128]{2,1,0:T(8,128)S(1)}, f32[3,129,128]{2,1,0:T(8,128)S(1)}, u32[]{:S(2)}, u32[]{:S(2)}) collective-permute-start(f32[3,129,128]{2,1,0:T(8,128)S(1)} %select_add_fusion.5), channel_id=1, source_target_pairs={{0,32},{4,36},{8,40},{12,44},{16,48},{20,52},{24,56},{28,60},{32,6... | collective-permute-start | bytes 594440 | tf_op jit(solution)/shard_map/ppermute | solution.py:121
  304.8 2.0 collective-permute-done.8
  306.9 7.1 %collective-permute-start.9 = (f32[3,129,128]{2,1,0:T(8,128)S(1)}, f32[3,129,128]{2,1,0:T(8,128)S(1)}, u32[]{:S(2)}, u32[]{:S(2)}) collective-permute-start(f32[3,129,128]{2,1,0:T(8,128)S(1)} %select_add_fusion.4), channel_id=1, source_target_pairs={{0,64},{4,68},{8,72},{12,76},{16,80},{20,84},{24,88},{28,92},{32,9... | collective-permute-start | bytes 594440 | tf_op jit(solution)/shard_map/ppermute | solution.py:121
  316.8 1.9 fusion.49
  318.7 2.4 fusion.47
  321.5 4.7 %gather_fusion.8 = bf16[1536,384]{1,0:T(8,128)(2,1)S(1)} fusion(bf16[1024,384]{1,0:T(8,128)(2,1)S(1)} %copy.75, s32[2048]{0:T(1024)S(1)} %get-tuple-element.156), kind=kCustom, calls=%fused_computation.8 | custom fusion | bytes 2365440 | tf_op jit(solution)/shard_map/jit(_take)/gather | solution.py:143
  326.2 26.8 %all_to_all.25 = bf16[32,48,384]{2,1,0:T(8,128)(2,1)S(1)} all-to-all(bf16[32,48,384]{2,1,0:T(8,128)(2,1)S(1)} %bitcast.234), channel_id=1, replica_groups=mesh['ctx'=32,'head'=4] {'ctx'}, dimensions={0} | all-to-all | bytes 2359296 | tf_op jit(solution)/shard_map/all_to_all | solution.py:144
  353.0 5.0 %gather_fusion.9 = bf16[1024,384]{1,0:T(8,128)(2,1)} fusion(bf16[1536,384]{1,0:T(8,128)(2,1)S(1)} %bitcast.213, s32[1024]{0:T(1024)S(1)} %broadcast_clamp_fusion), kind=kCustom, calls=%fused_computation.9 | custom fusion | bytes 1576960 | tf_op jit(solution)/shard_map/jit(_take)/gather | solution.py:145
  358.0 3.8 slice.231
  361.8 5.6 %slice.216 = bf16[4,5,128,1024]{3,2,1,0:T(8,128)(2,1)} slice(bf16[4,8,128,1024]{3,2,1,0:T(8,128)(2,1)} %bitcast.228), slice={[0:4], [0:5], [0:128], [0:1024]} | slice | bytes 10485760 | tf_op jit(solution)/shard_map/slice | solution.py:72
  367.5 10.6 %fusion.166 = f32[1024,1024]{1,0:T(8,128)} fusion(bf16[1024,2560]{1,0:T(8,128)(2,1)} %all-gather.5.cloned.1.call-done, bf16[2560,1024]{1,0:T(8,128)(2,1)} %bitcast.233), kind=kOutput, calls=%fused_computation.266 | convolution fusion | flops 5368709120 | bytes 14680064 | tf_op jit(solution)/shard_map/dot_general | solution.py:147
  378.1 18.4 %all-gather.7.cloned.1.call-done = bf16[1024,1536]{1,0:T(8,128)(2,1)} async-done(((bf16[1024,384]{1,0:T(8,128)(2,1)}), bf16[1024,1536]{1,0:T(8,128)(2,1)}) %all-gather.7.cloned.1.call-update) | async-done | bytes 3145744 | tf_op jit(solution)/shard_map/all_gather | solution.py:146
  396.5 8.9 %add_convert_fusion = bf16[1024,1024]{1,0:T(8,128)(2,1)} fusion(f32[1024,1024]{1,0:T(8,128)} %fusion.166, bf16[1024,1536]{1,0:T(8,128)(2,1)} %all-gather.7.cloned.1.call-done, bf16[1536,1024]{1,0:T(8,128)(2,1)} %bitcast.235), kind=kOutput, calls=%fused_computation.26 | convolution fusion | flops 3223322624 | bytes 12582912 | tf_op jit(solution)/shard_map/dot_general | solution.py:147
  (162 shorter events, 49.2 us)
Async XLA Ops:
  6.5 5.0 %copy-start = (bf16[1024,1024]{1,0:T(8,128)(2,1)S(1)}, bf16[1024,1024]{1,0:T(8,128)(2,1)}, u32[]{:S(2)}) copy-start(bf16[1024,1024]{1,0:T(8,128)(2,1)} %param.9) | copy-start | bytes 6291460
  7.6 9.8 %copy-start.17 = (s32[32,1024]{1,0:T(8,128)}, s32[32,1024]{1,0:T(8,128)S(1)}, u32[]{:S(2)}) copy-start(s32[32,1024]{1,0:T(8,128)S(1)} %reshape.467) | copy-start | bytes 393220
  17.4 8.8 %copy-start.2 = (bf16[1024,1024]{1,0:T(8,128)(2,1)S(1)}, bf16[1024,1024]{1,0:T(8,128)(2,1)}, u32[]{:S(2)}) copy-start(bf16[1024,1024]{1,0:T(8,128)(2,1)} %param.8) | copy-start | bytes 6291460
  17.4 48.6 %all-to-all-start.1 = ((bf16[32,48,1024]{2,1,0:T(8,128)(2,1)}), bf16[32,48,1024]{2,1,0:T(8,128)(2,1)}, u32[]{:S(2)}, u32[]{:S(2)}) async-start(bf16[32,48,1024]{2,1,0:T(8,128)(2,1)} %bitcast.224), calls=%async_computation.1 | async-start | bytes 6291456 | tf_op jit(solution)/shard_map/all_to_all | solution.py:67
  32.0 39.0 %copy-start.27 = (s32[32]{0:T(128)S(1)}, s32[32]{0:T(128)}, u32[]{:S(2)}) copy-start(s32[32]{0:T(128)} %param.11) | copy-start | bytes 388
  32.0 44.1 %copy-start.3 = (bf16[1024,1024]{1,0:T(8,128)(2,1)S(1)}, bf16[1024,1024]{1,0:T(8,128)(2,1)}, u32[]{:S(2)}) copy-start(bf16[1024,1024]{1,0:T(8,128)(2,1)} %param.7) | copy-start | bytes 6291460
  66.0 44.9 %all-to-all-start = ((bf16[32,48,1024]{2,1,0:T(8,128)(2,1)}), bf16[32,48,1024]{2,1,0:T(8,128)(2,1)}, u32[]{:S(2)}, u32[]{:S(2)}) async-start(bf16[32,48,1024]{2,1,0:T(8,128)(2,1)} %bitcast.223), calls=%async_computation | async-start | bytes 6291456 | tf_op jit(solution)/shard_map/all_to_all | solution.py:67
  82.0 34.2 %copy-start.28 = (f32[8]{0:T(128)S(1)}, f32[8]{0:T(128)}, u32[]{:S(2)}) copy-start(f32[8]{0:T(128)} %param.12) | copy-start | bytes 100
  110.9 45.0 %all-to-all-start.2 = ((bf16[32,48,1024]{2,1,0:T(8,128)(2,1)}), bf16[32,48,1024]{2,1,0:T(8,128)(2,1)S(1)}, u32[]{:S(2)}, u32[]{:S(2)}) async-start(bf16[32,48,1024]{2,1,0:T(8,128)(2,1)} %bitcast.222), calls=%async_computation.2 | async-start | bytes 6291456 | tf_op jit(solution)/shard_map/all_to_all | solution.py:67
  138.1 2.4 copy-start.7
  140.5 5.8 %copy-start.4 = (bf16[128,8,8,128]{3,2,1,0:T(8,128)(2,1)}, bf16[128,8,8,128]{3,2,1,0:T(8,128)(2,1)S(1)}, u32[]{:S(2)}) copy-start(bf16[128,8,8,128]{3,2,1,0:T(8,128)(2,1)S(1)} %copy.106) | copy-start | bytes 6291460
  161.2 2.3 copy-start.16
  163.4 53.1 %copy-start.5 = (bf16[128,8,8,128]{3,2,1,0:T(8,128)(2,1)}, bf16[128,8,8,128]{3,2,1,0:T(8,128)(2,1)S(1)}, u32[]{:S(2)}) copy-start(bf16[128,8,8,128]{3,2,1,0:T(8,128)(2,1)S(1)} %copy.107) | copy-start | bytes 6291460
  168.2 4.6 %copy-start.25 = (bf16[1024,1,128]{0,2,1:T(8,128)(2,1)S(1)}, bf16[1024,1,128]{0,2,1:T(8,128)(2,1)}, u32[]{:S(2)}) copy-start(bf16[1024,1,128]{0,2,1:T(8,128)(2,1)} %get-tuple-element.58) | copy-start | bytes 786436
  168.2 7.6 %collective-permute-start = (f32[5,129,128]{2,1,0:T(8,128)S(1)}, f32[5,129,128]{2,1,0:T(8,128)S(1)}, u32[]{:S(2)}, u32[]{:S(2)}) collective-permute-start(f32[5,129,128]{2,1,0:T(8,128)S(1)} %pad_maximum_fusion), channel_id=1, source_target_pairs={{0,4},{4,8},{8,12},{12,16},{16,20},{20,24},{24,28},{28,32},{32,36}... | collective-permute-start | bytes 990728 | tf_op jit(solution)/shard_map/ppermute | solution.py:121
  172.8 1.5 copy-start.15
  172.8 1.6 copy-start.14
  172.8 1.6 copy-start.13
  172.8 1.7 copy-start.12
  175.8 3.3 copy-start.24
  175.8 6.8 %collective-permute-start.1 = (f32[5,129,128]{2,1,0:T(8,128)S(1)}, f32[5,129,128]{2,1,0:T(8,128)S(1)}, u32[]{:S(2)}, u32[]{:S(2)}) collective-permute-start(f32[5,129,128]{2,1,0:T(8,128)S(1)} %select_add_fusion.3), channel_id=1, source_target_pairs={{0,8},{4,12},{8,16},{12,20},{16,24},{20,28},{24,32},{28,36},{32,40... | collective-permute-start | bytes 990728 | tf_op jit(solution)/shard_map/ppermute | solution.py:121
  182.6 7.5 %copy-start.23 = (bf16[1024,1,128]{0,2,1:T(8,128)(2,1)S(1)}, bf16[1024,1,128]{0,2,1:T(8,128)(2,1)}, u32[]{:S(2)}) copy-start(bf16[1024,1,128]{0,2,1:T(8,128)(2,1)} %get-tuple-element.68) | copy-start | bytes 786436
  182.6 10.9 %collective-permute-start.2 = (f32[5,129,128]{2,1,0:T(8,128)S(1)}, f32[5,129,128]{2,1,0:T(8,128)S(1)}, u32[]{:S(2)}, u32[]{:S(2)}) collective-permute-start(f32[5,129,128]{2,1,0:T(8,128)S(1)} %select_add_fusion.2), channel_id=1, source_target_pairs={{0,16},{4,20},{8,24},{12,28},{16,32},{20,36},{24,40},{28,44},{32,4... | collective-permute-start | bytes 990728 | tf_op jit(solution)/shard_map/ppermute | solution.py:121
  193.5 6.7 %copy-start.22 = (bf16[1024,1,128]{0,2,1:T(8,128)(2,1)S(1)}, bf16[1024,1,128]{0,2,1:T(8,128)(2,1)}, u32[]{:S(2)}) copy-start(bf16[1024,1,128]{0,2,1:T(8,128)(2,1)} %get-tuple-element.73) | copy-start | bytes 786436
  193.5 9.6 %collective-permute-start.3 = (f32[5,129,128]{2,1,0:T(8,128)S(1)}, f32[5,129,128]{2,1,0:T(8,128)S(1)}, u32[]{:S(2)}, u32[]{:S(2)}) collective-permute-start(f32[5,129,128]{2,1,0:T(8,128)S(1)} %select_add_fusion.1), channel_id=1, source_target_pairs={{0,32},{4,36},{8,40},{12,44},{16,48},{20,52},{24,56},{28,60},{32,6... | collective-permute-start | bytes 990728 | tf_op jit(solution)/shard_map/ppermute | solution.py:121
  203.2 7.1 %copy-start.21 = (bf16[1024,1,128]{0,2,1:T(8,128)(2,1)S(1)}, bf16[1024,1,128]{0,2,1:T(8,128)(2,1)}, u32[]{:S(2)}) copy-start(bf16[1024,1,128]{0,2,1:T(8,128)(2,1)} %get-tuple-element.78) | copy-start | bytes 786436
  203.2 10.1 %collective-permute-start.4 = (f32[5,129,128]{2,1,0:T(8,128)S(1)}, f32[5,129,128]{2,1,0:T(8,128)S(1)}, u32[]{:S(2)}, u32[]{:S(2)}) collective-permute-start(f32[5,129,128]{2,1,0:T(8,128)S(1)} %select_add_fusion), channel_id=1, source_target_pairs={{0,64},{4,68},{8,72},{12,76},{16,80},{20,84},{24,88},{28,92},{32,9... | collective-permute-start | bytes 990728 | tf_op jit(solution)/shard_map/ppermute | solution.py:121
  228.8 19.7 %copy-start.10 = (bf16[1024,1,128]{2,1,0:T(2,128)(2,1)S(1)}, bf16[1024,1,128]{2,1,0:T(2,128)(2,1)}, u32[]{:S(2)}) copy-start(bf16[1024,1,128]{2,1,0:T(2,128)(2,1)} %get-tuple-element.121) | copy-start | bytes 786436
  228.8 42.6 %all-to-all-start.3 = ((bf16[32,48,640]{2,1,0:T(8,128)(2,1)}), bf16[32,48,640]{2,1,0:T(8,128)(2,1)S(1)}, u32[]{:S(2)}, u32[]{:S(2)}) async-start(bf16[32,48,640]{2,1,0:T(8,128)(2,1)} %bitcast.232), calls=%async_computation.3 | async-start | bytes 3932160 | tf_op jit(solution)/shard_map/all_to_all | solution.py:144
  244.5 123.0 %all-gather.5.cloned.1.call-start = ((), (), s32[]{:S(2)}) async-start(), calls=%async_computation.5 | async-start | bytes 6553600 | tf_op jit(solution)/shard_map/all_gather | solution.py:146
  244.8 4.5 %copy-start.11 = (bf16[1024,1,128]{2,1,0:T(2,128)(2,1)S(1)}, bf16[1024,1,128]{2,1,0:T(2,128)(2,1)}, u32[]{:S(2)}) copy-start(bf16[1024,1,128]{2,1,0:T(2,128)(2,1)} %get-tuple-element.129) | copy-start | bytes 786436
  253.1 27.3 %collective-permute-start.5 = (f32[3,129,128]{2,1,0:T(8,128)S(1)}, f32[3,129,128]{2,1,0:T(8,128)}, u32[]{:S(2)}, u32[]{:S(2)}) collective-permute-start(f32[3,129,128]{2,1,0:T(8,128)S(1)} %pad_maximum_fusion.1), channel_id=1, source_target_pairs={{0,4},{4,8},{8,12},{12,16},{16,20},{20,24},{24,28},{28,32},{32,36}... | collective-permute-start | bytes 594440 | tf_op jit(solution)/shard_map/ppermute | solution.py:121
  271.4 5.2 %copy-start.26 = (bf16[1024,1,128]{2,0,1:T(8,128)(2,1)S(1)}, bf16[1024,1,128]{2,0,1:T(8,128)(2,1)}, u32[]{:S(2)}) copy-start(bf16[1024,1,128]{2,0,1:T(8,128)(2,1)} %copy.100) | copy-start | bytes 786436
  276.6 2.3 copy-start.20
  276.6 119.9 %all-gather.7.cloned.1.call-start = ((), (), s32[]{:S(2)}) async-start(), calls=%async_computation.6 | async-start | bytes 3932160 | tf_op jit(solution)/shard_map/all_gather | solution.py:146
  278.9 3.8 copy-start.9
  281.4 4.9 %collective-permute-start.6 = (f32[3,129,128]{2,1,0:T(8,128)S(1)}, f32[3,129,128]{2,1,0:T(8,128)S(1)}, u32[]{:S(2)}, u32[]{:S(2)}) collective-permute-start(f32[3,129,128]{2,1,0:T(8,128)S(1)} %select_add_fusion.7), channel_id=1, source_target_pairs={{0,8},{4,12},{8,16},{12,20},{16,24},{20,28},{24,32},{28,36},{32,40... | collective-permute-start | bytes 594440 | tf_op jit(solution)/shard_map/ppermute | solution.py:121
  286.4 6.7 %copy-start.19 = (bf16[1024,1,128]{0,2,1:T(8,128)(2,1)S(1)}, bf16[1024,1,128]{0,2,1:T(8,128)(2,1)}, u32[]{:S(2)}) copy-start(bf16[1024,1,128]{0,2,1:T(8,128)(2,1)} %get-tuple-element.96) | copy-start | bytes 786436
  286.4 8.2 %collective-permute-start.7 = (f32[3,129,128]{2,1,0:T(8,128)S(1)}, f32[3,129,128]{2,1,0:T(8,128)S(1)}, u32[]{:S(2)}, u32[]{:S(2)}) collective-permute-start(f32[3,129,128]{2,1,0:T(8,128)S(1)} %select_add_fusion.6), channel_id=1, source_target_pairs={{0,16},{4,20},{8,24},{12,28},{16,32},{20,36},{24,40},{28,44},{32,4... | collective-permute-start | bytes 594440 | tf_op jit(solution)/shard_map/ppermute | solution.py:121
  293.1 11.1 %copy-start.6 = (bf16[128,8,8,128]{3,2,1,0:T(8,128)(2,1)S(1)}, bf16[128,8,8,128]{3,2,1,0:T(8,128)(2,1)}, u32[]{:S(2)}) copy-start(bf16[128,8,8,128]{3,2,1,0:T(8,128)(2,1)} %copy-done.5) | copy-start | bytes 6291460
  293.1 11.7 %copy-start.8 = (bf16[1024,1,128]{2,1,0:T(2,128)(2,1)S(1)}, bf16[1024,1,128]{2,1,0:T(2,128)(2,1)}, u32[]{:S(2)}) copy-start(bf16[1024,1,128]{2,1,0:T(2,128)(2,1)} %get-tuple-element.119) | copy-start | bytes 786436
  294.6 12.2 %collective-permute-start.8 = (f32[3,129,128]{2,1,0:T(8,128)S(1)}, f32[3,129,128]{2,1,0:T(8,128)S(1)}, u32[]{:S(2)}, u32[]{:S(2)}) collective-permute-start(f32[3,129,128]{2,1,0:T(8,128)S(1)} %select_add_fusion.5), channel_id=1, source_target_pairs={{0,32},{4,36},{8,40},{12,44},{16,48},{20,52},{24,56},{28,60},{32,6... | collective-permute-start | bytes 594440 | tf_op jit(solution)/shard_map/ppermute | solution.py:121
  306.9 8.4 %copy-start.18 = (bf16[1024,1,128]{0,2,1:T(8,128)(2,1)S(1)}, bf16[1024,1,128]{0,2,1:T(8,128)(2,1)}, u32[]{:S(2)}) copy-start(bf16[1024,1,128]{0,2,1:T(8,128)(2,1)} %get-tuple-element.102) | copy-start | bytes 786436
  306.9 9.9 %collective-permute-start.9 = (f32[3,129,128]{2,1,0:T(8,128)S(1)}, f32[3,129,128]{2,1,0:T(8,128)S(1)}, u32[]{:S(2)}, u32[]{:S(2)}) collective-permute-start(f32[3,129,128]{2,1,0:T(8,128)S(1)} %select_add_fusion.4), channel_id=1, source_target_pairs={{0,64},{4,68},{8,72},{12,76},{16,80},{20,84},{24,88},{28,92},{32,9... | collective-permute-start | bytes 594440 | tf_op jit(solution)/shard_map/ppermute | solution.py:121
  396.5 8.9 %copy-start.1 = (bf16[1024,1024]{1,0:T(8,128)(2,1)S(1)}, bf16[1024,1024]{1,0:T(8,128)(2,1)}, u32[]{:S(2)}) copy-start(bf16[1024,1024]{1,0:T(8,128)(2,1)} %param.9) | copy-start | bytes 6291460
Sparse Core Ops, SparseCore 0:
  276.7 55.6 all-gather.4
  358.2 38.2 all-gather.6

commit v9 on v8

--- a/solution.py
+++ b/solution.py
@@ -53,7 +53,7 @@
     causal = r_idx[:, None] >= r_idx[None, :]
     head_count = lax.axis_size("head")
     out_cols = out_weight.shape[1]
-    bounds = [0, heads - (3 * heads) // 8, heads]
+    bounds = [0, heads - heads // 4, heads]
     weight_rows = out_weight.reshape(head_count, heads, dh, out_cols)
     gate_all = jax.nn.sigmoid(mem_gate)
     shifts = []

time: 419 us -> 438 us (1.045)
  waiting for transfers between devices: 114 us -> 130 us
  starting transfers between devices: 84.7 us -> 71.7 us
  matrix products: 58 us -> 65.2 us
    all_to_all x1, waiting for transfers between devices: 14.7 us -> 31 us  [one_group(): lax.all_to_all(outgoing, 'ctx', 0, 0, tiled=True)]
    ppermute x10, waiting for transfers between devices: 13 us -> 22.4 us  [one_group(): got = lax.ppermute(total, 'ctx', perm)]
    sub x0 -> x1, matrix products: none -> 7.97 us  [local_attention(): weights = jnp.exp(scores - row_max)]
    all_gather x2, waiting for transfers between devices: 18.4 us -> 10.6 us  [one_group(): gathered = lax.all_gather(rows, 'head', axis=1, tiled=True)]
    ppermute x10, starting transfers between devices: 49.7 us -> 42 us  [one_group(): got = lax.ppermute(total, 'ctx', perm)]
    all_to_all x1, starting transfers between devices: 15.7 us -> 9.75 us  [one_group(): lax.all_to_all(outgoing, 'ctx', 0, 0, tiled=True)]
    dot_general x8 -> x7, matrix products: 12.1 us -> 13.4 us  [local_attention(): jnp.einsum('hqk,khd->qhd', probabilities, value_part, preferred_element_t...]
  transfers between devices with their start and end apart: 16 -> 16, of which waited for: 12 -> 11; matrix products, arithmetic and copies ran while one was open for 29% -> 29% of each run, Pallas kernels for 0% -> 0%
where the time goes in v9:
time: 438 us; the launch traced here: 432 us
  waiting for transfers between devices  130 us (30%)
  local copies, waits for them, and re-layouts  101 us (23%)
  starting transfers between devices  71.7 us (16%)
  matrix products  65.2 us (15%)
  blocking collectives  29.2 us (7%)
  between operations  17.6 us (4%)
  other arithmetic  16.4 us (4%)
    all_to_all x3, waiting for transfers between devices, dispatch(): got = lax.all_to_all(buffer, 'ctx', 0, 0, tiled=True).reshape(slots, width)  66 us
    ppermute x10, starting transfers between devices, one_group(): got = lax.ppermute(total, 'ctx', perm)  42 us
    all_to_all x1, waiting for transfers between devices, one_group(): lax.all_to_all(outgoing, 'ctx', 0, 0, tiled=True)  31 us
    all_to_all x1, blocking collectives, one_group(): lax.all_to_all(outgoing, 'ctx', 0, 0, tiled=True)  29.2 us
    gather x4, local copies, waits for them, and re-layouts, dispatch(): return jnp.take(got, tok_slot, axis=0, mode='clip').reshape(seg, heads, dh)  25.9 us
    ppermute x10, waiting for transfers between devices, one_group(): got = lax.ppermute(total, 'ctx', perm)  22.4 us
    all_to_all x3, starting transfers between devices, dispatch(): got = lax.all_to_all(buffer, 'ctx', 0, 0, tiled=True).reshape(slots, width)  19.4 us
    dot_general x2, matrix products, one_group(): part = jnp.dot(gathered, weights[g], preferred_element_type=f32)  19.2 us
  transfers between devices with their start and end apart: 16, of which 11 were waited for; matrix products, arithmetic and copies ran while one was open for 29% of the time, Pallas kernels for 0%

profile of v9, /device:TPU:1, one launch (start us, length us, event | category | flops | bytes accessed | tf_op | source)
XLA Modules:
  0.0 431.6 jit_solution(8920230589287513574)
XLA Ops:
  11.6 5.8 %gather_fusion.2 = bf16[1536,1024]{1,0:T(8,128)(2,1)} fusion(bf16[1024,1024]{1,0:T(8,128)(2,1)S(1)} %copy-done, s32[2048]{0:T(1024)S(1)} %get-tuple-element.143), kind=kCustom, calls=%fused_computation.2 | custom fusion | bytes 6297600 | tf_op jit(solution)/shard_map/jit(_take)/gather | solution.py:66
  17.4 8.8 %all-to-all-start.1 = ((bf16[32,48,1024]{2,1,0:T(8,128)(2,1)}), bf16[32,48,1024]{2,1,0:T(8,128)(2,1)}, u32[]{:S(2)}, u32[]{:S(2)}) async-start(bf16[32,48,1024]{2,1,0:T(8,128)(2,1)} %bitcast.205), calls=%async_computation.1 | async-start | bytes 6291456 | tf_op jit(solution)/shard_map/all_to_all | solution.py:67
  26.2 5.8 %gather_fusion = bf16[1536,1024]{1,0:T(8,128)(2,1)} fusion(bf16[1024,1024]{1,0:T(8,128)(2,1)S(1)} %copy-done.2, s32[2048]{0:T(1024)S(1)} %get-tuple-element.143), kind=kCustom, calls=%fused_computation | custom fusion | bytes 6297600 | tf_op jit(solution)/shard_map/jit(_take)/gather | solution.py:66
  32.0 34.0 %all-to-all-done.1 = bf16[32,48,1024]{2,1,0:T(8,128)(2,1)} async-done(((bf16[32,48,1024]{2,1,0:T(8,128)(2,1)}), bf16[32,48,1024]{2,1,0:T(8,128)(2,1)}, u32[]{:S(2)}, u32[]{:S(2)}) %all-to-all-start.1) | async-done | bytes 3145760 | tf_op jit(solution)/shard_map/all_to_all | solution.py:67
  66.0 5.0 %all-to-all-start = ((bf16[32,48,1024]{2,1,0:T(8,128)(2,1)}), bf16[32,48,1024]{2,1,0:T(8,128)(2,1)}, u32[]{:S(2)}, u32[]{:S(2)}) async-start(bf16[32,48,1024]{2,1,0:T(8,128)(2,1)} %bitcast.204), calls=%async_computation | async-start | bytes 6291456 | tf_op jit(solution)/shard_map/all_to_all | solution.py:67
  71.0 5.8 %gather_fusion.4 = bf16[1536,1024]{1,0:T(8,128)(2,1)} fusion(bf16[1024,1024]{1,0:T(8,128)(2,1)S(1)} %copy-done.3, s32[2048]{0:T(1024)S(1)} %get-tuple-element.143), kind=kCustom, calls=%fused_computation.4 | custom fusion | bytes 6297600 | tf_op jit(solution)/shard_map/jit(_take)/gather | solution.py:66
  78.8 32.0 %all-to-all-done = bf16[32,48,1024]{2,1,0:T(8,128)(2,1)} async-done(((bf16[32,48,1024]{2,1,0:T(8,128)(2,1)}), bf16[32,48,1024]{2,1,0:T(8,128)(2,1)}, u32[]{:S(2)}, u32[]{:S(2)}) %all-to-all-start) | async-done | bytes 3145760 | tf_op jit(solution)/shard_map/all_to_all | solution.py:67
  110.8 5.6 %all-to-all-start.2 = ((bf16[32,48,1024]{2,1,0:T(8,128)(2,1)}), bf16[32,48,1024]{2,1,0:T(8,128)(2,1)S(1)}, u32[]{:S(2)}, u32[]{:S(2)}) async-start(bf16[32,48,1024]{2,1,0:T(8,128)(2,1)} %bitcast.203), calls=%async_computation.2 | async-start | bytes 6291456 | tf_op jit(solution)/shard_map/all_to_all | solution.py:67
  123.4 8.3 %gather_fusion.3 = bf16[1024,1024]{1,0:T(8,128)(2,1)} fusion(bf16[1536,1024]{1,0:T(8,128)(2,1)} %bitcast.6, s32[1024]{0:T(1024)S(1)} %broadcast_clamp_fusion.1), kind=kCustom, calls=%fused_computation.3 | custom fusion | bytes 4198400 | tf_op jit(solution)/shard_map/jit(_take)/gather | solution.py:68
  131.7 4.0 copy.51
  135.7 8.3 %gather_fusion.1 = bf16[1024,1024]{1,0:T(8,128)(2,1)} fusion(bf16[1536,1024]{1,0:T(8,128)(2,1)} %bitcast.4, s32[1024]{0:T(1024)S(1)} %broadcast_clamp_fusion.1), kind=kCustom, calls=%fused_computation.1 | custom fusion | bytes 4198400 | tf_op jit(solution)/shard_map/jit(_take)/gather | solution.py:68
  144.0 2.4 copy.107
  149.6 4.5 %fusion.28 = f32[6,128,128]{2,1,0:T(8,128)} fusion(bf16[1024,8,128]{0,2,1:T(8,128)(2,1)S(1)} %bitcast.214, bf16[1024,6,128]{2,1,0:T(8,128)(2,1)S(1)} %bitcast.195), kind=kOutput, calls=%fused_computation.75 | convolution fusion | flops 1211891712 | bytes 4063232 | tf_op jit(solution)/shard_map/khd,khe->hde/dot_general | solution.py:103
  154.0 3.6 fusion.155
  157.6 5.3 %gather_fusion.5 = bf16[1024,1024]{1,0:T(8,128)(2,1)} fusion(bf16[1536,1024]{1,0:T(8,128)(2,1)S(1)} %bitcast.192, s32[1024]{0:T(1024)S(1)} %broadcast_clamp_fusion.1), kind=kCustom, calls=%fused_computation.5 | custom fusion | bytes 4198400 | tf_op jit(solution)/shard_map/jit(_take)/gather | solution.py:68
  162.9 2.2 copy.108
  165.2 2.5 fusion.156
  173.3 3.5 collective-permute-start
  184.5 3.2 collective-permute-start.1
  191.5 5.3 %collective-permute-done.1 = f32[6,129,128]{2,1,0:T(8,128)S(1)} collective-permute-done((f32[6,129,128]{2,1,0:T(8,128)S(1)}, f32[6,129,128]{2,1,0:T(8,128)S(1)}, u32[]{:S(2)}, u32[]{:S(2)}) %collective-permute-start.1) | collective-permute-done | bytes 396320 | tf_op jit(solution)/shard_map/ppermute | solution.py:121
  197.5 6.2 %collective-permute-start.2 = (f32[6,129,128]{2,1,0:T(8,128)}, f32[6,129,128]{2,1,0:T(8,128)}, u32[]{:S(2)}, u32[]{:S(2)}) collective-permute-start(f32[6,129,128]{2,1,0:T(8,128)} %select_add_fusion.2), channel_id=1, source_target_pairs={{0,16},{4,20},{8,24},{12,28},{16,32},{20,36},{24,40},{28,44},{32,4... | collective-permute-start | bytes 1188872 | tf_op jit(solution)/shard_map/ppermute | solution.py:121
  203.7 8.0 %fusion.160 = (f32[2,1024]{1,0:T(2,128)S(1)}, f32[2,1024,1024]{1,2,0:T(8,128)}) fusion(pred[1024,1024]{0,1:T(8,128)(4,1)} %iota_compare_fusion.3, bf16[1024,2,128]{2,0,1:T(8,128)(2,1)} %copy.93, bf16[1024,2,128]{2,0,1:T(8,128)(2,1)} %copy.94), kind=kOutput, calls=%fused_computation.256 | convolution fusion | flops 545260544 | bytes 10493952 | tf_op jit(solution)/shard_map/sub | solution.py:86
  211.7 4.4 %fusion.49 = f32[1024,2,128]{0,2,1:T(8,128)S(1)} fusion(bf16[1024,2,128]{0,2,1:T(8,128)(2,1)} %slice.191, f32[2,1024,1024]{1,2,0:T(8,128)} %get-tuple-element.133, f32[2,1024]{1,0:T(2,128)S(1)} %get-tuple-element.132), kind=kOutput, calls=%fused_computation.95 | convolution fusion | flops 541065216 | bytes 9969664 | tf_op jit(solution)/shard_map/hqk,khd->qhd/dot_general | solution.py:88
  217.4 2.8 collective-permute-start.3
  223.2 5.1 %collective-permute-done.3 = f32[6,129,128]{2,1,0:T(8,128)S(1)} collective-permute-done((f32[6,129,128]{2,1,0:T(8,128)S(1)}, f32[6,129,128]{2,1,0:T(8,128)S(1)}, u32[]{:S(2)}, u32[]{:S(2)}) %collective-permute-start.3) | collective-permute-done | bytes 396320 | tf_op jit(solution)/shard_map/ppermute | solution.py:121
  228.3 5.8 %collective-permute-start.4 = (f32[6,129,128]{2,1,0:T(8,128)S(1)}, f32[6,129,128]{2,1,0:T(8,128)S(1)}, u32[]{:S(2)}, u32[]{:S(2)}) collective-permute-start(f32[6,129,128]{2,1,0:T(8,128)S(1)} %select_add_fusion), channel_id=1, source_target_pairs={{0,64},{4,68},{8,72},{12,76},{16,80},{20,84},{24,88},{28,92},{32,9... | collective-permute-start | bytes 1188872 | tf_op jit(solution)/shard_map/ppermute | solution.py:121
  236.9 4.4 %collective-permute-done.4 = f32[6,129,128]{2,1,0:T(8,128)S(1)} collective-permute-done((f32[6,129,128]{2,1,0:T(8,128)S(1)}, f32[6,129,128]{2,1,0:T(8,128)S(1)}, u32[]{:S(2)}, u32[]{:S(2)}) %collective-permute-start.4) | collective-permute-done | bytes 396320 | tf_op jit(solution)/shard_map/ppermute | solution.py:121
  241.5 3.7 fusion.23
  245.3 5.6 %fusion.22 = bf16[1024,6,128]{0,2,1:T(8,128)(2,1)} fusion(f32[1024,6,128]{0,2,1:T(8,128)S(1)} %constant_dynamic-update-slice_fusion, f32[6]{0:T(128)S(1)} %copy-done.34, f32[1024,6]{0,1:T(8,128)S(1)} %fusion.121, f32[6]{0:T(128)S(1)} %copy-done.33, bf16[1024,6,128]{2,1,0:T(8,128)(2,1)S(1)} %bitcast.202, f32[6,129,128]{2,1,0:T(8,128)S(1)} %add_subtract_fusion), kind=kOutput, calls=%fused_computation.71 | convolution fusion | flops 1215823872 | bytes 7242752 | tf_op jit(solution)/shard_map/qhd,hde->qhe/dot_general | solution.py:133
  252.6 5.6 %gather_fusion.6 = bf16[1536,768]{1,0:T(8,128)(2,1)} fusion(bf16[1024,768]{1,0:T(8,128)(2,1)S(1)} %copy.67, s32[2048]{0:T(1024)S(1)} %get-tuple-element.142), kind=kCustom, calls=%fused_computation.6 | custom fusion | bytes 4724736 | tf_op jit(solution)/shard_map/jit(_take)/gather | solution.py:143
  258.2 9.7 %all-to-all-start.3 = ((bf16[32,48,768]{2,1,0:T(8,128)(2,1)}), bf16[32,48,768]{2,1,0:T(8,128)(2,1)S(1)}, u32[]{:S(2)}, u32[]{:S(2)}) async-start(bf16[32,48,768]{2,1,0:T(8,128)(2,1)} %bitcast.206), calls=%async_computation.3 | async-start | bytes 4718592 | tf_op jit(solution)/shard_map/all_to_all | solution.py:144
  268.1 31.0 %all-to-all-done.3 = bf16[32,48,768]{2,1,0:T(8,128)(2,1)S(1)} async-done(((bf16[32,48,768]{2,1,0:T(8,128)(2,1)}), bf16[32,48,768]{2,1,0:T(8,128)(2,1)S(1)}, u32[]{:S(2)}, u32[]{:S(2)}) %all-to-all-start.3) | async-done | bytes 2359328 | tf_op jit(solution)/shard_map/all_to_all | solution.py:144
  299.1 5.2 %gather_fusion.7 = bf16[1024,768]{1,0:T(8,128)(2,1)} fusion(bf16[1536,768]{1,0:T(8,128)(2,1)S(1)} %bitcast.193, s32[1024]{0:T(1024)S(1)} %broadcast_clamp_fusion), kind=kCustom, calls=%fused_computation.7 | custom fusion | bytes 3149824 | tf_op jit(solution)/shard_map/jit(_take)/gather | solution.py:145
  306.4 2.6 fusion.76
  308.9 2.4 collective-permute-start.5
  314.7 2.5 collective-permute-start.6
  319.2 5.5 %collective-permute-start.7 = (f32[2,129,128]{2,1,0:T(8,128)S(1)}, f32[2,129,128]{2,1,0:T(8,128)S(1)}, u32[]{:S(2)}, u32[]{:S(2)}) collective-permute-start(f32[2,129,128]{2,1,0:T(8,128)S(1)} %select_add_fusion.6), channel_id=1, source_target_pairs={{0,16},{4,20},{8,24},{12,28},{16,32},{20,36},{24,40},{28,44},{32,4... | collective-permute-start | bytes 396296 | tf_op jit(solution)/shard_map/ppermute | solution.py:121
  326.8 5.9 %collective-permute-start.8 = (f32[2,129,128]{2,1,0:T(8,128)S(1)}, f32[2,129,128]{2,1,0:T(8,128)S(1)}, u32[]{:S(2)}, u32[]{:S(2)}) collective-permute-start(f32[2,129,128]{2,1,0:T(8,128)S(1)} %select_add_fusion.5), channel_id=1, source_target_pairs={{0,32},{4,36},{8,40},{12,44},{16,48},{20,52},{24,56},{28,60},{32,6... | collective-permute-start | bytes 396296 | tf_op jit(solution)/shard_map/ppermute | solution.py:121
  335.5 4.1 collective-permute-start.9
  339.7 3.3 collective-permute-done.9
  346.1 4.8 %gather_fusion.8 = bf16[1536,256]{1,0:T(8,128)(2,1)S(1)} fusion(bf16[1024,256]{1,0:T(8,128)(2,1)S(1)} %copy.77, s32[2048]{0:T(1024)S(1)} %get-tuple-element.142), kind=kCustom, calls=%fused_computation.8 | custom fusion | bytes 1579008 | tf_op jit(solution)/shard_map/jit(_take)/gather | solution.py:143
  350.9 29.2 %all_to_all.25 = bf16[32,48,256]{2,1,0:T(8,128)(2,1)S(1)} all-to-all(bf16[32,48,256]{2,1,0:T(8,128)(2,1)S(1)} %bitcast.216), channel_id=1, replica_groups=mesh['ctx'=32,'head'=4] {'ctx'}, dimensions={0} | all-to-all | bytes 1572864 | tf_op jit(solution)/shard_map/all_to_all | solution.py:144
  380.1 4.9 %gather_fusion.9 = bf16[1024,256]{1,0:T(8,128)(2,1)} fusion(bf16[1536,256]{1,0:T(8,128)(2,1)S(1)} %bitcast.198, s32[1024]{0:T(1024)S(1)} %broadcast_clamp_fusion), kind=kCustom, calls=%fused_computation.9 | custom fusion | bytes 1052672 | tf_op jit(solution)/shard_map/jit(_take)/gather | solution.py:145
  385.1 6.5 %slice.201 = bf16[4,6,128,1024]{3,2,1,0:T(8,128)(2,1)} slice(bf16[4,8,128,1024]{3,2,1,0:T(8,128)(2,1)} %bitcast.209), slice={[0:4], [0:6], [0:128], [0:1024]} | slice | bytes 12582912 | tf_op jit(solution)/shard_map/slice | solution.py:72
  391.6 3.2 slice.213
  394.8 12.0 %fusion.161 = f32[1024,1024]{1,0:T(8,128)} fusion(bf16[1024,3072]{1,0:T(8,128)(2,1)} %all-gather.5.cloned.1.call-done, bf16[3072,1024]{1,0:T(8,128)(2,1)} %bitcast.215), kind=kOutput, calls=%fused_computation.257 | convolution fusion | flops 6442450944 | bytes 16777216 | tf_op jit(solution)/shard_map/dot_general | solution.py:147
  406.8 10.6 %all-gather.7.cloned.1.call-done = bf16[1024,1024]{1,0:T(8,128)(2,1)} async-done(((bf16[1024,256]{1,0:T(8,128)(2,1)}), bf16[1024,1024]{1,0:T(8,128)(2,1)}) %all-gather.7.cloned.1.call-update) | async-done | bytes 2097168 | tf_op jit(solution)/shard_map/all_gather | solution.py:146
  417.3 7.3 %add_convert_fusion = bf16[1024,1024]{1,0:T(8,128)(2,1)} fusion(f32[1024,1024]{1,0:T(8,128)} %fusion.161, bf16[1024,1024]{1,0:T(8,128)(2,1)} %all-gather.7.cloned.1.call-done, bf16[1024,1024]{1,0:T(8,128)(2,1)} %bitcast.217), kind=kOutput, calls=%fused_computation.27 | convolution fusion | flops 2149580800 | bytes 10485760 | tf_op jit(solution)/shard_map/dot_general | solution.py:147
  (169 shorter events, 55.6 us)
Async XLA Ops:
  6.5 5.0 %copy-start = (bf16[1024,1024]{1,0:T(8,128)(2,1)S(1)}, bf16[1024,1024]{1,0:T(8,128)(2,1)}, u32[]{:S(2)}) copy-start(bf16[1024,1024]{1,0:T(8,128)(2,1)} %param.9) | copy-start | bytes 6291460
  17.4 8.8 %copy-start.2 = (bf16[1024,1024]{1,0:T(8,128)(2,1)S(1)}, bf16[1024,1024]{1,0:T(8,128)(2,1)}, u32[]{:S(2)}) copy-start(bf16[1024,1024]{1,0:T(8,128)(2,1)} %param.8) | copy-start | bytes 6291460
  17.4 48.6 %all-to-all-start.1 = ((bf16[32,48,1024]{2,1,0:T(8,128)(2,1)}), bf16[32,48,1024]{2,1,0:T(8,128)(2,1)}, u32[]{:S(2)}, u32[]{:S(2)}) async-start(bf16[32,48,1024]{2,1,0:T(8,128)(2,1)} %bitcast.205), calls=%async_computation.1 | async-start | bytes 6291456 | tf_op jit(solution)/shard_map/all_to_all | solution.py:67
  32.0 39.0 %copy-start.3 = (bf16[1024,1024]{1,0:T(8,128)(2,1)S(1)}, bf16[1024,1024]{1,0:T(8,128)(2,1)}, u32[]{:S(2)}) copy-start(bf16[1024,1024]{1,0:T(8,128)(2,1)} %param.7) | copy-start | bytes 6291460
  66.0 44.9 %all-to-all-start = ((bf16[32,48,1024]{2,1,0:T(8,128)(2,1)}), bf16[32,48,1024]{2,1,0:T(8,128)(2,1)}, u32[]{:S(2)}, u32[]{:S(2)}) async-start(bf16[32,48,1024]{2,1,0:T(8,128)(2,1)} %bitcast.204), calls=%async_computation | async-start | bytes 6291456 | tf_op jit(solution)/shard_map/all_to_all | solution.py:67
  71.0 5.8 %copy-start.29 = (s32[32]{0:T(128)S(1)}, s32[32]{0:T(128)}, u32[]{:S(2)}) copy-start(s32[32]{0:T(128)} %param.11) | copy-start | bytes 388
  76.9 44.1 %copy-start.30 = (f32[8]{0:T(128)S(1)}, f32[8]{0:T(128)}, u32[]{:S(2)}) copy-start(f32[8]{0:T(128)} %param.12) | copy-start | bytes 100
  110.8 46.8 %all-to-all-start.2 = ((bf16[32,48,1024]{2,1,0:T(8,128)(2,1)}), bf16[32,48,1024]{2,1,0:T(8,128)(2,1)S(1)}, u32[]{:S(2)}, u32[]{:S(2)}) async-start(bf16[32,48,1024]{2,1,0:T(8,128)(2,1)} %bitcast.203), calls=%async_computation.2 | async-start | bytes 6291456 | tf_op jit(solution)/shard_map/all_to_all | solution.py:67
  146.4 7.7 %copy-start.4 = (bf16[128,8,8,128]{3,2,1,0:T(8,128)(2,1)}, bf16[128,8,8,128]{3,2,1,0:T(8,128)(2,1)S(1)}, u32[]{:S(2)}) copy-start(bf16[128,8,8,128]{3,2,1,0:T(8,128)(2,1)S(1)} %copy.107) | copy-start | bytes 6291460
  165.1 4.3 %copy-start.5 = (bf16[128,8,8,128]{3,2,1,0:T(8,128)(2,1)S(1)}, bf16[128,8,8,128]{3,2,1,0:T(8,128)(2,1)}, u32[]{:S(2)}) copy-start(bf16[128,8,8,128]{3,2,1,0:T(8,128)(2,1)} %copy-done.4) | copy-start | bytes 6291460
  167.7 5.5 %copy-start.28 = (f32[6,128]{1,0:T(8,128)S(1)}, f32[6,128]{1,0:T(8,128)}, u32[]{:S(2)}) copy-start(f32[6,128]{1,0:T(8,128)} %fusion.27) | copy-start | bytes 9220
  167.7 5.5 %copy-start.12 = (bf16[1024,1,128]{2,1,0:T(2,128)(2,1)S(1)}, bf16[1024,1,128]{2,1,0:T(2,128)(2,1)}, u32[]{:S(2)}) copy-start(bf16[1024,1,128]{2,1,0:T(2,128)(2,1)} %get-tuple-element.114) | copy-start | bytes 786436
  167.7 5.6 %copy-start.13 = (f32[6,128,128]{2,1,0:T(8,128)S(1)}, f32[6,128,128]{2,1,0:T(8,128)}, u32[]{:S(2)}) copy-start(f32[6,128,128]{2,1,0:T(8,128)} %fusion.28) | copy-start | bytes 1179652
  167.7 9.2 %copy-start.11 = (bf16[1024,1,128]{2,1,0:T(2,128)(2,1)S(1)}, bf16[1024,1,128]{2,1,0:T(2,128)(2,1)}, u32[]{:S(2)}) copy-start(bf16[1024,1,128]{2,1,0:T(2,128)(2,1)} %get-tuple-element.113) | copy-start | bytes 786436
  171.2 8.2 %copy-start.10 = (bf16[1024,1,128]{2,1,0:T(2,128)(2,1)S(1)}, bf16[1024,1,128]{2,1,0:T(2,128)(2,1)}, u32[]{:S(2)}) copy-start(bf16[1024,1,128]{2,1,0:T(2,128)(2,1)} %get-tuple-element.112) | copy-start | bytes 786436
  173.2 7.7 %copy-start.9 = (bf16[1024,1,128]{2,1,0:T(2,128)(2,1)S(1)}, bf16[1024,1,128]{2,1,0:T(2,128)(2,1)}, u32[]{:S(2)}) copy-start(bf16[1024,1,128]{2,1,0:T(2,128)(2,1)} %get-tuple-element.111) | copy-start | bytes 786436
  173.3 11.1 %collective-permute-start = (f32[6,129,128]{2,1,0:T(8,128)S(1)}, f32[6,129,128]{2,1,0:T(8,128)S(1)}, u32[]{:S(2)}, u32[]{:S(2)}) collective-permute-start(f32[6,129,128]{2,1,0:T(8,128)S(1)} %pad_maximum_fusion), channel_id=1, source_target_pairs={{0,4},{4,8},{8,12},{12,16},{16,20},{20,24},{24,28},{28,32},{32,36}... | collective-permute-start | bytes 1188872 | tf_op jit(solution)/shard_map/ppermute | solution.py:121
  184.5 4.5 %copy-start.23 = (bf16[1024,1,128]{0,2,1:T(8,128)(2,1)S(1)}, bf16[1024,1,128]{0,2,1:T(8,128)(2,1)}, u32[]{:S(2)}) copy-start(bf16[1024,1,128]{0,2,1:T(8,128)(2,1)} %get-tuple-element.58) | copy-start | bytes 786436
  184.5 12.2 %collective-permute-start.1 = (f32[6,129,128]{2,1,0:T(8,128)S(1)}, f32[6,129,128]{2,1,0:T(8,128)S(1)}, u32[]{:S(2)}, u32[]{:S(2)}) collective-permute-start(f32[6,129,128]{2,1,0:T(8,128)S(1)} %select_add_fusion.3), channel_id=1, source_target_pairs={{0,8},{4,12},{8,16},{12,20},{16,24},{20,28},{24,32},{28,36},{32,40... | collective-permute-start | bytes 1188872 | tf_op jit(solution)/shard_map/ppermute | solution.py:121
  197.5 18.8 %collective-permute-start.2 = (f32[6,129,128]{2,1,0:T(8,128)}, f32[6,129,128]{2,1,0:T(8,128)}, u32[]{:S(2)}, u32[]{:S(2)}) collective-permute-start(f32[6,129,128]{2,1,0:T(8,128)} %select_add_fusion.2), channel_id=1, source_target_pairs={{0,16},{4,20},{8,24},{12,28},{16,32},{20,36},{24,40},{28,44},{32,4... | collective-permute-start | bytes 1188872 | tf_op jit(solution)/shard_map/ppermute | solution.py:121
  211.7 4.4 %copy-start.15 = (f32[1024,1,128]{0,2,1:T(8,128)S(1)}, f32[1024,1,128]{0,2,1:T(8,128)}, u32[]{:S(2)}) copy-start(f32[1024,1,128]{0,2,1:T(8,128)} %fusion.58) | copy-start | bytes 1572868
  211.7 4.6 %copy-start.27 = (f32[1024,6,128]{0,2,1:T(8,128)S(1)}, f32[1024,6,128]{0,2,1:T(8,128)}, u32[]{:S(2)}) copy-start(f32[1024,6,128]{0,2,1:T(8,128)} %constant_dynamic-update-slice_fusion.4) | copy-start | bytes 9437188
  211.7 8.6 %copy-start.24 = (bf16[1024,1,128]{2,0,1:T(8,128)(2,1)S(1)}, bf16[1024,1,128]{2,0,1:T(8,128)(2,1)}, u32[]{:S(2)}) copy-start(bf16[1024,1,128]{2,0,1:T(8,128)(2,1)} %copy.95) | copy-start | bytes 786436
  211.7 8.6 %copy-start.25 = (bf16[1024,1,128]{2,0,1:T(8,128)(2,1)S(1)}, bf16[1024,1,128]{2,0,1:T(8,128)(2,1)}, u32[]{:S(2)}) copy-start(bf16[1024,1,128]{2,0,1:T(8,128)(2,1)} %copy.96) | copy-start | bytes 786436
  217.4 4.1 copy-start.20
  217.4 10.8 %collective-permute-start.3 = (f32[6,129,128]{2,1,0:T(8,128)S(1)}, f32[6,129,128]{2,1,0:T(8,128)S(1)}, u32[]{:S(2)}, u32[]{:S(2)}) collective-permute-start(f32[6,129,128]{2,1,0:T(8,128)S(1)} %select_add_fusion.1), channel_id=1, source_target_pairs={{0,32},{4,36},{8,40},{12,44},{16,48},{20,52},{24,56},{28,60},{32,6... | collective-permute-start | bytes 1188872 | tf_op jit(solution)/shard_map/ppermute | solution.py:121
  221.6 12.5 %copy-start.21 = (bf16[1024,1,128]{2,0,1:T(8,128)(2,1)S(1)}, bf16[1024,1,128]{2,0,1:T(8,128)(2,1)}, u32[]{:S(2)}) copy-start(bf16[1024,1,128]{2,0,1:T(8,128)(2,1)} %copy.97) | copy-start | bytes 786436
  221.6 12.5 %copy-start.22 = (bf16[1024,1,128]{2,0,1:T(8,128)(2,1)S(1)}, bf16[1024,1,128]{2,0,1:T(8,128)(2,1)}, u32[]{:S(2)}) copy-start(bf16[1024,1,128]{2,0,1:T(8,128)(2,1)} %copy.98) | copy-start | bytes 786436
  228.3 7.0 %copy-start.19 = (bf16[1024,1,128]{0,2,1:T(8,128)(2,1)S(1)}, bf16[1024,1,128]{0,2,1:T(8,128)(2,1)}, u32[]{:S(2)}) copy-start(bf16[1024,1,128]{0,2,1:T(8,128)(2,1)} %get-tuple-element.73) | copy-start | bytes 786436
  228.3 13.0 %collective-permute-start.4 = (f32[6,129,128]{2,1,0:T(8,128)S(1)}, f32[6,129,128]{2,1,0:T(8,128)S(1)}, u32[]{:S(2)}, u32[]{:S(2)}) collective-permute-start(f32[6,129,128]{2,1,0:T(8,128)S(1)} %select_add_fusion), channel_id=1, source_target_pairs={{0,64},{4,68},{8,72},{12,76},{16,80},{20,84},{24,88},{28,92},{32,9... | collective-permute-start | bytes 1188872 | tf_op jit(solution)/shard_map/ppermute | solution.py:121
  235.4 6.0 %copy-start.14 = (f32[6,128,128]{2,1,0:T(8,128)S(1)}, f32[6,128,128]{2,1,0:T(8,128)}, u32[]{:S(2)}) copy-start(f32[6,128,128]{2,1,0:T(8,128)} %fusion.28) | copy-start | bytes 1179652
  241.5 3.8 copy-start.33
  241.5 3.8 copy-start.34
  258.2 40.9 %all-to-all-start.3 = ((bf16[32,48,768]{2,1,0:T(8,128)(2,1)}), bf16[32,48,768]{2,1,0:T(8,128)(2,1)S(1)}, u32[]{:S(2)}, u32[]{:S(2)}) async-start(bf16[32,48,768]{2,1,0:T(8,128)(2,1)} %bitcast.206), calls=%async_computation.3 | async-start | bytes 4718592 | tf_op jit(solution)/shard_map/all_to_all | solution.py:144
  268.0 126.8 %all-gather.5.cloned.1.call-start = ((), (), s32[]{:S(2)}) async-start(), calls=%async_computation.5 | async-start | bytes 7864320 | tf_op jit(solution)/shard_map/all_gather | solution.py:146
  304.3 7.1 %copy-start.8 = (bf16[1024,1,128]{2,1,0:T(2,128)(2,1)S(1)}, bf16[1024,1,128]{2,1,0:T(2,128)(2,1)}, u32[]{:S(2)}) copy-start(bf16[1024,1,128]{2,1,0:T(2,128)(2,1)} %get-tuple-element.110) | copy-start | bytes 786436
  304.4 113.0 %all-gather.7.cloned.1.call-start = ((), (), s32[]{:S(2)}) async-start(), calls=%async_computation.6 | async-start | bytes 2621440 | tf_op jit(solution)/shard_map/all_gather | solution.py:146
  308.9 4.5 %collective-permute-start.5 = (f32[2,129,128]{2,1,0:T(8,128)S(1)}, f32[2,129,128]{2,1,0:T(8,128)S(1)}, u32[]{:S(2)}, u32[]{:S(2)}) collective-permute-start(f32[2,129,128]{2,1,0:T(8,128)S(1)} %pad_maximum_fusion.1), channel_id=1, source_target_pairs={{0,4},{4,8},{8,12},{12,16},{16,20},{20,24},{24,28},{28,32},{32,36}... | collective-permute-start | bytes 396296 | tf_op jit(solution)/shard_map/ppermute | solution.py:121
  313.4 3.8 copy-start.18
  314.7 10.2 %copy-start.7 = (bf16[1024,1,128]{2,1,0:T(2,128)(2,1)S(1)}, bf16[1024,1,128]{2,1,0:T(2,128)(2,1)}, u32[]{:S(2)}) copy-start(bf16[1024,1,128]{2,1,0:T(2,128)(2,1)} %get-tuple-element.109) | copy-start | bytes 786436
  314.7 4.6 %collective-permute-start.6 = (f32[2,129,128]{2,1,0:T(8,128)S(1)}, f32[2,129,128]{2,1,0:T(8,128)S(1)}, u32[]{:S(2)}, u32[]{:S(2)}) collective-permute-start(f32[2,129,128]{2,1,0:T(8,128)S(1)} %select_add_fusion.7), channel_id=1, source_target_pairs={{0,8},{4,12},{8,16},{12,20},{16,24},{20,28},{24,32},{28,36},{32,40... | collective-permute-start | bytes 396296 | tf_op jit(solution)/shard_map/ppermute | solution.py:121
  319.2 7.5 %collective-permute-start.7 = (f32[2,129,128]{2,1,0:T(8,128)S(1)}, f32[2,129,128]{2,1,0:T(8,128)S(1)}, u32[]{:S(2)}, u32[]{:S(2)}) collective-permute-start(f32[2,129,128]{2,1,0:T(8,128)S(1)} %select_add_fusion.6), channel_id=1, source_target_pairs={{0,16},{4,20},{8,24},{12,28},{16,32},{20,36},{24,40},{28,44},{32,4... | collective-permute-start | bytes 396296 | tf_op jit(solution)/shard_map/ppermute | solution.py:121
  326.8 7.1 %copy-start.17 = (bf16[1024,1,128]{0,2,1:T(8,128)(2,1)S(1)}, bf16[1024,1,128]{0,2,1:T(8,128)(2,1)}, u32[]{:S(2)}) copy-start(bf16[1024,1,128]{0,2,1:T(8,128)(2,1)} %get-tuple-element.92) | copy-start | bytes 786436
  326.8 8.7 %collective-permute-start.8 = (f32[2,129,128]{2,1,0:T(8,128)S(1)}, f32[2,129,128]{2,1,0:T(8,128)S(1)}, u32[]{:S(2)}, u32[]{:S(2)}) collective-permute-start(f32[2,129,128]{2,1,0:T(8,128)S(1)} %select_add_fusion.5), channel_id=1, source_target_pairs={{0,32},{4,36},{8,40},{12,44},{16,48},{20,52},{24,56},{28,60},{32,6... | collective-permute-start | bytes 396296 | tf_op jit(solution)/shard_map/ppermute | solution.py:121
  334.0 5.6 %copy-start.32 = (f32[8]{0:T(128)S(1)}, f32[8]{0:T(128)}, u32[]{:S(2)}) copy-start(f32[8]{0:T(128)} %copy-done.31) | copy-start | bytes 100
  334.0 9.0 %copy-start.16 = (bf16[1024,2,128]{2,1,0:T(2,128)(2,1)S(1)}, bf16[1024,2,128]{2,1,0:T(2,128)(2,1)}, u32[]{:S(2)}) copy-start(bf16[1024,2,128]{2,1,0:T(2,128)(2,1)} %get-tuple-element.101) | copy-start | bytes 1572868
  335.5 7.5 %collective-permute-start.9 = (f32[2,129,128]{2,1,0:T(8,128)S(1)}, f32[2,129,128]{2,1,0:T(8,128)S(1)}, u32[]{:S(2)}, u32[]{:S(2)}) collective-permute-start(f32[2,129,128]{2,1,0:T(8,128)S(1)} %select_add_fusion.4), channel_id=1, source_target_pairs={{0,64},{4,68},{8,72},{12,76},{16,80},{20,84},{24,88},{28,92},{32,9... | collective-permute-start | bytes 396296 | tf_op jit(solution)/shard_map/ppermute | solution.py:121
  417.3 7.3 %copy-start.1 = (bf16[1024,1024]{1,0:T(8,128)(2,1)S(1)}, bf16[1024,1024]{1,0:T(8,128)(2,1)}, u32[]{:S(2)}) copy-start(bf16[1024,1024]{1,0:T(8,128)(2,1)} %param.9) | copy-start | bytes 6291460
  (3 other events, 4.2 us)
Sparse Core Ops, SparseCore 0:
  304.5 64.3 all-gather.4
  385.2 32.0 all-gather.6

commit v10 on v5

--- a/solution.py
+++ b/solution.py
@@ -69,7 +69,18 @@
 
     key_all = dispatch(keys)
     value_all = dispatch(values)
-    query_all = dispatch(queries)
+
+    def memory_terms(first, last):
+        key_feat = feature(key_all[:, first:last].astype(f32))
+        delta_m = jnp.einsum(
+            "khd,khe->hde", key_feat, value_all[:, first:last].astype(f32), precision=highest
+        )
+        delta_z = jnp.sum(key_feat, axis=0)
+        return jnp.concatenate([delta_m, delta_z[:, None, :]], axis=1)
+
+    first_delta = memory_terms(bounds[0], bounds[1])
+    queries_after, first_delta = lax.optimization_barrier((queries, first_delta))
+    query_all = dispatch(queries_after)
 
     def local_attention(query_part, key_part, value_part):
         scores = jnp.einsum(
@@ -87,18 +98,14 @@
         first, last = bounds[g], bounds[g + 1]
         group_heads = last - first
         group_width = group_heads * dh
-        cuts = [first + round(group_heads * i / len(shifts)) for i in range(len(shifts) + 1)]
-        cuts = [c - first for c in cuts]
+        skip = 2 if g == 0 and len(shifts) > 2 else 0
+        slots_used = len(shifts) - skip
+        cuts = [0] * skip + [round(group_heads * i / slots_used) for i in range(slots_used + 1)]
         key_heads = key_all[:, first:last]
         value_heads = value_all[:, first:last]
         query_heads = query_all[:, first:last]
 
-        key_feat = feature(key_heads.astype(f32))
-        delta_m = jnp.einsum(
-            "khd,khe->hde", key_feat, value_heads.astype(f32), precision=highest
-        )
-        delta_z = jnp.sum(key_feat, axis=0)
-        delta = jnp.concatenate([delta_m, delta_z[:, None, :]], axis=1)
+        delta = first_delta if g == 0 else memory_terms(first, last)
         if hold is not None:
             delta, _ = lax.optimization_barrier((delta, hold))
 
@@ -106,9 +113,11 @@
         total = delta
         for k, step in enumerate(shifts):
             lo, hi = cuts[k], cuts[k + 1]
-            total, operands = lax.optimization_barrier(
-                (total, (query_heads[:, lo:hi], key_heads[:, lo:hi], value_heads[:, lo:hi]))
-            )
+            operands = None
+            if hi > lo:
+                total, operands = lax.optimization_barrier(
+                    (total, (query_heads[:, lo:hi], key_heads[:, lo:hi], value_heads[:, lo:hi]))
+                )
             perm = [(j, j + step) for j in range(n - step)]
             got = lax.ppermute(total, "ctx", perm)
             if hi > lo:

time: 419 us -> 437 us (1.043)
  matrix products: 57.4 us -> 66.3 us
  local copies, waits for them, and re-layouts: 95.5 us -> 103 us
  other arithmetic: 12.7 us -> 19.1 us
  waiting for transfers between devices: 119 us -> 114 us
    all_to_all x3, waiting for transfers between devices: 64.5 us -> 56.7 us  [dispatch(): got = lax.all_to_all(buffer, 'ctx', 0, 0, tiled=True).reshape(slots, width)]
    sub x0 -> x1, matrix products: none -> 7.65 us  [local_attention(): weights = jnp.exp(scores - row_max)]
    slice x1 -> x2, local copies, waits for them, and re-layouts: 4.69 us -> 11.4 us  [one_group(): key_heads[:, lo:hi]]
    dot_general x8 -> x7, matrix products: 12.1 us -> 13.4 us  [local_attention(): jnp.einsum('hqk,khd->qhd', probabilities, value_part, preferred_element_t...]
  transfers between devices with their start and end apart: 16 -> 16, of which waited for: 11 -> 10; matrix products, arithmetic and copies ran while one was open for 31% -> 29% of each run, Pallas kernels for 0% -> 0%
where the time goes in v10:
time: 437 us; the launch traced here: 433 us
  waiting for transfers between devices  114 us (26%)
  local copies, waits for them, and re-layouts  103 us (24%)
  starting transfers between devices  81.3 us (19%)
  matrix products  66.3 us (15%)
  blocking collectives  31.7 us (7%)
  other arithmetic  19.1 us (4%)
  between operations  18.3 us (4%)
    all_to_all x3, waiting for transfers between devices, dispatch(): got = lax.all_to_all(buffer, 'ctx', 0, 0, tiled=True).reshape(slots, width)  56.7 us
    ppermute x10, starting transfers between devices, one_group(): got = lax.ppermute(total, 'ctx', perm)  52.7 us
    all_to_all x1, blocking collectives, one_group(): lax.all_to_all(outgoing, 'ctx', 0, 0, tiled=True)  31.7 us
    all_gather x2, waiting for transfers between devices, one_group(): gathered = lax.all_gather(rows, 'head', axis=1, tiled=True)  30.1 us
    ppermute x10, waiting for transfers between devices, one_group(): got = lax.ppermute(total, 'ctx', perm)  26.9 us
    gather x4, local copies, waits for them, and re-layouts, dispatch(): return jnp.take(got, tok_slot, axis=0, mode='clip').reshape(seg, heads, dh)  23.2 us
    dot_general x2, matrix products, one_group(): jnp.dot(gathered, weight_rows[:, first:last].reshape(head_count * group_w...  21.2 us
    all_to_all x3, starting transfers between devices, dispatch(): got = lax.all_to_all(buffer, 'ctx', 0, 0, tiled=True).reshape(slots, width)  19.1 us
  transfers between devices with their start and end apart: 16, of which 10 were waited for; matrix products, arithmetic and copies ran while one was open for 29% of the time, Pallas kernels for 0%

profile of v10, /device:TPU:1, one launch (start us, length us, event | category | flops | bytes accessed | tf_op | source)
XLA Modules:
  0.0 433.1 jit_solution(11581617036612681655)
XLA Ops:
  9.0 5.9 %gather_fusion.2 = bf16[1536,1024]{1,0:T(8,128)(2,1)} fusion(bf16[1024,1024]{1,0:T(8,128)(2,1)S(1)} %copy-done, s32[2048]{0:T(1024)S(1)} %pad_clamp_fusion.1), kind=kCustom, calls=%fused_computation.2 | custom fusion | bytes 6297600 | tf_op jit(solution)/shard_map/jit(_take)/gather | solution.py:66
  14.9 8.8 %all-to-all-start.1 = ((bf16[32,48,1024]{2,1,0:T(8,128)(2,1)}), bf16[32,48,1024]{2,1,0:T(8,128)(2,1)}, u32[]{:S(2)}, u32[]{:S(2)}) async-start(bf16[32,48,1024]{2,1,0:T(8,128)(2,1)} %bitcast.200), calls=%async_computation.1 | async-start | bytes 6291456 | tf_op jit(solution)/shard_map/all_to_all | solution.py:67
  23.6 5.8 %gather_fusion = bf16[1536,1024]{1,0:T(8,128)(2,1)} fusion(bf16[1024,1024]{1,0:T(8,128)(2,1)S(1)} %copy-done.2, s32[2048]{0:T(1024)S(1)} %pad_clamp_fusion.1), kind=kCustom, calls=%fused_computation | custom fusion | bytes 6297600 | tf_op jit(solution)/shard_map/jit(_take)/gather | solution.py:66
  29.5 34.0 %all-to-all-done.1 = bf16[32,48,1024]{2,1,0:T(8,128)(2,1)} async-done(((bf16[32,48,1024]{2,1,0:T(8,128)(2,1)}), bf16[32,48,1024]{2,1,0:T(8,128)(2,1)}, u32[]{:S(2)}, u32[]{:S(2)}) %all-to-all-start.1) | async-done | bytes 3145760 | tf_op jit(solution)/shard_map/all_to_all | solution.py:67
  63.5 5.3 %all-to-all-start = ((bf16[32,48,1024]{2,1,0:T(8,128)(2,1)}), bf16[32,48,1024]{2,1,0:T(8,128)(2,1)S(1)}, u32[]{:S(2)}, u32[]{:S(2)}) async-start(bf16[32,48,1024]{2,1,0:T(8,128)(2,1)} %bitcast.199), calls=%async_computation | async-start | bytes 6291456 | tf_op jit(solution)/shard_map/all_to_all | solution.py:67
  73.5 8.3 %gather_fusion.3 = bf16[1024,1024]{1,0:T(8,128)(2,1)} fusion(bf16[1536,1024]{1,0:T(8,128)(2,1)} %bitcast.6, s32[1024]{0:T(1024)S(1)} %broadcast_clamp_fusion.1), kind=kCustom, calls=%fused_computation.3 | custom fusion | bytes 4198400 | tf_op jit(solution)/shard_map/jit(_take)/gather | solution.py:68
  81.8 3.9 copy.51
  85.7 22.7 %all-to-all-done = bf16[32,48,1024]{2,1,0:T(8,128)(2,1)S(1)} async-done(((bf16[32,48,1024]{2,1,0:T(8,128)(2,1)}), bf16[32,48,1024]{2,1,0:T(8,128)(2,1)S(1)}, u32[]{:S(2)}, u32[]{:S(2)}) %all-to-all-start) | async-done | bytes 3145760 | tf_op jit(solution)/shard_map/all_to_all | solution.py:67
  108.4 5.3 %gather_fusion.1 = bf16[1024,1024]{1,0:T(8,128)(2,1)} fusion(bf16[1536,1024]{1,0:T(8,128)(2,1)S(1)} %bitcast.189, s32[1024]{0:T(1024)S(1)} %broadcast_clamp_fusion.1), kind=kCustom, calls=%fused_computation.1 | custom fusion | bytes 4198400 | tf_op jit(solution)/shard_map/jit(_take)/gather | solution.py:68
  113.8 2.2 copy.107
  117.3 2.5 fusion.46
  119.8 2.5 fusion.54
  123.1 5.8 %gather_fusion.4 = bf16[1536,1024]{1,0:T(8,128)(2,1)} fusion(bf16[1024,1024]{1,0:T(8,128)(2,1)S(1)} %copy-done.3, s32[2048]{0:T(1024)S(1)} %pad_clamp_fusion.1), kind=kCustom, calls=%fused_computation.4 | custom fusion | bytes 6297600 | tf_op jit(solution)/shard_map/jit(_take)/gather | solution.py:66
  128.9 5.0 %all-to-all-start.2 = ((bf16[32,48,1024]{2,1,0:T(8,128)(2,1)}), bf16[32,48,1024]{2,1,0:T(8,128)(2,1)S(1)}, u32[]{:S(2)}, u32[]{:S(2)}) async-start(bf16[32,48,1024]{2,1,0:T(8,128)(2,1)} %bitcast.198), calls=%async_computation.2 | async-start | bytes 6291456 | tf_op jit(solution)/shard_map/all_to_all | solution.py:67
  141.1 3.5 collective-permute-start
  144.7 9.3 %fusion.158 = (bf16[1024,1,128]{2,1,0:T(2,128)(2,1)}, bf16[1024,1,128]{2,1,0:T(2,128)(2,1)}, bf16[1024,1,128]{2,1,0:T(2,128)(2,1)S(1)}, bf16[1024,1,128]{2,1,0:T...) fusion(bf16[1024,8,128]{2,1,0:T(8,128)(2,1)} %bitcast.193), kind=kLoop, calls=%fused_computation.248 | loop fusion | bytes 3145728 | tf_op jit(solution)/shard_map/slice | solution.py:119
  154.0 2.5 fusion.47
  163.4 8.6 %collective-permute-done = f32[4,129,128]{2,1,0:T(8,128)S(1)} collective-permute-done((f32[4,129,128]{2,1,0:T(8,128)}, f32[4,129,128]{2,1,0:T(8,128)S(1)}, u32[]{:S(2)}, u32[]{:S(2)}) %collective-permute-start) | collective-permute-done | bytes 264224 | tf_op jit(solution)/shard_map/ppermute | solution.py:122
  173.0 2.7 collective-permute-start.1
  176.8 3.0 collective-permute-done.1
  180.5 5.6 %gather_fusion.5 = bf16[1024,1024]{1,0:T(8,128)(2,1)} fusion(bf16[1536,1024]{1,0:T(8,128)(2,1)S(1)} %bitcast.188, s32[1024]{0:T(1024)} %copy-done.31), kind=kCustom, calls=%fused_computation.5 | custom fusion | bytes 4198400 | tf_op jit(solution)/shard_map/jit(_take)/gather | solution.py:68
  186.1 2.2 copy.108
  188.9 3.1 fusion.159
  195.1 8.0 %collective-permute-start.2 = (f32[4,129,128]{2,1,0:T(8,128)S(1)}, f32[4,129,128]{2,1,0:T(8,128)S(1)}, u32[]{:S(2)}, u32[]{:S(2)}) collective-permute-start(f32[4,129,128]{2,1,0:T(8,128)S(1)} %copy-done.12), channel_id=1, source_target_pairs={{0,16},{4,20},{8,24},{12,28},{16,32},{20,36},{24,40},{28,44},{32,4... | collective-permute-start | bytes 792584 | tf_op jit(solution)/shard_map/ppermute | solution.py:122
  207.8 3.4 collective-permute-start.3
  211.2 7.6 %fusion.162 = (f32[2,1024]{1,0:T(2,128)S(1)}, f32[2,1024,1024]{1,2,0:T(8,128)}) fusion(pred[1024,1024]{0,1:T(8,128)(4,1)S(1)} %copy-done.13, bf16[1024,2,128]{2,0,1:T(8,128)(2,1)} %copy.91, bf16[1024,2,128]{2,0,1:T(8,128)(2,1)} %copy.92), kind=kOutput, calls=%fused_computation.252 | convolution fusion | flops 545260544 | bytes 10493952 | tf_op jit(solution)/shard_map/sub | solution.py:91
  218.9 4.3 %fusion.56 = f32[1024,2,128]{0,2,1:T(8,128)S(1)} fusion(bf16[1024,2,128]{0,2,1:T(8,128)(2,1)} %slice.192, f32[2,1024,1024]{1,2,0:T(8,128)} %get-tuple-element.129, f32[2,1024]{1,0:T(2,128)S(1)} %get-tuple-element.128), kind=kOutput, calls=%fused_computation.102 | convolution fusion | flops 541065216 | bytes 9969664 | tf_op jit(solution)/shard_map/hqk,khd->qhd/dot_general | solution.py:93
  223.3 4.8 %collective-permute-start.4 = (f32[4,129,128]{2,1,0:T(8,128)S(1)}, f32[4,129,128]{2,1,0:T(8,128)S(1)}, u32[]{:S(2)}, u32[]{:S(2)}) collective-permute-start(f32[4,129,128]{2,1,0:T(8,128)S(1)} %select_add_fusion.4), channel_id=1, source_target_pairs={{0,64},{4,68},{8,72},{12,76},{16,80},{20,84},{24,88},{28,92},{32,9... | collective-permute-start | bytes 792584 | tf_op jit(solution)/shard_map/ppermute | solution.py:122
  232.6 2.5 fusion.49
  235.1 4.4 %fusion.31 = bf16[1024,4,128]{0,2,1:T(8,128)(2,1)S(1)} fusion(f32[1024,1,128]{0,2,1:T(8,128)S(1)} %fusion.61, f32[1024,2,128]{0,2,1:T(8,128)S(1)} %fusion.56, f32[1024,1,128]{0,2,1:T(8,128)S(1)} %copy-done.41, f32[4]{0:T(128)S(1)} %copy-done.37, f32[1024,4]{0,1:T(4,128)S(1)} %fusion.124, f32[4]{0:T(128)S(1)} %copy-done.38, ...), kind=kOutput, calls=%fused_computation.80 | convolution fusion | flops 811597824 | bytes 4473856 | tf_op jit(solution)/shard_map/qhd,hde->qhe/dot_general | solution.py:134
  240.1 7.3 %collective-permute-start.5 = (f32[4,129,128]{2,1,0:T(8,128)S(1)}, f32[4,129,128]{2,1,0:T(8,128)S(1)}, u32[]{:S(2)}, u32[]{:S(2)}) collective-permute-start(f32[4,129,128]{2,1,0:T(8,128)S(1)} %pad_maximum_fusion.1), channel_id=1, source_target_pairs={{0,4},{4,8},{8,12},{12,16},{16,20},{20,24},{24,28},{28,32},{32,36}... | collective-permute-start | bytes 792584 | tf_op jit(solution)/shard_map/ppermute | solution.py:122
  247.4 5.4 %gather_fusion.6 = bf16[1536,512]{1,0:T(8,128)(2,1)} fusion(bf16[1024,512]{1,0:T(8,128)(2,1)S(1)} %copy.63, s32[2048]{0:T(1024)S(1)} %copy-done.29), kind=kCustom, calls=%fused_computation.6 | custom fusion | bytes 3151872 | tf_op jit(solution)/shard_map/jit(_take)/gather | solution.py:144
  252.8 9.4 %all-to-all-start.3 = ((bf16[32,48,512]{2,1,0:T(8,128)(2,1)}), bf16[32,48,512]{2,1,0:T(8,128)(2,1)S(1)}, u32[]{:S(2)}, u32[]{:S(2)}) async-start(bf16[32,48,512]{2,1,0:T(8,128)(2,1)} %bitcast.30), calls=%async_computation.3 | async-start | bytes 3145728 | tf_op jit(solution)/shard_map/all_to_all | solution.py:145
  266.1 3.4 collective-permute-start.6
  272.4 12.9 %collective-permute-done.6 = f32[4,129,128]{2,1,0:T(8,128)S(1)} collective-permute-done((f32[4,129,128]{2,1,0:T(8,128)S(1)}, f32[4,129,128]{2,1,0:T(8,128)S(1)}, u32[]{:S(2)}, u32[]{:S(2)}) %collective-permute-start.6) | collective-permute-done | bytes 264224 | tf_op jit(solution)/shard_map/ppermute | solution.py:122
  286.1 6.5 %collective-permute-start.7 = (f32[4,129,128]{2,1,0:T(8,128)}, f32[4,129,128]{2,1,0:T(8,128)}, u32[]{:S(2)}, u32[]{:S(2)}) collective-permute-start(f32[4,129,128]{2,1,0:T(8,128)} %select_add_fusion.2), channel_id=1, source_target_pairs={{0,16},{4,20},{8,24},{12,28},{16,32},{20,36},{24,40},{28,44},{32,4... | collective-permute-start | bytes 792584 | tf_op jit(solution)/shard_map/ppermute | solution.py:122
  293.6 5.1 %gather_fusion.7 = bf16[1024,512]{1,0:T(8,128)(2,1)} fusion(bf16[1536,512]{1,0:T(8,128)(2,1)S(1)} %bitcast.190, s32[1024]{0:T(1024)S(1)} %broadcast_clamp_fusion), kind=kCustom, calls=%fused_computation.7 | custom fusion | bytes 2101248 | tf_op jit(solution)/shard_map/jit(_take)/gather | solution.py:146
  299.7 5.8 %collective-permute-start.8 = (f32[4,129,128]{2,1,0:T(8,128)S(1)}, f32[4,129,128]{2,1,0:T(8,128)S(1)}, u32[]{:S(2)}, u32[]{:S(2)}) collective-permute-start(f32[4,129,128]{2,1,0:T(8,128)S(1)} %select_add_fusion.1), channel_id=1, source_target_pairs={{0,32},{4,36},{8,40},{12,44},{16,48},{20,52},{24,56},{28,60},{32,6... | collective-permute-start | bytes 792584 | tf_op jit(solution)/shard_map/ppermute | solution.py:122
  309.7 7.3 %collective-permute-start.9 = (f32[4,129,128]{2,1,0:T(8,128)S(1)}, f32[4,129,128]{2,1,0:T(8,128)S(1)}, u32[]{:S(2)}, u32[]{:S(2)}) collective-permute-start(f32[4,129,128]{2,1,0:T(8,128)S(1)} %select_add_fusion), channel_id=1, source_target_pairs={{0,64},{4,68},{8,72},{12,76},{16,80},{20,84},{24,88},{28,92},{32,9... | collective-permute-start | bytes 792584 | tf_op jit(solution)/shard_map/ppermute | solution.py:122
  320.3 2.5 fusion.42
  322.9 3.2 fusion.33
  326.6 4.8 %gather_fusion.8 = bf16[1536,512]{1,0:T(8,128)(2,1)S(1)} fusion(bf16[1024,512]{1,0:T(8,128)(2,1)S(1)} %copy.77, s32[2048]{0:T(1024)S(1)} %copy-done.30), kind=kCustom, calls=%fused_computation.8 | custom fusion | bytes 3151872 | tf_op jit(solution)/shard_map/jit(_take)/gather | solution.py:144
  331.5 31.7 %all_to_all.25 = bf16[32,48,512]{2,1,0:T(8,128)(2,1)S(1)} all-to-all(bf16[32,48,512]{2,1,0:T(8,128)(2,1)S(1)} %bitcast.208), channel_id=1, replica_groups=mesh['ctx'=32,'head'=4] {'ctx'}, dimensions={0} | all-to-all | bytes 3145728 | tf_op jit(solution)/shard_map/all_to_all | solution.py:145
  363.2 5.1 %gather_fusion.9 = bf16[1024,512]{1,0:T(8,128)(2,1)} fusion(bf16[1536,512]{1,0:T(8,128)(2,1)S(1)} %bitcast.191, s32[1024]{0:T(1024)S(1)} %broadcast_clamp_fusion), kind=kCustom, calls=%fused_computation.9 | custom fusion | bytes 2101248 | tf_op jit(solution)/shard_map/jit(_take)/gather | solution.py:146
  368.3 6.1 %fusion.155 = (bf16[4,4,128,1024]{3,2,1,0:T(8,128)(2,1)}, bf16[4,4,128,1024]{3,2,1,0:T(8,128)(2,1)}) fusion(bf16[4,8,128,1024]{3,2,1,0:T(8,128)(2,1)} %bitcast.203), kind=kLoop, calls=%fused_computation.245 | loop fusion | bytes 16777216 | tf_op jit(solution)/shard_map/slice | solution.py:150
  374.4 10.6 %fusion.163 = f32[1024,1024]{1,0:T(8,128)} fusion(bf16[1024,2048]{1,0:T(8,128)(2,1)} %all-gather.5.cloned.1.call-done, bf16[2048,1024]{1,0:T(8,128)(2,1)} %bitcast.210), kind=kOutput, calls=%fused_computation.253 | convolution fusion | flops 4294967296 | bytes 12582912 | tf_op jit(solution)/shard_map/dot_general | solution.py:148
  385.0 30.1 %all-gather.7.cloned.1.call-done = bf16[1024,2048]{1,0:T(8,128)(2,1)} async-done(((bf16[1024,512]{1,0:T(8,128)(2,1)}), bf16[1024,2048]{1,0:T(8,128)(2,1)}) %all-gather.7.cloned.1.call-update) | async-done | bytes 4194320 | tf_op jit(solution)/shard_map/all_gather | solution.py:147
  415.2 10.6 %add_convert_fusion = bf16[1024,1024]{1,0:T(8,128)(2,1)} fusion(f32[1024,1024]{1,0:T(8,128)} %fusion.163, bf16[1024,2048]{1,0:T(8,128)(2,1)} %all-gather.7.cloned.1.call-done, bf16[2048,1024]{1,0:T(8,128)(2,1)} %bitcast.209), kind=kOutput, calls=%fused_computation.31 | convolution fusion | flops 4297064448 | bytes 14680064 | tf_op jit(solution)/shard_map/dot_general | solution.py:148
  (181 shorter events, 53.3 us)
Async XLA Ops:
  8.2 6.7 %copy-start.32 = (s32[1024]{0:T(1024)}, s32[1024]{0:T(1024)S(1)}, u32[]{:S(2)}) copy-start(s32[1024]{0:T(1024)S(1)} %convert_element_type.85) | copy-start | bytes 12292
  14.9 8.8 %copy-start.2 = (bf16[1024,1024]{1,0:T(8,128)(2,1)S(1)}, bf16[1024,1024]{1,0:T(8,128)(2,1)}, u32[]{:S(2)}) copy-start(bf16[1024,1024]{1,0:T(8,128)(2,1)} %param.8) | copy-start | bytes 6291460
  14.9 48.6 %all-to-all-start.1 = ((bf16[32,48,1024]{2,1,0:T(8,128)(2,1)}), bf16[32,48,1024]{2,1,0:T(8,128)(2,1)}, u32[]{:S(2)}, u32[]{:S(2)}) async-start(bf16[32,48,1024]{2,1,0:T(8,128)(2,1)} %bitcast.200), calls=%async_computation.1 | async-start | bytes 6291456 | tf_op jit(solution)/shard_map/all_to_all | solution.py:67
  29.5 39.3 %copy-start.39 = (s32[32]{0:T(128)S(1)}, s32[32]{0:T(128)}, u32[]{:S(2)}) copy-start(s32[32]{0:T(128)} %param.11) | copy-start | bytes 388
  63.5 45.0 %all-to-all-start = ((bf16[32,48,1024]{2,1,0:T(8,128)(2,1)}), bf16[32,48,1024]{2,1,0:T(8,128)(2,1)S(1)}, u32[]{:S(2)}, u32[]{:S(2)}) async-start(bf16[32,48,1024]{2,1,0:T(8,128)(2,1)} %bitcast.199), calls=%async_computation | async-start | bytes 6291456 | tf_op jit(solution)/shard_map/all_to_all | solution.py:67
  73.4 35.0 %copy-start.31 = (s32[1024]{0:T(1024)}, s32[1024]{0:T(1024)S(1)}, u32[]{:S(2)}) copy-start(s32[1024]{0:T(1024)S(1)} %broadcast_clamp_fusion.1) | copy-start | bytes 12292
  116.7 5.6 %copy-start.7 = (bf16[1024,4,128]{2,1,0:T(4,128)(2,1)}, bf16[1024,4,128]{2,1,0:T(4,128)(2,1)S(1)}, u32[]{:S(2)}) copy-start(bf16[1024,4,128]{2,1,0:T(4,128)(2,1)S(1)} %get-tuple-element.119) | copy-start | bytes 3145732
  117.3 5.8 %copy-start.3 = (bf16[1024,1024]{1,0:T(8,128)(2,1)S(1)}, bf16[1024,1024]{1,0:T(8,128)(2,1)}, u32[]{:S(2)}) copy-start(bf16[1024,1024]{1,0:T(8,128)(2,1)} %param.7) | copy-start | bytes 6291460
  128.9 11.6 %copy-start.40 = (f32[8]{0:T(128)S(1)}, f32[8]{0:T(128)}, u32[]{:S(2)}) copy-start(f32[8]{0:T(128)} %param.12) | copy-start | bytes 100
  128.9 51.7 %all-to-all-start.2 = ((bf16[32,48,1024]{2,1,0:T(8,128)(2,1)}), bf16[32,48,1024]{2,1,0:T(8,128)(2,1)S(1)}, u32[]{:S(2)}, u32[]{:S(2)}) async-start(bf16[32,48,1024]{2,1,0:T(8,128)(2,1)} %bitcast.198), calls=%async_computation.2 | async-start | bytes 6291456 | tf_op jit(solution)/shard_map/all_to_all | solution.py:67
  138.5 15.5 %copy-start.6 = (bf16[1024,1024]{0,1:T(8,128)(2,1)S(1)}, bf16[1024,1024]{0,1:T(8,128)(2,1)}, u32[]{:S(2)}) copy-start(bf16[1024,1024]{0,1:T(8,128)(2,1)} %copy.51) | copy-start | bytes 6291460
  138.5 15.5 %copy-start.8 = (bf16[1024,4,128]{2,1,0:T(4,128)(2,1)S(1)}, bf16[1024,4,128]{2,1,0:T(4,128)(2,1)}, u32[]{:S(2)}) copy-start(bf16[1024,4,128]{2,1,0:T(4,128)(2,1)} %copy-done.7) | copy-start | bytes 3145732
  141.1 30.8 %collective-permute-start = (f32[4,129,128]{2,1,0:T(8,128)}, f32[4,129,128]{2,1,0:T(8,128)S(1)}, u32[]{:S(2)}, u32[]{:S(2)}) collective-permute-start(f32[4,129,128]{2,1,0:T(8,128)} %pad_maximum_fusion), channel_id=1, source_target_pairs={{0,4},{4,8},{8,12},{12,16},{16,20},{20,24},{24,28},{28,32},{32,36}... | collective-permute-start | bytes 792584 | tf_op jit(solution)/shard_map/ppermute | solution.py:122
  156.5 6.8 %copy-start.34 = (f32[4,128]{1,0:T(4,128)S(1)}, f32[4,128]{1,0:T(4,128)}, u32[]{:S(2)}) copy-start(f32[4,128]{1,0:T(4,128)} %get-tuple-element.140) | copy-start | bytes 6148
  173.0 6.8 %collective-permute-start.1 = (f32[4,129,128]{2,1,0:T(8,128)S(1)}, f32[4,129,128]{2,1,0:T(8,128)S(1)}, u32[]{:S(2)}, u32[]{:S(2)}) collective-permute-start(f32[4,129,128]{2,1,0:T(8,128)S(1)} %select_add_fusion.7), channel_id=1, source_target_pairs={{0,8},{4,12},{8,16},{12,20},{16,24},{20,28},{24,32},{28,36},{32,40... | collective-permute-start | bytes 792584 | tf_op jit(solution)/shard_map/ppermute | solution.py:122
  188.9 6.2 %copy-start.12 = (f32[4,129,128]{2,1,0:T(8,128)S(1)}, f32[4,129,128]{2,1,0:T(8,128)}, u32[]{:S(2)}) copy-start(f32[4,129,128]{2,1,0:T(8,128)} %select_add_fusion.6) | copy-start | bytes 792580
  188.9 14.2 %copy-start.26 = (bf16[1024,1,128]{2,0,1:T(8,128)(2,1)S(1)}, bf16[1024,1,128]{2,0,1:T(8,128)(2,1)}, u32[]{:S(2)}) copy-start(bf16[1024,1,128]{2,0,1:T(8,128)(2,1)} %copy.90) | copy-start | bytes 786436
  195.1 9.3 %copy-start.28 = (bf16[1024,1,128]{0,2,1:T(8,128)(2,1)S(1)}, bf16[1024,1,128]{0,2,1:T(8,128)(2,1)}, u32[]{:S(2)}) copy-start(bf16[1024,1,128]{0,2,1:T(8,128)(2,1)} %get-tuple-element.53) | copy-start | bytes 786436
  195.1 12.6 %collective-permute-start.2 = (f32[4,129,128]{2,1,0:T(8,128)S(1)}, f32[4,129,128]{2,1,0:T(8,128)S(1)}, u32[]{:S(2)}, u32[]{:S(2)}) collective-permute-start(f32[4,129,128]{2,1,0:T(8,128)S(1)} %copy-done.12), channel_id=1, source_target_pairs={{0,16},{4,20},{8,24},{12,28},{16,32},{20,36},{24,40},{28,44},{32,4... | collective-permute-start | bytes 792584 | tf_op jit(solution)/shard_map/ppermute | solution.py:122
  205.9 5.3 %copy-start.13 = (pred[1024,1024]{0,1:T(8,128)(4,1)S(1)}, pred[1024,1024]{0,1:T(8,128)(4,1)}, u32[]{:S(2)}) copy-start(pred[1024,1024]{0,1:T(8,128)(4,1)} %iota_compare_fusion.3) | copy-start | bytes 3145732
  207.7 24.9 %copy-start.15 = (bf16[1024,4,128]{2,1,0:T(4,128)(2,1)}, bf16[1024,4,128]{2,1,0:T(4,128)(2,1)S(1)}, u32[]{:S(2)}) copy-start(bf16[1024,4,128]{2,1,0:T(4,128)(2,1)S(1)} %get-tuple-element.100) | copy-start | bytes 3145732
  207.8 15.4 %collective-permute-start.3 = (f32[4,129,128]{2,1,0:T(8,128)S(1)}, f32[4,129,128]{2,1,0:T(8,128)}, u32[]{:S(2)}, u32[]{:S(2)}) collective-permute-start(f32[4,129,128]{2,1,0:T(8,128)S(1)} %select_add_fusion.5), channel_id=1, source_target_pairs={{0,32},{4,36},{8,40},{12,44},{16,48},{20,52},{24,56},{28,60},{32,6... | collective-permute-start | bytes 792584 | tf_op jit(solution)/shard_map/ppermute | solution.py:122
  218.9 9.2 %copy-start.23 = (bf16[1024,1,128]{2,0,1:T(8,128)(2,1)S(1)}, bf16[1024,1,128]{2,0,1:T(8,128)(2,1)}, u32[]{:S(2)}) copy-start(bf16[1024,1,128]{2,0,1:T(8,128)(2,1)} %copy.94) | copy-start | bytes 786436
  218.9 9.2 %copy-start.27 = (bf16[1024,1,128]{2,0,1:T(8,128)(2,1)S(1)}, bf16[1024,1,128]{2,0,1:T(8,128)(2,1)}, u32[]{:S(2)}) copy-start(bf16[1024,1,128]{2,0,1:T(8,128)(2,1)} %copy.93) | copy-start | bytes 786436
  223.3 6.1 %copy-start.24 = (bf16[1024,1,128]{0,2,1:T(8,128)(2,1)S(1)}, bf16[1024,1,128]{0,2,1:T(8,128)(2,1)}, u32[]{:S(2)}) copy-start(bf16[1024,1,128]{0,2,1:T(8,128)(2,1)} %get-tuple-element.63) | copy-start | bytes 786436
  223.3 8.3 %collective-permute-start.4 = (f32[4,129,128]{2,1,0:T(8,128)S(1)}, f32[4,129,128]{2,1,0:T(8,128)S(1)}, u32[]{:S(2)}, u32[]{:S(2)}) collective-permute-start(f32[4,129,128]{2,1,0:T(8,128)S(1)} %select_add_fusion.4), channel_id=1, source_target_pairs={{0,64},{4,68},{8,72},{12,76},{16,80},{20,84},{24,88},{28,92},{32,9... | collective-permute-start | bytes 792584 | tf_op jit(solution)/shard_map/ppermute | solution.py:122
  230.9 4.2 copy-start.37
  235.1 12.3 %copy-start.29 = (s32[2048]{0:T(1024)S(1)}, s32[2048]{0:T(1024)}, u32[]{:S(2)}) copy-start(s32[2048]{0:T(1024)} %pad_clamp_fusion) | copy-start | bytes 24580
  240.1 22.2 %copy-start.20 = (bf16[1024,1,128]{2,0,1:T(8,128)(2,1)S(1)}, bf16[1024,1,128]{2,0,1:T(8,128)(2,1)}, u32[]{:S(2)}) copy-start(bf16[1024,1,128]{2,0,1:T(8,128)(2,1)} %copy.99) | copy-start | bytes 786436
  240.1 26.0 %collective-permute-start.5 = (f32[4,129,128]{2,1,0:T(8,128)S(1)}, f32[4,129,128]{2,1,0:T(8,128)S(1)}, u32[]{:S(2)}, u32[]{:S(2)}) collective-permute-start(f32[4,129,128]{2,1,0:T(8,128)S(1)} %pad_maximum_fusion.1), channel_id=1, source_target_pairs={{0,4},{4,8},{8,12},{12,16},{16,20},{20,24},{24,28},{28,32},{32,36}... | collective-permute-start | bytes 792584 | tf_op jit(solution)/shard_map/ppermute | solution.py:122
  252.8 40.7 %all-to-all-start.3 = ((bf16[32,48,512]{2,1,0:T(8,128)(2,1)}), bf16[32,48,512]{2,1,0:T(8,128)(2,1)S(1)}, u32[]{:S(2)}, u32[]{:S(2)}) async-start(bf16[32,48,512]{2,1,0:T(8,128)(2,1)} %bitcast.30), calls=%async_computation.3 | async-start | bytes 3145728 | tf_op jit(solution)/shard_map/all_to_all | solution.py:145
  262.2 112.2 %all-gather.5.cloned.1.call-start = ((), (), s32[]{:S(2)}) async-start(), calls=%async_computation.5 | async-start | bytes 5242880 | tf_op jit(solution)/shard_map/all_gather | solution.py:147
  264.5 5.1 %copy-start.18 = (bf16[1024,1,128]{2,0,1:T(8,128)(2,1)S(1)}, bf16[1024,1,128]{2,0,1:T(8,128)(2,1)}, u32[]{:S(2)}) copy-start(bf16[1024,1,128]{2,0,1:T(8,128)(2,1)} %copy.101) | copy-start | bytes 786436
  264.5 5.1 %copy-start.22 = (bf16[1024,1,128]{2,0,1:T(8,128)(2,1)S(1)}, bf16[1024,1,128]{2,0,1:T(8,128)(2,1)}, u32[]{:S(2)}) copy-start(bf16[1024,1,128]{2,0,1:T(8,128)(2,1)} %copy.100) | copy-start | bytes 786436
  266.1 4.7 %copy-start.19 = (bf16[1024,1,128]{0,2,1:T(8,128)(2,1)S(1)}, bf16[1024,1,128]{0,2,1:T(8,128)(2,1)}, u32[]{:S(2)}) copy-start(bf16[1024,1,128]{0,2,1:T(8,128)(2,1)} %get-tuple-element.77) | copy-start | bytes 786436
  266.1 19.2 %collective-permute-start.6 = (f32[4,129,128]{2,1,0:T(8,128)S(1)}, f32[4,129,128]{2,1,0:T(8,128)S(1)}, u32[]{:S(2)}, u32[]{:S(2)}) collective-permute-start(f32[4,129,128]{2,1,0:T(8,128)S(1)} %select_add_fusion.3), channel_id=1, source_target_pairs={{0,8},{4,12},{8,16},{12,20},{16,24},{20,28},{24,32},{28,36},{32,40... | collective-permute-start | bytes 792584 | tf_op jit(solution)/shard_map/ppermute | solution.py:122
  270.9 21.8 %copy-start.33 = (s32[1024]{0:T(1024)S(1)}, s32[1024]{0:T(1024)}, u32[]{:S(2)}) copy-start(s32[1024]{0:T(1024)} %copy-done.32) | copy-start | bytes 12292
  270.9 21.8 %copy-start.10 = (bf16[1024,1,128]{2,1,0:T(2,128)(2,1)S(1)}, bf16[1024,1,128]{2,1,0:T(2,128)(2,1)}, u32[]{:S(2)}) copy-start(bf16[1024,1,128]{2,1,0:T(2,128)(2,1)} %get-tuple-element.107) | copy-start | bytes 786436
  270.9 22.5 %copy-start.9 = (bf16[1024,1,128]{2,1,0:T(2,128)(2,1)S(1)}, bf16[1024,1,128]{2,1,0:T(2,128)(2,1)}, u32[]{:S(2)}) copy-start(bf16[1024,1,128]{2,1,0:T(2,128)(2,1)} %get-tuple-element.108) | copy-start | bytes 786436
  270.9 22.6 %copy-start.11 = (bf16[1024,1,128]{2,1,0:T(2,128)(2,1)S(1)}, bf16[1024,1,128]{2,1,0:T(2,128)(2,1)}, u32[]{:S(2)}) copy-start(bf16[1024,1,128]{2,1,0:T(2,128)(2,1)} %get-tuple-element.113) | copy-start | bytes 786436
  286.1 12.6 %collective-permute-start.7 = (f32[4,129,128]{2,1,0:T(8,128)}, f32[4,129,128]{2,1,0:T(8,128)}, u32[]{:S(2)}, u32[]{:S(2)}) collective-permute-start(f32[4,129,128]{2,1,0:T(8,128)} %select_add_fusion.2), channel_id=1, source_target_pairs={{0,16},{4,20},{8,24},{12,28},{16,32},{20,36},{24,40},{28,44},{32,4... | collective-permute-start | bytes 792584 | tf_op jit(solution)/shard_map/ppermute | solution.py:122
  298.7 116.5 %all-gather.7.cloned.1.call-start = ((), (), s32[]{:S(2)}) async-start(), calls=%async_computation.6 | async-start | bytes 5242880 | tf_op jit(solution)/shard_map/all_gather | solution.py:147
  299.7 7.1 %copy-start.17 = (bf16[1024,1,128]{0,2,1:T(8,128)(2,1)S(1)}, bf16[1024,1,128]{0,2,1:T(8,128)(2,1)}, u32[]{:S(2)}) copy-start(bf16[1024,1,128]{0,2,1:T(8,128)(2,1)} %get-tuple-element.82) | copy-start | bytes 786436
  299.7 9.9 %collective-permute-start.8 = (f32[4,129,128]{2,1,0:T(8,128)S(1)}, f32[4,129,128]{2,1,0:T(8,128)S(1)}, u32[]{:S(2)}, u32[]{:S(2)}) collective-permute-start(f32[4,129,128]{2,1,0:T(8,128)S(1)} %select_add_fusion.1), channel_id=1, source_target_pairs={{0,32},{4,36},{8,40},{12,44},{16,48},{20,52},{24,56},{28,60},{32,6... | collective-permute-start | bytes 792584 | tf_op jit(solution)/shard_map/ppermute | solution.py:122
  306.8 10.2 %copy-start.25 = (bf16[1024,1,128]{2,0,1:T(8,128)(2,1)S(1)}, bf16[1024,1,128]{2,0,1:T(8,128)(2,1)}, u32[]{:S(2)}) copy-start(bf16[1024,1,128]{2,0,1:T(8,128)(2,1)} %copy.105) | copy-start | bytes 786436
  309.7 8.6 %copy-start.16 = (bf16[1024,1,128]{0,2,1:T(8,128)(2,1)S(1)}, bf16[1024,1,128]{0,2,1:T(8,128)(2,1)}, u32[]{:S(2)}) copy-start(bf16[1024,1,128]{0,2,1:T(8,128)(2,1)} %get-tuple-element.87) | copy-start | bytes 786436
  309.7 10.5 %collective-permute-start.9 = (f32[4,129,128]{2,1,0:T(8,128)S(1)}, f32[4,129,128]{2,1,0:T(8,128)S(1)}, u32[]{:S(2)}, u32[]{:S(2)}) collective-permute-start(f32[4,129,128]{2,1,0:T(8,128)S(1)} %select_add_fusion), channel_id=1, source_target_pairs={{0,64},{4,68},{8,72},{12,76},{16,80},{20,84},{24,88},{28,92},{32,9... | collective-permute-start | bytes 792584 | tf_op jit(solution)/shard_map/ppermute | solution.py:122
  415.1 10.6 %copy-start.1 = (bf16[1024,1024]{1,0:T(8,128)(2,1)S(1)}, bf16[1024,1024]{1,0:T(8,128)(2,1)}, u32[]{:S(2)}) copy-start(bf16[1024,1024]{1,0:T(8,128)(2,1)} %param.9) | copy-start | bytes 6291460
  (12 other events, 36.3 us)
Sparse Core Ops, SparseCore 0:
  298.8 50.8 all-gather.4
  368.4 46.6 all-gather.6

commit v11 on v5

--- a/solution.py
+++ b/solution.py
@@ -135,12 +135,22 @@
         outgoing = jnp.take(combined, pslot, axis=0, mode="clip").reshape(n, cap, group_width)
         incoming = lax.all_to_all(outgoing, "ctx", 0, 0, tiled=True).reshape(slots, group_width)
         rows = jnp.take(incoming, send_slot, axis=0, mode="clip")
-        gathered = lax.all_gather(rows, "head", axis=1, tiled=True)
-        part = jnp.dot(
-            gathered,
-            weight_rows[:, first:last].reshape(head_count * group_width, out_cols),
-            preferred_element_type=f32,
-        )
+        if last == heads:
+            spread = jnp.broadcast_to(rows[None], (head_count, seg, group_width))
+            blocks = lax.all_to_all(spread, "head", 0, 0, tiled=True)
+            part = jnp.einsum(
+                "hrc,hcd->rd",
+                blocks,
+                weight_rows[:, first:last].reshape(head_count, group_width, out_cols),
+                preferred_element_type=f32,
+            )
+        else:
+            gathered = lax.all_gather(rows, "head", axis=1, tiled=True)
+            part = jnp.dot(
+                gathered,
+                weight_rows[:, first:last].reshape(head_count * group_width, out_cols),
+                preferred_element_type=f32,
+            )
         return part, combined
 
     summed, hold = one_group(0, None)

time: 419 us -> 428 us (1.021)
  waiting for transfers between devices: 119 us -> 127 us
    all_to_all x0 -> x1, waiting for transfers between devices: none -> 33.9 us  [one_group(): blocks = lax.all_to_all(spread, 'head', 0, 0, tiled=True)]
    all_gather x2 -> x1, waiting for transfers between devices: 30.1 us -> 0.01 us  [one_group(): gathered = lax.all_gather(rows, 'head', axis=1, tiled=True)]
    dot_general x2 -> x1, matrix products: 21.2 us -> 9.89 us  [one_group(): jnp.dot(gathered, weight_rows[:, first:last].reshape(head_count * group_w...]
    dot_general x0 -> x1, matrix products: none -> 10.6 us  [one_group(): jnp.einsum('hrc,hcd->rd', blocks, weight_rows[:, first:last].reshape(head...]
    ppermute x10, starting transfers between devices: 50 us -> 44.6 us  [one_group(): got = lax.ppermute(total, 'ctx', perm)]
    all_to_all x0 -> x1, starting transfers between devices: none -> 5.29 us  [one_group(): blocks = lax.all_to_all(spread, 'head', 0, 0, tiled=True)]
    all_to_all x1, starting transfers between devices: 8.23 us -> 12.9 us  [one_group(): lax.all_to_all(outgoing, 'ctx', 0, 0, tiled=True)]
  transfers between devices with their start and end apart: 16 -> 16, of which waited for: 11 -> 11; matrix products, arithmetic and copies ran while one was open for 31% -> 29% of each run, Pallas kernels for 0% -> 0%
where the time goes in v11:
time: 428 us; the launch traced here: 420 us
  waiting for transfers between devices  127 us (30%)
  local copies, waits for them, and re-layouts  95.9 us (22%)
  starting transfers between devices  81.9 us (19%)
  matrix products  55.7 us (13%)
  blocking collectives  29.8 us (7%)
  between operations  17.9 us (4%)
  other arithmetic  12.1 us (3%)
    all_to_all x3, waiting for transfers between devices, dispatch(): got = lax.all_to_all(buffer, 'ctx', 0, 0, tiled=True).reshape(slots, width)  66.1 us
    ppermute x10, starting transfers between devices, one_group(): got = lax.ppermute(total, 'ctx', perm)  44.6 us
    all_to_all x1, waiting for transfers between devices, one_group(): blocks = lax.all_to_all(spread, 'head', 0, 0, tiled=True)  33.9 us
    all_to_all x1, blocking collectives, one_group(): lax.all_to_all(outgoing, 'ctx', 0, 0, tiled=True)  29.8 us
    ppermute x10, waiting for transfers between devices, one_group(): got = lax.ppermute(total, 'ctx', perm)  27 us
    gather x4, local copies, waits for them, and re-layouts, dispatch(): return jnp.take(got, tok_slot, axis=0, mode='clip').reshape(seg, heads, dh)  25.3 us
    all_to_all x3, starting transfers between devices, dispatch(): got = lax.all_to_all(buffer, 'ctx', 0, 0, tiled=True).reshape(slots, width)  19.1 us
    gather x3, local copies, waits for them, and re-layouts, dispatch(): jnp.take(source, slot_row, axis=0, mode='clip').reshape(n, cap, width)  17.4 us
  transfers between devices with their start and end apart: 16, of which 11 were waited for; matrix products, arithmetic and copies ran while one was open for 29% of the time, Pallas kernels for 0%

profile of v11, /device:TPU:1, one launch (start us, length us, event | category | flops | bytes accessed | tf_op | source)
XLA Modules:
  0.0 420.4 jit_solution(15899838261600653302)
XLA Ops:
  9.0 5.8 %gather_fusion.4 = bf16[1536,1024]{1,0:T(8,128)(2,1)} fusion(bf16[1024,1024]{1,0:T(8,128)(2,1)S(1)} %copy-done, s32[2048]{0:T(1024)S(1)} %pad_clamp_fusion.1), kind=kCustom, calls=%fused_computation.4 | custom fusion | bytes 6297600 | tf_op jit(solution)/shard_map/jit(_take)/gather | solution.py:66
  14.8 8.8 %all-to-all-start.2 = ((bf16[32,48,1024]{2,1,0:T(8,128)(2,1)}), bf16[32,48,1024]{2,1,0:T(8,128)(2,1)}, u32[]{:S(2)}, u32[]{:S(2)}) async-start(bf16[32,48,1024]{2,1,0:T(8,128)(2,1)} %bitcast.228), calls=%async_computation.2 | async-start | bytes 6291456 | tf_op jit(solution)/shard_map/all_to_all | solution.py:67
  23.6 5.8 %gather_fusion = bf16[1536,1024]{1,0:T(8,128)(2,1)} fusion(bf16[1024,1024]{1,0:T(8,128)(2,1)S(1)} %copy-done.2, s32[2048]{0:T(1024)S(1)} %pad_clamp_fusion.1), kind=kCustom, calls=%fused_computation | custom fusion | bytes 6297600 | tf_op jit(solution)/shard_map/jit(_take)/gather | solution.py:66
  29.4 34.0 %all-to-all-done.2 = bf16[32,48,1024]{2,1,0:T(8,128)(2,1)} async-done(((bf16[32,48,1024]{2,1,0:T(8,128)(2,1)}), bf16[32,48,1024]{2,1,0:T(8,128)(2,1)}, u32[]{:S(2)}, u32[]{:S(2)}) %all-to-all-start.2) | async-done | bytes 3145760 | tf_op jit(solution)/shard_map/all_to_all | solution.py:67
  63.4 5.0 %all-to-all-start = ((bf16[32,48,1024]{2,1,0:T(8,128)(2,1)}), bf16[32,48,1024]{2,1,0:T(8,128)(2,1)}, u32[]{:S(2)}, u32[]{:S(2)}) async-start(bf16[32,48,1024]{2,1,0:T(8,128)(2,1)} %bitcast.227), calls=%async_computation | async-start | bytes 6291456 | tf_op jit(solution)/shard_map/all_to_all | solution.py:67
  71.8 5.8 %gather_fusion.2 = bf16[1536,1024]{1,0:T(8,128)(2,1)} fusion(bf16[1024,1024]{1,0:T(8,128)(2,1)S(1)} %copy-done.3, s32[2048]{0:T(1024)S(1)} %pad_clamp_fusion.1), kind=kCustom, calls=%fused_computation.2 | custom fusion | bytes 6297600 | tf_op jit(solution)/shard_map/jit(_take)/gather | solution.py:66
  79.1 29.2 %all-to-all-done = bf16[32,48,1024]{2,1,0:T(8,128)(2,1)} async-done(((bf16[32,48,1024]{2,1,0:T(8,128)(2,1)}), bf16[32,48,1024]{2,1,0:T(8,128)(2,1)}, u32[]{:S(2)}, u32[]{:S(2)}) %all-to-all-start) | async-done | bytes 3145760 | tf_op jit(solution)/shard_map/all_to_all | solution.py:67
  108.3 5.3 %all-to-all-start.1 = ((bf16[32,48,1024]{2,1,0:T(8,128)(2,1)}), bf16[32,48,1024]{2,1,0:T(8,128)(2,1)S(1)}, u32[]{:S(2)}, u32[]{:S(2)}) async-start(bf16[32,48,1024]{2,1,0:T(8,128)(2,1)} %bitcast.226), calls=%async_computation.1 | async-start | bytes 6291456 | tf_op jit(solution)/shard_map/all_to_all | solution.py:67
  118.0 8.3 %gather_fusion.5 = bf16[1024,1024]{1,0:T(8,128)(2,1)} fusion(bf16[1536,1024]{1,0:T(8,128)(2,1)} %bitcast.10, s32[1024]{0:T(1024)S(1)} %broadcast_clamp_fusion.1), kind=kCustom, calls=%fused_computation.5 | custom fusion | bytes 4198400 | tf_op jit(solution)/shard_map/jit(_take)/gather | solution.py:68
  126.3 2.2 copy.107
  128.6 4.6 %fusion.169 = (bf16[1024,1,128]{2,1,0:T(2,128)(2,1)}, bf16[1024,1,128]{2,1,0:T(2,128)(2,1)}, bf16[1024,1,128]{2,1,0:T(2,128)(2,1)}, bf16[1024,1,128]{2,1,0:T(2,1...) fusion(bf16[1024,8,128]{2,1,0:T(8,128)(2,1)S(1)} %bitcast.222), kind=kLoop, calls=%fused_computation.263 | loop fusion | bytes 4194304 | tf_op jit(solution)/shard_map/slice | solution.py:110
  133.2 8.3 %gather_fusion.1 = bf16[1024,1024]{1,0:T(8,128)(2,1)} fusion(bf16[1536,1024]{1,0:T(8,128)(2,1)} %bitcast.4, s32[1024]{0:T(1024)S(1)} %broadcast_clamp_fusion.1), kind=kCustom, calls=%fused_computation.1 | custom fusion | bytes 4198400 | tf_op jit(solution)/shard_map/jit(_take)/gather | solution.py:68
  141.5 2.2 copy.106
  143.7 2.0 fusion.170
  145.7 4.6 %fusion.168 = (bf16[1024,1,128]{2,1,0:T(2,128)(2,1)}, bf16[1024,1,128]{2,1,0:T(2,128)(2,1)}, bf16[1024,1,128]{2,1,0:T(2,128)(2,1)}, bf16[1024,1,128]{2,1,0:T(2,1...) fusion(bf16[1024,8,128]{2,1,0:T(8,128)(2,1)S(1)} %bitcast.225), kind=kLoop, calls=%fused_computation.262 | loop fusion | bytes 4194304 | tf_op jit(solution)/shard_map/slice | solution.py:110
  150.3 2.9 all-to-all-done.1
  153.2 5.3 %gather_fusion.3 = bf16[1024,1024]{1,0:T(8,128)(2,1)} fusion(bf16[1536,1024]{1,0:T(8,128)(2,1)S(1)} %bitcast.219, s32[1024]{0:T(1024)S(1)} %broadcast_clamp_fusion.1), kind=kCustom, calls=%fused_computation.3 | custom fusion | bytes 4198400 | tf_op jit(solution)/shard_map/jit(_take)/gather | solution.py:68
  158.6 3.3 copy.48
  163.0 2.5 fusion.55
  165.5 1.9 fusion.47
  167.5 3.2 collective-permute-start
  173.6 2.5 fusion.48
  182.3 3.1 collective-permute-done.1
  185.4 5.6 %collective-permute-start.2 = (f32[4,129,128]{2,1,0:T(8,128)S(1)}, f32[4,129,128]{2,1,0:T(8,128)S(1)}, u32[]{:S(2)}, u32[]{:S(2)}) collective-permute-start(f32[4,129,128]{2,1,0:T(8,128)S(1)} %select_add_fusion.6), channel_id=1, source_target_pairs={{0,16},{4,20},{8,24},{12,28},{16,32},{20,36},{24,40},{28,44},{32,4... | collective-permute-start | bytes 792584 | tf_op jit(solution)/shard_map/ppermute | solution.py:113
  192.6 3.8 collective-permute-done.2
  196.4 6.2 %collective-permute-start.3 = (f32[4,129,128]{2,1,0:T(8,128)S(1)}, f32[4,129,128]{2,1,0:T(8,128)S(1)}, u32[]{:S(2)}, u32[]{:S(2)}) collective-permute-start(f32[4,129,128]{2,1,0:T(8,128)S(1)} %select_add_fusion.5), channel_id=1, source_target_pairs={{0,32},{4,36},{8,40},{12,44},{16,48},{20,52},{24,56},{28,60},{32,6... | collective-permute-start | bytes 792584 | tf_op jit(solution)/shard_map/ppermute | solution.py:113
  206.9 4.4 %collective-permute-start.4 = (f32[4,129,128]{2,1,0:T(8,128)S(1)}, f32[4,129,128]{2,1,0:T(8,128)S(1)}, u32[]{:S(2)}, u32[]{:S(2)}) collective-permute-start(f32[4,129,128]{2,1,0:T(8,128)S(1)} %select_add_fusion.4), channel_id=1, source_target_pairs={{0,64},{4,68},{8,72},{12,76},{16,80},{20,84},{24,88},{28,92},{32,9... | collective-permute-start | bytes 792584 | tf_op jit(solution)/shard_map/ppermute | solution.py:113
  214.8 2.5 fusion.50
  217.3 3.1 fusion.30
  220.4 6.6 %collective-permute-start.5 = (f32[4,129,128]{2,1,0:T(8,128)S(1)}, f32[4,129,128]{2,1,0:T(8,128)S(1)}, u32[]{:S(2)}, u32[]{:S(2)}) collective-permute-start(f32[4,129,128]{2,1,0:T(8,128)S(1)} %pad_maximum_fusion.1), channel_id=1, source_target_pairs={{0,4},{4,8},{8,12},{12,16},{16,20},{20,24},{24,28},{28,32},{32,36}... | collective-permute-start | bytes 792584 | tf_op jit(solution)/shard_map/ppermute | solution.py:113
  235.4 6.2 %collective-permute-start.7 = (f32[4,129,128]{2,1,0:T(8,128)S(1)}, f32[4,129,128]{2,1,0:T(8,128)S(1)}, u32[]{:S(2)}, u32[]{:S(2)}) collective-permute-start(f32[4,129,128]{2,1,0:T(8,128)S(1)} %select_add_fusion.2), channel_id=1, source_target_pairs={{0,16},{4,20},{8,24},{12,28},{16,32},{20,36},{24,40},{28,44},{32,4... | collective-permute-start | bytes 792584 | tf_op jit(solution)/shard_map/ppermute | solution.py:113
  245.1 5.4 %gather_fusion.6 = bf16[1536,512]{1,0:T(8,128)(2,1)} fusion(bf16[1024,512]{1,0:T(8,128)(2,1)S(1)} %copy.61, s32[2048]{0:T(1024)S(1)} %pad_clamp_fusion), kind=kCustom, calls=%fused_computation.6 | custom fusion | bytes 3151872 | tf_op jit(solution)/shard_map/jit(_take)/gather | solution.py:135
  250.5 12.9 %all-to-all-start.3 = ((bf16[32,48,512]{2,1,0:T(8,128)(2,1)}), bf16[32,48,512]{2,1,0:T(8,128)(2,1)S(1)}, u32[]{:S(2)}, u32[]{:S(2)}) async-start(bf16[32,48,512]{2,1,0:T(8,128)(2,1)} %bitcast.39), calls=%async_computation.3 | async-start | bytes 3145728 | tf_op jit(solution)/shard_map/all_to_all | solution.py:136
  263.5 3.4 collective-permute-start.8
  269.8 16.9 %collective-permute-done.8 = f32[4,129,128]{2,1,0:T(8,128)S(1)} collective-permute-done((f32[4,129,128]{2,1,0:T(8,128)S(1)}, f32[4,129,128]{2,1,0:T(8,128)S(1)}, u32[]{:S(2)}, u32[]{:S(2)}) %collective-permute-start.8) | collective-permute-done | bytes 264224 | tf_op jit(solution)/shard_map/ppermute | solution.py:113
  286.7 5.5 %collective-permute-start.9 = (f32[4,129,128]{2,1,0:T(8,128)S(1)}, f32[4,129,128]{2,1,0:T(8,128)S(1)}, u32[]{:S(2)}, u32[]{:S(2)}) collective-permute-start(f32[4,129,128]{2,1,0:T(8,128)S(1)} %select_add_fusion), channel_id=1, source_target_pairs={{0,64},{4,68},{8,72},{12,76},{16,80},{20,84},{24,88},{28,92},{32,9... | collective-permute-start | bytes 792584 | tf_op jit(solution)/shard_map/ppermute | solution.py:113
  292.2 5.1 %gather_fusion.7 = bf16[1024,512]{1,0:T(8,128)(2,1)} fusion(bf16[1536,512]{1,0:T(8,128)(2,1)S(1)} %bitcast.220, s32[1024]{0:T(1024)S(1)} %broadcast_clamp_fusion), kind=kCustom, calls=%fused_computation.7 | custom fusion | bytes 2101248 | tf_op jit(solution)/shard_map/jit(_take)/gather | solution.py:137
  300.3 2.5 fusion.43
  302.8 3.2 fusion.32
  306.5 4.8 %gather_fusion.8 = bf16[1536,512]{1,0:T(8,128)(2,1)S(1)} fusion(bf16[1024,512]{1,0:T(8,128)(2,1)S(1)} %copy.75, s32[2048]{0:T(1024)S(1)} %pad_clamp_fusion), kind=kCustom, calls=%fused_computation.8 | custom fusion | bytes 3151872 | tf_op jit(solution)/shard_map/jit(_take)/gather | solution.py:135
  311.4 29.8 %all_to_all.30 = bf16[32,48,512]{2,1,0:T(8,128)(2,1)S(1)} all-to-all(bf16[32,48,512]{2,1,0:T(8,128)(2,1)S(1)} %bitcast.235), channel_id=1, replica_groups=mesh['ctx'=32,'head'=4] {'ctx'}, dimensions={0} | all-to-all | bytes 3145728 | tf_op jit(solution)/shard_map/all_to_all | solution.py:136
  341.1 4.0 gather_fusion.9
  345.1 2.3 broadcast_in_dim.152
  347.4 5.3 %all-to-all-start.5 = ((bf16[4,1024,512]{2,1,0:T(8,128)(2,1)}), bf16[4,1024,512]{2,1,0:T(8,128)(2,1)}, u32[]{:S(2)}, u32[]{:S(2)}) async-start(bf16[4,1024,512]{2,1,0:T(8,128)(2,1)} %broadcast_in_dim.152), calls=%async_computation.5 | async-start | bytes 8388608 | tf_op jit(solution)/shard_map/all_to_all | solution.py:140
  352.6 6.1 %fusion.165 = (bf16[4,4,128,1024]{3,2,1,0:T(8,128)(2,1)}, bf16[4,4,128,1024]{3,2,1,0:T(8,128)(2,1)}) fusion(bf16[4,8,128,1024]{3,2,1,0:T(8,128)(2,1)} %bitcast.231), kind=kLoop, calls=%fused_computation.259 | loop fusion | bytes 16777216 | tf_op jit(solution)/shard_map/slice | solution.py:144
  358.7 9.9 %fusion.172 = f32[1024,1024]{1,0:T(8,128)} fusion(bf16[1024,2048]{1,0:T(8,128)(2,1)} %all-gather.3.cloned.1.call-done, bf16[2048,1024]{1,0:T(8,128)(2,1)} %bitcast.237), kind=kOutput, calls=%fused_computation.266 | convolution fusion | flops 4294967296 | bytes 12582912 | tf_op jit(solution)/shard_map/dot_general | solution.py:149
  368.6 33.9 %all-to-all-done.5 = bf16[4,1024,512]{2,1,0:T(8,128)(2,1)} async-done(((bf16[4,1024,512]{2,1,0:T(8,128)(2,1)}), bf16[4,1024,512]{2,1,0:T(8,128)(2,1)}, u32[]{:S(2)}, u32[]{:S(2)}) %all-to-all-start.5) | async-done | bytes 4194336 | tf_op jit(solution)/shard_map/all_to_all | solution.py:140
  402.5 10.6 %fusion.2 = bf16[1024,1024]{1,0:T(8,128)(2,1)} fusion(f32[1024,1024]{1,0:T(8,128)} %fusion.172, bf16[4,1024,512]{2,1,0:T(8,128)(2,1)} %all-to-all-done.5, bf16[4,512,1024]{2,1,0:T(8,128)(2,1)} %bitcast.236), kind=kOutput, calls=%fused_computation.27 | convolution fusion | flops 4297064448 | bytes 14680064 | tf_op jit(solution)/shard_map/hrc,hcd->rd/dot_general | solution.py:141
  (165 shorter events, 45.9 us)
Async XLA Ops:
  6.5 2.5 copy-start
  14.8 8.8 %copy-start.2 = (bf16[1024,1024]{1,0:T(8,128)(2,1)S(1)}, bf16[1024,1024]{1,0:T(8,128)(2,1)}, u32[]{:S(2)}) copy-start(bf16[1024,1024]{1,0:T(8,128)(2,1)} %param.8) | copy-start | bytes 6291460
  14.8 48.6 %all-to-all-start.2 = ((bf16[32,48,1024]{2,1,0:T(8,128)(2,1)}), bf16[32,48,1024]{2,1,0:T(8,128)(2,1)}, u32[]{:S(2)}, u32[]{:S(2)}) async-start(bf16[32,48,1024]{2,1,0:T(8,128)(2,1)} %bitcast.228), calls=%async_computation.2 | async-start | bytes 6291456 | tf_op jit(solution)/shard_map/all_to_all | solution.py:67
  29.4 39.1 %copy-start.31 = (s32[32]{0:T(128)S(1)}, s32[32]{0:T(128)}, u32[]{:S(2)}) copy-start(s32[32]{0:T(128)} %param.11) | copy-start | bytes 388
  29.4 42.4 %copy-start.3 = (bf16[1024,1024]{1,0:T(8,128)(2,1)S(1)}, bf16[1024,1024]{1,0:T(8,128)(2,1)}, u32[]{:S(2)}) copy-start(bf16[1024,1024]{1,0:T(8,128)(2,1)} %param.9) | copy-start | bytes 6291460
  63.4 44.9 %all-to-all-start = ((bf16[32,48,1024]{2,1,0:T(8,128)(2,1)}), bf16[32,48,1024]{2,1,0:T(8,128)(2,1)}, u32[]{:S(2)}, u32[]{:S(2)}) async-start(bf16[32,48,1024]{2,1,0:T(8,128)(2,1)} %bitcast.227), calls=%async_computation | async-start | bytes 6291456 | tf_op jit(solution)/shard_map/all_to_all | solution.py:67
  71.8 5.8 %copy-start.30 = (f32[8]{0:T(128)S(1)}, f32[8]{0:T(128)}, u32[]{:S(2)}) copy-start(f32[8]{0:T(128)} %param.12) | copy-start | bytes 100
  108.3 45.0 %all-to-all-start.1 = ((bf16[32,48,1024]{2,1,0:T(8,128)(2,1)}), bf16[32,48,1024]{2,1,0:T(8,128)(2,1)S(1)}, u32[]{:S(2)}, u32[]{:S(2)}) async-start(bf16[32,48,1024]{2,1,0:T(8,128)(2,1)} %bitcast.226), calls=%async_computation.1 | async-start | bytes 6291456 | tf_op jit(solution)/shard_map/all_to_all | solution.py:67
  128.6 4.6 %copy-start.4 = (bf16[128,8,8,128]{3,2,1,0:T(8,128)(2,1)}, bf16[128,8,8,128]{3,2,1,0:T(8,128)(2,1)S(1)}, u32[]{:S(2)}) copy-start(bf16[128,8,8,128]{3,2,1,0:T(8,128)(2,1)S(1)} %copy.107) | copy-start | bytes 6291460
  158.6 4.4 %copy-start.7 = (bf16[1024,4,128]{2,1,0:T(4,128)(2,1)S(1)}, bf16[1024,4,128]{2,1,0:T(4,128)(2,1)}, u32[]{:S(2)}) copy-start(bf16[1024,4,128]{2,1,0:T(4,128)(2,1)} %get-tuple-element.138) | copy-start | bytes 3145732
  161.9 3.6 copy-start.6
  163.0 4.5 %copy-start.22 = (bf16[1024,1,128]{2,1,0:T(2,128)(2,1)S(1)}, bf16[1024,1,128]{2,1,0:T(2,128)(2,1)}, u32[]{:S(2)}) copy-start(bf16[1024,1,128]{2,1,0:T(2,128)(2,1)} %get-tuple-element.128) | copy-start | bytes 786436
  167.5 10.0 %collective-permute-start = (f32[4,129,128]{2,1,0:T(8,128)S(1)}, f32[4,129,128]{2,1,0:T(8,128)S(1)}, u32[]{:S(2)}, u32[]{:S(2)}) collective-permute-start(f32[4,129,128]{2,1,0:T(8,128)S(1)} %pad_maximum_fusion), channel_id=1, source_target_pairs={{0,4},{4,8},{8,12},{12,16},{16,20},{20,24},{24,28},{28,32},{32,36}... | collective-permute-start | bytes 792584 | tf_op jit(solution)/shard_map/ppermute | solution.py:113
  173.5 2.7 copy-start.16
  173.5 2.7 copy-start.15
  173.5 2.7 copy-start.14
  173.5 2.8 copy-start.13
  173.6 2.8 copy-start.12
  173.6 2.9 copy-start.21
  173.6 2.9 copy-start.20
  176.2 1.3 copy-start.17
  177.6 7.7 %collective-permute-start.1 = (f32[4,129,128]{2,1,0:T(8,128)S(1)}, f32[4,129,128]{2,1,0:T(8,128)S(1)}, u32[]{:S(2)}, u32[]{:S(2)}) collective-permute-start(f32[4,129,128]{2,1,0:T(8,128)S(1)} %select_add_fusion.7), channel_id=1, source_target_pairs={{0,8},{4,12},{8,16},{12,20},{16,24},{20,28},{24,32},{28,36},{32,40... | collective-permute-start | bytes 792584 | tf_op jit(solution)/shard_map/ppermute | solution.py:113
  180.7 10.2 %copy-start.5 = (bf16[128,8,8,128]{3,2,1,0:T(8,128)(2,1)S(1)}, bf16[128,8,8,128]{3,2,1,0:T(8,128)(2,1)}, u32[]{:S(2)}) copy-start(bf16[128,8,8,128]{3,2,1,0:T(8,128)(2,1)} %copy-done.4) | copy-start | bytes 6291460
  185.4 11.0 %collective-permute-start.2 = (f32[4,129,128]{2,1,0:T(8,128)S(1)}, f32[4,129,128]{2,1,0:T(8,128)S(1)}, u32[]{:S(2)}, u32[]{:S(2)}) collective-permute-start(f32[4,129,128]{2,1,0:T(8,128)S(1)} %select_add_fusion.6), channel_id=1, source_target_pairs={{0,16},{4,20},{8,24},{12,28},{16,32},{20,36},{24,40},{28,44},{32,4... | collective-permute-start | bytes 792584 | tf_op jit(solution)/shard_map/ppermute | solution.py:113
  196.4 10.4 %collective-permute-start.3 = (f32[4,129,128]{2,1,0:T(8,128)S(1)}, f32[4,129,128]{2,1,0:T(8,128)S(1)}, u32[]{:S(2)}, u32[]{:S(2)}) collective-permute-start(f32[4,129,128]{2,1,0:T(8,128)S(1)} %select_add_fusion.5), channel_id=1, source_target_pairs={{0,32},{4,36},{8,40},{12,44},{16,48},{20,52},{24,56},{28,60},{32,6... | collective-permute-start | bytes 792584 | tf_op jit(solution)/shard_map/ppermute | solution.py:113
  206.9 7.8 %collective-permute-start.4 = (f32[4,129,128]{2,1,0:T(8,128)S(1)}, f32[4,129,128]{2,1,0:T(8,128)S(1)}, u32[]{:S(2)}, u32[]{:S(2)}) collective-permute-start(f32[4,129,128]{2,1,0:T(8,128)S(1)} %select_add_fusion.4), channel_id=1, source_target_pairs={{0,64},{4,68},{8,72},{12,76},{16,80},{20,84},{24,88},{28,92},{32,9... | collective-permute-start | bytes 792584 | tf_op jit(solution)/shard_map/ppermute | solution.py:113
  220.4 10.1 %collective-permute-start.5 = (f32[4,129,128]{2,1,0:T(8,128)S(1)}, f32[4,129,128]{2,1,0:T(8,128)S(1)}, u32[]{:S(2)}, u32[]{:S(2)}) collective-permute-start(f32[4,129,128]{2,1,0:T(8,128)S(1)} %pad_maximum_fusion.1), channel_id=1, source_target_pairs={{0,4},{4,8},{8,12},{12,16},{16,20},{20,24},{24,28},{28,32},{32,36}... | collective-permute-start | bytes 792584 | tf_op jit(solution)/shard_map/ppermute | solution.py:113
  230.6 4.8 %collective-permute-start.6 = (f32[4,129,128]{2,1,0:T(8,128)S(1)}, f32[4,129,128]{2,1,0:T(8,128)S(1)}, u32[]{:S(2)}, u32[]{:S(2)}) collective-permute-start(f32[4,129,128]{2,1,0:T(8,128)S(1)} %select_add_fusion.3), channel_id=1, source_target_pairs={{0,8},{4,12},{8,16},{12,20},{16,24},{20,28},{24,32},{28,36},{32,40... | collective-permute-start | bytes 792584 | tf_op jit(solution)/shard_map/ppermute | solution.py:113
  233.3 8.2 %copy-start.9 = (bf16[1024,1,128]{2,1,0:T(2,128)(2,1)S(1)}, bf16[1024,1,128]{2,1,0:T(2,128)(2,1)}, u32[]{:S(2)}) copy-start(bf16[1024,1,128]{2,1,0:T(2,128)(2,1)} %get-tuple-element.129) | copy-start | bytes 786436
  233.3 9.0 %copy-start.8 = (bf16[1024,1,128]{2,1,0:T(2,128)(2,1)S(1)}, bf16[1024,1,128]{2,1,0:T(2,128)(2,1)}, u32[]{:S(2)}) copy-start(bf16[1024,1,128]{2,1,0:T(2,128)(2,1)} %get-tuple-element.130) | copy-start | bytes 786436
  233.3 9.7 %copy-start.11 = (bf16[1024,1,128]{2,1,0:T(2,128)(2,1)S(1)}, bf16[1024,1,128]{2,1,0:T(2,128)(2,1)}, u32[]{:S(2)}) copy-start(bf16[1024,1,128]{2,1,0:T(2,128)(2,1)} %get-tuple-element.121) | copy-start | bytes 786436
  233.4 10.4 %copy-start.10 = (bf16[1024,1,128]{2,1,0:T(2,128)(2,1)S(1)}, bf16[1024,1,128]{2,1,0:T(2,128)(2,1)}, u32[]{:S(2)}) copy-start(bf16[1024,1,128]{2,1,0:T(2,128)(2,1)} %get-tuple-element.122) | copy-start | bytes 786436
  235.4 28.1 %collective-permute-start.7 = (f32[4,129,128]{2,1,0:T(8,128)S(1)}, f32[4,129,128]{2,1,0:T(8,128)S(1)}, u32[]{:S(2)}, u32[]{:S(2)}) collective-permute-start(f32[4,129,128]{2,1,0:T(8,128)S(1)} %select_add_fusion.2), channel_id=1, source_target_pairs={{0,16},{4,20},{8,24},{12,28},{16,32},{20,36},{24,40},{28,44},{32,4... | collective-permute-start | bytes 792584 | tf_op jit(solution)/shard_map/ppermute | solution.py:113
  245.1 21.9 %copy-start.28 = (bf16[1024,1,128]{2,0,1:T(8,128)(2,1)S(1)}, bf16[1024,1,128]{2,0,1:T(8,128)(2,1)}, u32[]{:S(2)}) copy-start(bf16[1024,1,128]{2,0,1:T(8,128)(2,1)} %copy.101) | copy-start | bytes 786436
  245.1 21.9 %copy-start.29 = (bf16[1024,1,128]{2,0,1:T(8,128)(2,1)S(1)}, bf16[1024,1,128]{2,0,1:T(8,128)(2,1)}, u32[]{:S(2)}) copy-start(bf16[1024,1,128]{2,0,1:T(8,128)(2,1)} %copy.102) | copy-start | bytes 786436
  250.5 41.7 %all-to-all-start.3 = ((bf16[32,48,512]{2,1,0:T(8,128)(2,1)}), bf16[32,48,512]{2,1,0:T(8,128)(2,1)S(1)}, u32[]{:S(2)}, u32[]{:S(2)}) async-start(bf16[32,48,512]{2,1,0:T(8,128)(2,1)} %bitcast.39), calls=%async_computation.3 | async-start | bytes 3145728 | tf_op jit(solution)/shard_map/all_to_all | solution.py:136
  263.4 95.3 %all-gather.3.cloned.1.call-start = ((), (), s32[]{:S(2)}) async-start(), calls=%async_computation.6 | async-start | bytes 5242880 | tf_op jit(solution)/shard_map/all_gather | solution.py:148
  263.5 4.7 %copy-start.25 = (bf16[1024,1,128]{0,2,1:T(8,128)(2,1)S(1)}, bf16[1024,1,128]{0,2,1:T(8,128)(2,1)}, u32[]{:S(2)}) copy-start(bf16[1024,1,128]{0,2,1:T(8,128)(2,1)} %get-tuple-element.94) | copy-start | bytes 786436
  263.5 23.2 %collective-permute-start.8 = (f32[4,129,128]{2,1,0:T(8,128)S(1)}, f32[4,129,128]{2,1,0:T(8,128)S(1)}, u32[]{:S(2)}, u32[]{:S(2)}) collective-permute-start(f32[4,129,128]{2,1,0:T(8,128)S(1)} %select_add_fusion.1), channel_id=1, source_target_pairs={{0,32},{4,36},{8,40},{12,44},{16,48},{20,52},{24,56},{28,60},{32,6... | collective-permute-start | bytes 792584 | tf_op jit(solution)/shard_map/ppermute | solution.py:113
  286.7 13.5 %collective-permute-start.9 = (f32[4,129,128]{2,1,0:T(8,128)S(1)}, f32[4,129,128]{2,1,0:T(8,128)S(1)}, u32[]{:S(2)}, u32[]{:S(2)}) collective-permute-start(f32[4,129,128]{2,1,0:T(8,128)S(1)} %select_add_fusion), channel_id=1, source_target_pairs={{0,64},{4,68},{8,72},{12,76},{16,80},{20,84},{24,88},{28,92},{32,9... | collective-permute-start | bytes 792584 | tf_op jit(solution)/shard_map/ppermute | solution.py:113
  292.2 5.1 %copy-start.26 = (bf16[1024,1,128]{2,0,1:T(8,128)(2,1)S(1)}, bf16[1024,1,128]{2,0,1:T(8,128)(2,1)}, u32[]{:S(2)}) copy-start(bf16[1024,1,128]{2,0,1:T(8,128)(2,1)} %copy.103) | copy-start | bytes 786436
  292.2 5.1 %copy-start.27 = (bf16[1024,1,128]{2,0,1:T(8,128)(2,1)S(1)}, bf16[1024,1,128]{2,0,1:T(8,128)(2,1)}, u32[]{:S(2)}) copy-start(bf16[1024,1,128]{2,0,1:T(8,128)(2,1)} %copy.104) | copy-start | bytes 786436
  298.6 1.6 copy-start.23
  300.2 2.6 copy-start.32
  300.2 2.6 copy-start.33
  300.2 2.6 copy-start.34
  347.4 55.2 %all-to-all-start.5 = ((bf16[4,1024,512]{2,1,0:T(8,128)(2,1)}), bf16[4,1024,512]{2,1,0:T(8,128)(2,1)}, u32[]{:S(2)}, u32[]{:S(2)}) async-start(bf16[4,1024,512]{2,1,0:T(8,128)(2,1)} %broadcast_in_dim.152), calls=%async_computation.5 | async-start | bytes 8388608 | tf_op jit(solution)/shard_map/all_to_all | solution.py:140
  402.5 10.6 %copy-start.1 = (bf16[1024,1024]{1,0:T(8,128)(2,1)S(1)}, bf16[1024,1024]{1,0:T(8,128)(2,1)}, u32[]{:S(2)}) copy-start(bf16[1024,1024]{1,0:T(8,128)(2,1)} %param.7) | copy-start | bytes 6291460
  (3 other events, 3.5 us)
Sparse Core Ops, SparseCore 0:
  297.5 48.9 all-gather.2

commit v12 on v5

--- a/solution.py
+++ b/solution.py
@@ -135,10 +135,11 @@
         outgoing = jnp.take(combined, pslot, axis=0, mode="clip").reshape(n, cap, group_width)
         incoming = lax.all_to_all(outgoing, "ctx", 0, 0, tiled=True).reshape(slots, group_width)
         rows = jnp.take(incoming, send_slot, axis=0, mode="clip")
-        gathered = lax.all_gather(rows, "head", axis=1, tiled=True)
-        part = jnp.dot(
+        gathered = lax.all_gather(rows, "head", axis=0, tiled=False)
+        part = jnp.einsum(
+            "hrc,hcd->rd",
             gathered,
-            weight_rows[:, first:last].reshape(head_count * group_width, out_cols),
+            weight_rows[:, first:last].reshape(head_count, group_width, out_cols),
             preferred_element_type=f32,
         )
         return part, combined

time: 419 us -> 419 us (level)
  no operation moved by 1% of the time
where the time goes in v12:
time: 419 us; the launch traced here: 412 us
  waiting for transfers between devices  119 us (28%)
  local copies, waits for them, and re-layouts  95.5 us (23%)
  starting transfers between devices  77.7 us (19%)
  matrix products  57.4 us (14%)
  blocking collectives  31.7 us (8%)
  between operations  18.3 us (4%)
  other arithmetic  12.7 us (3%)
    all_to_all x3, waiting for transfers between devices, dispatch(): got = lax.all_to_all(buffer, 'ctx', 0, 0, tiled=True).reshape(slots, width)  64.5 us
    ppermute x10, starting transfers between devices, one_group(): got = lax.ppermute(total, 'ctx', perm)  50 us
    all_to_all x1, blocking collectives, one_group(): lax.all_to_all(outgoing, 'ctx', 0, 0, tiled=True)  31.7 us
    all_gather x2, waiting for transfers between devices, one_group(): gathered = lax.all_gather(rows, 'head', axis=0, tiled=False)  30.2 us
    gather x4, local copies, waits for them, and re-layouts, dispatch(): return jnp.take(got, tok_slot, axis=0, mode='clip').reshape(seg, heads, dh)  25.3 us
    ppermute x10, waiting for transfers between devices, one_group(): got = lax.ppermute(total, 'ctx', perm)  24 us
    dot_general x2, matrix products, one_group(): jnp.einsum('hrc,hcd->rd', gathered, weight_rows[:, first:last].reshape(he...  21.2 us
    all_to_all x3, starting transfers between devices, dispatch(): got = lax.all_to_all(buffer, 'ctx', 0, 0, tiled=True).reshape(slots, width)  19.1 us
  transfers between devices with their start and end apart: 16, of which 11 were waited for; matrix products, arithmetic and copies ran while one was open for 31% of the time, Pallas kernels for 0%

profile of v12, /device:TPU:1, one launch (start us, length us, event | category | flops | bytes accessed | tf_op | source)
XLA Modules:
  0.0 412.1 jit_solution(15766064702177981891)
XLA Ops:
  9.0 5.8 %gather_fusion.4 = bf16[1536,1024]{1,0:T(8,128)(2,1)} fusion(bf16[1024,1024]{1,0:T(8,128)(2,1)S(1)} %copy-done, s32[2048]{0:T(1024)S(1)} %pad_clamp_fusion.1), kind=kCustom, calls=%fused_computation.4 | custom fusion | bytes 6297600 | tf_op jit(solution)/shard_map/jit(_take)/gather | solution.py:66
  14.8 8.8 %all-to-all-start.2 = ((bf16[32,48,1024]{2,1,0:T(8,128)(2,1)}), bf16[32,48,1024]{2,1,0:T(8,128)(2,1)}, u32[]{:S(2)}, u32[]{:S(2)}) async-start(bf16[32,48,1024]{2,1,0:T(8,128)(2,1)} %bitcast.232), calls=%async_computation.2 | async-start | bytes 6291456 | tf_op jit(solution)/shard_map/all_to_all | solution.py:67
  23.6 5.8 %gather_fusion = bf16[1536,1024]{1,0:T(8,128)(2,1)} fusion(bf16[1024,1024]{1,0:T(8,128)(2,1)S(1)} %copy-done.2, s32[2048]{0:T(1024)S(1)} %pad_clamp_fusion.1), kind=kCustom, calls=%fused_computation | custom fusion | bytes 6297600 | tf_op jit(solution)/shard_map/jit(_take)/gather | solution.py:66
  29.4 34.0 %all-to-all-done.2 = bf16[32,48,1024]{2,1,0:T(8,128)(2,1)} async-done(((bf16[32,48,1024]{2,1,0:T(8,128)(2,1)}), bf16[32,48,1024]{2,1,0:T(8,128)(2,1)}, u32[]{:S(2)}, u32[]{:S(2)}) %all-to-all-start.2) | async-done | bytes 3145760 | tf_op jit(solution)/shard_map/all_to_all | solution.py:67
  63.4 5.0 %all-to-all-start = ((bf16[32,48,1024]{2,1,0:T(8,128)(2,1)}), bf16[32,48,1024]{2,1,0:T(8,128)(2,1)}, u32[]{:S(2)}, u32[]{:S(2)}) async-start(bf16[32,48,1024]{2,1,0:T(8,128)(2,1)} %bitcast.230), calls=%async_computation | async-start | bytes 6291456 | tf_op jit(solution)/shard_map/all_to_all | solution.py:67
  76.6 5.8 %gather_fusion.2 = bf16[1536,1024]{1,0:T(8,128)(2,1)} fusion(bf16[1024,1024]{1,0:T(8,128)(2,1)S(1)} %copy-done.3, s32[2048]{0:T(1024)S(1)} %pad_clamp_fusion.1), kind=kCustom, calls=%fused_computation.2 | custom fusion | bytes 6297600 | tf_op jit(solution)/shard_map/jit(_take)/gather | solution.py:66
  84.3 24.0 %all-to-all-done = bf16[32,48,1024]{2,1,0:T(8,128)(2,1)} async-done(((bf16[32,48,1024]{2,1,0:T(8,128)(2,1)}), bf16[32,48,1024]{2,1,0:T(8,128)(2,1)}, u32[]{:S(2)}, u32[]{:S(2)}) %all-to-all-start) | async-done | bytes 3145760 | tf_op jit(solution)/shard_map/all_to_all | solution.py:67
  108.3 5.3 %all-to-all-start.1 = ((bf16[32,48,1024]{2,1,0:T(8,128)(2,1)}), bf16[32,48,1024]{2,1,0:T(8,128)(2,1)S(1)}, u32[]{:S(2)}, u32[]{:S(2)}) async-start(bf16[32,48,1024]{2,1,0:T(8,128)(2,1)} %bitcast.231), calls=%async_computation.1 | async-start | bytes 6291456 | tf_op jit(solution)/shard_map/all_to_all | solution.py:67
  113.6 8.3 %gather_fusion.5 = bf16[1024,1024]{1,0:T(8,128)(2,1)} fusion(bf16[1536,1024]{1,0:T(8,128)(2,1)} %bitcast.10, s32[1024]{0:T(1024)S(1)} %broadcast_clamp_fusion.1), kind=kCustom, calls=%fused_computation.5 | custom fusion | bytes 4198400 | tf_op jit(solution)/shard_map/jit(_take)/gather | solution.py:68
  121.9 2.2 copy.107
  124.1 4.6 %fusion.169 = (bf16[1024,1,128]{2,1,0:T(2,128)(2,1)}, bf16[1024,1,128]{2,1,0:T(2,128)(2,1)}, bf16[1024,1,128]{2,1,0:T(2,128)(2,1)}, bf16[1024,1,128]{2,1,0:T(2,1...) fusion(bf16[1024,8,128]{2,1,0:T(8,128)(2,1)S(1)} %bitcast.226), kind=kLoop, calls=%fused_computation.263 | loop fusion | bytes 4194304 | tf_op jit(solution)/shard_map/slice | solution.py:110
  129.5 8.3 %gather_fusion.1 = bf16[1024,1024]{1,0:T(8,128)(2,1)} fusion(bf16[1536,1024]{1,0:T(8,128)(2,1)} %bitcast.4, s32[1024]{0:T(1024)S(1)} %broadcast_clamp_fusion.1), kind=kCustom, calls=%fused_computation.1 | custom fusion | bytes 4198400 | tf_op jit(solution)/shard_map/jit(_take)/gather | solution.py:68
  137.8 2.2 copy.106
  140.0 2.0 fusion.170
  142.0 4.7 %fusion.168 = (bf16[1024,1,128]{2,1,0:T(2,128)(2,1)}, bf16[1024,1,128]{2,1,0:T(2,128)(2,1)}, bf16[1024,1,128]{2,1,0:T(2,128)(2,1)}, bf16[1024,1,128]{2,1,0:T(2,1...) fusion(bf16[1024,8,128]{2,1,0:T(8,128)(2,1)S(1)} %bitcast.229), kind=kLoop, calls=%fused_computation.262 | loop fusion | bytes 4194304 | tf_op jit(solution)/shard_map/slice | solution.py:110
  146.7 6.5 %all-to-all-done.1 = bf16[32,48,1024]{2,1,0:T(8,128)(2,1)S(1)} async-done(((bf16[32,48,1024]{2,1,0:T(8,128)(2,1)}), bf16[32,48,1024]{2,1,0:T(8,128)(2,1)S(1)}, u32[]{:S(2)}, u32[]{:S(2)}) %all-to-all-start.1) | async-done | bytes 3145760 | tf_op jit(solution)/shard_map/all_to_all | solution.py:67
  153.2 5.3 %gather_fusion.3 = bf16[1024,1024]{1,0:T(8,128)(2,1)} fusion(bf16[1536,1024]{1,0:T(8,128)(2,1)S(1)} %bitcast.223, s32[1024]{0:T(1024)S(1)} %broadcast_clamp_fusion.1), kind=kCustom, calls=%fused_computation.3 | custom fusion | bytes 4198400 | tf_op jit(solution)/shard_map/jit(_take)/gather | solution.py:68
  158.6 3.3 copy.48
  162.9 2.5 fusion.55
  165.5 1.9 fusion.47
  167.5 3.2 collective-permute-start
  173.5 2.5 fusion.48
  184.1 3.1 collective-permute-done.1
  187.3 5.6 %collective-permute-start.2 = (f32[4,129,128]{2,1,0:T(8,128)S(1)}, f32[4,129,128]{2,1,0:T(8,128)S(1)}, u32[]{:S(2)}, u32[]{:S(2)}) collective-permute-start(f32[4,129,128]{2,1,0:T(8,128)S(1)} %select_add_fusion.6), channel_id=1, source_target_pairs={{0,16},{4,20},{8,24},{12,28},{16,32},{20,36},{24,40},{28,44},{32,4... | collective-permute-start | bytes 792584 | tf_op jit(solution)/shard_map/ppermute | solution.py:113
  194.5 3.8 collective-permute-done.2
  198.3 6.5 %collective-permute-start.3 = (f32[4,129,128]{2,1,0:T(8,128)S(1)}, f32[4,129,128]{2,1,0:T(8,128)S(1)}, u32[]{:S(2)}, u32[]{:S(2)}) collective-permute-start(f32[4,129,128]{2,1,0:T(8,128)S(1)} %select_add_fusion.5), channel_id=1, source_target_pairs={{0,32},{4,36},{8,40},{12,44},{16,48},{20,52},{24,56},{28,60},{32,6... | collective-permute-start | bytes 792584 | tf_op jit(solution)/shard_map/ppermute | solution.py:113
  207.6 1.9 collective-permute-done.3
  209.6 4.2 %collective-permute-start.4 = (f32[4,129,128]{2,1,0:T(8,128)S(1)}, f32[4,129,128]{2,1,0:T(8,128)S(1)}, u32[]{:S(2)}, u32[]{:S(2)}) collective-permute-start(f32[4,129,128]{2,1,0:T(8,128)S(1)} %select_add_fusion.4), channel_id=1, source_target_pairs={{0,64},{4,68},{8,72},{12,76},{16,80},{20,84},{24,88},{28,92},{32,9... | collective-permute-start | bytes 792584 | tf_op jit(solution)/shard_map/ppermute | solution.py:113
  217.4 2.5 fusion.50
  219.9 3.1 fusion.30
  223.6 6.1 %collective-permute-start.5 = (f32[4,129,128]{2,1,0:T(8,128)S(1)}, f32[4,129,128]{2,1,0:T(8,128)S(1)}, u32[]{:S(2)}, u32[]{:S(2)}) collective-permute-start(f32[4,129,128]{2,1,0:T(8,128)S(1)} %pad_maximum_fusion.1), channel_id=1, source_target_pairs={{0,4},{4,8},{8,12},{12,16},{16,20},{20,24},{24,28},{28,32},{32,36}... | collective-permute-start | bytes 792584 | tf_op jit(solution)/shard_map/ppermute | solution.py:113
  229.8 5.4 %gather_fusion.6 = bf16[1536,512]{1,0:T(8,128)(2,1)} fusion(bf16[1024,512]{1,0:T(8,128)(2,1)S(1)} %copy.61, s32[2048]{0:T(1024)S(1)} %pad_clamp_fusion), kind=kCustom, calls=%fused_computation.6 | custom fusion | bytes 3151872 | tf_op jit(solution)/shard_map/jit(_take)/gather | solution.py:135
  235.2 8.2 %all-to-all-start.3 = ((bf16[32,48,512]{2,1,0:T(8,128)(2,1)}), bf16[32,48,512]{2,1,0:T(8,128)(2,1)S(1)}, u32[]{:S(2)}, u32[]{:S(2)}) async-start(bf16[32,48,512]{2,1,0:T(8,128)(2,1)} %bitcast.39), calls=%async_computation.3 | async-start | bytes 3145728 | tf_op jit(solution)/shard_map/all_to_all | solution.py:136
  246.6 3.4 collective-permute-start.6
  252.9 13.7 %collective-permute-done.6 = f32[4,129,128]{2,1,0:T(8,128)S(1)} collective-permute-done((f32[4,129,128]{2,1,0:T(8,128)S(1)}, f32[4,129,128]{2,1,0:T(8,128)S(1)}, u32[]{:S(2)}, u32[]{:S(2)}) %collective-permute-start.6) | collective-permute-done | bytes 264224 | tf_op jit(solution)/shard_map/ppermute | solution.py:113
  266.6 5.8 %collective-permute-start.7 = (f32[4,129,128]{2,1,0:T(8,128)S(1)}, f32[4,129,128]{2,1,0:T(8,128)S(1)}, u32[]{:S(2)}, u32[]{:S(2)}) collective-permute-start(f32[4,129,128]{2,1,0:T(8,128)S(1)} %select_add_fusion.2), channel_id=1, source_target_pairs={{0,16},{4,20},{8,24},{12,28},{16,32},{20,36},{24,40},{28,44},{32,4... | collective-permute-start | bytes 792584 | tf_op jit(solution)/shard_map/ppermute | solution.py:113
  273.4 5.1 %gather_fusion.7 = bf16[1024,512]{1,0:T(8,128)(2,1)} fusion(bf16[1536,512]{1,0:T(8,128)(2,1)S(1)} %bitcast.224, s32[1024]{0:T(1024)S(1)} %broadcast_clamp_fusion), kind=kCustom, calls=%fused_computation.7 | custom fusion | bytes 2101248 | tf_op jit(solution)/shard_map/jit(_take)/gather | solution.py:137
  278.6 6.1 %collective-permute-start.8 = (f32[4,129,128]{2,1,0:T(8,128)S(1)}, f32[4,129,128]{2,1,0:T(8,128)S(1)}, u32[]{:S(2)}, u32[]{:S(2)}) collective-permute-start(f32[4,129,128]{2,1,0:T(8,128)S(1)} %select_add_fusion.1), channel_id=1, source_target_pairs={{0,32},{4,36},{8,40},{12,44},{16,48},{20,52},{24,56},{28,60},{32,6... | collective-permute-start | bytes 792584 | tf_op jit(solution)/shard_map/ppermute | solution.py:113
  288.8 7.2 %collective-permute-start.9 = (f32[4,129,128]{2,1,0:T(8,128)S(1)}, f32[4,129,128]{2,1,0:T(8,128)S(1)}, u32[]{:S(2)}, u32[]{:S(2)}) collective-permute-start(f32[4,129,128]{2,1,0:T(8,128)S(1)} %select_add_fusion), channel_id=1, source_target_pairs={{0,64},{4,68},{8,72},{12,76},{16,80},{20,84},{24,88},{28,92},{32,9... | collective-permute-start | bytes 792584 | tf_op jit(solution)/shard_map/ppermute | solution.py:113
  299.3 2.5 fusion.43
  301.8 3.2 fusion.32
  305.5 4.8 %gather_fusion.8 = bf16[1536,512]{1,0:T(8,128)(2,1)S(1)} fusion(bf16[1024,512]{1,0:T(8,128)(2,1)S(1)} %copy.75, s32[2048]{0:T(1024)S(1)} %pad_clamp_fusion), kind=kCustom, calls=%fused_computation.8 | custom fusion | bytes 3151872 | tf_op jit(solution)/shard_map/jit(_take)/gather | solution.py:135
  310.4 31.7 %all_to_all.25 = bf16[32,48,512]{2,1,0:T(8,128)(2,1)S(1)} all-to-all(bf16[32,48,512]{2,1,0:T(8,128)(2,1)S(1)} %bitcast.239), channel_id=1, replica_groups=mesh['ctx'=32,'head'=4] {'ctx'}, dimensions={0} | all-to-all | bytes 3145728 | tf_op jit(solution)/shard_map/all_to_all | solution.py:136
  342.1 5.1 %gather_fusion.9 = bf16[1024,512]{1,0:T(8,128)(2,1)} fusion(bf16[1536,512]{1,0:T(8,128)(2,1)S(1)} %bitcast.225, s32[1024]{0:T(1024)S(1)} %broadcast_clamp_fusion), kind=kCustom, calls=%fused_computation.9 | custom fusion | bytes 2101248 | tf_op jit(solution)/shard_map/jit(_take)/gather | solution.py:137
  347.2 6.1 %fusion.165 = (bf16[4,4,128,1024]{3,2,1,0:T(8,128)(2,1)}, bf16[4,4,128,1024]{3,2,1,0:T(8,128)(2,1)}) fusion(bf16[4,8,128,1024]{3,2,1,0:T(8,128)(2,1)} %bitcast.235), kind=kLoop, calls=%fused_computation.259 | loop fusion | bytes 16777216 | tf_op jit(solution)/shard_map/slice | solution.py:142
  353.3 10.6 %fusion.172 = f32[1024,1024,1]{1,0,2:T(8,128)} fusion(bf16[4,1024,512]{2,1,0:T(8,128)(2,1)} %bitcast.252, bf16[4,512,1024]{2,1,0:T(8,128)(2,1)} %bitcast.241), kind=kOutput, calls=%fused_computation.266 | convolution fusion | flops 4294967296 | bytes 12582912 | tf_op jit(solution)/shard_map/hrc,hcd->rd/dot_general | solution.py:139
  363.9 30.2 %all-gather.7.cloned.1.call-done = bf16[4096,512]{1,0:T(8,128)(2,1)} async-done(((bf16[1024,512]{1,0:T(8,128)(2,1)}), bf16[4096,512]{1,0:T(8,128)(2,1)}) %all-gather.7.cloned.1.call-update) | async-done | bytes 4194320 | tf_op jit(solution)/shard_map/all_gather | solution.py:138
  394.1 10.6 %fusion.2 = bf16[1024,1024]{1,0:T(8,128)(2,1)} fusion(f32[1024,1024,1]{1,0,2:T(8,128)} %fusion.172, bf16[4,1024,512]{2,1,0:T(8,128)(2,1)} %bitcast.253, bf16[4,512,1024]{2,1,0:T(8,128)(2,1)} %bitcast.240), kind=kOutput, calls=%fused_computation.27 | convolution fusion | flops 4297064448 | bytes 14680064 | tf_op jit(solution)/shard_map/hrc,hcd->rd/dot_general | solution.py:139
  (173 shorter events, 44.9 us)
Async XLA Ops:
  14.8 8.8 %copy-start.2 = (bf16[1024,1024]{1,0:T(8,128)(2,1)S(1)}, bf16[1024,1024]{1,0:T(8,128)(2,1)}, u32[]{:S(2)}) copy-start(bf16[1024,1024]{1,0:T(8,128)(2,1)} %param.8) | copy-start | bytes 6291460
  14.8 48.6 %all-to-all-start.2 = ((bf16[32,48,1024]{2,1,0:T(8,128)(2,1)}), bf16[32,48,1024]{2,1,0:T(8,128)(2,1)}, u32[]{:S(2)}, u32[]{:S(2)}) async-start(bf16[32,48,1024]{2,1,0:T(8,128)(2,1)} %bitcast.232), calls=%async_computation.2 | async-start | bytes 6291456 | tf_op jit(solution)/shard_map/all_to_all | solution.py:67
  29.4 39.0 %copy-start.35 = (s32[32]{0:T(128)S(1)}, s32[32]{0:T(128)}, u32[]{:S(2)}) copy-start(s32[32]{0:T(128)} %param.11) | copy-start | bytes 388
  29.4 47.1 %copy-start.3 = (bf16[1024,1024]{1,0:T(8,128)(2,1)S(1)}, bf16[1024,1024]{1,0:T(8,128)(2,1)}, u32[]{:S(2)}) copy-start(bf16[1024,1024]{1,0:T(8,128)(2,1)} %param.9) | copy-start | bytes 6291460
  63.4 44.9 %all-to-all-start = ((bf16[32,48,1024]{2,1,0:T(8,128)(2,1)}), bf16[32,48,1024]{2,1,0:T(8,128)(2,1)}, u32[]{:S(2)}, u32[]{:S(2)}) async-start(bf16[32,48,1024]{2,1,0:T(8,128)(2,1)} %bitcast.230), calls=%async_computation | async-start | bytes 6291456 | tf_op jit(solution)/shard_map/all_to_all | solution.py:67
  76.5 5.8 %copy-start.36 = (f32[8]{0:T(128)S(1)}, f32[8]{0:T(128)}, u32[]{:S(2)}) copy-start(f32[8]{0:T(128)} %param.12) | copy-start | bytes 100
  108.3 45.0 %all-to-all-start.1 = ((bf16[32,48,1024]{2,1,0:T(8,128)(2,1)}), bf16[32,48,1024]{2,1,0:T(8,128)(2,1)S(1)}, u32[]{:S(2)}, u32[]{:S(2)}) async-start(bf16[32,48,1024]{2,1,0:T(8,128)(2,1)} %bitcast.231), calls=%async_computation.1 | async-start | bytes 6291456 | tf_op jit(solution)/shard_map/all_to_all | solution.py:67
  124.1 4.6 %copy-start.4 = (bf16[128,8,8,128]{3,2,1,0:T(8,128)(2,1)}, bf16[128,8,8,128]{3,2,1,0:T(8,128)(2,1)S(1)}, u32[]{:S(2)}) copy-start(bf16[128,8,8,128]{3,2,1,0:T(8,128)(2,1)S(1)} %copy.107) | copy-start | bytes 6291460
  158.6 4.4 %copy-start.7 = (bf16[1024,4,128]{2,1,0:T(4,128)(2,1)S(1)}, bf16[1024,4,128]{2,1,0:T(4,128)(2,1)}, u32[]{:S(2)}) copy-start(bf16[1024,4,128]{2,1,0:T(4,128)(2,1)} %get-tuple-element.138) | copy-start | bytes 3145732
  161.9 3.6 copy-start.6
  162.9 4.5 %copy-start.22 = (bf16[1024,1,128]{2,1,0:T(2,128)(2,1)S(1)}, bf16[1024,1,128]{2,1,0:T(2,128)(2,1)}, u32[]{:S(2)}) copy-start(bf16[1024,1,128]{2,1,0:T(2,128)(2,1)} %get-tuple-element.128) | copy-start | bytes 786436
  162.9 7.8 %copy-start.31 = (bf16[1024,1,128]{2,0,1:T(8,128)(2,1)S(1)}, bf16[1024,1,128]{2,0,1:T(8,128)(2,1)}, u32[]{:S(2)}) copy-start(bf16[1024,1,128]{2,0,1:T(8,128)(2,1)} %copy.86) | copy-start | bytes 786436
  167.5 12.0 %collective-permute-start = (f32[4,129,128]{2,1,0:T(8,128)S(1)}, f32[4,129,128]{2,1,0:T(8,128)S(1)}, u32[]{:S(2)}, u32[]{:S(2)}) collective-permute-start(f32[4,129,128]{2,1,0:T(8,128)S(1)} %pad_maximum_fusion), channel_id=1, source_target_pairs={{0,4},{4,8},{8,12},{12,16},{16,20},{20,24},{24,28},{28,32},{32,36}... | collective-permute-start | bytes 792584 | tf_op jit(solution)/shard_map/ppermute | solution.py:113
  173.5 3.4 copy-start.15
  173.5 4.1 %copy-start.14 = (bf16[1024,1,128]{2,1,0:T(2,128)(2,1)S(1)}, bf16[1024,1,128]{2,1,0:T(2,128)(2,1)}, u32[]{:S(2)}) copy-start(bf16[1024,1,128]{2,1,0:T(2,128)(2,1)} %get-tuple-element.133) | copy-start | bytes 786436
  173.5 4.2 %copy-start.13 = (bf16[1024,1,128]{2,1,0:T(2,128)(2,1)S(1)}, bf16[1024,1,128]{2,1,0:T(2,128)(2,1)}, u32[]{:S(2)}) copy-start(bf16[1024,1,128]{2,1,0:T(2,128)(2,1)} %get-tuple-element.134) | copy-start | bytes 786436
  173.5 4.2 %copy-start.12 = (bf16[1024,1,128]{2,1,0:T(2,128)(2,1)S(1)}, bf16[1024,1,128]{2,1,0:T(2,128)(2,1)}, u32[]{:S(2)}) copy-start(bf16[1024,1,128]{2,1,0:T(2,128)(2,1)} %get-tuple-element.135) | copy-start | bytes 786436
  173.5 4.2 %copy-start.21 = (bf16[1024,1,128]{2,1,0:T(2,128)(2,1)S(1)}, bf16[1024,1,128]{2,1,0:T(2,128)(2,1)}, u32[]{:S(2)}) copy-start(bf16[1024,1,128]{2,1,0:T(2,128)(2,1)} %get-tuple-element.123) | copy-start | bytes 786436
  173.5 5.0 %copy-start.20 = (bf16[1024,1,128]{2,1,0:T(2,128)(2,1)S(1)}, bf16[1024,1,128]{2,1,0:T(2,128)(2,1)}, u32[]{:S(2)}) copy-start(bf16[1024,1,128]{2,1,0:T(2,128)(2,1)} %get-tuple-element.124) | copy-start | bytes 786436
  176.1 3.2 copy-start.19
  176.1 3.2 copy-start.18
  176.1 3.2 copy-start.17
  179.5 7.7 %collective-permute-start.1 = (f32[4,129,128]{2,1,0:T(8,128)S(1)}, f32[4,129,128]{2,1,0:T(8,128)S(1)}, u32[]{:S(2)}, u32[]{:S(2)}) collective-permute-start(f32[4,129,128]{2,1,0:T(8,128)S(1)} %select_add_fusion.7), channel_id=1, source_target_pairs={{0,8},{4,12},{8,16},{12,20},{16,24},{20,28},{24,32},{28,36},{32,40... | collective-permute-start | bytes 792584 | tf_op jit(solution)/shard_map/ppermute | solution.py:113
  182.6 10.2 %copy-start.5 = (bf16[128,8,8,128]{3,2,1,0:T(8,128)(2,1)S(1)}, bf16[128,8,8,128]{3,2,1,0:T(8,128)(2,1)}, u32[]{:S(2)}) copy-start(bf16[128,8,8,128]{3,2,1,0:T(8,128)(2,1)} %copy-done.4) | copy-start | bytes 6291460
  187.3 11.0 %collective-permute-start.2 = (f32[4,129,128]{2,1,0:T(8,128)S(1)}, f32[4,129,128]{2,1,0:T(8,128)S(1)}, u32[]{:S(2)}, u32[]{:S(2)}) collective-permute-start(f32[4,129,128]{2,1,0:T(8,128)S(1)} %select_add_fusion.6), channel_id=1, source_target_pairs={{0,16},{4,20},{8,24},{12,28},{16,32},{20,36},{24,40},{28,44},{32,4... | collective-permute-start | bytes 792584 | tf_op jit(solution)/shard_map/ppermute | solution.py:113
  198.3 11.2 %collective-permute-start.3 = (f32[4,129,128]{2,1,0:T(8,128)S(1)}, f32[4,129,128]{2,1,0:T(8,128)S(1)}, u32[]{:S(2)}, u32[]{:S(2)}) collective-permute-start(f32[4,129,128]{2,1,0:T(8,128)S(1)} %select_add_fusion.5), channel_id=1, source_target_pairs={{0,32},{4,36},{8,40},{12,44},{16,48},{20,52},{24,56},{28,60},{32,6... | collective-permute-start | bytes 792584 | tf_op jit(solution)/shard_map/ppermute | solution.py:113
  209.6 7.7 %collective-permute-start.4 = (f32[4,129,128]{2,1,0:T(8,128)S(1)}, f32[4,129,128]{2,1,0:T(8,128)S(1)}, u32[]{:S(2)}, u32[]{:S(2)}) collective-permute-start(f32[4,129,128]{2,1,0:T(8,128)S(1)} %select_add_fusion.4), channel_id=1, source_target_pairs={{0,64},{4,68},{8,72},{12,76},{16,80},{20,84},{24,88},{28,92},{32,9... | collective-permute-start | bytes 792584 | tf_op jit(solution)/shard_map/ppermute | solution.py:113
  216.6 3.3 copy-start.33
  216.6 3.3 copy-start.34
  223.6 20.1 %copy-start.29 = (bf16[1024,1,128]{2,0,1:T(8,128)(2,1)S(1)}, bf16[1024,1,128]{2,0,1:T(8,128)(2,1)}, u32[]{:S(2)}) copy-start(bf16[1024,1,128]{2,0,1:T(8,128)(2,1)} %copy.97) | copy-start | bytes 786436
  223.6 20.1 %copy-start.30 = (bf16[1024,1,128]{2,0,1:T(8,128)(2,1)S(1)}, bf16[1024,1,128]{2,0,1:T(8,128)(2,1)}, u32[]{:S(2)}) copy-start(bf16[1024,1,128]{2,0,1:T(8,128)(2,1)} %copy.98) | copy-start | bytes 786436
  223.6 22.9 %collective-permute-start.5 = (f32[4,129,128]{2,1,0:T(8,128)S(1)}, f32[4,129,128]{2,1,0:T(8,128)S(1)}, u32[]{:S(2)}, u32[]{:S(2)}) collective-permute-start(f32[4,129,128]{2,1,0:T(8,128)S(1)} %pad_maximum_fusion.1), channel_id=1, source_target_pairs={{0,4},{4,8},{8,12},{12,16},{16,20},{20,24},{24,28},{28,32},{32,36}... | collective-permute-start | bytes 792584 | tf_op jit(solution)/shard_map/ppermute | solution.py:113
  235.2 38.2 %all-to-all-start.3 = ((bf16[32,48,512]{2,1,0:T(8,128)(2,1)}), bf16[32,48,512]{2,1,0:T(8,128)(2,1)S(1)}, u32[]{:S(2)}, u32[]{:S(2)}) async-start(bf16[32,48,512]{2,1,0:T(8,128)(2,1)} %bitcast.39), calls=%async_computation.3 | async-start | bytes 3145728 | tf_op jit(solution)/shard_map/all_to_all | solution.py:136
  243.4 109.9 %all-gather.5.cloned.1.call-start = ((), (), s32[]{:S(2)}) async-start(), calls=%async_computation.5 | async-start | bytes 5242880 | tf_op jit(solution)/shard_map/all_gather | solution.py:138
  244.9 5.1 %copy-start.27 = (bf16[1024,1,128]{2,0,1:T(8,128)(2,1)S(1)}, bf16[1024,1,128]{2,0,1:T(8,128)(2,1)}, u32[]{:S(2)}) copy-start(bf16[1024,1,128]{2,0,1:T(8,128)(2,1)} %copy.99) | copy-start | bytes 786436
  245.0 5.1 %copy-start.28 = (bf16[1024,1,128]{2,0,1:T(8,128)(2,1)S(1)}, bf16[1024,1,128]{2,0,1:T(8,128)(2,1)}, u32[]{:S(2)}) copy-start(bf16[1024,1,128]{2,0,1:T(8,128)(2,1)} %copy.100) | copy-start | bytes 786436
  246.6 4.7 %copy-start.25 = (bf16[1024,1,128]{0,2,1:T(8,128)(2,1)S(1)}, bf16[1024,1,128]{0,2,1:T(8,128)(2,1)}, u32[]{:S(2)}) copy-start(bf16[1024,1,128]{0,2,1:T(8,128)(2,1)} %get-tuple-element.88) | copy-start | bytes 786436
  246.6 20.0 %collective-permute-start.6 = (f32[4,129,128]{2,1,0:T(8,128)S(1)}, f32[4,129,128]{2,1,0:T(8,128)S(1)}, u32[]{:S(2)}, u32[]{:S(2)}) collective-permute-start(f32[4,129,128]{2,1,0:T(8,128)S(1)} %select_add_fusion.3), channel_id=1, source_target_pairs={{0,8},{4,12},{8,16},{12,20},{16,24},{20,28},{24,32},{28,36},{32,40... | collective-permute-start | bytes 792584 | tf_op jit(solution)/shard_map/ppermute | solution.py:113
  251.3 21.2 %copy-start.9 = (bf16[1024,1,128]{2,1,0:T(2,128)(2,1)S(1)}, bf16[1024,1,128]{2,1,0:T(2,128)(2,1)}, u32[]{:S(2)}) copy-start(bf16[1024,1,128]{2,1,0:T(2,128)(2,1)} %get-tuple-element.129) | copy-start | bytes 786436
  251.3 21.2 %copy-start.8 = (bf16[1024,1,128]{2,1,0:T(2,128)(2,1)S(1)}, bf16[1024,1,128]{2,1,0:T(2,128)(2,1)}, u32[]{:S(2)}) copy-start(bf16[1024,1,128]{2,1,0:T(2,128)(2,1)} %get-tuple-element.130) | copy-start | bytes 786436
  251.3 21.3 %copy-start.11 = (bf16[1024,1,128]{2,1,0:T(2,128)(2,1)S(1)}, bf16[1024,1,128]{2,1,0:T(2,128)(2,1)}, u32[]{:S(2)}) copy-start(bf16[1024,1,128]{2,1,0:T(2,128)(2,1)} %get-tuple-element.121) | copy-start | bytes 786436
  251.3 21.3 %copy-start.10 = (bf16[1024,1,128]{2,1,0:T(2,128)(2,1)S(1)}, bf16[1024,1,128]{2,1,0:T(2,128)(2,1)}, u32[]{:S(2)}) copy-start(bf16[1024,1,128]{2,1,0:T(2,128)(2,1)} %get-tuple-element.122) | copy-start | bytes 786436
  266.6 11.9 %collective-permute-start.7 = (f32[4,129,128]{2,1,0:T(8,128)S(1)}, f32[4,129,128]{2,1,0:T(8,128)S(1)}, u32[]{:S(2)}, u32[]{:S(2)}) collective-permute-start(f32[4,129,128]{2,1,0:T(8,128)S(1)} %select_add_fusion.2), channel_id=1, source_target_pairs={{0,16},{4,20},{8,24},{12,28},{16,32},{20,36},{24,40},{28,44},{32,4... | collective-permute-start | bytes 792584 | tf_op jit(solution)/shard_map/ppermute | solution.py:113
  278.5 115.6 %all-gather.7.cloned.1.call-start = ((), (), s32[]{:S(2)}) async-start(), calls=%async_computation.6 | async-start | bytes 5242880 | tf_op jit(solution)/shard_map/all_gather | solution.py:138
  278.6 8.3 %copy-start.24 = (bf16[1024,1,128]{0,2,1:T(8,128)(2,1)S(1)}, bf16[1024,1,128]{0,2,1:T(8,128)(2,1)}, u32[]{:S(2)}) copy-start(bf16[1024,1,128]{0,2,1:T(8,128)(2,1)} %get-tuple-element.94) | copy-start | bytes 786436
  278.6 10.2 %collective-permute-start.8 = (f32[4,129,128]{2,1,0:T(8,128)S(1)}, f32[4,129,128]{2,1,0:T(8,128)S(1)}, u32[]{:S(2)}, u32[]{:S(2)}) collective-permute-start(f32[4,129,128]{2,1,0:T(8,128)S(1)} %select_add_fusion.1), channel_id=1, source_target_pairs={{0,32},{4,36},{8,40},{12,44},{16,48},{20,52},{24,56},{28,60},{32,6... | collective-permute-start | bytes 792584 | tf_op jit(solution)/shard_map/ppermute | solution.py:113
  288.8 10.4 %collective-permute-start.9 = (f32[4,129,128]{2,1,0:T(8,128)S(1)}, f32[4,129,128]{2,1,0:T(8,128)S(1)}, u32[]{:S(2)}, u32[]{:S(2)}) collective-permute-start(f32[4,129,128]{2,1,0:T(8,128)S(1)} %select_add_fusion), channel_id=1, source_target_pairs={{0,64},{4,68},{8,72},{12,76},{16,80},{20,84},{24,88},{28,92},{32,9... | collective-permute-start | bytes 792584 | tf_op jit(solution)/shard_map/ppermute | solution.py:113
  394.1 10.6 %copy-start.1 = (bf16[1024,1024]{1,0:T(8,128)(2,1)S(1)}, bf16[1024,1024]{1,0:T(8,128)(2,1)}, u32[]{:S(2)}) copy-start(bf16[1024,1024]{1,0:T(8,128)(2,1)} %param.7) | copy-start | bytes 6291460
  (7 other events, 17.9 us)
Sparse Core Ops, SparseCore 0:
  278.6 51.5 all-gather.4
  347.3 46.7 all-gather.6

commit v13 on v5

--- a/solution.py
+++ b/solution.py
@@ -83,43 +83,48 @@
             "hqk,khd->qhd", probabilities, value_part, preferred_element_type=f32
         )
 
+    key_feat = feature(key_all.astype(f32))
+    delta_m = jnp.einsum(
+        "khd,khe->hde", key_feat, value_all.astype(f32), precision=highest
+    )
+    delta_z = jnp.sum(key_feat, axis=0)
+    delta = jnp.concatenate([delta_m, delta_z[:, None, :]], axis=1)
+
+    first_heads = bounds[1]
+    cuts = [round(first_heads * i / len(shifts)) for i in range(len(shifts) + 1)]
+    pieces = []
+    total = delta
+    for k, step in enumerate(shifts):
+        lo, hi = cuts[k], cuts[k + 1]
+        operands = None
+        if hi > lo:
+            total, operands = lax.optimization_barrier(
+                (total, (query_all[:, lo:hi], key_all[:, lo:hi], value_all[:, lo:hi]))
+            )
+        perm = [(j, j + step) for j in range(n - step)]
+        got = lax.ppermute(total, "ctx", perm)
+        if hi > lo:
+            piece = local_attention(*operands)
+            got, piece = lax.optimization_barrier((got, piece))
+            pieces.append(piece)
+        total = total + jnp.where(me - step >= start, got, jnp.zeros_like(got))
+    memory = total - delta
+    first_local = jnp.concatenate(pieces, axis=1)
+
     def one_group(g, hold):
         first, last = bounds[g], bounds[g + 1]
         group_heads = last - first
         group_width = group_heads * dh
-        cuts = [first + round(group_heads * i / len(shifts)) for i in range(len(shifts) + 1)]
-        cuts = [c - first for c in cuts]
-        key_heads = key_all[:, first:last]
-        value_heads = value_all[:, first:last]
         query_heads = query_all[:, first:last]
-
-        key_feat = feature(key_heads.astype(f32))
-        delta_m = jnp.einsum(
-            "khd,khe->hde", key_feat, value_heads.astype(f32), precision=highest
-        )
-        delta_z = jnp.sum(key_feat, axis=0)
-        delta = jnp.concatenate([delta_m, delta_z[:, None, :]], axis=1)
-        if hold is not None:
-            delta, _ = lax.optimization_barrier((delta, hold))
-
-        pieces = []
-        total = delta
-        for k, step in enumerate(shifts):
-            lo, hi = cuts[k], cuts[k + 1]
-            total, operands = lax.optimization_barrier(
-                (total, (query_heads[:, lo:hi], key_heads[:, lo:hi], value_heads[:, lo:hi]))
-            )
-            perm = [(j, j + step) for j in range(n - step)]
-            got = lax.ppermute(total, "ctx", perm)
-            if hi > lo:
-                piece = local_attention(*operands)
-                got, piece = lax.optimization_barrier((got, piece))
-                pieces.append(piece)
-            total = total + jnp.where(me - step >= start, got, jnp.zeros_like(got))
-        local_out = jnp.concatenate(pieces, axis=1)
-        memory = total - delta
-        mem_m = memory[:, :dh, :]
-        mem_z = memory[:, dh, :]
+        if g == 0:
+            local_out = first_local
+        else:
+            operands = (query_heads, key_all[:, first:last], value_all[:, first:last])
+            if hold is not None:
+                operands, _ = lax.optimization_barrier((operands, hold))
+            local_out = local_attention(*operands)
+        mem_m = memory[first:last, :dh, :]
+        mem_z = memory[first:last, dh, :]
 
         query_feat = feature(query_heads.astype(f32))
         numerator = jnp.einsum("qhd,hde->qhe", query_feat, mem_m, precision=highest)
@@ -141,7 +146,7 @@
             weight_rows[:, first:last].reshape(head_count * group_width, out_cols),
             preferred_element_type=f32,
         )
-        return part, combined
+        return part, outgoing
 
     summed, hold = one_group(0, None)
     for g in range(1, len(bounds) - 1):

time: 419 us -> 436 us (1.041)
  waiting for transfers between devices: 119 us -> 134 us
  starting transfers between devices: 77.7 us -> 66 us
  matrix products: 57.4 us -> 67.5 us
  local copies, waits for them, and re-layouts: 95.5 us -> 105 us
  blocking collectives: 31.7 us -> 26.8 us
    all_to_all x1, waiting for transfers between devices: 0.01 us -> 22.6 us  [one_group(): lax.all_to_all(outgoing, 'ctx', 0, 0, tiled=True)]
    ppermute x10 -> x5, starting transfers between devices: 50 us -> 34.6 us  [per_device(): got = lax.ppermute(total, 'ctx', perm)]
    sub x0 -> x1, matrix products: none -> 10.8 us  [local_attention(): weights = jnp.exp(scores - row_max)]
    ppermute x10 -> x5, waiting for transfers between devices: 24 us -> 15.5 us  [per_device(): got = lax.ppermute(total, 'ctx', perm)]
    all_to_all x1, blocking collectives: 31.7 us -> 26.8 us  [one_group(): lax.all_to_all(outgoing, 'ctx', 0, 0, tiled=True)]
    optimization_barrier x16 -> x15, local copies, waits for them, and re-layouts: 4.83 us -> 9.56 us  [the longest x12 5.59 us: per_device(): lax.optimization_barrier((total, (query_all[:, lo:hi], key_all[:, lo:hi],...]
    reshape x0 -> x2, local copies, waits for them, and re-layouts: none -> 4.48 us  [dispatch(): return jnp.take(got, tok_slot, axis=0, mode='clip').reshape(seg, heads, dh)]
    gather x4 -> x3, local copies, waits for them, and re-layouts: 25.3 us -> 22 us  [dispatch(): return jnp.take(got, tok_slot, axis=0, mode='clip').reshape(seg, heads, dh)]
  transfers between devices with their start and end apart: 16 -> 11, of which waited for: 11 -> 8; matrix products, arithmetic and copies ran while one was open for 31% -> 32% of each run, Pallas kernels for 0% -> 0%
where the time goes in v13:
time: 436 us; the launch traced here: 429 us
  waiting for transfers between devices  134 us (31%)
  local copies, waits for them, and re-layouts  105 us (24%)
  matrix products  67.5 us (15%)
  starting transfers between devices  66 us (15%)
  blocking collectives  26.8 us (6%)
  between operations  17.3 us (4%)
  other arithmetic  12.7 us (3%)
    all_to_all x3, waiting for transfers between devices, dispatch(): got = lax.all_to_all(buffer, 'ctx', 0, 0, tiled=True).reshape(slots, width)  65.5 us
    ppermute x5, starting transfers between devices, per_device(): got = lax.ppermute(total, 'ctx', perm)  34.6 us
    all_gather x2, waiting for transfers between devices, one_group(): gathered = lax.all_gather(rows, 'head', axis=1, tiled=True)  30.1 us
    all_to_all x1, blocking collectives, one_group(): lax.all_to_all(outgoing, 'ctx', 0, 0, tiled=True)  26.8 us
    all_to_all x1, waiting for transfers between devices, one_group(): lax.all_to_all(outgoing, 'ctx', 0, 0, tiled=True)  22.6 us
    gather x3, local copies, waits for them, and re-layouts, dispatch(): return jnp.take(got, tok_slot, axis=0, mode='clip').reshape(seg, heads, dh)  22 us
    dot_general x2, matrix products, one_group(): jnp.dot(gathered, weight_rows[:, first:last].reshape(head_count * group_w...  21.2 us
    all_to_all x3, starting transfers between devices, dispatch(): got = lax.all_to_all(buffer, 'ctx', 0, 0, tiled=True).reshape(slots, width)  19.1 us
  transfers between devices with their start and end apart: 11, of which 8 were waited for; matrix products, arithmetic and copies ran while one was open for 32% of the time, Pallas kernels for 0%

profile of v13, /device:TPU:1, one launch (start us, length us, event | category | flops | bytes accessed | tf_op | source)
XLA Modules:
  0.0 429.0 jit_solution(4079985967987815462)
XLA Ops:
  9.0 5.8 %gather_fusion = bf16[1536,1024]{1,0:T(8,128)(2,1)} fusion(bf16[1024,1024]{1,0:T(8,128)(2,1)S(1)} %copy-done, s32[2048]{0:T(1024)S(1)} %pad_clamp_fusion.1), kind=kCustom, calls=%fused_computation | custom fusion | bytes 6297600 | tf_op jit(solution)/shard_map/jit(_take)/gather | solution.py:66
  14.8 8.8 %all-to-all-start = ((bf16[32,48,1024]{2,1,0:T(8,128)(2,1)}), bf16[32,48,1024]{2,1,0:T(8,128)(2,1)}, u32[]{:S(2)}, u32[]{:S(2)}) async-start(bf16[32,48,1024]{2,1,0:T(8,128)(2,1)} %bitcast.177), calls=%async_computation | async-start | bytes 6291456 | tf_op jit(solution)/shard_map/all_to_all | solution.py:67
  23.6 5.8 %gather_fusion.2 = bf16[1536,1024]{1,0:T(8,128)(2,1)} fusion(bf16[1024,1024]{1,0:T(8,128)(2,1)S(1)} %copy-done.2, s32[2048]{0:T(1024)S(1)} %pad_clamp_fusion.1), kind=kCustom, calls=%fused_computation.2 | custom fusion | bytes 6297600 | tf_op jit(solution)/shard_map/jit(_take)/gather | solution.py:66
  29.4 34.0 %all-to-all-done = bf16[32,48,1024]{2,1,0:T(8,128)(2,1)} async-done(((bf16[32,48,1024]{2,1,0:T(8,128)(2,1)}), bf16[32,48,1024]{2,1,0:T(8,128)(2,1)}, u32[]{:S(2)}, u32[]{:S(2)}) %all-to-all-start) | async-done | bytes 3145760 | tf_op jit(solution)/shard_map/all_to_all | solution.py:67
  63.4 5.0 %all-to-all-start.1 = ((bf16[32,48,1024]{2,1,0:T(8,128)(2,1)}), bf16[32,48,1024]{2,1,0:T(8,128)(2,1)}, u32[]{:S(2)}, u32[]{:S(2)}) async-start(bf16[32,48,1024]{2,1,0:T(8,128)(2,1)} %bitcast.176), calls=%async_computation.1 | async-start | bytes 6291456 | tf_op jit(solution)/shard_map/all_to_all | solution.py:67
  69.2 1.7 select_reduce_fusion.1
  71.0 5.8 %gather_fusion.4 = bf16[1536,1024]{1,0:T(8,128)(2,1)} fusion(bf16[1024,1024]{1,0:T(8,128)(2,1)S(1)} %copy-done.3, s32[2048]{0:T(1024)S(1)} %pad_clamp_fusion.1), kind=kCustom, calls=%fused_computation.4 | custom fusion | bytes 6297600 | tf_op jit(solution)/shard_map/jit(_take)/gather | solution.py:66
  76.8 31.4 %all-to-all-done.1 = bf16[32,48,1024]{2,1,0:T(8,128)(2,1)} async-done(((bf16[32,48,1024]{2,1,0:T(8,128)(2,1)}), bf16[32,48,1024]{2,1,0:T(8,128)(2,1)}, u32[]{:S(2)}, u32[]{:S(2)}) %all-to-all-start.1) | async-done | bytes 3145760 | tf_op jit(solution)/shard_map/all_to_all | solution.py:67
  108.3 5.3 %all-to-all-start.2 = ((bf16[32,48,1024]{2,1,0:T(8,128)(2,1)}), bf16[32,48,1024]{2,1,0:T(8,128)(2,1)S(1)}, u32[]{:S(2)}, u32[]{:S(2)}) async-start(bf16[32,48,1024]{2,1,0:T(8,128)(2,1)} %bitcast.175), calls=%async_computation.2 | async-start | bytes 6291456 | tf_op jit(solution)/shard_map/all_to_all | solution.py:67
  118.1 8.3 %gather_fusion.1 = bf16[1024,1024]{1,0:T(8,128)(2,1)} fusion(bf16[1536,1024]{1,0:T(8,128)(2,1)} %bitcast.4, s32[1024]{0:T(1024)S(1)} %broadcast_clamp_fusion.1), kind=kCustom, calls=%fused_computation.1 | custom fusion | bytes 4198400 | tf_op jit(solution)/shard_map/jit(_take)/gather | solution.py:68
  126.4 3.6 copy.128
  130.0 4.1 copy.75
  134.1 8.4 %gather_fusion.3 = bf16[1024,1024]{1,0:T(8,128)(2,1)} fusion(bf16[1536,1024]{1,0:T(8,128)(2,1)} %bitcast.6, s32[1024]{0:T(1024)S(1)} %broadcast_clamp_fusion.1), kind=kCustom, calls=%fused_computation.3 | custom fusion | bytes 4198400 | tf_op jit(solution)/shard_map/jit(_take)/gather | solution.py:68
  142.5 7.0 %fusion.129 = (bf16[1024,1,128]{2,1,0:T(2,128)(2,1)}, bf16[1024,1,128]{2,1,0:T(2,128)(2,1)}, bf16[1024,1,128]{2,1,0:T(2,128)(2,1)}, bf16[1024,1,128]{2,1,0:T(2,128)(2,1)S(1)}) fusion(bf16[1024,8,128]{2,1,0:T(8,128)(2,1)} %bitcast.169), kind=kLoop, calls=%fused_computation.211 | loop fusion | bytes 2097152 | tf_op jit(solution)/shard_map/slice | solution.py:102
  151.7 1.9 fusion.14
  153.6 4.7 %fusion.10 = f32[8,128,128]{2,1,0:T(8,128)} fusion(bf16[1024,8,128]{0,2,1:T(8,128)(2,1)S(1)} %copy-done.9, bf16[1024,1024]{1,0:T(8,128)(2,1)S(1)} %copy-done.4), kind=kOutput, calls=%fused_computation.37 | convolution fusion | flops 1615855616 | bytes 4718592 | tf_op jit(solution)/shard_map/khd,khe->hde/dot_general | solution.py:87
  158.3 5.3 %gather_fusion.5 = bf16[1024,1024]{1,0:T(8,128)(2,1)} fusion(bf16[1536,1024]{1,0:T(8,128)(2,1)S(1)} %bitcast.165, s32[1024]{0:T(1024)S(1)} %broadcast_clamp_fusion.1), kind=kCustom, calls=%fused_computation.5 | custom fusion | bytes 4198400 | tf_op jit(solution)/shard_map/jit(_take)/gather | solution.py:68
  163.6 2.3 copy.129
  165.9 2.3 fusion.130
  168.5 3.5 collective-permute-start
  173.4 1.6 fusion.53
  175.0 3.2 collective-permute-done
  178.4 15.3 %collective-permute-start.1 = (f32[8,129,128]{2,0,1:T(8,128)S(1)}, f32[8,129,128]{2,0,1:T(8,128)S(1)}, u32[]{:S(2)}, u32[]{:S(2)}) collective-permute-start(f32[8,129,128]{2,0,1:T(8,128)S(1)} %copy.85), channel_id=1, source_target_pairs={{0,8},{4,12},{8,16},{12,20},{16,24},{20,28},{24,32},{28,36},{32,40... | collective-permute-start | bytes 1585160 | tf_op jit(solution)/shard_map/ppermute | solution.py:105
  197.6 5.1 %collective-permute-start.2 = (f32[8,129,128]{2,0,1:T(8,128)}, f32[8,129,128]{2,0,1:T(8,128)}, u32[]{:S(2)}, u32[]{:S(2)}) collective-permute-start(f32[8,129,128]{2,0,1:T(8,128)} %copy.87), channel_id=1, source_target_pairs={{0,16},{4,20},{8,24},{12,28},{16,32},{20,36},{24,40},{28,44},{32,4... | collective-permute-start | bytes 1585160 | tf_op jit(solution)/shard_map/ppermute | solution.py:105
  208.8 1.6 fusion.127
  213.1 4.8 %collective-permute-start.3 = (f32[8,129,128]{2,0,1:T(8,128)S(1)}, f32[8,129,128]{2,0,1:T(8,128)S(1)}, u32[]{:S(2)}, u32[]{:S(2)}) collective-permute-start(f32[8,129,128]{2,0,1:T(8,128)S(1)} %copy.92), channel_id=1, source_target_pairs={{0,32},{4,36},{8,40},{12,44},{16,48},{20,52},{24,56},{28,60},{32,6... | collective-permute-start | bytes 1585160 | tf_op jit(solution)/shard_map/ppermute | solution.py:105
  219.9 6.0 %collective-permute-done.3 = f32[8,129,128]{2,0,1:T(8,128)S(1)} collective-permute-done((f32[8,129,128]{2,0,1:T(8,128)S(1)}, f32[8,129,128]{2,0,1:T(8,128)S(1)}, u32[]{:S(2)}, u32[]{:S(2)}) %collective-permute-start.3) | collective-permute-done | bytes 528416 | tf_op jit(solution)/shard_map/ppermute | solution.py:105
  226.1 5.8 %collective-permute-start.4 = (f32[8,129,128]{2,0,1:T(8,128)S(1)}, f32[8,129,128]{2,0,1:T(8,128)S(1)}, u32[]{:S(2)}, u32[]{:S(2)}) collective-permute-start(f32[8,129,128]{2,0,1:T(8,128)S(1)} %copy.97), channel_id=1, source_target_pairs={{0,64},{4,68},{8,72},{12,76},{16,80},{20,84},{24,88},{28,92},{32,9... | collective-permute-start | bytes 1585160 | tf_op jit(solution)/shard_map/ppermute | solution.py:105
  234.0 5.0 %collective-permute-done.4 = f32[8,129,128]{2,0,1:T(8,128)S(1)} collective-permute-done((f32[8,129,128]{2,0,1:T(8,128)S(1)}, f32[8,129,128]{2,0,1:T(8,128)S(1)}, u32[]{:S(2)}, u32[]{:S(2)}) %collective-permute-start.4) | collective-permute-done | bytes 528416 | tf_op jit(solution)/shard_map/ppermute | solution.py:105
  239.2 2.5 fusion.44
  241.8 3.1 fusion.30
  245.5 5.4 %gather_fusion.6 = bf16[1536,512]{1,0:T(8,128)(2,1)} fusion(bf16[1024,512]{1,0:T(8,128)(2,1)S(1)} %copy.101, s32[2048]{0:T(1024)S(1)} %pad_clamp_fusion), kind=kCustom, calls=%fused_computation.6 | custom fusion | bytes 3151872 | tf_op jit(solution)/shard_map/jit(_take)/gather | solution.py:140
  250.9 12.2 %all-to-all-start.3 = ((bf16[32,48,512]{2,1,0:T(8,128)(2,1)}), bf16[32,48,512]{2,1,0:T(8,128)(2,1)S(1)}, u32[]{:S(2)}, u32[]{:S(2)}) async-start(bf16[32,48,512]{2,1,0:T(8,128)(2,1)} %bitcast.38), calls=%async_computation.3 | async-start | bytes 3145728 | tf_op jit(solution)/shard_map/all_to_all | solution.py:141
  263.2 22.6 %all-to-all-done.3 = bf16[32,48,512]{2,1,0:T(8,128)(2,1)S(1)} async-done(((bf16[32,48,512]{2,1,0:T(8,128)(2,1)}), bf16[32,48,512]{2,1,0:T(8,128)(2,1)S(1)}, u32[]{:S(2)}, u32[]{:S(2)}) %all-to-all-start.3) | async-done | bytes 1572896 | tf_op jit(solution)/shard_map/all_to_all | solution.py:141
  285.8 5.1 %gather_fusion.7 = bf16[1024,512]{1,0:T(8,128)(2,1)} fusion(bf16[1536,512]{1,0:T(8,128)(2,1)S(1)} %bitcast.166, s32[1024]{0:T(1024)S(1)} %broadcast_clamp_fusion), kind=kCustom, calls=%fused_computation.7 | custom fusion | bytes 2101248 | tf_op jit(solution)/shard_map/jit(_take)/gather | solution.py:142
  292.3 2.1 slice.135
  297.8 1.7 copy.126
  299.6 3.4 fusion.40
  303.0 5.0 %fusion.42 = f32[4,128,1024]{2,1,0:T(8,128)} fusion(f32[8,129,128]{2,1,0:T(8,128)} %copy-done.14, bf16[1024,4,128]{2,1,0:T(4,128)(2,1)S(1)} %copy-done.7), kind=kOutput, calls=%fused_computation.87 | convolution fusion | flops 807927808 | bytes 3407872 | tf_op jit(solution)/shard_map/qhd,hde->qhe/dot_general | solution.py:130
  308.0 10.8 %fusion.132 = (f32[4,1024]{1,0:T(4,128)S(1)}, f32[4,1024,1024]{1,2,0:T(8,128)}) fusion(pred[1024,1024]{0,1:T(8,128)(4,1)S(1)} %copy-done.11, bf16[1024,4,128]{2,0,1:T(8,128)(2,1)S(1)} %copy-done.12, bf16[1024,4,128]{2,0,1:T(8,128)(2,1)} %copy.125), kind=kOutput, calls=%fused_computation.214 | convolution fusion | flops 1090520064 | bytes 19939328 | tf_op jit(solution)/shard_map/sub | solution.py:80
  318.8 8.1 %fusion.31 = bf16[1024,4,128]{0,2,1:T(8,128)(2,1)S(1)} fusion(f32[4,128,1024]{2,1,0:T(8,128)} %fusion.42, bf16[1024,4,128]{0,2,1:T(8,128)(2,1)S(1)} %copy-done.13, f32[4,1024,1024]{1,2,0:T(8,128)} %get-tuple-element.91, f32[4,1024]{1,0:T(4,128)S(1)} %get-tuple-element.90, f32[4]{0:T(128)S(1)} %get-tuple-element.80, f32[1024,4]{0,1:T(4,128)S(1)} %fusion.98, ...), kind=kOutput, calls=%fused_computation.75 | convolution fusion | flops 1084751872 | bytes 21004320 | tf_op jit(solution)/shard_map/hqk,khd->qhd/dot_general | solution.py:82
  327.5 4.8 %gather_fusion.8 = bf16[1536,512]{1,0:T(8,128)(2,1)S(1)} fusion(bf16[1024,512]{1,0:T(8,128)(2,1)S(1)} %copy.107, s32[2048]{0:T(1024)S(1)} %pad_clamp_fusion), kind=kCustom, calls=%fused_computation.8 | custom fusion | bytes 3151872 | tf_op jit(solution)/shard_map/jit(_take)/gather | solution.py:140
  332.4 26.8 %all_to_all.25 = bf16[32,48,512]{2,1,0:T(8,128)(2,1)S(1)} all-to-all(bf16[32,48,512]{2,1,0:T(8,128)(2,1)S(1)} %bitcast.180), channel_id=1, replica_groups=mesh['ctx'=32,'head'=4] {'ctx'}, dimensions={0} | all-to-all | bytes 3145728 | tf_op jit(solution)/shard_map/all_to_all | solution.py:141
  359.1 5.1 %gather_fusion.9 = bf16[1024,512]{1,0:T(8,128)(2,1)} fusion(bf16[1536,512]{1,0:T(8,128)(2,1)S(1)} %bitcast.167, s32[1024]{0:T(1024)S(1)} %broadcast_clamp_fusion), kind=kCustom, calls=%fused_computation.9 | custom fusion | bytes 2101248 | tf_op jit(solution)/shard_map/jit(_take)/gather | solution.py:142
  364.2 6.1 %fusion.126 = (bf16[4,4,128,1024]{3,2,1,0:T(8,128)(2,1)}, bf16[4,4,128,1024]{3,2,1,0:T(8,128)(2,1)}) fusion(bf16[4,8,128,1024]{3,2,1,0:T(8,128)(2,1)} %bitcast.179), kind=kLoop, calls=%fused_computation.208 | loop fusion | bytes 16777216 | tf_op jit(solution)/shard_map/slice | solution.py:146
  370.4 10.6 %fusion.133 = f32[1024,1024]{1,0:T(8,128)} fusion(bf16[1024,2048]{1,0:T(8,128)(2,1)} %all-gather.5.cloned.1.call-done, bf16[2048,1024]{1,0:T(8,128)(2,1)} %bitcast.183), kind=kOutput, calls=%fused_computation.215 | convolution fusion | flops 4294967296 | bytes 12582912 | tf_op jit(solution)/shard_map/dot_general | solution.py:144
  381.0 30.1 %all-gather.7.cloned.1.call-done = bf16[1024,2048]{1,0:T(8,128)(2,1)} async-done(((bf16[1024,512]{1,0:T(8,128)(2,1)}), bf16[1024,2048]{1,0:T(8,128)(2,1)}) %all-gather.7.cloned.1.call-update) | async-done | bytes 4194320 | tf_op jit(solution)/shard_map/all_gather | solution.py:143
  411.1 10.6 %add_convert_fusion = bf16[1024,1024]{1,0:T(8,128)(2,1)} fusion(f32[1024,1024]{1,0:T(8,128)} %fusion.133, bf16[1024,2048]{1,0:T(8,128)(2,1)} %all-gather.7.cloned.1.call-done, bf16[2048,1024]{1,0:T(8,128)(2,1)} %bitcast.182), kind=kOutput, calls=%fused_computation.41 | convolution fusion | flops 4297064448 | bytes 14680064 | tf_op jit(solution)/shard_map/dot_general | solution.py:144
  (120 shorter events, 31.8 us)
Async XLA Ops:
  6.5 2.5 copy-start
  14.8 8.8 %copy-start.2 = (bf16[1024,1024]{1,0:T(8,128)(2,1)S(1)}, bf16[1024,1024]{1,0:T(8,128)(2,1)}, u32[]{:S(2)}) copy-start(bf16[1024,1024]{1,0:T(8,128)(2,1)} %param.9) | copy-start | bytes 6291460
  14.8 48.6 %all-to-all-start = ((bf16[32,48,1024]{2,1,0:T(8,128)(2,1)}), bf16[32,48,1024]{2,1,0:T(8,128)(2,1)}, u32[]{:S(2)}, u32[]{:S(2)}) async-start(bf16[32,48,1024]{2,1,0:T(8,128)(2,1)} %bitcast.177), calls=%async_computation | async-start | bytes 6291456 | tf_op jit(solution)/shard_map/all_to_all | solution.py:67
  29.4 41.6 %copy-start.3 = (bf16[1024,1024]{1,0:T(8,128)(2,1)S(1)}, bf16[1024,1024]{1,0:T(8,128)(2,1)}, u32[]{:S(2)}) copy-start(bf16[1024,1024]{1,0:T(8,128)(2,1)} %param.7) | copy-start | bytes 6291460
  63.4 44.9 %all-to-all-start.1 = ((bf16[32,48,1024]{2,1,0:T(8,128)(2,1)}), bf16[32,48,1024]{2,1,0:T(8,128)(2,1)}, u32[]{:S(2)}, u32[]{:S(2)}) async-start(bf16[32,48,1024]{2,1,0:T(8,128)(2,1)} %bitcast.176), calls=%async_computation.1 | async-start | bytes 6291456 | tf_op jit(solution)/shard_map/all_to_all | solution.py:67
  76.8 36.9 %copy-start.20 = (s32[32]{0:T(128)S(1)}, s32[32]{0:T(128)}, u32[]{:S(2)}) copy-start(s32[32]{0:T(128)} %param.11) | copy-start | bytes 388
  76.8 40.0 %copy-start.21 = (f32[8]{0:T(128)S(1)}, f32[8]{0:T(128)}, u32[]{:S(2)}) copy-start(f32[8]{0:T(128)} %param.12) | copy-start | bytes 100
  108.3 50.0 %all-to-all-start.2 = ((bf16[32,48,1024]{2,1,0:T(8,128)(2,1)}), bf16[32,48,1024]{2,1,0:T(8,128)(2,1)S(1)}, u32[]{:S(2)}, u32[]{:S(2)}) async-start(bf16[32,48,1024]{2,1,0:T(8,128)(2,1)} %bitcast.175), calls=%async_computation.2 | async-start | bytes 6291456 | tf_op jit(solution)/shard_map/all_to_all | solution.py:67
  142.5 7.8 %copy-start.4 = (bf16[1024,1024]{1,0:T(8,128)(2,1)S(1)}, bf16[1024,1024]{1,0:T(8,128)(2,1)}, u32[]{:S(2)}) copy-start(bf16[1024,1024]{1,0:T(8,128)(2,1)} %gather_fusion.3) | copy-start | bytes 6291460
  149.5 2.2 copy-start.6
  150.3 3.3 copy-start.9
  163.6 4.7 %copy-start.8 = (f32[8,128,128]{2,1,0:T(8,128)S(1)}, f32[8,128,128]{2,1,0:T(8,128)}, u32[]{:S(2)}) copy-start(f32[8,128,128]{2,1,0:T(8,128)} %fusion.10) | copy-start | bytes 1572868
  165.9 6.1 %copy-start.10 = (bf16[1024,1,128]{2,1,0:T(2,128)(2,1)S(1)}, bf16[1024,1,128]{2,1,0:T(2,128)(2,1)}, u32[]{:S(2)}) copy-start(bf16[1024,1,128]{2,1,0:T(2,128)(2,1)} %get-tuple-element.71) | copy-start | bytes 786436
  165.9 6.2 %copy-start.15 = (bf16[1024,1,128]{2,0,1:T(8,128)(2,1)S(1)}, bf16[1024,1,128]{2,0,1:T(8,128)(2,1)}, u32[]{:S(2)}) copy-start(bf16[1024,1,128]{2,0,1:T(8,128)(2,1)} %copy.116) | copy-start | bytes 786436
  168.5 9.7 %collective-permute-start = (f32[8,129,128]{2,0,1:T(8,128)S(1)}, f32[8,129,128]{2,0,1:T(8,128)S(1)}, u32[]{:S(2)}, u32[]{:S(2)}) collective-permute-start(f32[8,129,128]{2,0,1:T(8,128)S(1)} %copy.80), channel_id=1, source_target_pairs={{0,4},{4,8},{8,12},{12,16},{16,20},{20,24},{24,28},{28,32},{32,36}... | collective-permute-start | bytes 1585160 | tf_op jit(solution)/shard_map/ppermute | solution.py:105
  172.1 1.3 copy-start.19
  178.4 16.6 %copy-start.18 = (bf16[1024,1,128]{2,0,1:T(8,128)(2,1)S(1)}, bf16[1024,1,128]{2,0,1:T(8,128)(2,1)}, u32[]{:S(2)}) copy-start(bf16[1024,1,128]{2,0,1:T(8,128)(2,1)} %get-tuple-element.38) | copy-start | bytes 786436
  178.4 18.2 %collective-permute-start.1 = (f32[8,129,128]{2,0,1:T(8,128)S(1)}, f32[8,129,128]{2,0,1:T(8,128)S(1)}, u32[]{:S(2)}, u32[]{:S(2)}) collective-permute-start(f32[8,129,128]{2,0,1:T(8,128)S(1)} %copy.85), channel_id=1, source_target_pairs={{0,8},{4,12},{8,16},{12,20},{16,24},{20,28},{24,32},{28,36},{32,40... | collective-permute-start | bytes 1585160 | tf_op jit(solution)/shard_map/ppermute | solution.py:105
  197.6 14.2 %collective-permute-start.2 = (f32[8,129,128]{2,0,1:T(8,128)}, f32[8,129,128]{2,0,1:T(8,128)}, u32[]{:S(2)}, u32[]{:S(2)}) collective-permute-start(f32[8,129,128]{2,0,1:T(8,128)} %copy.87), channel_id=1, source_target_pairs={{0,16},{4,20},{8,24},{12,28},{16,32},{20,36},{24,40},{28,44},{32,4... | collective-permute-start | bytes 1585160 | tf_op jit(solution)/shard_map/ppermute | solution.py:105
  213.1 6.1 %copy-start.17 = (bf16[1024,1,128]{2,0,1:T(8,128)(2,1)S(1)}, bf16[1024,1,128]{2,0,1:T(8,128)(2,1)}, u32[]{:S(2)}) copy-start(bf16[1024,1,128]{2,0,1:T(8,128)(2,1)} %get-tuple-element.43) | copy-start | bytes 786436
  213.1 12.8 %collective-permute-start.3 = (f32[8,129,128]{2,0,1:T(8,128)S(1)}, f32[8,129,128]{2,0,1:T(8,128)S(1)}, u32[]{:S(2)}, u32[]{:S(2)}) collective-permute-start(f32[8,129,128]{2,0,1:T(8,128)S(1)} %copy.92), channel_id=1, source_target_pairs={{0,32},{4,36},{8,40},{12,44},{16,48},{20,52},{24,56},{28,60},{32,6... | collective-permute-start | bytes 1585160 | tf_op jit(solution)/shard_map/ppermute | solution.py:105
  226.1 7.1 %copy-start.16 = (bf16[1024,1,128]{2,0,1:T(8,128)(2,1)S(1)}, bf16[1024,1,128]{2,0,1:T(8,128)(2,1)}, u32[]{:S(2)}) copy-start(bf16[1024,1,128]{2,0,1:T(8,128)(2,1)} %get-tuple-element.48) | copy-start | bytes 786436
  226.1 12.9 %collective-permute-start.4 = (f32[8,129,128]{2,0,1:T(8,128)S(1)}, f32[8,129,128]{2,0,1:T(8,128)S(1)}, u32[]{:S(2)}, u32[]{:S(2)}) collective-permute-start(f32[8,129,128]{2,0,1:T(8,128)S(1)} %copy.97), channel_id=1, source_target_pairs={{0,64},{4,68},{8,72},{12,76},{16,80},{20,84},{24,88},{28,92},{32,9... | collective-permute-start | bytes 1585160 | tf_op jit(solution)/shard_map/ppermute | solution.py:105
  234.0 7.8 %copy-start.22 = (f32[1024,1,128]{0,2,1:T(8,128)S(1)}, f32[1024,1,128]{0,2,1:T(8,128)}, u32[]{:S(2)}) copy-start(f32[1024,1,128]{0,2,1:T(8,128)} %fusion.53) | copy-start | bytes 1572868
  234.0 7.8 %copy-start.23 = (f32[1024,1,128]{0,2,1:T(8,128)S(1)}, f32[1024,1,128]{0,2,1:T(8,128)}, u32[]{:S(2)}) copy-start(f32[1024,1,128]{0,2,1:T(8,128)} %fusion.52) | copy-start | bytes 1572868
  239.2 5.7 %copy-start.14 = (f32[8,129,128]{2,1,0:T(8,128)}, f32[8,129,128]{2,1,0:T(8,128)S(1)}, u32[]{:S(2)}) copy-start(f32[8,129,128]{2,1,0:T(8,128)S(1)} %fusion.70) | copy-start | bytes 1585156
  250.9 34.9 %all-to-all-start.3 = ((bf16[32,48,512]{2,1,0:T(8,128)(2,1)}), bf16[32,48,512]{2,1,0:T(8,128)(2,1)S(1)}, u32[]{:S(2)}, u32[]{:S(2)}) async-start(bf16[32,48,512]{2,1,0:T(8,128)(2,1)} %bitcast.38), calls=%async_computation.3 | async-start | bytes 3145728 | tf_op jit(solution)/shard_map/all_to_all | solution.py:141
  263.1 107.3 %all-gather.5.cloned.1.call-start = ((), (), s32[]{:S(2)}) async-start(), calls=%async_computation.5 | async-start | bytes 5242880 | tf_op jit(solution)/shard_map/all_gather | solution.py:143
  290.9 3.5 copy-start.7
  290.9 5.8 %copy-start.5 = (bf16[1024,1024]{1,0:T(8,128)(2,1)S(1)}, bf16[1024,1024]{1,0:T(8,128)(2,1)}, u32[]{:S(2)}) copy-start(bf16[1024,1024]{1,0:T(8,128)(2,1)} %gather_fusion.3) | copy-start | bytes 6291460
  290.9 120.2 %all-gather.7.cloned.1.call-start = ((), (), s32[]{:S(2)}) async-start(), calls=%async_computation.6 | async-start | bytes 5242880 | tf_op jit(solution)/shard_map/all_gather | solution.py:143
  299.6 8.4 %copy-start.11 = (pred[1024,1024]{0,1:T(8,128)(4,1)S(1)}, pred[1024,1024]{0,1:T(8,128)(4,1)}, u32[]{:S(2)}) copy-start(pred[1024,1024]{0,1:T(8,128)(4,1)} %iota_compare_fusion.3) | copy-start | bytes 3145732
  299.6 8.4 %copy-start.12 = (bf16[1024,4,128]{2,0,1:T(8,128)(2,1)S(1)}, bf16[1024,4,128]{2,0,1:T(8,128)(2,1)}, u32[]{:S(2)}) copy-start(bf16[1024,4,128]{2,0,1:T(8,128)(2,1)} %copy.124) | copy-start | bytes 3145732
  308.0 10.9 %copy-start.13 = (bf16[1024,4,128]{0,2,1:T(8,128)(2,1)S(1)}, bf16[1024,4,128]{0,2,1:T(8,128)(2,1)}, u32[]{:S(2)}) copy-start(bf16[1024,4,128]{0,2,1:T(8,128)(2,1)} %copy.126) | copy-start | bytes 3145732
  411.1 10.6 %copy-start.1 = (bf16[1024,1024]{1,0:T(8,128)(2,1)S(1)}, bf16[1024,1024]{1,0:T(8,128)(2,1)}, u32[]{:S(2)}) copy-start(bf16[1024,1024]{1,0:T(8,128)(2,1)} %param.8) | copy-start | bytes 6291460
Sparse Core Ops, SparseCore 0:
  291.0 46.9 all-gather.4
  364.4 46.6 all-gather.6

commit v14 on v5

--- a/solution.py
+++ b/solution.py
@@ -87,8 +87,9 @@
         first, last = bounds[g], bounds[g + 1]
         group_heads = last - first
         group_width = group_heads * dh
-        cuts = [first + round(group_heads * i / len(shifts)) for i in range(len(shifts) + 1)]
-        cuts = [c - first for c in cuts]
+        skip = 1 if g == 0 and len(shifts) > 1 else 0
+        used = len(shifts) - skip
+        cuts = [0] * skip + [round(group_heads * i / used) for i in range(used + 1)]
         key_heads = key_all[:, first:last]
         value_heads = value_all[:, first:last]
         query_heads = query_all[:, first:last]
@@ -106,9 +107,11 @@
         total = delta
         for k, step in enumerate(shifts):
             lo, hi = cuts[k], cuts[k + 1]
-            total, operands = lax.optimization_barrier(
-                (total, (query_heads[:, lo:hi], key_heads[:, lo:hi], value_heads[:, lo:hi]))
-            )
+            operands = None
+            if hi > lo:
+                total, operands = lax.optimization_barrier(
+                    (total, (query_heads[:, lo:hi], key_heads[:, lo:hi], value_heads[:, lo:hi]))
+                )
             perm = [(j, j + step) for j in range(n - step)]
             got = lax.ppermute(total, "ctx", perm)
             if hi > lo:

time: 419 us -> 422 us (level)
  starting transfers between devices: 77.7 us -> 82.8 us
  transfers between devices with their start and end apart: 16 -> 16, of which waited for: 11 -> 12; matrix products, arithmetic and copies ran while one was open for 31% -> 29% of each run, Pallas kernels for 0% -> 0%
where the time goes in v14:
time: 422 us; the launch traced here: 417 us
  waiting for transfers between devices  115 us (27%)
  local copies, waits for them, and re-layouts  99.6 us (24%)
  starting transfers between devices  82.8 us (20%)
  matrix products  58.7 us (14%)
  blocking collectives  30.5 us (7%)
  between operations  18.2 us (4%)
  other arithmetic  12.2 us (3%)
    all_to_all x3, waiting for transfers between devices, dispatch(): got = lax.all_to_all(buffer, 'ctx', 0, 0, tiled=True).reshape(slots, width)  64.7 us
    ppermute x10, starting transfers between devices, one_group(): got = lax.ppermute(total, 'ctx', perm)  53.1 us
    all_to_all x1, blocking collectives, one_group(): lax.all_to_all(outgoing, 'ctx', 0, 0, tiled=True)  30.5 us
    all_gather x2, waiting for transfers between devices, one_group(): gathered = lax.all_gather(rows, 'head', axis=1, tiled=True)  30.2 us
    gather x4, local copies, waits for them, and re-layouts, dispatch(): return jnp.take(got, tok_slot, axis=0, mode='clip').reshape(seg, heads, dh)  26.3 us
    dot_general x2, matrix products, one_group(): jnp.dot(gathered, weight_rows[:, first:last].reshape(head_count * group_w...  21.2 us
    ppermute x10, waiting for transfers between devices, one_group(): got = lax.ppermute(total, 'ctx', perm)  20.5 us
    all_to_all x3, starting transfers between devices, dispatch(): got = lax.all_to_all(buffer, 'ctx', 0, 0, tiled=True).reshape(slots, width)  19.1 us
  transfers between devices with their start and end apart: 16, of which 12 were waited for; matrix products, arithmetic and copies ran while one was open for 29% of the time, Pallas kernels for 0%

profile of v14, /device:TPU:1, one launch (start us, length us, event | category | flops | bytes accessed | tf_op | source)
XLA Modules:
  0.0 417.4 jit_solution(12597771410992876366)
XLA Ops:
  9.0 5.8 %gather_fusion.4 = bf16[1536,1024]{1,0:T(8,128)(2,1)} fusion(bf16[1024,1024]{1,0:T(8,128)(2,1)S(1)} %copy-done, s32[2048]{0:T(1024)S(1)} %pad_clamp_fusion.1), kind=kCustom, calls=%fused_computation.4 | custom fusion | bytes 6297600 | tf_op jit(solution)/shard_map/jit(_take)/gather | solution.py:66
  14.8 8.8 %all-to-all-start.2 = ((bf16[32,48,1024]{2,1,0:T(8,128)(2,1)}), bf16[32,48,1024]{2,1,0:T(8,128)(2,1)}, u32[]{:S(2)}, u32[]{:S(2)}) async-start(bf16[32,48,1024]{2,1,0:T(8,128)(2,1)} %bitcast.224), calls=%async_computation.2 | async-start | bytes 6291456 | tf_op jit(solution)/shard_map/all_to_all | solution.py:67
  23.6 5.8 %gather_fusion.2 = bf16[1536,1024]{1,0:T(8,128)(2,1)} fusion(bf16[1024,1024]{1,0:T(8,128)(2,1)S(1)} %copy-done.2, s32[2048]{0:T(1024)S(1)} %pad_clamp_fusion.1), kind=kCustom, calls=%fused_computation.2 | custom fusion | bytes 6297600 | tf_op jit(solution)/shard_map/jit(_take)/gather | solution.py:66
  29.5 34.0 %all-to-all-done.2 = bf16[32,48,1024]{2,1,0:T(8,128)(2,1)} async-done(((bf16[32,48,1024]{2,1,0:T(8,128)(2,1)}), bf16[32,48,1024]{2,1,0:T(8,128)(2,1)}, u32[]{:S(2)}, u32[]{:S(2)}) %all-to-all-start.2) | async-done | bytes 3145760 | tf_op jit(solution)/shard_map/all_to_all | solution.py:67
  63.4 5.0 %all-to-all-start.1 = ((bf16[32,48,1024]{2,1,0:T(8,128)(2,1)}), bf16[32,48,1024]{2,1,0:T(8,128)(2,1)}, u32[]{:S(2)}, u32[]{:S(2)}) async-start(bf16[32,48,1024]{2,1,0:T(8,128)(2,1)} %bitcast.223), calls=%async_computation.1 | async-start | bytes 6291456 | tf_op jit(solution)/shard_map/all_to_all | solution.py:67
  74.3 5.8 %gather_fusion = bf16[1536,1024]{1,0:T(8,128)(2,1)} fusion(bf16[1024,1024]{1,0:T(8,128)(2,1)S(1)} %copy-done.3, s32[2048]{0:T(1024)S(1)} %pad_clamp_fusion.1), kind=kCustom, calls=%fused_computation | custom fusion | bytes 6297600 | tf_op jit(solution)/shard_map/jit(_take)/gather | solution.py:66
  80.2 28.1 %all-to-all-done.1 = bf16[32,48,1024]{2,1,0:T(8,128)(2,1)} async-done(((bf16[32,48,1024]{2,1,0:T(8,128)(2,1)}), bf16[32,48,1024]{2,1,0:T(8,128)(2,1)}, u32[]{:S(2)}, u32[]{:S(2)}) %all-to-all-start.1) | async-done | bytes 3145760 | tf_op jit(solution)/shard_map/all_to_all | solution.py:67
  108.3 5.3 %all-to-all-start = ((bf16[32,48,1024]{2,1,0:T(8,128)(2,1)}), bf16[32,48,1024]{2,1,0:T(8,128)(2,1)S(1)}, u32[]{:S(2)}, u32[]{:S(2)}) async-start(bf16[32,48,1024]{2,1,0:T(8,128)(2,1)} %bitcast.222), calls=%async_computation | async-start | bytes 6291456 | tf_op jit(solution)/shard_map/all_to_all | solution.py:67
  117.4 8.3 %gather_fusion.5 = bf16[1024,1024]{1,0:T(8,128)(2,1)} fusion(bf16[1536,1024]{1,0:T(8,128)(2,1)} %bitcast.11, s32[1024]{0:T(1024)S(1)} %broadcast_clamp_fusion.1), kind=kCustom, calls=%fused_computation.5 | custom fusion | bytes 4198400 | tf_op jit(solution)/shard_map/jit(_take)/gather | solution.py:68
  125.7 3.5 copy.107
  129.2 8.3 %gather_fusion.3 = bf16[1024,1024]{1,0:T(8,128)(2,1)} fusion(bf16[1536,1024]{1,0:T(8,128)(2,1)} %bitcast.6, s32[1024]{0:T(1024)S(1)} %broadcast_clamp_fusion.1), kind=kCustom, calls=%fused_computation.3 | custom fusion | bytes 4198400 | tf_op jit(solution)/shard_map/jit(_take)/gather | solution.py:68
  137.5 4.0 copy.48
  141.5 4.5 %fusion.165 = (bf16[1024,4,128]{2,1,0:T(4,128)(2,1)}, bf16[1024,4,128]{2,1,0:T(4,128)(2,1)}) fusion(bf16[1024,8,128]{2,1,0:T(8,128)(2,1)} %bitcast.220), kind=kLoop, calls=%fused_computation.259 | loop fusion | bytes 4194304 | tf_op jit(solution)/shard_map/slice | solution.py:95
  146.0 4.6 %fusion.168 = (bf16[1024,1,128]{2,1,0:T(2,128)(2,1)}, bf16[1024,1,128]{2,1,0:T(2,128)(2,1)}, bf16[1024,1,128]{2,1,0:T(2,128)(2,1)}, bf16[1024,1,128]{2,1,0:T(2,1...) fusion(bf16[1024,8,128]{2,1,0:T(8,128)(2,1)S(1)} %bitcast.221), kind=kLoop, calls=%fused_computation.262 | loop fusion | bytes 4194304 | tf_op jit(solution)/shard_map/slice | solution.py:113
  150.6 2.6 all-to-all-done
  153.3 5.8 %gather_fusion.1 = bf16[1024,1024]{1,0:T(8,128)(2,1)} fusion(bf16[1536,1024]{1,0:T(8,128)(2,1)S(1)} %bitcast.215, s32[1024]{0:T(1024)S(1)} %broadcast_clamp_fusion.1), kind=kCustom, calls=%fused_computation.1 | custom fusion | bytes 4198400 | tf_op jit(solution)/shard_map/jit(_take)/gather | solution.py:68
  159.1 2.4 copy.106
  163.1 2.5 fusion.47
  165.6 2.5 fusion.54
  169.2 3.5 fusion.167
  174.5 3.2 collective-permute-start
  181.2 1.9 collective-permute-start.1
  186.6 5.9 %collective-permute-start.2 = (f32[4,129,128]{2,1,0:T(8,128)S(1)}, f32[4,129,128]{2,1,0:T(8,128)S(1)}, u32[]{:S(2)}, u32[]{:S(2)}) collective-permute-start(f32[4,129,128]{2,1,0:T(8,128)S(1)} %select_add_fusion.6), channel_id=1, source_target_pairs={{0,16},{4,20},{8,24},{12,28},{16,32},{20,36},{24,40},{28,44},{32,4... | collective-permute-start | bytes 792584 | tf_op jit(solution)/shard_map/ppermute | solution.py:116
  196.0 5.8 %collective-permute-start.3 = (f32[4,129,128]{2,1,0:T(8,128)S(1)}, f32[4,129,128]{2,1,0:T(8,128)S(1)}, u32[]{:S(2)}, u32[]{:S(2)}) collective-permute-start(f32[4,129,128]{2,1,0:T(8,128)S(1)} %select_add_fusion.5), channel_id=1, source_target_pairs={{0,32},{4,36},{8,40},{12,44},{16,48},{20,52},{24,56},{28,60},{32,6... | collective-permute-start | bytes 792584 | tf_op jit(solution)/shard_map/ppermute | solution.py:116
  205.2 4.8 %collective-permute-start.4 = (f32[4,129,128]{2,1,0:T(8,128)S(1)}, f32[4,129,128]{2,1,0:T(8,128)S(1)}, u32[]{:S(2)}, u32[]{:S(2)}) collective-permute-start(f32[4,129,128]{2,1,0:T(8,128)S(1)} %select_add_fusion.4), channel_id=1, source_target_pairs={{0,64},{4,68},{8,72},{12,76},{16,80},{20,84},{24,88},{28,92},{32,9... | collective-permute-start | bytes 792584 | tf_op jit(solution)/shard_map/ppermute | solution.py:116
  212.8 2.4 collective-permute-done.4
  215.3 2.5 fusion.49
  217.8 4.2 fusion.29
  223.5 7.3 %collective-permute-start.5 = (f32[4,129,128]{2,1,0:T(8,128)S(1)}, f32[4,129,128]{2,1,0:T(8,128)S(1)}, u32[]{:S(2)}, u32[]{:S(2)}) collective-permute-start(f32[4,129,128]{2,1,0:T(8,128)S(1)} %pad_maximum_fusion.1), channel_id=1, source_target_pairs={{0,4},{4,8},{8,12},{12,16},{16,20},{20,24},{24,28},{28,32},{32,36}... | collective-permute-start | bytes 792584 | tf_op jit(solution)/shard_map/ppermute | solution.py:116
  230.8 5.4 %gather_fusion.6 = bf16[1536,512]{1,0:T(8,128)(2,1)} fusion(bf16[1024,512]{1,0:T(8,128)(2,1)S(1)} %copy.61, s32[2048]{0:T(1024)S(1)} %pad_clamp_fusion), kind=kCustom, calls=%fused_computation.6 | custom fusion | bytes 3151872 | tf_op jit(solution)/shard_map/jit(_take)/gather | solution.py:138
  236.2 10.5 %all-to-all-start.3 = ((bf16[32,48,512]{2,1,0:T(8,128)(2,1)}), bf16[32,48,512]{2,1,0:T(8,128)(2,1)S(1)}, u32[]{:S(2)}, u32[]{:S(2)}) async-start(bf16[32,48,512]{2,1,0:T(8,128)(2,1)} %bitcast.39), calls=%async_computation.3 | async-start | bytes 3145728 | tf_op jit(solution)/shard_map/all_to_all | solution.py:139
  246.8 1.8 fusion.16
  250.7 3.5 collective-permute-start.6
  257.0 12.9 %collective-permute-done.6 = f32[4,129,128]{2,1,0:T(8,128)S(1)} collective-permute-done((f32[4,129,128]{2,1,0:T(8,128)S(1)}, f32[4,129,128]{2,1,0:T(8,128)S(1)}, u32[]{:S(2)}, u32[]{:S(2)}) %collective-permute-start.6) | collective-permute-done | bytes 264224 | tf_op jit(solution)/shard_map/ppermute | solution.py:116
  269.9 6.5 %collective-permute-start.7 = (f32[4,129,128]{2,1,0:T(8,128)S(1)}, f32[4,129,128]{2,1,0:T(8,128)}, u32[]{:S(2)}, u32[]{:S(2)}) collective-permute-start(f32[4,129,128]{2,1,0:T(8,128)S(1)} %select_add_fusion.2), channel_id=1, source_target_pairs={{0,16},{4,20},{8,24},{12,28},{16,32},{20,36},{24,40},{28,44},{32,4... | collective-permute-start | bytes 792584 | tf_op jit(solution)/shard_map/ppermute | solution.py:116
  278.1 5.3 %gather_fusion.7 = bf16[1024,512]{1,0:T(8,128)(2,1)} fusion(bf16[1536,512]{1,0:T(8,128)(2,1)S(1)} %bitcast.216, s32[1024]{0:T(1024)S(1)} %broadcast_clamp_fusion), kind=kCustom, calls=%fused_computation.7 | custom fusion | bytes 2101248 | tf_op jit(solution)/shard_map/jit(_take)/gather | solution.py:140
  283.5 4.6 %collective-permute-start.8 = (f32[4,129,128]{2,1,0:T(8,128)S(1)}, f32[4,129,128]{2,1,0:T(8,128)S(1)}, u32[]{:S(2)}, u32[]{:S(2)}) collective-permute-start(f32[4,129,128]{2,1,0:T(8,128)S(1)} %select_add_fusion.1), channel_id=1, source_target_pairs={{0,32},{4,36},{8,40},{12,44},{16,48},{20,52},{24,56},{28,60},{32,6... | collective-permute-start | bytes 792584 | tf_op jit(solution)/shard_map/ppermute | solution.py:116
  291.6 9.7 %collective-permute-start.9 = (f32[4,129,128]{2,1,0:T(8,128)S(1)}, f32[4,129,128]{2,1,0:T(8,128)S(1)}, u32[]{:S(2)}, u32[]{:S(2)}) collective-permute-start(f32[4,129,128]{2,1,0:T(8,128)S(1)} %select_add_fusion), channel_id=1, source_target_pairs={{0,64},{4,68},{8,72},{12,76},{16,80},{20,84},{24,88},{28,92},{32,9... | collective-permute-start | bytes 792584 | tf_op jit(solution)/shard_map/ppermute | solution.py:116
  304.1 1.9 collective-permute-done.9
  306.1 2.5 fusion.42
  308.6 3.1 fusion.31
  312.3 4.8 %gather_fusion.8 = bf16[1536,512]{1,0:T(8,128)(2,1)S(1)} fusion(bf16[1024,512]{1,0:T(8,128)(2,1)S(1)} %copy.75, s32[2048]{0:T(1024)S(1)} %pad_clamp_fusion), kind=kCustom, calls=%fused_computation.8 | custom fusion | bytes 3151872 | tf_op jit(solution)/shard_map/jit(_take)/gather | solution.py:138
  317.2 30.5 %all_to_all.25 = bf16[32,48,512]{2,1,0:T(8,128)(2,1)S(1)} all-to-all(bf16[32,48,512]{2,1,0:T(8,128)(2,1)S(1)} %bitcast.231), channel_id=1, replica_groups=mesh['ctx'=32,'head'=4] {'ctx'}, dimensions={0} | all-to-all | bytes 3145728 | tf_op jit(solution)/shard_map/all_to_all | solution.py:139
  347.6 5.0 %gather_fusion.9 = bf16[1024,512]{1,0:T(8,128)(2,1)} fusion(bf16[1536,512]{1,0:T(8,128)(2,1)S(1)} %bitcast.217, s32[1024]{0:T(1024)S(1)} %broadcast_clamp_fusion), kind=kCustom, calls=%fused_computation.9 | custom fusion | bytes 2101248 | tf_op jit(solution)/shard_map/jit(_take)/gather | solution.py:140
  352.7 6.1 %fusion.164 = (bf16[4,4,128,1024]{3,2,1,0:T(8,128)(2,1)}, bf16[4,4,128,1024]{3,2,1,0:T(8,128)(2,1)}) fusion(bf16[4,8,128,1024]{3,2,1,0:T(8,128)(2,1)} %bitcast.227), kind=kLoop, calls=%fused_computation.258 | loop fusion | bytes 16777216 | tf_op jit(solution)/shard_map/slice | solution.py:144
  358.8 10.6 %fusion.171 = f32[1024,1024]{1,0:T(8,128)} fusion(bf16[1024,2048]{1,0:T(8,128)(2,1)} %all-gather.5.cloned.1.call-done, bf16[2048,1024]{1,0:T(8,128)(2,1)} %bitcast.233), kind=kOutput, calls=%fused_computation.265 | convolution fusion | flops 4294967296 | bytes 12582912 | tf_op jit(solution)/shard_map/dot_general | solution.py:142
  369.4 30.2 %all-gather.7.cloned.1.call-done = bf16[1024,2048]{1,0:T(8,128)(2,1)} async-done(((bf16[1024,512]{1,0:T(8,128)(2,1)}), bf16[1024,2048]{1,0:T(8,128)(2,1)}) %all-gather.7.cloned.1.call-update) | async-done | bytes 4194320 | tf_op jit(solution)/shard_map/all_gather | solution.py:141
  399.6 10.6 %add_convert_fusion = bf16[1024,1024]{1,0:T(8,128)(2,1)} fusion(f32[1024,1024]{1,0:T(8,128)} %fusion.171, bf16[1024,2048]{1,0:T(8,128)(2,1)} %all-gather.7.cloned.1.call-done, bf16[2048,1024]{1,0:T(8,128)(2,1)} %bitcast.232), kind=kOutput, calls=%fused_computation.26 | convolution fusion | flops 4297064448 | bytes 14680064 | tf_op jit(solution)/shard_map/dot_general | solution.py:142
  (152 shorter events, 44.6 us)
Async XLA Ops:
  6.5 2.5 copy-start
  14.8 8.8 %copy-start.2 = (bf16[1024,1024]{1,0:T(8,128)(2,1)S(1)}, bf16[1024,1024]{1,0:T(8,128)(2,1)}, u32[]{:S(2)}) copy-start(bf16[1024,1024]{1,0:T(8,128)(2,1)} %param.9) | copy-start | bytes 6291460
  14.8 48.6 %all-to-all-start.2 = ((bf16[32,48,1024]{2,1,0:T(8,128)(2,1)}), bf16[32,48,1024]{2,1,0:T(8,128)(2,1)}, u32[]{:S(2)}, u32[]{:S(2)}) async-start(bf16[32,48,1024]{2,1,0:T(8,128)(2,1)} %bitcast.224), calls=%async_computation.2 | async-start | bytes 6291456 | tf_op jit(solution)/shard_map/all_to_all | solution.py:67
  29.5 39.0 %copy-start.24 = (s32[32]{0:T(128)S(1)}, s32[32]{0:T(128)}, u32[]{:S(2)}) copy-start(s32[32]{0:T(128)} %param.11) | copy-start | bytes 388
  29.5 44.9 %copy-start.3 = (bf16[1024,1024]{1,0:T(8,128)(2,1)S(1)}, bf16[1024,1024]{1,0:T(8,128)(2,1)}, u32[]{:S(2)}) copy-start(bf16[1024,1024]{1,0:T(8,128)(2,1)} %param.8) | copy-start | bytes 6291460
  63.4 44.9 %all-to-all-start.1 = ((bf16[32,48,1024]{2,1,0:T(8,128)(2,1)}), bf16[32,48,1024]{2,1,0:T(8,128)(2,1)}, u32[]{:S(2)}, u32[]{:S(2)}) async-start(bf16[32,48,1024]{2,1,0:T(8,128)(2,1)} %bitcast.223), calls=%async_computation.1 | async-start | bytes 6291456 | tf_op jit(solution)/shard_map/all_to_all | solution.py:67
  80.2 35.8 %copy-start.25 = (f32[8]{0:T(128)S(1)}, f32[8]{0:T(128)}, u32[]{:S(2)}) copy-start(f32[8]{0:T(128)} %param.12) | copy-start | bytes 100
  108.3 45.0 %all-to-all-start = ((bf16[32,48,1024]{2,1,0:T(8,128)(2,1)}), bf16[32,48,1024]{2,1,0:T(8,128)(2,1)S(1)}, u32[]{:S(2)}, u32[]{:S(2)}) async-start(bf16[32,48,1024]{2,1,0:T(8,128)(2,1)} %bitcast.222), calls=%async_computation | async-start | bytes 6291456 | tf_op jit(solution)/shard_map/all_to_all | solution.py:67
  141.5 4.5 %copy-start.4 = (bf16[128,8,8,128]{3,2,1,0:T(8,128)(2,1)S(1)}, bf16[128,8,8,128]{3,2,1,0:T(8,128)(2,1)}, u32[]{:S(2)}) copy-start(bf16[128,8,8,128]{3,2,1,0:T(8,128)(2,1)} %copy.107) | copy-start | bytes 6291460
  159.0 4.0 copy-start.5
  169.1 3.6 copy-start.13
  169.2 4.3 %copy-start.12 = (bf16[1024,1,128]{2,1,0:T(2,128)(2,1)S(1)}, bf16[1024,1,128]{2,1,0:T(2,128)(2,1)}, u32[]{:S(2)}) copy-start(bf16[1024,1,128]{2,1,0:T(2,128)(2,1)} %get-tuple-element.128) | copy-start | bytes 786436
  169.2 5.1 %copy-start.11 = (bf16[1024,1,128]{2,1,0:T(2,128)(2,1)S(1)}, bf16[1024,1,128]{2,1,0:T(2,128)(2,1)}, u32[]{:S(2)}) copy-start(bf16[1024,1,128]{2,1,0:T(2,128)(2,1)} %get-tuple-element.129) | copy-start | bytes 786436
  169.2 5.1 %copy-start.10 = (bf16[1024,1,128]{2,1,0:T(2,128)(2,1)S(1)}, bf16[1024,1,128]{2,1,0:T(2,128)(2,1)}, u32[]{:S(2)}) copy-start(bf16[1024,1,128]{2,1,0:T(2,128)(2,1)} %get-tuple-element.130) | copy-start | bytes 786436
  169.2 5.1 %copy-start.9 = (bf16[1024,1,128]{2,1,0:T(2,128)(2,1)S(1)}, bf16[1024,1,128]{2,1,0:T(2,128)(2,1)}, u32[]{:S(2)}) copy-start(bf16[1024,1,128]{2,1,0:T(2,128)(2,1)} %get-tuple-element.131) | copy-start | bytes 786436
  169.2 5.2 %copy-start.8 = (bf16[1024,1,128]{2,1,0:T(2,128)(2,1)S(1)}, bf16[1024,1,128]{2,1,0:T(2,128)(2,1)}, u32[]{:S(2)}) copy-start(bf16[1024,1,128]{2,1,0:T(2,128)(2,1)} %get-tuple-element.132) | copy-start | bytes 786436
  174.5 6.7 %collective-permute-start = (f32[4,129,128]{2,1,0:T(8,128)S(1)}, f32[4,129,128]{2,1,0:T(8,128)S(1)}, u32[]{:S(2)}, u32[]{:S(2)}) collective-permute-start(f32[4,129,128]{2,1,0:T(8,128)S(1)} %pad_maximum_fusion), channel_id=1, source_target_pairs={{0,4},{4,8},{8,12},{12,16},{16,20},{20,24},{24,28},{28,32},{32,36}... | collective-permute-start | bytes 792584 | tf_op jit(solution)/shard_map/ppermute | solution.py:116
  181.2 5.3 %collective-permute-start.1 = (f32[4,129,128]{2,1,0:T(8,128)S(1)}, f32[4,129,128]{2,1,0:T(8,128)S(1)}, u32[]{:S(2)}, u32[]{:S(2)}) collective-permute-start(f32[4,129,128]{2,1,0:T(8,128)S(1)} %select_add_fusion.7), channel_id=1, source_target_pairs={{0,8},{4,12},{8,16},{12,20},{16,24},{20,28},{24,32},{28,36},{32,40... | collective-permute-start | bytes 792584 | tf_op jit(solution)/shard_map/ppermute | solution.py:116
  186.6 9.3 %collective-permute-start.2 = (f32[4,129,128]{2,1,0:T(8,128)S(1)}, f32[4,129,128]{2,1,0:T(8,128)S(1)}, u32[]{:S(2)}, u32[]{:S(2)}) collective-permute-start(f32[4,129,128]{2,1,0:T(8,128)S(1)} %select_add_fusion.6), channel_id=1, source_target_pairs={{0,16},{4,20},{8,24},{12,28},{16,32},{20,36},{24,40},{28,44},{32,4... | collective-permute-start | bytes 792584 | tf_op jit(solution)/shard_map/ppermute | solution.py:116
  196.0 9.2 %collective-permute-start.3 = (f32[4,129,128]{2,1,0:T(8,128)S(1)}, f32[4,129,128]{2,1,0:T(8,128)S(1)}, u32[]{:S(2)}, u32[]{:S(2)}) collective-permute-start(f32[4,129,128]{2,1,0:T(8,128)S(1)} %select_add_fusion.5), channel_id=1, source_target_pairs={{0,32},{4,36},{8,40},{12,44},{16,48},{20,52},{24,56},{28,60},{32,6... | collective-permute-start | bytes 792584 | tf_op jit(solution)/shard_map/ppermute | solution.py:116
  205.2 10.0 %collective-permute-start.4 = (f32[4,129,128]{2,1,0:T(8,128)S(1)}, f32[4,129,128]{2,1,0:T(8,128)S(1)}, u32[]{:S(2)}, u32[]{:S(2)}) collective-permute-start(f32[4,129,128]{2,1,0:T(8,128)S(1)} %select_add_fusion.4), channel_id=1, source_target_pairs={{0,64},{4,68},{8,72},{12,76},{16,80},{20,84},{24,88},{28,92},{32,9... | collective-permute-start | bytes 792584 | tf_op jit(solution)/shard_map/ppermute | solution.py:116
  211.3 4.0 copy-start.15
  223.5 27.2 %collective-permute-start.5 = (f32[4,129,128]{2,1,0:T(8,128)S(1)}, f32[4,129,128]{2,1,0:T(8,128)S(1)}, u32[]{:S(2)}, u32[]{:S(2)}) collective-permute-start(f32[4,129,128]{2,1,0:T(8,128)S(1)} %pad_maximum_fusion.1), channel_id=1, source_target_pairs={{0,4},{4,8},{8,12},{12,16},{16,20},{20,24},{24,28},{28,32},{32,36}... | collective-permute-start | bytes 792584 | tf_op jit(solution)/shard_map/ppermute | solution.py:116
  236.2 41.9 %all-to-all-start.3 = ((bf16[32,48,512]{2,1,0:T(8,128)(2,1)}), bf16[32,48,512]{2,1,0:T(8,128)(2,1)S(1)}, u32[]{:S(2)}, u32[]{:S(2)}) async-start(bf16[32,48,512]{2,1,0:T(8,128)(2,1)} %bitcast.39), calls=%async_computation.3 | async-start | bytes 3145728 | tf_op jit(solution)/shard_map/all_to_all | solution.py:139
  246.7 112.0 %all-gather.5.cloned.1.call-start = ((), (), s32[]{:S(2)}) async-start(), calls=%async_computation.5 | async-start | bytes 5242880 | tf_op jit(solution)/shard_map/all_gather | solution.py:141
  246.8 2.3 copy-start.21
  249.1 5.1 %copy-start.18 = (bf16[1024,1,128]{2,0,1:T(8,128)(2,1)S(1)}, bf16[1024,1,128]{2,0,1:T(8,128)(2,1)}, u32[]{:S(2)}) copy-start(bf16[1024,1,128]{2,0,1:T(8,128)(2,1)} %copy.99) | copy-start | bytes 786436
  249.1 5.1 %copy-start.19 = (bf16[1024,1,128]{2,0,1:T(8,128)(2,1)S(1)}, bf16[1024,1,128]{2,0,1:T(8,128)(2,1)}, u32[]{:S(2)}) copy-start(bf16[1024,1,128]{2,0,1:T(8,128)(2,1)} %copy.100) | copy-start | bytes 786436
  250.7 4.7 %copy-start.20 = (bf16[1024,1,128]{0,2,1:T(8,128)(2,1)S(1)}, bf16[1024,1,128]{0,2,1:T(8,128)(2,1)}, u32[]{:S(2)}) copy-start(bf16[1024,1,128]{0,2,1:T(8,128)(2,1)} %get-tuple-element.85) | copy-start | bytes 786436
  250.7 19.2 %collective-permute-start.6 = (f32[4,129,128]{2,1,0:T(8,128)S(1)}, f32[4,129,128]{2,1,0:T(8,128)S(1)}, u32[]{:S(2)}, u32[]{:S(2)}) collective-permute-start(f32[4,129,128]{2,1,0:T(8,128)S(1)} %select_add_fusion.3), channel_id=1, source_target_pairs={{0,8},{4,12},{8,16},{12,20},{16,24},{20,28},{24,32},{28,36},{32,40... | collective-permute-start | bytes 792584 | tf_op jit(solution)/shard_map/ppermute | solution.py:116
  255.5 21.0 %copy-start.7 = (bf16[1024,1,128]{2,1,0:T(2,128)(2,1)S(1)}, bf16[1024,1,128]{2,1,0:T(2,128)(2,1)}, u32[]{:S(2)}) copy-start(bf16[1024,1,128]{2,1,0:T(2,128)(2,1)} %get-tuple-element.125) | copy-start | bytes 786436
  255.5 21.1 %copy-start.6 = (bf16[1024,1,128]{2,1,0:T(2,128)(2,1)S(1)}, bf16[1024,1,128]{2,1,0:T(2,128)(2,1)}, u32[]{:S(2)}) copy-start(bf16[1024,1,128]{2,1,0:T(2,128)(2,1)} %get-tuple-element.126) | copy-start | bytes 786436
  269.9 13.5 %collective-permute-start.7 = (f32[4,129,128]{2,1,0:T(8,128)S(1)}, f32[4,129,128]{2,1,0:T(8,128)}, u32[]{:S(2)}, u32[]{:S(2)}) collective-permute-start(f32[4,129,128]{2,1,0:T(8,128)S(1)} %select_add_fusion.2), channel_id=1, source_target_pairs={{0,16},{4,20},{8,24},{12,28},{16,32},{20,36},{24,40},{28,44},{32,4... | collective-permute-start | bytes 792584 | tf_op jit(solution)/shard_map/ppermute | solution.py:116
  278.1 10.0 %copy-start.23 = (bf16[1024,1,128]{2,0,1:T(8,128)(2,1)S(1)}, bf16[1024,1,128]{2,0,1:T(8,128)(2,1)}, u32[]{:S(2)}) copy-start(bf16[1024,1,128]{2,0,1:T(8,128)(2,1)} %copy.101) | copy-start | bytes 786436
  283.4 116.1 %all-gather.7.cloned.1.call-start = ((), (), s32[]{:S(2)}) async-start(), calls=%async_computation.6 | async-start | bytes 5242880 | tf_op jit(solution)/shard_map/all_gather | solution.py:141
  283.5 5.9 %copy-start.17 = (bf16[1024,1,128]{0,2,1:T(8,128)(2,1)S(1)}, bf16[1024,1,128]{0,2,1:T(8,128)(2,1)}, u32[]{:S(2)}) copy-start(bf16[1024,1,128]{0,2,1:T(8,128)(2,1)} %get-tuple-element.90) | copy-start | bytes 786436
  283.5 8.0 %collective-permute-start.8 = (f32[4,129,128]{2,1,0:T(8,128)S(1)}, f32[4,129,128]{2,1,0:T(8,128)S(1)}, u32[]{:S(2)}, u32[]{:S(2)}) collective-permute-start(f32[4,129,128]{2,1,0:T(8,128)S(1)} %select_add_fusion.1), channel_id=1, source_target_pairs={{0,32},{4,36},{8,40},{12,44},{16,48},{20,52},{24,56},{28,60},{32,6... | collective-permute-start | bytes 792584 | tf_op jit(solution)/shard_map/ppermute | solution.py:116
  289.4 11.9 %copy-start.22 = (bf16[1024,1,128]{2,0,1:T(8,128)(2,1)S(1)}, bf16[1024,1,128]{2,0,1:T(8,128)(2,1)}, u32[]{:S(2)}) copy-start(bf16[1024,1,128]{2,0,1:T(8,128)(2,1)} %copy.104) | copy-start | bytes 786436
  291.6 10.9 %copy-start.16 = (bf16[1024,1,128]{0,2,1:T(8,128)(2,1)S(1)}, bf16[1024,1,128]{0,2,1:T(8,128)(2,1)}, u32[]{:S(2)}) copy-start(bf16[1024,1,128]{0,2,1:T(8,128)(2,1)} %get-tuple-element.95) | copy-start | bytes 786436
  291.6 14.4 %collective-permute-start.9 = (f32[4,129,128]{2,1,0:T(8,128)S(1)}, f32[4,129,128]{2,1,0:T(8,128)S(1)}, u32[]{:S(2)}, u32[]{:S(2)}) collective-permute-start(f32[4,129,128]{2,1,0:T(8,128)S(1)} %select_add_fusion), channel_id=1, source_target_pairs={{0,64},{4,68},{8,72},{12,76},{16,80},{20,84},{24,88},{28,92},{32,9... | collective-permute-start | bytes 792584 | tf_op jit(solution)/shard_map/ppermute | solution.py:116
  302.6 3.5 copy-start.14
  304.1 4.5 %copy-start.26 = (f32[1024,1,128]{0,2,1:T(8,128)S(1)}, f32[1024,1,128]{0,2,1:T(8,128)}, u32[]{:S(2)}) copy-start(f32[1024,1,128]{0,2,1:T(8,128)} %fusion.59) | copy-start | bytes 1572868
  304.1 4.5 %copy-start.27 = (f32[1024,1,128]{0,2,1:T(8,128)S(1)}, f32[1024,1,128]{0,2,1:T(8,128)}, u32[]{:S(2)}) copy-start(f32[1024,1,128]{0,2,1:T(8,128)} %fusion.58) | copy-start | bytes 1572868
  399.6 10.6 %copy-start.1 = (bf16[1024,1024]{1,0:T(8,128)(2,1)S(1)}, bf16[1024,1024]{1,0:T(8,128)(2,1)}, u32[]{:S(2)}) copy-start(bf16[1024,1024]{1,0:T(8,128)(2,1)} %param.7) | copy-start | bytes 6291460
Sparse Core Ops, SparseCore 0:
  283.5 50.8 all-gather.4
  352.8 46.6 all-gather.6

commit v15 on v14

--- a/solution.py
+++ b/solution.py
@@ -53,7 +53,7 @@
     causal = r_idx[:, None] >= r_idx[None, :]
     head_count = lax.axis_size("head")
     out_cols = out_weight.shape[1]
-    bounds = [0, heads // 2, heads]
+    bounds = [0, heads - (3 * heads) // 8, heads]
     weight_rows = out_weight.reshape(head_count, heads, dh, out_cols)
     gate_all = jax.nn.sigmoid(mem_gate)
     shifts = []

time: 422 us -> 430 us (1.019)
  matrix products: 58.7 us -> 67.9 us
  other arithmetic: 12.2 us -> 19.2 us
  waiting for transfers between devices: 115 us -> 109 us
  starting transfers between devices: 82.8 us -> 77.3 us
  local copies, waits for them, and re-layouts: 99.6 us -> 104 us
    all_to_all x1, waiting for transfers between devices: 0.01 us -> 12.8 us  [one_group(): lax.all_to_all(outgoing, 'ctx', 0, 0, tiled=True)]
    all_gather x2, waiting for transfers between devices: 30.2 us -> 18.3 us  [one_group(): gathered = lax.all_gather(rows, 'head', axis=1, tiled=True)]
    sub x0 -> x1, matrix products: none -> 7.96 us  [local_attention(): weights = jnp.exp(scores - row_max)]
    all_to_all x3, waiting for transfers between devices: 64.7 us -> 60.3 us  [dispatch(): got = lax.all_to_all(buffer, 'ctx', 0, 0, tiled=True).reshape(slots, width)]
    slice x1 -> x2, local copies, waits for them, and re-layouts: 6.06 us -> 9.52 us  [one_group(): weight_rows[:, first:last].reshape(head_count * group_width, out_cols)]
    dot_general x8 -> x7, matrix products: 12.2 us -> 13.4 us  [local_attention(): jnp.einsum('hqk,khd->qhd', probabilities, value_part, preferred_element_t...]
  transfers between devices with their start and end apart: 16 -> 16, of which waited for: 12 -> 9; matrix products, arithmetic and copies ran while one was open for 29% -> 37% of each run, Pallas kernels for 0% -> 0%
where the time goes in v15:
time: 430 us; the launch traced here: 423 us
  waiting for transfers between devices  109 us (25%)
  local copies, waits for them, and re-layouts  104 us (24%)
  starting transfers between devices  77.3 us (18%)
  matrix products  67.9 us (16%)
  blocking collectives  27.4 us (6%)
  other arithmetic  19.2 us (4%)
  between operations  17.7 us (4%)
    all_to_all x3, waiting for transfers between devices, dispatch(): got = lax.all_to_all(buffer, 'ctx', 0, 0, tiled=True).reshape(slots, width)  60.3 us
    ppermute x10, starting transfers between devices, one_group(): got = lax.ppermute(total, 'ctx', perm)  50.2 us
    all_to_all x1, blocking collectives, one_group(): lax.all_to_all(outgoing, 'ctx', 0, 0, tiled=True)  27.4 us
    gather x4, local copies, waits for them, and re-layouts, dispatch(): return jnp.take(got, tok_slot, axis=0, mode='clip').reshape(seg, heads, dh)  25.9 us
    dot_general x2, matrix products, one_group(): jnp.dot(gathered, weight_rows[:, first:last].reshape(head_count * group_w...  19.5 us
    all_to_all x3, starting transfers between devices, dispatch(): got = lax.all_to_all(buffer, 'ctx', 0, 0, tiled=True).reshape(slots, width)  19.1 us
    all_gather x2, waiting for transfers between devices, one_group(): gathered = lax.all_gather(rows, 'head', axis=1, tiled=True)  18.3 us
    ppermute x10, waiting for transfers between devices, one_group(): got = lax.ppermute(total, 'ctx', perm)  17.9 us
  transfers between devices with their start and end apart: 16, of which 9 were waited for; matrix products, arithmetic and copies ran while one was open for 37% of the time, Pallas kernels for 0%

profile of v15, /device:TPU:1, one launch (start us, length us, event | category | flops | bytes accessed | tf_op | source)
XLA Modules:
  0.0 422.8 jit_solution(5869128798970931603)
XLA Ops:
  9.0 5.8 %gather_fusion = bf16[1536,1024]{1,0:T(8,128)(2,1)} fusion(bf16[1024,1024]{1,0:T(8,128)(2,1)S(1)} %copy-done, s32[2048]{0:T(1024)S(1)} %pad_clamp_fusion.1), kind=kCustom, calls=%fused_computation | custom fusion | bytes 6297600 | tf_op jit(solution)/shard_map/jit(_take)/gather | solution.py:66
  14.8 8.8 %all-to-all-start = ((bf16[32,48,1024]{2,1,0:T(8,128)(2,1)}), bf16[32,48,1024]{2,1,0:T(8,128)(2,1)}, u32[]{:S(2)}, u32[]{:S(2)}) async-start(bf16[32,48,1024]{2,1,0:T(8,128)(2,1)} %bitcast.197), calls=%async_computation | async-start | bytes 6291456 | tf_op jit(solution)/shard_map/all_to_all | solution.py:67
  23.6 5.8 %gather_fusion.2 = bf16[1536,1024]{1,0:T(8,128)(2,1)} fusion(bf16[1024,1024]{1,0:T(8,128)(2,1)S(1)} %copy-done.2, s32[2048]{0:T(1024)S(1)} %pad_clamp_fusion.1), kind=kCustom, calls=%fused_computation.2 | custom fusion | bytes 6297600 | tf_op jit(solution)/shard_map/jit(_take)/gather | solution.py:66
  29.5 34.0 %all-to-all-done = bf16[32,48,1024]{2,1,0:T(8,128)(2,1)} async-done(((bf16[32,48,1024]{2,1,0:T(8,128)(2,1)}), bf16[32,48,1024]{2,1,0:T(8,128)(2,1)}, u32[]{:S(2)}, u32[]{:S(2)}) %all-to-all-start) | async-done | bytes 3145760 | tf_op jit(solution)/shard_map/all_to_all | solution.py:67
  63.4 5.0 %all-to-all-start.1 = ((bf16[32,48,1024]{2,1,0:T(8,128)(2,1)}), bf16[32,48,1024]{2,1,0:T(8,128)(2,1)}, u32[]{:S(2)}, u32[]{:S(2)}) async-start(bf16[32,48,1024]{2,1,0:T(8,128)(2,1)} %bitcast.196), calls=%async_computation.1 | async-start | bytes 6291456 | tf_op jit(solution)/shard_map/all_to_all | solution.py:67
  71.8 5.8 %gather_fusion.4 = bf16[1536,1024]{1,0:T(8,128)(2,1)} fusion(bf16[1024,1024]{1,0:T(8,128)(2,1)S(1)} %copy-done.3, s32[2048]{0:T(1024)S(1)} %pad_clamp_fusion.1), kind=kCustom, calls=%fused_computation.4 | custom fusion | bytes 6297600 | tf_op jit(solution)/shard_map/jit(_take)/gather | solution.py:66
  82.0 26.3 %all-to-all-done.1 = bf16[32,48,1024]{2,1,0:T(8,128)(2,1)} async-done(((bf16[32,48,1024]{2,1,0:T(8,128)(2,1)}), bf16[32,48,1024]{2,1,0:T(8,128)(2,1)}, u32[]{:S(2)}, u32[]{:S(2)}) %all-to-all-start.1) | async-done | bytes 3145760 | tf_op jit(solution)/shard_map/all_to_all | solution.py:67
  108.3 5.3 %all-to-all-start.2 = ((bf16[32,48,1024]{2,1,0:T(8,128)(2,1)}), bf16[32,48,1024]{2,1,0:T(8,128)(2,1)S(1)}, u32[]{:S(2)}, u32[]{:S(2)}) async-start(bf16[32,48,1024]{2,1,0:T(8,128)(2,1)} %bitcast.195), calls=%async_computation.2 | async-start | bytes 6291456 | tf_op jit(solution)/shard_map/all_to_all | solution.py:67
  116.3 8.3 %gather_fusion.1 = bf16[1024,1024]{1,0:T(8,128)(2,1)} fusion(bf16[1536,1024]{1,0:T(8,128)(2,1)} %bitcast.4, s32[1024]{0:T(1024)S(1)} %broadcast_clamp_fusion.1), kind=kCustom, calls=%fused_computation.1 | custom fusion | bytes 4198400 | tf_op jit(solution)/shard_map/jit(_take)/gather | solution.py:68
  124.7 3.5 copy.107
  128.2 8.3 %gather_fusion.3 = bf16[1024,1024]{1,0:T(8,128)(2,1)} fusion(bf16[1536,1024]{1,0:T(8,128)(2,1)} %bitcast.6, s32[1024]{0:T(1024)S(1)} %broadcast_clamp_fusion.1), kind=kCustom, calls=%fused_computation.3 | custom fusion | bytes 4198400 | tf_op jit(solution)/shard_map/jit(_take)/gather | solution.py:68
  136.5 3.9 copy.51
  140.4 2.8 fusion.33
  143.2 5.2 %fusion.34 = f32[5,128,128]{2,1,0:T(8,128)S(1)} fusion(bf16[1024,8,128]{0,2,1:T(8,128)(2,1)} %bitcast.202, bf16[1024,5,128]{2,1,0:T(8,128)(2,1)} %bitcast.186), kind=kOutput, calls=%fused_computation.82 | convolution fusion | flops 1009909760 | bytes 3735552 | tf_op jit(solution)/shard_map/khd,khe->hde/dot_general | solution.py:98
  149.2 3.9 collective-permute-start
  153.1 3.7 fusion.153
  156.8 5.3 %gather_fusion.5 = bf16[1024,1024]{1,0:T(8,128)(2,1)} fusion(bf16[1536,1024]{1,0:T(8,128)(2,1)S(1)} %bitcast.182, s32[1024]{0:T(1024)S(1)} %broadcast_clamp_fusion.1), kind=kCustom, calls=%fused_computation.5 | custom fusion | bytes 4198400 | tf_op jit(solution)/shard_map/jit(_take)/gather | solution.py:68
  164.4 3.0 fusion.154
  176.4 3.1 collective-permute-start.1
  182.4 4.7 %collective-permute-done.1 = f32[5,129,128]{2,1,0:T(8,128)S(1)} collective-permute-done((f32[5,129,128]{2,1,0:T(8,128)S(1)}, f32[5,129,128]{2,1,0:T(8,128)S(1)}, u32[]{:S(2)}, u32[]{:S(2)}) %collective-permute-start.1) | collective-permute-done | bytes 330272 | tf_op jit(solution)/shard_map/ppermute | solution.py:116
  187.1 5.5 %collective-permute-start.2 = (f32[5,129,128]{2,1,0:T(8,128)S(1)}, f32[5,129,128]{2,1,0:T(8,128)S(1)}, u32[]{:S(2)}, u32[]{:S(2)}) collective-permute-start(f32[5,129,128]{2,1,0:T(8,128)S(1)} %select_add_fusion.2), channel_id=1, source_target_pairs={{0,16},{4,20},{8,24},{12,28},{16,32},{20,36},{24,40},{28,44},{32,4... | collective-permute-start | bytes 990728 | tf_op jit(solution)/shard_map/ppermute | solution.py:116
  195.3 4.3 %collective-permute-done.2 = f32[5,129,128]{2,1,0:T(8,128)S(1)} collective-permute-done((f32[5,129,128]{2,1,0:T(8,128)S(1)}, f32[5,129,128]{2,1,0:T(8,128)S(1)}, u32[]{:S(2)}, u32[]{:S(2)}) %collective-permute-start.2) | collective-permute-done | bytes 330272 | tf_op jit(solution)/shard_map/ppermute | solution.py:116
  200.4 7.0 %collective-permute-start.3 = (f32[5,129,128]{2,1,0:T(8,128)}, f32[5,129,128]{2,1,0:T(8,128)}, u32[]{:S(2)}, u32[]{:S(2)}) collective-permute-start(f32[5,129,128]{2,1,0:T(8,128)} %select_add_fusion.1), channel_id=1, source_target_pairs={{0,32},{4,36},{8,40},{12,44},{16,48},{20,52},{24,56},{28,60},{32,6... | collective-permute-start | bytes 990728 | tf_op jit(solution)/shard_map/ppermute | solution.py:116
  207.4 8.0 %fusion.157 = (f32[2,1024]{1,0:T(2,128)S(1)}, f32[2,1024,1024]{1,2,0:T(8,128)}) fusion(pred[1024,1024]{0,1:T(8,128)(4,1)} %iota_compare_fusion.3, bf16[1024,2,128]{2,0,1:T(8,128)(2,1)} %copy.93, bf16[1024,2,128]{2,0,1:T(8,128)(2,1)} %copy.94), kind=kOutput, calls=%fused_computation.249 | convolution fusion | flops 545260544 | bytes 10493952 | tf_op jit(solution)/shard_map/sub | solution.py:80
  215.4 4.3 %fusion.55 = f32[1024,2,128]{0,2,1:T(8,128)S(1)} fusion(bf16[1024,2,128]{0,2,1:T(8,128)(2,1)} %slice.191, f32[2,1024,1024]{1,2,0:T(8,128)} %get-tuple-element.121, f32[2,1024]{1,0:T(2,128)S(1)} %get-tuple-element.120), kind=kOutput, calls=%fused_computation.101 | convolution fusion | flops 541065216 | bytes 9969664 | tf_op jit(solution)/shard_map/hqk,khd->qhd/dot_general | solution.py:82
  220.7 4.8 %collective-permute-start.4 = (f32[5,129,128]{2,1,0:T(8,128)S(1)}, f32[5,129,128]{2,1,0:T(8,128)S(1)}, u32[]{:S(2)}, u32[]{:S(2)}) collective-permute-start(f32[5,129,128]{2,1,0:T(8,128)S(1)} %select_add_fusion), channel_id=1, source_target_pairs={{0,64},{4,68},{8,72},{12,76},{16,80},{20,84},{24,88},{28,92},{32,9... | collective-permute-start | bytes 990728 | tf_op jit(solution)/shard_map/ppermute | solution.py:116
  228.4 3.1 collective-permute-done.4
  231.5 3.1 fusion.29
  234.7 5.0 %fusion.27 = bf16[1024,5,128]{0,2,1:T(8,128)(2,1)} fusion(f32[1024,1,128]{0,2,1:T(8,128)S(1)} %fusion.66, f32[1024,2,128]{0,2,1:T(8,128)S(1)} %fusion.55, f32[1024,1,128]{0,2,1:T(8,128)S(1)} %copy-done.23, f32[1024,1,128]{0,2,1:T(8,128)S(1)} %copy-done.22, f32[5]{0:T(128)S(1)} %get-tuple-element.115, f32[1024,5]{0,1:T(8,128)S(1)} %fusion.120, ...), kind=kOutput, calls=%fused_computation.76 | convolution fusion | flops 1015152640 | bytes 6390784 | tf_op jit(solution)/shard_map/qhd,hde->qhe/dot_general | solution.py:128
  241.4 5.6 %gather_fusion.6 = bf16[1536,640]{1,0:T(8,128)(2,1)} fusion(bf16[1024,640]{1,0:T(8,128)(2,1)S(1)} %copy.65, s32[2048]{0:T(1024)S(1)} %pad_clamp_fusion), kind=kCustom, calls=%fused_computation.6 | custom fusion | bytes 3938304 | tf_op jit(solution)/shard_map/jit(_take)/gather | solution.py:138
  246.9 7.7 %all-to-all-start.3 = ((bf16[32,48,640]{2,1,0:T(8,128)(2,1)}), bf16[32,48,640]{2,1,0:T(8,128)(2,1)S(1)}, u32[]{:S(2)}, u32[]{:S(2)}) async-start(bf16[32,48,640]{2,1,0:T(8,128)(2,1)} %bitcast.206), calls=%async_computation.3 | async-start | bytes 3932160 | tf_op jit(solution)/shard_map/all_to_all | solution.py:139
  262.1 3.1 fusion.53
  265.3 3.5 collective-permute-start.5
  268.8 12.8 %all-to-all-done.3 = bf16[32,48,640]{2,1,0:T(8,128)(2,1)S(1)} async-done(((bf16[32,48,640]{2,1,0:T(8,128)(2,1)}), bf16[32,48,640]{2,1,0:T(8,128)(2,1)S(1)}, u32[]{:S(2)}, u32[]{:S(2)}) %all-to-all-start.3) | async-done | bytes 1966112 | tf_op jit(solution)/shard_map/all_to_all | solution.py:139
  281.6 5.2 %gather_fusion.7 = bf16[1024,640]{1,0:T(8,128)(2,1)} fusion(bf16[1536,640]{1,0:T(8,128)(2,1)S(1)} %bitcast.183, s32[1024]{0:T(1024)S(1)} %broadcast_clamp_fusion), kind=kCustom, calls=%fused_computation.7 | custom fusion | bytes 2625536 | tf_op jit(solution)/shard_map/jit(_take)/gather | solution.py:140
  293.0 3.5 collective-permute-done.6
  296.6 5.4 %collective-permute-start.7 = (f32[3,129,128]{2,1,0:T(8,128)S(1)}, f32[3,129,128]{2,1,0:T(8,128)S(1)}, u32[]{:S(2)}, u32[]{:S(2)}) collective-permute-start(f32[3,129,128]{2,1,0:T(8,128)S(1)} %select_add_fusion.6), channel_id=1, source_target_pairs={{0,16},{4,20},{8,24},{12,28},{16,32},{20,36},{24,40},{28,44},{32,4... | collective-permute-start | bytes 594440 | tf_op jit(solution)/shard_map/ppermute | solution.py:116
  304.8 9.9 %collective-permute-start.8 = (f32[3,129,128]{2,1,0:T(8,128)S(1)}, f32[3,129,128]{2,1,0:T(8,128)S(1)}, u32[]{:S(2)}, u32[]{:S(2)}) collective-permute-start(f32[3,129,128]{2,1,0:T(8,128)S(1)} %select_add_fusion.5), channel_id=1, source_target_pairs={{0,32},{4,36},{8,40},{12,44},{16,48},{20,52},{24,56},{28,60},{32,6... | collective-permute-start | bytes 594440 | tf_op jit(solution)/shard_map/ppermute | solution.py:116
  317.8 5.8 %collective-permute-start.9 = (f32[3,129,128]{2,1,0:T(8,128)S(1)}, f32[3,129,128]{2,1,0:T(8,128)S(1)}, u32[]{:S(2)}, u32[]{:S(2)}) collective-permute-start(f32[3,129,128]{2,1,0:T(8,128)S(1)} %select_add_fusion.4), channel_id=1, source_target_pairs={{0,64},{4,68},{8,72},{12,76},{16,80},{20,84},{24,88},{28,92},{32,9... | collective-permute-start | bytes 594440 | tf_op jit(solution)/shard_map/ppermute | solution.py:116
  328.4 2.4 fusion.47
  331.1 4.7 %gather_fusion.8 = bf16[1536,384]{1,0:T(8,128)(2,1)S(1)} fusion(bf16[1024,384]{1,0:T(8,128)(2,1)S(1)} %copy.77, s32[2048]{0:T(1024)S(1)} %pad_clamp_fusion), kind=kCustom, calls=%fused_computation.8 | custom fusion | bytes 2365440 | tf_op jit(solution)/shard_map/jit(_take)/gather | solution.py:138
  335.8 27.4 %all_to_all.25 = bf16[32,48,384]{2,1,0:T(8,128)(2,1)S(1)} all-to-all(bf16[32,48,384]{2,1,0:T(8,128)(2,1)S(1)} %bitcast.208), channel_id=1, replica_groups=mesh['ctx'=32,'head'=4] {'ctx'}, dimensions={0} | all-to-all | bytes 2359296 | tf_op jit(solution)/shard_map/all_to_all | solution.py:139
  363.2 5.0 %gather_fusion.9 = bf16[1024,384]{1,0:T(8,128)(2,1)} fusion(bf16[1536,384]{1,0:T(8,128)(2,1)S(1)} %bitcast.184, s32[1024]{0:T(1024)S(1)} %broadcast_clamp_fusion), kind=kCustom, calls=%fused_computation.9 | custom fusion | bytes 1576960 | tf_op jit(solution)/shard_map/jit(_take)/gather | solution.py:140
  368.2 5.7 %slice.198 = bf16[4,5,128,1024]{3,2,1,0:T(8,128)(2,1)} slice(bf16[4,8,128,1024]{3,2,1,0:T(8,128)(2,1)} %bitcast.200), slice={[0:4], [0:5], [0:128], [0:1024]} | slice | bytes 10485760 | tf_op jit(solution)/shard_map/slice | solution.py:144
  373.9 3.9 slice.213
  377.8 10.6 %fusion.158 = f32[1024,1024]{1,0:T(8,128)} fusion(bf16[1024,2560]{1,0:T(8,128)(2,1)} %all-gather.5.cloned.1.call-done, bf16[2560,1024]{1,0:T(8,128)(2,1)} %bitcast.207), kind=kOutput, calls=%fused_computation.250 | convolution fusion | flops 5368709120 | bytes 14680064 | tf_op jit(solution)/shard_map/dot_general | solution.py:142
  388.3 18.3 %all-gather.7.cloned.1.call-done = bf16[1024,1536]{1,0:T(8,128)(2,1)} async-done(((bf16[1024,384]{1,0:T(8,128)(2,1)}), bf16[1024,1536]{1,0:T(8,128)(2,1)}) %all-gather.7.cloned.1.call-update) | async-done | bytes 3145744 | tf_op jit(solution)/shard_map/all_gather | solution.py:141
  406.6 8.9 %add_convert_fusion = bf16[1024,1024]{1,0:T(8,128)(2,1)} fusion(f32[1024,1024]{1,0:T(8,128)} %fusion.158, bf16[1024,1536]{1,0:T(8,128)(2,1)} %all-gather.7.cloned.1.call-done, bf16[1536,1024]{1,0:T(8,128)(2,1)} %bitcast.209), kind=kOutput, calls=%fused_computation.31 | convolution fusion | flops 3223322624 | bytes 12582912 | tf_op jit(solution)/shard_map/dot_general | solution.py:142
  (146 shorter events, 58.4 us)
Async XLA Ops:
  6.5 2.5 copy-start
  7.6 60.9 %copy-start.13 = (s32[32,1024]{1,0:T(8,128)}, s32[32,1024]{1,0:T(8,128)S(1)}, u32[]{:S(2)}) copy-start(s32[32,1024]{1,0:T(8,128)S(1)} %reshape.423) | copy-start | bytes 393220
  14.8 8.8 %copy-start.2 = (bf16[1024,1024]{1,0:T(8,128)(2,1)S(1)}, bf16[1024,1024]{1,0:T(8,128)(2,1)}, u32[]{:S(2)}) copy-start(bf16[1024,1024]{1,0:T(8,128)(2,1)} %param.9) | copy-start | bytes 6291460
  14.8 48.6 %all-to-all-start = ((bf16[32,48,1024]{2,1,0:T(8,128)(2,1)}), bf16[32,48,1024]{2,1,0:T(8,128)(2,1)}, u32[]{:S(2)}, u32[]{:S(2)}) async-start(bf16[32,48,1024]{2,1,0:T(8,128)(2,1)} %bitcast.197), calls=%async_computation | async-start | bytes 6291456 | tf_op jit(solution)/shard_map/all_to_all | solution.py:67
  29.5 41.8 %copy-start.20 = (s32[32]{0:T(128)S(1)}, s32[32]{0:T(128)}, u32[]{:S(2)}) copy-start(s32[32]{0:T(128)} %param.11) | copy-start | bytes 388
  29.5 42.4 %copy-start.3 = (bf16[1024,1024]{1,0:T(8,128)(2,1)S(1)}, bf16[1024,1024]{1,0:T(8,128)(2,1)}, u32[]{:S(2)}) copy-start(bf16[1024,1024]{1,0:T(8,128)(2,1)} %param.7) | copy-start | bytes 6291460
  63.4 44.9 %all-to-all-start.1 = ((bf16[32,48,1024]{2,1,0:T(8,128)(2,1)}), bf16[32,48,1024]{2,1,0:T(8,128)(2,1)}, u32[]{:S(2)}, u32[]{:S(2)}) async-start(bf16[32,48,1024]{2,1,0:T(8,128)(2,1)} %bitcast.196), calls=%async_computation.1 | async-start | bytes 6291456 | tf_op jit(solution)/shard_map/all_to_all | solution.py:67
  77.7 37.3 %copy-start.21 = (f32[8]{0:T(128)S(1)}, f32[8]{0:T(128)}, u32[]{:S(2)}) copy-start(f32[8]{0:T(128)} %param.12) | copy-start | bytes 100
  108.3 48.5 %all-to-all-start.2 = ((bf16[32,48,1024]{2,1,0:T(8,128)(2,1)}), bf16[32,48,1024]{2,1,0:T(8,128)(2,1)S(1)}, u32[]{:S(2)}, u32[]{:S(2)}) async-start(bf16[32,48,1024]{2,1,0:T(8,128)(2,1)} %bitcast.195), calls=%async_computation.2 | async-start | bytes 6291456 | tf_op jit(solution)/shard_map/all_to_all | solution.py:67
  143.2 9.9 %copy-start.4 = (bf16[128,8,8,128]{3,2,1,0:T(8,128)(2,1)S(1)}, bf16[128,8,8,128]{3,2,1,0:T(8,128)(2,1)}, u32[]{:S(2)}) copy-start(bf16[128,8,8,128]{3,2,1,0:T(8,128)(2,1)} %copy.107) | copy-start | bytes 6291460
  149.2 26.2 %collective-permute-start = (f32[5,129,128]{2,1,0:T(8,128)}, f32[5,129,128]{2,1,0:T(8,128)}, u32[]{:S(2)}, u32[]{:S(2)}) collective-permute-start(f32[5,129,128]{2,1,0:T(8,128)} %pad_maximum_fusion), channel_id=1, source_target_pairs={{0,4},{4,8},{8,12},{12,16},{16,20},{20,24},{24,28},{28,32},{32,36}... | collective-permute-start | bytes 990728 | tf_op jit(solution)/shard_map/ppermute | solution.py:116
  164.4 70.3 %copy-start.5 = (bf16[128,8,8,128]{3,2,1,0:T(8,128)(2,1)}, bf16[128,8,8,128]{3,2,1,0:T(8,128)(2,1)S(1)}, u32[]{:S(2)}) copy-start(bf16[128,8,8,128]{3,2,1,0:T(8,128)(2,1)S(1)} %copy.108) | copy-start | bytes 6291460
  164.4 3.6 copy-start.7
  164.4 6.6 %copy-start.12 = (bf16[1024,1,128]{2,1,0:T(2,128)(2,1)S(1)}, bf16[1024,1,128]{2,1,0:T(2,128)(2,1)}, u32[]{:S(2)}) copy-start(bf16[1024,1,128]{2,1,0:T(2,128)(2,1)} %get-tuple-element.104) | copy-start | bytes 786436
  167.4 3.7 copy-start.11
  168.0 5.7 %copy-start.10 = (bf16[1024,1,128]{2,1,0:T(2,128)(2,1)S(1)}, bf16[1024,1,128]{2,1,0:T(2,128)(2,1)}, u32[]{:S(2)}) copy-start(bf16[1024,1,128]{2,1,0:T(2,128)(2,1)} %get-tuple-element.102) | copy-start | bytes 786436
  176.4 10.6 %collective-permute-start.1 = (f32[5,129,128]{2,1,0:T(8,128)S(1)}, f32[5,129,128]{2,1,0:T(8,128)S(1)}, u32[]{:S(2)}, u32[]{:S(2)}) collective-permute-start(f32[5,129,128]{2,1,0:T(8,128)S(1)} %select_add_fusion.3), channel_id=1, source_target_pairs={{0,8},{4,12},{8,16},{12,20},{16,24},{20,28},{24,32},{28,36},{32,40... | collective-permute-start | bytes 990728 | tf_op jit(solution)/shard_map/ppermute | solution.py:116
  187.1 12.6 %collective-permute-start.2 = (f32[5,129,128]{2,1,0:T(8,128)S(1)}, f32[5,129,128]{2,1,0:T(8,128)S(1)}, u32[]{:S(2)}, u32[]{:S(2)}) collective-permute-start(f32[5,129,128]{2,1,0:T(8,128)S(1)} %select_add_fusion.2), channel_id=1, source_target_pairs={{0,16},{4,20},{8,24},{12,28},{16,32},{20,36},{24,40},{28,44},{32,4... | collective-permute-start | bytes 990728 | tf_op jit(solution)/shard_map/ppermute | solution.py:116
  200.4 19.3 %collective-permute-start.3 = (f32[5,129,128]{2,1,0:T(8,128)}, f32[5,129,128]{2,1,0:T(8,128)}, u32[]{:S(2)}, u32[]{:S(2)}) collective-permute-start(f32[5,129,128]{2,1,0:T(8,128)} %select_add_fusion.1), channel_id=1, source_target_pairs={{0,32},{4,36},{8,40},{12,44},{16,48},{20,52},{24,56},{28,60},{32,6... | collective-permute-start | bytes 990728 | tf_op jit(solution)/shard_map/ppermute | solution.py:116
  215.4 10.2 %copy-start.17 = (bf16[1024,1,128]{2,0,1:T(8,128)(2,1)S(1)}, bf16[1024,1,128]{2,0,1:T(8,128)(2,1)}, u32[]{:S(2)}) copy-start(bf16[1024,1,128]{2,0,1:T(8,128)(2,1)} %copy.95) | copy-start | bytes 786436
  215.4 10.2 %copy-start.18 = (bf16[1024,1,128]{2,0,1:T(8,128)(2,1)S(1)}, bf16[1024,1,128]{2,0,1:T(8,128)(2,1)}, u32[]{:S(2)}) copy-start(bf16[1024,1,128]{2,0,1:T(8,128)(2,1)} %copy.96) | copy-start | bytes 786436
  220.7 6.1 %copy-start.19 = (bf16[1024,1,128]{0,2,1:T(8,128)(2,1)S(1)}, bf16[1024,1,128]{0,2,1:T(8,128)(2,1)}, u32[]{:S(2)}) copy-start(bf16[1024,1,128]{0,2,1:T(8,128)(2,1)} %get-tuple-element.64) | copy-start | bytes 786436
  220.7 10.7 %collective-permute-start.4 = (f32[5,129,128]{2,1,0:T(8,128)S(1)}, f32[5,129,128]{2,1,0:T(8,128)S(1)}, u32[]{:S(2)}, u32[]{:S(2)}) collective-permute-start(f32[5,129,128]{2,1,0:T(8,128)S(1)} %select_add_fusion), channel_id=1, source_target_pairs={{0,64},{4,68},{8,72},{12,76},{16,80},{20,84},{24,88},{28,92},{32,9... | collective-permute-start | bytes 990728 | tf_op jit(solution)/shard_map/ppermute | solution.py:116
  228.4 6.3 %copy-start.22 = (f32[1024,1,128]{0,2,1:T(8,128)S(1)}, f32[1024,1,128]{0,2,1:T(8,128)}, u32[]{:S(2)}) copy-start(f32[1024,1,128]{0,2,1:T(8,128)} %fusion.68) | copy-start | bytes 1572868
  228.4 6.3 %copy-start.23 = (f32[1024,1,128]{0,2,1:T(8,128)S(1)}, f32[1024,1,128]{0,2,1:T(8,128)}, u32[]{:S(2)}) copy-start(f32[1024,1,128]{0,2,1:T(8,128)} %fusion.67) | copy-start | bytes 1572868
  246.9 34.6 %all-to-all-start.3 = ((bf16[32,48,640]{2,1,0:T(8,128)(2,1)}), bf16[32,48,640]{2,1,0:T(8,128)(2,1)S(1)}, u32[]{:S(2)}, u32[]{:S(2)}) async-start(bf16[32,48,640]{2,1,0:T(8,128)(2,1)} %bitcast.206), calls=%async_computation.3 | async-start | bytes 3932160 | tf_op jit(solution)/shard_map/all_to_all | solution.py:139
  254.6 123.1 %all-gather.5.cloned.1.call-start = ((), (), s32[]{:S(2)}) async-start(), calls=%async_computation.5 | async-start | bytes 6553600 | tf_op jit(solution)/shard_map/all_gather | solution.py:141
  265.3 25.4 %collective-permute-start.5 = (f32[3,129,128]{2,1,0:T(8,128)S(1)}, f32[3,129,128]{2,1,0:T(8,128)}, u32[]{:S(2)}, u32[]{:S(2)}) collective-permute-start(f32[3,129,128]{2,1,0:T(8,128)S(1)} %pad_maximum_fusion.1), channel_id=1, source_target_pairs={{0,4},{4,8},{8,12},{12,16},{16,20},{20,24},{24,28},{28,32},{32,36}... | collective-permute-start | bytes 594440 | tf_op jit(solution)/shard_map/ppermute | solution.py:116
  286.7 2.4 copy-start.16
  286.7 119.8 %all-gather.7.cloned.1.call-start = ((), (), s32[]{:S(2)}) async-start(), calls=%async_computation.6 | async-start | bytes 3932160 | tf_op jit(solution)/shard_map/all_gather | solution.py:141
  289.1 3.9 copy-start.9
  291.6 4.9 %collective-permute-start.6 = (f32[3,129,128]{2,1,0:T(8,128)S(1)}, f32[3,129,128]{2,1,0:T(8,128)S(1)}, u32[]{:S(2)}, u32[]{:S(2)}) collective-permute-start(f32[3,129,128]{2,1,0:T(8,128)S(1)} %select_add_fusion.7), channel_id=1, source_target_pairs={{0,8},{4,12},{8,16},{12,20},{16,24},{20,28},{24,32},{28,36},{32,40... | collective-permute-start | bytes 594440 | tf_op jit(solution)/shard_map/ppermute | solution.py:116
  296.6 6.7 %copy-start.15 = (bf16[1024,1,128]{0,2,1:T(8,128)(2,1)S(1)}, bf16[1024,1,128]{0,2,1:T(8,128)(2,1)}, u32[]{:S(2)}) copy-start(bf16[1024,1,128]{0,2,1:T(8,128)(2,1)} %get-tuple-element.79) | copy-start | bytes 786436
  296.6 8.2 %collective-permute-start.7 = (f32[3,129,128]{2,1,0:T(8,128)S(1)}, f32[3,129,128]{2,1,0:T(8,128)S(1)}, u32[]{:S(2)}, u32[]{:S(2)}) collective-permute-start(f32[3,129,128]{2,1,0:T(8,128)S(1)} %select_add_fusion.6), channel_id=1, source_target_pairs={{0,16},{4,20},{8,24},{12,28},{16,32},{20,36},{24,40},{28,44},{32,4... | collective-permute-start | bytes 594440 | tf_op jit(solution)/shard_map/ppermute | solution.py:116
  303.3 11.5 %copy-start.6 = (bf16[128,8,8,128]{3,2,1,0:T(8,128)(2,1)S(1)}, bf16[128,8,8,128]{3,2,1,0:T(8,128)(2,1)}, u32[]{:S(2)}) copy-start(bf16[128,8,8,128]{3,2,1,0:T(8,128)(2,1)} %copy-done.5) | copy-start | bytes 6291460
  303.3 12.1 %copy-start.8 = (bf16[1024,1,128]{2,1,0:T(2,128)(2,1)S(1)}, bf16[1024,1,128]{2,1,0:T(2,128)(2,1)}, u32[]{:S(2)}) copy-start(bf16[1024,1,128]{2,1,0:T(2,128)(2,1)} %get-tuple-element.99) | copy-start | bytes 786436
  304.8 13.0 %collective-permute-start.8 = (f32[3,129,128]{2,1,0:T(8,128)S(1)}, f32[3,129,128]{2,1,0:T(8,128)S(1)}, u32[]{:S(2)}, u32[]{:S(2)}) collective-permute-start(f32[3,129,128]{2,1,0:T(8,128)S(1)} %select_add_fusion.5), channel_id=1, source_target_pairs={{0,32},{4,36},{8,40},{12,44},{16,48},{20,52},{24,56},{28,60},{32,6... | collective-permute-start | bytes 594440 | tf_op jit(solution)/shard_map/ppermute | solution.py:116
  317.8 7.0 %copy-start.14 = (bf16[1024,1,128]{0,2,1:T(8,128)(2,1)S(1)}, bf16[1024,1,128]{0,2,1:T(8,128)(2,1)}, u32[]{:S(2)}) copy-start(bf16[1024,1,128]{0,2,1:T(8,128)(2,1)} %get-tuple-element.84) | copy-start | bytes 786436
  317.8 8.6 %collective-permute-start.9 = (f32[3,129,128]{2,1,0:T(8,128)S(1)}, f32[3,129,128]{2,1,0:T(8,128)S(1)}, u32[]{:S(2)}, u32[]{:S(2)}) collective-permute-start(f32[3,129,128]{2,1,0:T(8,128)S(1)} %select_add_fusion.4), channel_id=1, source_target_pairs={{0,64},{4,68},{8,72},{12,76},{16,80},{20,84},{24,88},{28,92},{32,9... | collective-permute-start | bytes 594440 | tf_op jit(solution)/shard_map/ppermute | solution.py:116
  406.6 8.9 %copy-start.1 = (bf16[1024,1024]{1,0:T(8,128)(2,1)S(1)}, bf16[1024,1024]{1,0:T(8,128)(2,1)}, u32[]{:S(2)}) copy-start(bf16[1024,1024]{1,0:T(8,128)(2,1)} %param.8) | copy-start | bytes 6291460
Sparse Core Ops, SparseCore 0:
  286.9 55.6 all-gather.4
  368.4 38.1 all-gather.6

commit v16 on v5

--- a/solution.py
+++ b/solution.py
@@ -99,8 +99,6 @@
         )
         delta_z = jnp.sum(key_feat, axis=0)
         delta = jnp.concatenate([delta_m, delta_z[:, None, :]], axis=1)
-        if hold is not None:
-            delta, _ = lax.optimization_barrier((delta, hold))
 
         pieces = []
         total = delta

time: 419 us -> 410 us (0.979)
  waiting for transfers between devices: 119 us -> 112 us
  starting transfers between devices: 77.7 us -> 73.5 us
    ppermute x10, waiting for transfers between devices: 24 us -> 8.61 us  [one_group(): got = lax.ppermute(total, 'ctx', perm)]
    all_to_all x1, waiting for transfers between devices: 0.01 us -> 9.89 us  [one_group(): lax.all_to_all(outgoing, 'ctx', 0, 0, tiled=True)]
    ppermute x10, starting transfers between devices: 50 us -> 43.3 us  [one_group(): got = lax.ppermute(total, 'ctx', perm)]
  transfers between devices with their start and end apart: 16 -> 16, of which waited for: 11 -> 9; matrix products, arithmetic and copies ran while one was open for 31% -> 34% of each run, Pallas kernels for 0% -> 0%
where the time goes in v16:
time: 410 us; the launch traced here: 402 us
  waiting for transfers between devices  112 us (27%)
  local copies, waits for them, and re-layouts  92.6 us (23%)
  starting transfers between devices  73.5 us (18%)
  matrix products  60.1 us (15%)
  blocking collectives  31.2 us (8%)
  between operations  17.9 us (4%)
  other arithmetic  15.3 us (4%)
    all_to_all x3, waiting for transfers between devices, dispatch(): got = lax.all_to_all(buffer, 'ctx', 0, 0, tiled=True).reshape(slots, width)  63.2 us
    ppermute x10, starting transfers between devices, one_group(): got = lax.ppermute(total, 'ctx', perm)  43.3 us
    all_to_all x1, blocking collectives, one_group(): lax.all_to_all(outgoing, 'ctx', 0, 0, tiled=True)  31.2 us
    all_gather x2, waiting for transfers between devices, one_group(): gathered = lax.all_gather(rows, 'head', axis=1, tiled=True)  30.2 us
    gather x4, local copies, waits for them, and re-layouts, dispatch(): return jnp.take(got, tok_slot, axis=0, mode='clip').reshape(seg, heads, dh)  25.9 us
    dot_general x2, matrix products, one_group(): jnp.dot(gathered, weight_rows[:, first:last].reshape(head_count * group_w...  21.2 us
    all_to_all x3, starting transfers between devices, dispatch(): got = lax.all_to_all(buffer, 'ctx', 0, 0, tiled=True).reshape(slots, width)  19.1 us
    gather x3, local copies, waits for them, and re-layouts, dispatch(): jnp.take(source, slot_row, axis=0, mode='clip').reshape(n, cap, width)  17.5 us
  transfers between devices with their start and end apart: 16, of which 9 were waited for; matrix products, arithmetic and copies ran while one was open for 34% of the time, Pallas kernels for 0%

profile of v16, /device:TPU:1, one launch (start us, length us, event | category | flops | bytes accessed | tf_op | source)
XLA Modules:
  0.0 402.4 jit_solution(4213001769700298006)
XLA Ops:
  9.0 5.8 %gather_fusion.2 = bf16[1536,1024]{1,0:T(8,128)(2,1)} fusion(bf16[1024,1024]{1,0:T(8,128)(2,1)S(1)} %copy-done, s32[2048]{0:T(1024)S(1)} %pad_clamp_fusion.1), kind=kCustom, calls=%fused_computation.2 | custom fusion | bytes 6297600 | tf_op jit(solution)/shard_map/jit(_take)/gather | solution.py:66
  14.8 8.8 %all-to-all-start.1 = ((bf16[32,48,1024]{2,1,0:T(8,128)(2,1)}), bf16[32,48,1024]{2,1,0:T(8,128)(2,1)}, u32[]{:S(2)}, u32[]{:S(2)}) async-start(bf16[32,48,1024]{2,1,0:T(8,128)(2,1)} %bitcast.224), calls=%async_computation.1 | async-start | bytes 6291456 | tf_op jit(solution)/shard_map/all_to_all | solution.py:67
  23.6 5.8 %gather_fusion = bf16[1536,1024]{1,0:T(8,128)(2,1)} fusion(bf16[1024,1024]{1,0:T(8,128)(2,1)S(1)} %copy-done.2, s32[2048]{0:T(1024)S(1)} %pad_clamp_fusion.1), kind=kCustom, calls=%fused_computation | custom fusion | bytes 6297600 | tf_op jit(solution)/shard_map/jit(_take)/gather | solution.py:66
  29.5 34.0 %all-to-all-done.1 = bf16[32,48,1024]{2,1,0:T(8,128)(2,1)} async-done(((bf16[32,48,1024]{2,1,0:T(8,128)(2,1)}), bf16[32,48,1024]{2,1,0:T(8,128)(2,1)}, u32[]{:S(2)}, u32[]{:S(2)}) %all-to-all-start.1) | async-done | bytes 3145760 | tf_op jit(solution)/shard_map/all_to_all | solution.py:67
  63.4 5.0 %all-to-all-start = ((bf16[32,48,1024]{2,1,0:T(8,128)(2,1)}), bf16[32,48,1024]{2,1,0:T(8,128)(2,1)}, u32[]{:S(2)}, u32[]{:S(2)}) async-start(bf16[32,48,1024]{2,1,0:T(8,128)(2,1)} %bitcast.223), calls=%async_computation | async-start | bytes 6291456 | tf_op jit(solution)/shard_map/all_to_all | solution.py:67
  71.9 5.8 %gather_fusion.4 = bf16[1536,1024]{1,0:T(8,128)(2,1)} fusion(bf16[1024,1024]{1,0:T(8,128)(2,1)S(1)} %copy-done.3, s32[2048]{0:T(1024)S(1)} %pad_clamp_fusion.1), kind=kCustom, calls=%fused_computation.4 | custom fusion | bytes 6297600 | tf_op jit(solution)/shard_map/jit(_take)/gather | solution.py:66
  79.1 29.2 %all-to-all-done = bf16[32,48,1024]{2,1,0:T(8,128)(2,1)} async-done(((bf16[32,48,1024]{2,1,0:T(8,128)(2,1)}), bf16[32,48,1024]{2,1,0:T(8,128)(2,1)}, u32[]{:S(2)}, u32[]{:S(2)}) %all-to-all-start) | async-done | bytes 3145760 | tf_op jit(solution)/shard_map/all_to_all | solution.py:67
  108.3 5.3 %all-to-all-start.2 = ((bf16[32,48,1024]{2,1,0:T(8,128)(2,1)}), bf16[32,48,1024]{2,1,0:T(8,128)(2,1)S(1)}, u32[]{:S(2)}, u32[]{:S(2)}) async-start(bf16[32,48,1024]{2,1,0:T(8,128)(2,1)} %bitcast.222), calls=%async_computation.2 | async-start | bytes 6291456 | tf_op jit(solution)/shard_map/all_to_all | solution.py:67
  118.1 8.3 %gather_fusion.3 = bf16[1024,1024]{1,0:T(8,128)(2,1)} fusion(bf16[1536,1024]{1,0:T(8,128)(2,1)} %bitcast.6, s32[1024]{0:T(1024)S(1)} %broadcast_clamp_fusion.1), kind=kCustom, calls=%fused_computation.3 | custom fusion | bytes 4198400 | tf_op jit(solution)/shard_map/jit(_take)/gather | solution.py:68
  126.4 4.0 copy.48
  130.4 8.3 %gather_fusion.1 = bf16[1024,1024]{1,0:T(8,128)(2,1)} fusion(bf16[1536,1024]{1,0:T(8,128)(2,1)} %bitcast.4, s32[1024]{0:T(1024)S(1)} %broadcast_clamp_fusion.1), kind=kCustom, calls=%fused_computation.1 | custom fusion | bytes 4198400 | tf_op jit(solution)/shard_map/jit(_take)/gather | solution.py:68
  138.7 2.4 copy.106
  143.2 3.2 fusion.54
  146.4 2.5 fusion.47
  149.0 1.9 fusion.46
  150.9 5.0 %fusion.167 = (bf16[1024,1,128]{2,1,0:T(2,128)(2,1)}, bf16[1024,1,128]{2,1,0:T(2,128)(2,1)}, bf16[1024,1,128]{2,1,0:T(2,128)(2,1)}, bf16[1024,1,128]{2,1,0:T(2,1...) fusion(bf16[1024,8,128]{2,1,0:T(8,128)(2,1)S(1)} %bitcast.221), kind=kLoop, calls=%fused_computation.261 | loop fusion | bytes 4194304 | tf_op jit(solution)/shard_map/slice | solution.py:108
  155.9 5.3 %gather_fusion.5 = bf16[1024,1024]{1,0:T(8,128)(2,1)} fusion(bf16[1536,1024]{1,0:T(8,128)(2,1)S(1)} %bitcast.215, s32[1024]{0:T(1024)S(1)} %broadcast_clamp_fusion.1), kind=kCustom, calls=%fused_computation.5 | custom fusion | bytes 4198400 | tf_op jit(solution)/shard_map/jit(_take)/gather | solution.py:68
  161.2 2.2 copy.107
  163.5 3.5 fusion.168
  167.3 3.7 collective-permute-start
  171.0 2.1 collective-permute-start.5
  180.7 3.1 collective-permute-start.1
  183.9 3.6 collective-permute-start.6
  190.3 4.5 %collective-permute-start.2 = (f32[4,129,128]{2,1,0:T(8,128)S(1)}, f32[4,129,128]{2,1,0:T(8,128)S(1)}, u32[]{:S(2)}, u32[]{:S(2)}) collective-permute-start(f32[4,129,128]{2,1,0:T(8,128)S(1)} %select_add_fusion.6), channel_id=1, source_target_pairs={{0,16},{4,20},{8,24},{12,28},{16,32},{20,36},{24,40},{28,44},{32,4... | collective-permute-start | bytes 792584 | tf_op jit(solution)/shard_map/ppermute | solution.py:111
  194.9 2.6 fusion.17
  197.5 3.1 collective-permute-done.2
  200.6 6.2 %collective-permute-start.3 = (f32[4,129,128]{2,1,0:T(8,128)S(1)}, f32[4,129,128]{2,1,0:T(8,128)S(1)}, u32[]{:S(2)}, u32[]{:S(2)}) collective-permute-start(f32[4,129,128]{2,1,0:T(8,128)S(1)} %select_add_fusion.5), channel_id=1, source_target_pairs={{0,32},{4,36},{8,40},{12,44},{16,48},{20,52},{24,56},{28,60},{32,6... | collective-permute-start | bytes 792584 | tf_op jit(solution)/shard_map/ppermute | solution.py:111
  210.3 5.5 %collective-permute-start.4 = (f32[4,129,128]{2,1,0:T(8,128)S(1)}, f32[4,129,128]{2,1,0:T(8,128)S(1)}, u32[]{:S(2)}, u32[]{:S(2)}) collective-permute-start(f32[4,129,128]{2,1,0:T(8,128)S(1)} %select_add_fusion.4), channel_id=1, source_target_pairs={{0,64},{4,68},{8,72},{12,76},{16,80},{20,84},{24,88},{28,92},{32,9... | collective-permute-start | bytes 792584 | tf_op jit(solution)/shard_map/ppermute | solution.py:111
  219.3 2.5 fusion.49
  221.8 4.1 %fusion.29 = bf16[1024,4,128]{0,2,1:T(8,128)(2,1)} fusion(f32[1024,1,128]{0,2,1:T(8,128)S(1)} %fusion.60, f32[1024,1,128]{0,2,1:T(8,128)S(1)} %fusion.61, f32[1024,1,128]{0,2,1:T(8,128)S(1)} %fusion.62, f32[1024,1,128]{0,2,1:T(8,128)S(1)} %fusion.63, f32[4]{0:T(128)S(1)} %get-tuple-element.139, f32[1024,4]{0,1:T(4,128)S(1)} %fusion.131, ...), kind=kOutput, calls=%fused_computation.81 | convolution fusion | flops 812122112 | bytes 4473856 | tf_op jit(solution)/shard_map/qhd,hde->qhe/dot_general | solution.py:123
  227.5 5.4 %gather_fusion.6 = bf16[1536,512]{1,0:T(8,128)(2,1)} fusion(bf16[1024,512]{1,0:T(8,128)(2,1)S(1)} %copy.61, s32[2048]{0:T(1024)S(1)} %pad_clamp_fusion), kind=kCustom, calls=%fused_computation.6 | custom fusion | bytes 3151872 | tf_op jit(solution)/shard_map/jit(_take)/gather | solution.py:133
  232.9 11.0 %all-to-all-start.3 = ((bf16[32,48,512]{2,1,0:T(8,128)(2,1)}), bf16[32,48,512]{2,1,0:T(8,128)(2,1)S(1)}, u32[]{:S(2)}, u32[]{:S(2)}) async-start(bf16[32,48,512]{2,1,0:T(8,128)(2,1)} %bitcast.39), calls=%async_computation.3 | async-start | bytes 3145728 | tf_op jit(solution)/shard_map/all_to_all | solution.py:134
  244.0 2.9 fusion.9
  249.0 6.0 %collective-permute-start.7 = (f32[4,129,128]{2,1,0:T(8,128)S(1)}, f32[4,129,128]{2,1,0:T(8,128)S(1)}, u32[]{:S(2)}, u32[]{:S(2)}) collective-permute-start(f32[4,129,128]{2,1,0:T(8,128)S(1)} %select_add_fusion.2), channel_id=1, source_target_pairs={{0,16},{4,20},{8,24},{12,28},{16,32},{20,36},{24,40},{28,44},{32,4... | collective-permute-start | bytes 792584 | tf_op jit(solution)/shard_map/ppermute | solution.py:111
  256.7 9.9 %all-to-all-done.3 = bf16[32,48,512]{2,1,0:T(8,128)(2,1)S(1)} async-done(((bf16[32,48,512]{2,1,0:T(8,128)(2,1)}), bf16[32,48,512]{2,1,0:T(8,128)(2,1)S(1)}, u32[]{:S(2)}, u32[]{:S(2)}) %all-to-all-start.3) | async-done | bytes 1572896 | tf_op jit(solution)/shard_map/all_to_all | solution.py:134
  266.6 5.1 %gather_fusion.7 = bf16[1024,512]{1,0:T(8,128)(2,1)} fusion(bf16[1536,512]{1,0:T(8,128)(2,1)S(1)} %bitcast.216, s32[1024]{0:T(1024)S(1)} %broadcast_clamp_fusion), kind=kCustom, calls=%fused_computation.7 | custom fusion | bytes 2101248 | tf_op jit(solution)/shard_map/jit(_take)/gather | solution.py:135
  271.8 2.0 collective-permute-start.8
  276.6 2.2 collective-permute-done.8
  278.8 6.7 %collective-permute-start.9 = (f32[4,129,128]{2,1,0:T(8,128)S(1)}, f32[4,129,128]{2,1,0:T(8,128)S(1)}, u32[]{:S(2)}, u32[]{:S(2)}) collective-permute-start(f32[4,129,128]{2,1,0:T(8,128)S(1)} %select_add_fusion), channel_id=1, source_target_pairs={{0,64},{4,68},{8,72},{12,76},{16,80},{20,84},{24,88},{28,92},{32,9... | collective-permute-start | bytes 792584 | tf_op jit(solution)/shard_map/ppermute | solution.py:111
  290.3 2.5 fusion.42
  292.9 3.2 fusion.31
  296.6 4.8 %gather_fusion.8 = bf16[1536,512]{1,0:T(8,128)(2,1)S(1)} fusion(bf16[1024,512]{1,0:T(8,128)(2,1)S(1)} %copy.75, s32[2048]{0:T(1024)S(1)} %pad_clamp_fusion), kind=kCustom, calls=%fused_computation.8 | custom fusion | bytes 3151872 | tf_op jit(solution)/shard_map/jit(_take)/gather | solution.py:133
  301.4 31.2 %all_to_all.25 = bf16[32,48,512]{2,1,0:T(8,128)(2,1)S(1)} all-to-all(bf16[32,48,512]{2,1,0:T(8,128)(2,1)S(1)} %bitcast.231), channel_id=1, replica_groups=mesh['ctx'=32,'head'=4] {'ctx'}, dimensions={0} | all-to-all | bytes 3145728 | tf_op jit(solution)/shard_map/all_to_all | solution.py:134
  332.6 5.0 %gather_fusion.9 = bf16[1024,512]{1,0:T(8,128)(2,1)} fusion(bf16[1536,512]{1,0:T(8,128)(2,1)S(1)} %bitcast.217, s32[1024]{0:T(1024)S(1)} %broadcast_clamp_fusion), kind=kCustom, calls=%fused_computation.9 | custom fusion | bytes 2101248 | tf_op jit(solution)/shard_map/jit(_take)/gather | solution.py:135
  337.7 6.1 %fusion.164 = (bf16[4,4,128,1024]{3,2,1,0:T(8,128)(2,1)}, bf16[4,4,128,1024]{3,2,1,0:T(8,128)(2,1)}) fusion(bf16[4,8,128,1024]{3,2,1,0:T(8,128)(2,1)} %bitcast.227), kind=kLoop, calls=%fused_computation.258 | loop fusion | bytes 16777216 | tf_op jit(solution)/shard_map/slice | solution.py:139
  343.8 10.6 %fusion.171 = f32[1024,1024]{1,0:T(8,128)} fusion(bf16[1024,2048]{1,0:T(8,128)(2,1)} %all-gather.5.cloned.1.call-done, bf16[2048,1024]{1,0:T(8,128)(2,1)} %bitcast.233), kind=kOutput, calls=%fused_computation.265 | convolution fusion | flops 4294967296 | bytes 12582912 | tf_op jit(solution)/shard_map/dot_general | solution.py:137
  354.4 30.2 %all-gather.7.cloned.1.call-done = bf16[1024,2048]{1,0:T(8,128)(2,1)} async-done(((bf16[1024,512]{1,0:T(8,128)(2,1)}), bf16[1024,2048]{1,0:T(8,128)(2,1)}) %all-gather.7.cloned.1.call-update) | async-done | bytes 4194320 | tf_op jit(solution)/shard_map/all_gather | solution.py:136
  384.5 10.6 %add_convert_fusion = bf16[1024,1024]{1,0:T(8,128)(2,1)} fusion(f32[1024,1024]{1,0:T(8,128)} %fusion.171, bf16[1024,2048]{1,0:T(8,128)(2,1)} %all-gather.7.cloned.1.call-done, bf16[2048,1024]{1,0:T(8,128)(2,1)} %bitcast.232), kind=kOutput, calls=%fused_computation.26 | convolution fusion | flops 4297064448 | bytes 14680064 | tf_op jit(solution)/shard_map/dot_general | solution.py:137
  (155 shorter events, 41.7 us)
Async XLA Ops:
  6.5 2.5 copy-start
  7.6 61.5 %copy-start.16 = (s32[32,1024]{1,0:T(8,128)}, s32[32,1024]{1,0:T(8,128)S(1)}, u32[]{:S(2)}) copy-start(s32[32,1024]{1,0:T(8,128)S(1)} %reshape.467) | copy-start | bytes 393220
  14.8 8.8 %copy-start.2 = (bf16[1024,1024]{1,0:T(8,128)(2,1)S(1)}, bf16[1024,1024]{1,0:T(8,128)(2,1)}, u32[]{:S(2)}) copy-start(bf16[1024,1024]{1,0:T(8,128)(2,1)} %param.8) | copy-start | bytes 6291460
  14.8 48.6 %all-to-all-start.1 = ((bf16[32,48,1024]{2,1,0:T(8,128)(2,1)}), bf16[32,48,1024]{2,1,0:T(8,128)(2,1)}, u32[]{:S(2)}, u32[]{:S(2)}) async-start(bf16[32,48,1024]{2,1,0:T(8,128)(2,1)} %bitcast.224), calls=%async_computation.1 | async-start | bytes 6291456 | tf_op jit(solution)/shard_map/all_to_all | solution.py:67
  29.5 39.0 %copy-start.27 = (s32[32]{0:T(128)S(1)}, s32[32]{0:T(128)}, u32[]{:S(2)}) copy-start(s32[32]{0:T(128)} %param.11) | copy-start | bytes 388
  29.5 42.4 %copy-start.3 = (bf16[1024,1024]{1,0:T(8,128)(2,1)S(1)}, bf16[1024,1024]{1,0:T(8,128)(2,1)}, u32[]{:S(2)}) copy-start(bf16[1024,1024]{1,0:T(8,128)(2,1)} %param.7) | copy-start | bytes 6291460
  63.4 44.9 %all-to-all-start = ((bf16[32,48,1024]{2,1,0:T(8,128)(2,1)}), bf16[32,48,1024]{2,1,0:T(8,128)(2,1)}, u32[]{:S(2)}, u32[]{:S(2)}) async-start(bf16[32,48,1024]{2,1,0:T(8,128)(2,1)} %bitcast.223), calls=%async_computation | async-start | bytes 6291456 | tf_op jit(solution)/shard_map/all_to_all | solution.py:67
  71.8 5.8 %copy-start.26 = (f32[8]{0:T(128)S(1)}, f32[8]{0:T(128)}, u32[]{:S(2)}) copy-start(f32[8]{0:T(128)} %param.12) | copy-start | bytes 100
  108.3 47.6 %all-to-all-start.2 = ((bf16[32,48,1024]{2,1,0:T(8,128)(2,1)}), bf16[32,48,1024]{2,1,0:T(8,128)(2,1)S(1)}, u32[]{:S(2)}, u32[]{:S(2)}) async-start(bf16[32,48,1024]{2,1,0:T(8,128)(2,1)} %bitcast.222), calls=%async_computation.2 | async-start | bytes 6291456 | tf_op jit(solution)/shard_map/all_to_all | solution.py:67
  138.7 2.4 copy-start.4
  163.5 3.6 copy-start.13
  163.5 3.7 copy-start.12
  163.5 3.8 copy-start.14
  167.3 7.0 %copy-start.24 = (bf16[1024,1,128]{0,2,1:T(8,128)(2,1)S(1)}, bf16[1024,1,128]{0,2,1:T(8,128)(2,1)}, u32[]{:S(2)}) copy-start(bf16[1024,1,128]{0,2,1:T(8,128)(2,1)} %get-tuple-element.56) | copy-start | bytes 786436
  167.3 13.4 %collective-permute-start = (f32[4,129,128]{2,1,0:T(8,128)S(1)}, f32[4,129,128]{2,1,0:T(8,128)S(1)}, u32[]{:S(2)}, u32[]{:S(2)}) collective-permute-start(f32[4,129,128]{2,1,0:T(8,128)S(1)} %pad_maximum_fusion), channel_id=1, source_target_pairs={{0,4},{4,8},{8,12},{12,16},{16,20},{20,24},{24,28},{28,32},{32,36}... | collective-permute-start | bytes 792584 | tf_op jit(solution)/shard_map/ppermute | solution.py:111
  171.0 12.9 %collective-permute-start.5 = (f32[4,129,128]{2,1,0:T(8,128)S(1)}, f32[4,129,128]{2,1,0:T(8,128)S(1)}, u32[]{:S(2)}, u32[]{:S(2)}) collective-permute-start(f32[4,129,128]{2,1,0:T(8,128)S(1)} %pad_maximum_fusion.1), channel_id=1, source_target_pairs={{0,4},{4,8},{8,12},{12,16},{16,20},{20,24},{24,28},{28,32},{32,36}... | collective-permute-start | bytes 792584 | tf_op jit(solution)/shard_map/ppermute | solution.py:111
  175.8 1.3 copy-start.23
  178.6 1.8 copy-start.11
  178.6 1.9 copy-start.10
  178.6 1.9 copy-start.9
  178.6 2.0 copy-start.8
  180.7 9.6 %collective-permute-start.1 = (f32[4,129,128]{2,1,0:T(8,128)S(1)}, f32[4,129,128]{2,1,0:T(8,128)S(1)}, u32[]{:S(2)}, u32[]{:S(2)}) collective-permute-start(f32[4,129,128]{2,1,0:T(8,128)S(1)} %select_add_fusion.7), channel_id=1, source_target_pairs={{0,8},{4,12},{8,16},{12,20},{16,24},{20,28},{24,32},{28,36},{32,40... | collective-permute-start | bytes 792584 | tf_op jit(solution)/shard_map/ppermute | solution.py:111
  183.9 4.9 %copy-start.22 = (bf16[1024,1,128]{0,2,1:T(8,128)(2,1)S(1)}, bf16[1024,1,128]{0,2,1:T(8,128)(2,1)}, u32[]{:S(2)}) copy-start(bf16[1024,1,128]{0,2,1:T(8,128)(2,1)} %get-tuple-element.61) | copy-start | bytes 786436
  183.9 65.1 %collective-permute-start.6 = (f32[4,129,128]{2,1,0:T(8,128)S(1)}, f32[4,129,128]{2,1,0:T(8,128)}, u32[]{:S(2)}, u32[]{:S(2)}) collective-permute-start(f32[4,129,128]{2,1,0:T(8,128)S(1)} %select_add_fusion.3), channel_id=1, source_target_pairs={{0,8},{4,12},{8,16},{12,20},{16,24},{20,28},{24,32},{28,36},{32,40... | collective-permute-start | bytes 792584 | tf_op jit(solution)/shard_map/ppermute | solution.py:111
  190.3 10.3 %collective-permute-start.2 = (f32[4,129,128]{2,1,0:T(8,128)S(1)}, f32[4,129,128]{2,1,0:T(8,128)S(1)}, u32[]{:S(2)}, u32[]{:S(2)}) collective-permute-start(f32[4,129,128]{2,1,0:T(8,128)S(1)} %select_add_fusion.6), channel_id=1, source_target_pairs={{0,16},{4,20},{8,24},{12,28},{16,32},{20,36},{24,40},{28,44},{32,4... | collective-permute-start | bytes 792584 | tf_op jit(solution)/shard_map/ppermute | solution.py:111
  200.6 7.4 %copy-start.21 = (bf16[1024,1,128]{0,2,1:T(8,128)(2,1)S(1)}, bf16[1024,1,128]{0,2,1:T(8,128)(2,1)}, u32[]{:S(2)}) copy-start(bf16[1024,1,128]{0,2,1:T(8,128)(2,1)} %get-tuple-element.67) | copy-start | bytes 786436
  200.6 9.6 %collective-permute-start.3 = (f32[4,129,128]{2,1,0:T(8,128)S(1)}, f32[4,129,128]{2,1,0:T(8,128)S(1)}, u32[]{:S(2)}, u32[]{:S(2)}) collective-permute-start(f32[4,129,128]{2,1,0:T(8,128)S(1)} %select_add_fusion.5), channel_id=1, source_target_pairs={{0,32},{4,36},{8,40},{12,44},{16,48},{20,52},{24,56},{28,60},{32,6... | collective-permute-start | bytes 792584 | tf_op jit(solution)/shard_map/ppermute | solution.py:111
  210.3 6.7 %copy-start.20 = (bf16[1024,1,128]{0,2,1:T(8,128)(2,1)S(1)}, bf16[1024,1,128]{0,2,1:T(8,128)(2,1)}, u32[]{:S(2)}) copy-start(bf16[1024,1,128]{0,2,1:T(8,128)(2,1)} %get-tuple-element.72) | copy-start | bytes 786436
  210.3 8.9 %collective-permute-start.4 = (f32[4,129,128]{2,1,0:T(8,128)S(1)}, f32[4,129,128]{2,1,0:T(8,128)S(1)}, u32[]{:S(2)}, u32[]{:S(2)}) collective-permute-start(f32[4,129,128]{2,1,0:T(8,128)S(1)} %select_add_fusion.4), channel_id=1, source_target_pairs={{0,64},{4,68},{8,72},{12,76},{16,80},{20,84},{24,88},{28,92},{32,9... | collective-permute-start | bytes 792584 | tf_op jit(solution)/shard_map/ppermute | solution.py:111
  232.9 14.0 %copy-start.19 = (bf16[1024,1,128]{0,2,1:T(8,128)(2,1)S(1)}, bf16[1024,1,128]{0,2,1:T(8,128)(2,1)}, u32[]{:S(2)}) copy-start(bf16[1024,1,128]{0,2,1:T(8,128)(2,1)} %get-tuple-element.86) | copy-start | bytes 786436
  232.9 33.7 %all-to-all-start.3 = ((bf16[32,48,512]{2,1,0:T(8,128)(2,1)}), bf16[32,48,512]{2,1,0:T(8,128)(2,1)S(1)}, u32[]{:S(2)}, u32[]{:S(2)}) async-start(bf16[32,48,512]{2,1,0:T(8,128)(2,1)} %bitcast.39), calls=%async_computation.3 | async-start | bytes 3145728 | tf_op jit(solution)/shard_map/all_to_all | solution.py:134
  243.9 99.8 %all-gather.5.cloned.1.call-start = ((), (), s32[]{:S(2)}) async-start(), calls=%async_computation.5 | async-start | bytes 5242880 | tf_op jit(solution)/shard_map/all_gather | solution.py:136
  244.0 3.5 copy-start.5
  247.4 9.2 %copy-start.7 = (bf16[1024,1,128]{2,1,0:T(2,128)(2,1)S(1)}, bf16[1024,1,128]{2,1,0:T(2,128)(2,1)}, u32[]{:S(2)}) copy-start(bf16[1024,1,128]{2,1,0:T(2,128)(2,1)} %get-tuple-element.119) | copy-start | bytes 786436
  247.4 9.2 %copy-start.6 = (bf16[1024,1,128]{2,1,0:T(2,128)(2,1)S(1)}, bf16[1024,1,128]{2,1,0:T(2,128)(2,1)}, u32[]{:S(2)}) copy-start(bf16[1024,1,128]{2,1,0:T(2,128)(2,1)} %get-tuple-element.120) | copy-start | bytes 786436
  249.0 22.7 %collective-permute-start.7 = (f32[4,129,128]{2,1,0:T(8,128)S(1)}, f32[4,129,128]{2,1,0:T(8,128)S(1)}, u32[]{:S(2)}, u32[]{:S(2)}) collective-permute-start(f32[4,129,128]{2,1,0:T(8,128)S(1)} %select_add_fusion.2), channel_id=1, source_target_pairs={{0,16},{4,20},{8,24},{12,28},{16,32},{20,36},{24,40},{28,44},{32,4... | collective-permute-start | bytes 792584 | tf_op jit(solution)/shard_map/ppermute | solution.py:111
  271.7 112.8 %all-gather.7.cloned.1.call-start = ((), (), s32[]{:S(2)}) async-start(), calls=%async_computation.6 | async-start | bytes 5242880 | tf_op jit(solution)/shard_map/all_gather | solution.py:136
  271.8 3.2 copy-start.18
  271.8 7.0 %collective-permute-start.8 = (f32[4,129,128]{2,1,0:T(8,128)S(1)}, f32[4,129,128]{2,1,0:T(8,128)S(1)}, u32[]{:S(2)}, u32[]{:S(2)}) collective-permute-start(f32[4,129,128]{2,1,0:T(8,128)S(1)} %select_add_fusion.1), channel_id=1, source_target_pairs={{0,32},{4,36},{8,40},{12,44},{16,48},{20,52},{24,56},{28,60},{32,6... | collective-permute-start | bytes 792584 | tf_op jit(solution)/shard_map/ppermute | solution.py:111
  275.1 10.5 %copy-start.25 = (bf16[1024,1,128]{2,0,1:T(8,128)(2,1)S(1)}, bf16[1024,1,128]{2,0,1:T(8,128)(2,1)}, u32[]{:S(2)}) copy-start(bf16[1024,1,128]{2,0,1:T(8,128)(2,1)} %copy.103) | copy-start | bytes 786436
  278.8 8.0 %copy-start.17 = (bf16[1024,1,128]{0,2,1:T(8,128)(2,1)S(1)}, bf16[1024,1,128]{0,2,1:T(8,128)(2,1)}, u32[]{:S(2)}) copy-start(bf16[1024,1,128]{0,2,1:T(8,128)(2,1)} %get-tuple-element.97) | copy-start | bytes 786436
  278.8 11.4 %collective-permute-start.9 = (f32[4,129,128]{2,1,0:T(8,128)S(1)}, f32[4,129,128]{2,1,0:T(8,128)S(1)}, u32[]{:S(2)}, u32[]{:S(2)}) collective-permute-start(f32[4,129,128]{2,1,0:T(8,128)S(1)} %select_add_fusion), channel_id=1, source_target_pairs={{0,64},{4,68},{8,72},{12,76},{16,80},{20,84},{24,88},{28,92},{32,9... | collective-permute-start | bytes 792584 | tf_op jit(solution)/shard_map/ppermute | solution.py:111
  286.9 3.4 copy-start.15
  288.4 4.5 %copy-start.28 = (f32[1024,1,128]{0,2,1:T(8,128)S(1)}, f32[1024,1,128]{0,2,1:T(8,128)}, u32[]{:S(2)}) copy-start(f32[1024,1,128]{0,2,1:T(8,128)} %fusion.59) | copy-start | bytes 1572868
  288.4 4.5 %copy-start.29 = (f32[1024,1,128]{0,2,1:T(8,128)S(1)}, f32[1024,1,128]{0,2,1:T(8,128)}, u32[]{:S(2)}) copy-start(f32[1024,1,128]{0,2,1:T(8,128)} %fusion.58) | copy-start | bytes 1572868
  384.5 10.6 %copy-start.1 = (bf16[1024,1024]{1,0:T(8,128)(2,1)S(1)}, bf16[1024,1024]{1,0:T(8,128)(2,1)}, u32[]{:S(2)}) copy-start(bf16[1024,1024]{1,0:T(8,128)(2,1)} %param.9) | copy-start | bytes 6291460
Sparse Core Ops, SparseCore 0:
  271.8 51.0 all-gather.4
  337.8 46.6 all-gather.6

commit v17 on v16

--- a/solution.py
+++ b/solution.py
@@ -53,7 +53,7 @@
     causal = r_idx[:, None] >= r_idx[None, :]
     head_count = lax.axis_size("head")
     out_cols = out_weight.shape[1]
-    bounds = [0, heads // 2, heads]
+    bounds = [0, heads - (3 * heads) // 8, heads]
     weight_rows = out_weight.reshape(head_count, heads, dh, out_cols)
     gate_all = jax.nn.sigmoid(mem_gate)
     shifts = []

time: 410 us -> 419 us (1.022)
  starting transfers between devices: 73.5 us -> 84.1 us
  local copies, waits for them, and re-layouts: 92.6 us -> 97.5 us
    all_gather x2, waiting for transfers between devices: 30.2 us -> 18.3 us  [one_group(): gathered = lax.all_gather(rows, 'head', axis=1, tiled=True)]
    ppermute x10, starting transfers between devices: 43.3 us -> 49.1 us  [one_group(): got = lax.ppermute(total, 'ctx', perm)]
    all_to_all x1, waiting for transfers between devices: 9.89 us -> 14.7 us  [one_group(): lax.all_to_all(outgoing, 'ctx', 0, 0, tiled=True)]
    all_to_all x1, starting transfers between devices: 11 us -> 15.7 us  [one_group(): lax.all_to_all(outgoing, 'ctx', 0, 0, tiled=True)]
    all_to_all x3, waiting for transfers between devices: 63.2 us -> 67.7 us  [dispatch(): got = lax.all_to_all(buffer, 'ctx', 0, 0, tiled=True).reshape(slots, width)]
    ppermute x10, waiting for transfers between devices: 8.61 us -> 13 us  [one_group(): got = lax.ppermute(total, 'ctx', perm)]
    slice x1 -> x2, local copies, waits for them, and re-layouts: 6.06 us -> 9.46 us  [one_group(): weight_rows[:, first:last].reshape(head_count * group_width, out_cols)]
  transfers between devices with their start and end apart: 16 -> 16, of which waited for: 9 -> 12; matrix products, arithmetic and copies ran while one was open for 34% -> 30% of each run, Pallas kernels for 0% -> 0%
where the time goes in v17:
time: 419 us; the launch traced here: 413 us
  waiting for transfers between devices  114 us (27%)
  local copies, waits for them, and re-layouts  97.5 us (23%)
  starting transfers between devices  84.1 us (20%)
  matrix products  58.1 us (14%)
  blocking collectives  27.4 us (7%)
  between operations  17.9 us (4%)
  other arithmetic  13.9 us (3%)
    all_to_all x3, waiting for transfers between devices, dispatch(): got = lax.all_to_all(buffer, 'ctx', 0, 0, tiled=True).reshape(slots, width)  67.7 us
    ppermute x10, starting transfers between devices, one_group(): got = lax.ppermute(total, 'ctx', perm)  49.1 us
    all_to_all x1, blocking collectives, one_group(): lax.all_to_all(outgoing, 'ctx', 0, 0, tiled=True)  27.4 us
    gather x4, local copies, waits for them, and re-layouts, dispatch(): return jnp.take(got, tok_slot, axis=0, mode='clip').reshape(seg, heads, dh)  25.9 us
    dot_general x2, matrix products, one_group(): jnp.dot(gathered, weight_rows[:, first:last].reshape(head_count * group_w...  19.5 us
    all_to_all x3, starting transfers between devices, dispatch(): got = lax.all_to_all(buffer, 'ctx', 0, 0, tiled=True).reshape(slots, width)  19.1 us
    all_gather x2, waiting for transfers between devices, one_group(): gathered = lax.all_gather(rows, 'head', axis=1, tiled=True)  18.3 us
    gather x3, local copies, waits for them, and re-layouts, dispatch(): jnp.take(source, slot_row, axis=0, mode='clip').reshape(n, cap, width)  17.5 us
  transfers between devices with their start and end apart: 16, of which 12 were waited for; matrix products, arithmetic and copies ran while one was open for 30% of the time, Pallas kernels for 0%

profile of v17, /device:TPU:1, one launch (start us, length us, event | category | flops | bytes accessed | tf_op | source)
XLA Modules:
  0.0 412.7 jit_solution(6673595519970400491)
XLA Ops:
  11.6 5.8 %gather_fusion.2 = bf16[1536,1024]{1,0:T(8,128)(2,1)} fusion(bf16[1024,1024]{1,0:T(8,128)(2,1)S(1)} %copy-done, s32[2048]{0:T(1024)S(1)} %get-tuple-element.153), kind=kCustom, calls=%fused_computation.2 | custom fusion | bytes 6297600 | tf_op jit(solution)/shard_map/jit(_take)/gather | solution.py:66
  17.4 8.8 %all-to-all-start.1 = ((bf16[32,48,1024]{2,1,0:T(8,128)(2,1)}), bf16[32,48,1024]{2,1,0:T(8,128)(2,1)}, u32[]{:S(2)}, u32[]{:S(2)}) async-start(bf16[32,48,1024]{2,1,0:T(8,128)(2,1)} %bitcast.224), calls=%async_computation.1 | async-start | bytes 6291456 | tf_op jit(solution)/shard_map/all_to_all | solution.py:67
  26.2 5.8 %gather_fusion = bf16[1536,1024]{1,0:T(8,128)(2,1)} fusion(bf16[1024,1024]{1,0:T(8,128)(2,1)S(1)} %copy-done.2, s32[2048]{0:T(1024)S(1)} %get-tuple-element.153), kind=kCustom, calls=%fused_computation | custom fusion | bytes 6297600 | tf_op jit(solution)/shard_map/jit(_take)/gather | solution.py:66
  32.0 34.0 %all-to-all-done.1 = bf16[32,48,1024]{2,1,0:T(8,128)(2,1)} async-done(((bf16[32,48,1024]{2,1,0:T(8,128)(2,1)}), bf16[32,48,1024]{2,1,0:T(8,128)(2,1)}, u32[]{:S(2)}, u32[]{:S(2)}) %all-to-all-start.1) | async-done | bytes 3145760 | tf_op jit(solution)/shard_map/all_to_all | solution.py:67
  66.0 5.0 %all-to-all-start = ((bf16[32,48,1024]{2,1,0:T(8,128)(2,1)}), bf16[32,48,1024]{2,1,0:T(8,128)(2,1)}, u32[]{:S(2)}, u32[]{:S(2)}) async-start(bf16[32,48,1024]{2,1,0:T(8,128)(2,1)} %bitcast.223), calls=%async_computation | async-start | bytes 6291456 | tf_op jit(solution)/shard_map/all_to_all | solution.py:67
  76.1 5.8 %gather_fusion.4 = bf16[1536,1024]{1,0:T(8,128)(2,1)} fusion(bf16[1024,1024]{1,0:T(8,128)(2,1)S(1)} %copy-done.3, s32[2048]{0:T(1024)S(1)} %get-tuple-element.153), kind=kCustom, calls=%fused_computation.4 | custom fusion | bytes 6297600 | tf_op jit(solution)/shard_map/jit(_take)/gather | solution.py:66
  82.0 28.9 %all-to-all-done = bf16[32,48,1024]{2,1,0:T(8,128)(2,1)} async-done(((bf16[32,48,1024]{2,1,0:T(8,128)(2,1)}), bf16[32,48,1024]{2,1,0:T(8,128)(2,1)}, u32[]{:S(2)}, u32[]{:S(2)}) %all-to-all-start) | async-done | bytes 3145760 | tf_op jit(solution)/shard_map/all_to_all | solution.py:67
  110.9 5.3 %all-to-all-start.2 = ((bf16[32,48,1024]{2,1,0:T(8,128)(2,1)}), bf16[32,48,1024]{2,1,0:T(8,128)(2,1)S(1)}, u32[]{:S(2)}, u32[]{:S(2)}) async-start(bf16[32,48,1024]{2,1,0:T(8,128)(2,1)} %bitcast.222), calls=%async_computation.2 | async-start | bytes 6291456 | tf_op jit(solution)/shard_map/all_to_all | solution.py:67
  117.5 8.3 %gather_fusion.3 = bf16[1024,1024]{1,0:T(8,128)(2,1)} fusion(bf16[1536,1024]{1,0:T(8,128)(2,1)} %bitcast.6, s32[1024]{0:T(1024)S(1)} %broadcast_clamp_fusion.1), kind=kCustom, calls=%fused_computation.3 | custom fusion | bytes 4198400 | tf_op jit(solution)/shard_map/jit(_take)/gather | solution.py:68
  125.9 4.0 copy.48
  129.8 8.3 %gather_fusion.1 = bf16[1024,1024]{1,0:T(8,128)(2,1)} fusion(bf16[1536,1024]{1,0:T(8,128)(2,1)} %bitcast.4, s32[1024]{0:T(1024)S(1)} %broadcast_clamp_fusion.1), kind=kCustom, calls=%fused_computation.1 | custom fusion | bytes 4198400 | tf_op jit(solution)/shard_map/jit(_take)/gather | solution.py:68
  138.1 2.4 copy.106
  143.2 3.1 fusion.32
  146.3 4.7 %fusion.162 = (bf16[1024,1,128]{2,1,0:T(2,128)(2,1)}, bf16[1024,1,128]{2,1,0:T(2,128)(2,1)}, bf16[1024,1,128]{2,1,0:T(2,128)(2,1)}, bf16[1024,1,128]{2,1,0:T(2,1...) fusion(bf16[1024,8,128]{2,1,0:T(8,128)(2,1)S(1)} %bitcast.216), kind=kLoop, calls=%fused_computation.262 | loop fusion | bytes 4194304 | tf_op jit(solution)/shard_map/slice | solution.py:108
  151.0 4.8 %all-to-all-done.2 = bf16[32,48,1024]{2,1,0:T(8,128)(2,1)S(1)} async-done(((bf16[32,48,1024]{2,1,0:T(8,128)(2,1)}), bf16[32,48,1024]{2,1,0:T(8,128)(2,1)S(1)}, u32[]{:S(2)}, u32[]{:S(2)}) %all-to-all-start.2) | async-done | bytes 3145760 | tf_op jit(solution)/shard_map/all_to_all | solution.py:67
  155.8 5.3 %gather_fusion.5 = bf16[1024,1024]{1,0:T(8,128)(2,1)} fusion(bf16[1536,1024]{1,0:T(8,128)(2,1)S(1)} %bitcast.211, s32[1024]{0:T(1024)S(1)} %broadcast_clamp_fusion.1), kind=kCustom, calls=%fused_computation.5 | custom fusion | bytes 4198400 | tf_op jit(solution)/shard_map/jit(_take)/gather | solution.py:68
  161.2 2.3 copy.107
  163.5 4.6 %fusion.163 = (bf16[1024,1,128]{2,1,0:T(2,128)(2,1)S(1)}, bf16[1024,1,128]{2,1,0:T(2,128)(2,1)S(1)}, bf16[1024,1,128]{2,1,0:T(2,128)(2,1)}, bf16[1024,1,128]{2,1...) fusion(bf16[1024,8,128]{2,1,0:T(8,128)(2,1)S(1)} %bitcast.218), kind=kLoop, calls=%fused_computation.263 | loop fusion | bytes 4194304 | tf_op jit(solution)/shard_map/slice | solution.py:108
  168.2 3.4 collective-permute-start
  175.8 2.0 collective-permute-start.1
  180.6 2.0 collective-permute-done.1
  182.6 6.2 %collective-permute-start.2 = (f32[5,129,128]{2,1,0:T(8,128)S(1)}, f32[5,129,128]{2,1,0:T(8,128)S(1)}, u32[]{:S(2)}, u32[]{:S(2)}) collective-permute-start(f32[5,129,128]{2,1,0:T(8,128)S(1)} %select_add_fusion.2), channel_id=1, source_target_pairs={{0,16},{4,20},{8,24},{12,28},{16,32},{20,36},{24,40},{28,44},{32,4... | collective-permute-start | bytes 990728 | tf_op jit(solution)/shard_map/ppermute | solution.py:111
  193.5 5.4 %collective-permute-start.3 = (f32[5,129,128]{2,1,0:T(8,128)S(1)}, f32[5,129,128]{2,1,0:T(8,128)S(1)}, u32[]{:S(2)}, u32[]{:S(2)}) collective-permute-start(f32[5,129,128]{2,1,0:T(8,128)S(1)} %select_add_fusion.1), channel_id=1, source_target_pairs={{0,32},{4,36},{8,40},{12,44},{16,48},{20,52},{24,56},{28,60},{32,6... | collective-permute-start | bytes 990728 | tf_op jit(solution)/shard_map/ppermute | solution.py:111
  203.2 5.9 %collective-permute-start.4 = (f32[5,129,128]{2,1,0:T(8,128)S(1)}, f32[5,129,128]{2,1,0:T(8,128)S(1)}, u32[]{:S(2)}, u32[]{:S(2)}) collective-permute-start(f32[5,129,128]{2,1,0:T(8,128)S(1)} %select_add_fusion), channel_id=1, source_target_pairs={{0,64},{4,68},{8,72},{12,76},{16,80},{20,84},{24,88},{28,92},{32,9... | collective-permute-start | bytes 990728 | tf_op jit(solution)/shard_map/ppermute | solution.py:111
  213.4 3.1 fusion.27
  216.6 5.0 %fusion.26 = bf16[1024,5,128]{0,2,1:T(8,128)(2,1)} fusion(f32[1024,5,128]{0,2,1:T(8,128)S(1)} %constant_dynamic-update-slice_fusion, f32[5]{0:T(128)S(1)} %get-tuple-element.135, f32[1024,5]{0,1:T(8,128)S(1)} %fusion.127, f32[5]{0:T(128)S(1)} %get-tuple-element.134, bf16[1024,5,128]{2,1,0:T(8,128)(2,1)S(1)} %bitcast.220, ...), kind=kOutput, calls=%fused_computation.78 | convolution fusion | flops 1013186560 | bytes 6390784 | tf_op jit(solution)/shard_map/qhd,hde->qhe/dot_general | solution.py:123
  223.3 5.6 %gather_fusion.6 = bf16[1536,640]{1,0:T(8,128)(2,1)} fusion(bf16[1024,640]{1,0:T(8,128)(2,1)S(1)} %copy.63, s32[2048]{0:T(1024)S(1)} %get-tuple-element.152), kind=kCustom, calls=%fused_computation.6 | custom fusion | bytes 3938304 | tf_op jit(solution)/shard_map/jit(_take)/gather | solution.py:133
  228.8 15.7 %all-to-all-start.3 = ((bf16[32,48,640]{2,1,0:T(8,128)(2,1)}), bf16[32,48,640]{2,1,0:T(8,128)(2,1)S(1)}, u32[]{:S(2)}, u32[]{:S(2)}) async-start(bf16[32,48,640]{2,1,0:T(8,128)(2,1)} %bitcast.232), calls=%async_computation.3 | async-start | bytes 3932160 | tf_op jit(solution)/shard_map/all_to_all | solution.py:134
  245.6 2.1 slice.217
  250.0 3.1 fusion.53
  253.1 3.5 collective-permute-start.5
  256.7 14.7 %all-to-all-done.3 = bf16[32,48,640]{2,1,0:T(8,128)(2,1)S(1)} async-done(((bf16[32,48,640]{2,1,0:T(8,128)(2,1)}), bf16[32,48,640]{2,1,0:T(8,128)(2,1)S(1)}, u32[]{:S(2)}, u32[]{:S(2)}) %all-to-all-start.3) | async-done | bytes 1966112 | tf_op jit(solution)/shard_map/all_to_all | solution.py:134
  271.4 5.2 %gather_fusion.7 = bf16[1024,640]{1,0:T(8,128)(2,1)} fusion(bf16[1536,640]{1,0:T(8,128)(2,1)S(1)} %bitcast.212, s32[1024]{0:T(1024)S(1)} %broadcast_clamp_fusion), kind=kCustom, calls=%fused_computation.7 | custom fusion | bytes 2625536 | tf_op jit(solution)/shard_map/jit(_take)/gather | solution.py:135
  282.9 3.5 collective-permute-done.6
  286.5 5.4 %collective-permute-start.7 = (f32[3,129,128]{2,1,0:T(8,128)S(1)}, f32[3,129,128]{2,1,0:T(8,128)S(1)}, u32[]{:S(2)}, u32[]{:S(2)}) collective-permute-start(f32[3,129,128]{2,1,0:T(8,128)S(1)} %select_add_fusion.6), channel_id=1, source_target_pairs={{0,16},{4,20},{8,24},{12,28},{16,32},{20,36},{24,40},{28,44},{32,4... | collective-permute-start | bytes 594440 | tf_op jit(solution)/shard_map/ppermute | solution.py:111
  294.7 6.6 %collective-permute-start.8 = (f32[3,129,128]{2,1,0:T(8,128)S(1)}, f32[3,129,128]{2,1,0:T(8,128)S(1)}, u32[]{:S(2)}, u32[]{:S(2)}) collective-permute-start(f32[3,129,128]{2,1,0:T(8,128)S(1)} %select_add_fusion.5), channel_id=1, source_target_pairs={{0,32},{4,36},{8,40},{12,44},{16,48},{20,52},{24,56},{28,60},{32,6... | collective-permute-start | bytes 594440 | tf_op jit(solution)/shard_map/ppermute | solution.py:111
  302.0 2.0 collective-permute-done.8
  304.1 9.4 %collective-permute-start.9 = (f32[3,129,128]{2,1,0:T(8,128)S(1)}, f32[3,129,128]{2,1,0:T(8,128)S(1)}, u32[]{:S(2)}, u32[]{:S(2)}) collective-permute-start(f32[3,129,128]{2,1,0:T(8,128)S(1)} %select_add_fusion.4), channel_id=1, source_target_pairs={{0,64},{4,68},{8,72},{12,76},{16,80},{20,84},{24,88},{28,92},{32,9... | collective-permute-start | bytes 594440 | tf_op jit(solution)/shard_map/ppermute | solution.py:111
  316.3 1.9 fusion.49
  318.2 2.4 fusion.47
  321.0 4.7 %gather_fusion.8 = bf16[1536,384]{1,0:T(8,128)(2,1)S(1)} fusion(bf16[1024,384]{1,0:T(8,128)(2,1)S(1)} %copy.75, s32[2048]{0:T(1024)S(1)} %get-tuple-element.152), kind=kCustom, calls=%fused_computation.8 | custom fusion | bytes 2365440 | tf_op jit(solution)/shard_map/jit(_take)/gather | solution.py:133
  325.7 27.4 %all_to_all.25 = bf16[32,48,384]{2,1,0:T(8,128)(2,1)S(1)} all-to-all(bf16[32,48,384]{2,1,0:T(8,128)(2,1)S(1)} %bitcast.234), channel_id=1, replica_groups=mesh['ctx'=32,'head'=4] {'ctx'}, dimensions={0} | all-to-all | bytes 2359296 | tf_op jit(solution)/shard_map/all_to_all | solution.py:134
  353.1 5.0 %gather_fusion.9 = bf16[1024,384]{1,0:T(8,128)(2,1)} fusion(bf16[1536,384]{1,0:T(8,128)(2,1)S(1)} %bitcast.213, s32[1024]{0:T(1024)S(1)} %broadcast_clamp_fusion), kind=kCustom, calls=%fused_computation.9 | custom fusion | bytes 1576960 | tf_op jit(solution)/shard_map/jit(_take)/gather | solution.py:135
  358.1 3.8 slice.231
  361.9 5.6 %slice.216 = bf16[4,5,128,1024]{3,2,1,0:T(8,128)(2,1)} slice(bf16[4,8,128,1024]{3,2,1,0:T(8,128)(2,1)} %bitcast.228), slice={[0:4], [0:5], [0:128], [0:1024]} | slice | bytes 10485760 | tf_op jit(solution)/shard_map/slice | solution.py:139
  367.6 10.6 %fusion.166 = f32[1024,1024]{1,0:T(8,128)} fusion(bf16[1024,2560]{1,0:T(8,128)(2,1)} %all-gather.5.cloned.1.call-done, bf16[2560,1024]{1,0:T(8,128)(2,1)} %bitcast.233), kind=kOutput, calls=%fused_computation.266 | convolution fusion | flops 5368709120 | bytes 14680064 | tf_op jit(solution)/shard_map/dot_general | solution.py:137
  378.1 18.3 %all-gather.7.cloned.1.call-done = bf16[1024,1536]{1,0:T(8,128)(2,1)} async-done(((bf16[1024,384]{1,0:T(8,128)(2,1)}), bf16[1024,1536]{1,0:T(8,128)(2,1)}) %all-gather.7.cloned.1.call-update) | async-done | bytes 3145744 | tf_op jit(solution)/shard_map/all_gather | solution.py:136
  396.4 8.9 %add_convert_fusion = bf16[1024,1024]{1,0:T(8,128)(2,1)} fusion(f32[1024,1024]{1,0:T(8,128)} %fusion.166, bf16[1024,1536]{1,0:T(8,128)(2,1)} %all-gather.7.cloned.1.call-done, bf16[1536,1024]{1,0:T(8,128)(2,1)} %bitcast.235), kind=kOutput, calls=%fused_computation.26 | convolution fusion | flops 3223322624 | bytes 12582912 | tf_op jit(solution)/shard_map/dot_general | solution.py:137
  (164 shorter events, 49.3 us)
Async XLA Ops:
  6.5 5.0 %copy-start = (bf16[1024,1024]{1,0:T(8,128)(2,1)S(1)}, bf16[1024,1024]{1,0:T(8,128)(2,1)}, u32[]{:S(2)}) copy-start(bf16[1024,1024]{1,0:T(8,128)(2,1)} %param.9) | copy-start | bytes 6291460
  7.6 9.8 %copy-start.17 = (s32[32,1024]{1,0:T(8,128)}, s32[32,1024]{1,0:T(8,128)S(1)}, u32[]{:S(2)}) copy-start(s32[32,1024]{1,0:T(8,128)S(1)} %reshape.467) | copy-start | bytes 393220
  17.4 8.8 %copy-start.2 = (bf16[1024,1024]{1,0:T(8,128)(2,1)S(1)}, bf16[1024,1024]{1,0:T(8,128)(2,1)}, u32[]{:S(2)}) copy-start(bf16[1024,1024]{1,0:T(8,128)(2,1)} %param.8) | copy-start | bytes 6291460
  17.4 48.6 %all-to-all-start.1 = ((bf16[32,48,1024]{2,1,0:T(8,128)(2,1)}), bf16[32,48,1024]{2,1,0:T(8,128)(2,1)}, u32[]{:S(2)}, u32[]{:S(2)}) async-start(bf16[32,48,1024]{2,1,0:T(8,128)(2,1)} %bitcast.224), calls=%async_computation.1 | async-start | bytes 6291456 | tf_op jit(solution)/shard_map/all_to_all | solution.py:67
  32.0 39.0 %copy-start.26 = (s32[32]{0:T(128)S(1)}, s32[32]{0:T(128)}, u32[]{:S(2)}) copy-start(s32[32]{0:T(128)} %param.11) | copy-start | bytes 388
  32.0 44.1 %copy-start.3 = (bf16[1024,1024]{1,0:T(8,128)(2,1)S(1)}, bf16[1024,1024]{1,0:T(8,128)(2,1)}, u32[]{:S(2)}) copy-start(bf16[1024,1024]{1,0:T(8,128)(2,1)} %param.7) | copy-start | bytes 6291460
  66.0 44.9 %all-to-all-start = ((bf16[32,48,1024]{2,1,0:T(8,128)(2,1)}), bf16[32,48,1024]{2,1,0:T(8,128)(2,1)}, u32[]{:S(2)}, u32[]{:S(2)}) async-start(bf16[32,48,1024]{2,1,0:T(8,128)(2,1)} %bitcast.223), calls=%async_computation | async-start | bytes 6291456 | tf_op jit(solution)/shard_map/all_to_all | solution.py:67
  82.0 34.2 %copy-start.27 = (f32[8]{0:T(128)S(1)}, f32[8]{0:T(128)}, u32[]{:S(2)}) copy-start(f32[8]{0:T(128)} %param.12) | copy-start | bytes 100
  110.9 45.0 %all-to-all-start.2 = ((bf16[32,48,1024]{2,1,0:T(8,128)(2,1)}), bf16[32,48,1024]{2,1,0:T(8,128)(2,1)S(1)}, u32[]{:S(2)}, u32[]{:S(2)}) async-start(bf16[32,48,1024]{2,1,0:T(8,128)(2,1)} %bitcast.222), calls=%async_computation.2 | async-start | bytes 6291456 | tf_op jit(solution)/shard_map/all_to_all | solution.py:67
  116.2 9.7 %copy-start.28 = (f32[8]{0:T(128)}, f32[8]{0:T(128)S(1)}, u32[]{:S(2)}) copy-start(f32[8]{0:T(128)S(1)} %add_divide_fusion) | copy-start | bytes 100
  138.1 2.4 copy-start.7
  140.5 5.8 %copy-start.4 = (bf16[128,8,8,128]{3,2,1,0:T(8,128)(2,1)}, bf16[128,8,8,128]{3,2,1,0:T(8,128)(2,1)S(1)}, u32[]{:S(2)}) copy-start(bf16[128,8,8,128]{3,2,1,0:T(8,128)(2,1)S(1)} %copy.106) | copy-start | bytes 6291460
  161.2 2.3 copy-start.16
  163.4 53.1 %copy-start.5 = (bf16[128,8,8,128]{3,2,1,0:T(8,128)(2,1)}, bf16[128,8,8,128]{3,2,1,0:T(8,128)(2,1)S(1)}, u32[]{:S(2)}) copy-start(bf16[128,8,8,128]{3,2,1,0:T(8,128)(2,1)S(1)} %copy.107) | copy-start | bytes 6291460
  168.2 4.6 %copy-start.25 = (bf16[1024,1,128]{0,2,1:T(8,128)(2,1)S(1)}, bf16[1024,1,128]{0,2,1:T(8,128)(2,1)}, u32[]{:S(2)}) copy-start(bf16[1024,1,128]{0,2,1:T(8,128)(2,1)} %get-tuple-element.56) | copy-start | bytes 786436
  168.2 7.6 %collective-permute-start = (f32[5,129,128]{2,1,0:T(8,128)S(1)}, f32[5,129,128]{2,1,0:T(8,128)S(1)}, u32[]{:S(2)}, u32[]{:S(2)}) collective-permute-start(f32[5,129,128]{2,1,0:T(8,128)S(1)} %pad_maximum_fusion), channel_id=1, source_target_pairs={{0,4},{4,8},{8,12},{12,16},{16,20},{20,24},{24,28},{28,32},{32,36}... | collective-permute-start | bytes 990728 | tf_op jit(solution)/shard_map/ppermute | solution.py:111
  172.8 1.5 copy-start.15
  172.8 1.6 copy-start.14
  172.8 1.6 copy-start.13
  172.8 1.7 copy-start.12
  175.8 3.3 copy-start.24
  175.8 6.8 %collective-permute-start.1 = (f32[5,129,128]{2,1,0:T(8,128)S(1)}, f32[5,129,128]{2,1,0:T(8,128)S(1)}, u32[]{:S(2)}, u32[]{:S(2)}) collective-permute-start(f32[5,129,128]{2,1,0:T(8,128)S(1)} %select_add_fusion.3), channel_id=1, source_target_pairs={{0,8},{4,12},{8,16},{12,20},{16,24},{20,28},{24,32},{28,36},{32,40... | collective-permute-start | bytes 990728 | tf_op jit(solution)/shard_map/ppermute | solution.py:111
  182.6 7.5 %copy-start.23 = (bf16[1024,1,128]{0,2,1:T(8,128)(2,1)S(1)}, bf16[1024,1,128]{0,2,1:T(8,128)(2,1)}, u32[]{:S(2)}) copy-start(bf16[1024,1,128]{0,2,1:T(8,128)(2,1)} %get-tuple-element.66) | copy-start | bytes 786436
  182.6 10.9 %collective-permute-start.2 = (f32[5,129,128]{2,1,0:T(8,128)S(1)}, f32[5,129,128]{2,1,0:T(8,128)S(1)}, u32[]{:S(2)}, u32[]{:S(2)}) collective-permute-start(f32[5,129,128]{2,1,0:T(8,128)S(1)} %select_add_fusion.2), channel_id=1, source_target_pairs={{0,16},{4,20},{8,24},{12,28},{16,32},{20,36},{24,40},{28,44},{32,4... | collective-permute-start | bytes 990728 | tf_op jit(solution)/shard_map/ppermute | solution.py:111
  193.5 6.7 %copy-start.22 = (bf16[1024,1,128]{0,2,1:T(8,128)(2,1)S(1)}, bf16[1024,1,128]{0,2,1:T(8,128)(2,1)}, u32[]{:S(2)}) copy-start(bf16[1024,1,128]{0,2,1:T(8,128)(2,1)} %get-tuple-element.71) | copy-start | bytes 786436
  193.5 9.6 %collective-permute-start.3 = (f32[5,129,128]{2,1,0:T(8,128)S(1)}, f32[5,129,128]{2,1,0:T(8,128)S(1)}, u32[]{:S(2)}, u32[]{:S(2)}) collective-permute-start(f32[5,129,128]{2,1,0:T(8,128)S(1)} %select_add_fusion.1), channel_id=1, source_target_pairs={{0,32},{4,36},{8,40},{12,44},{16,48},{20,52},{24,56},{28,60},{32,6... | collective-permute-start | bytes 990728 | tf_op jit(solution)/shard_map/ppermute | solution.py:111
  203.2 7.1 %copy-start.21 = (bf16[1024,1,128]{0,2,1:T(8,128)(2,1)S(1)}, bf16[1024,1,128]{0,2,1:T(8,128)(2,1)}, u32[]{:S(2)}) copy-start(bf16[1024,1,128]{0,2,1:T(8,128)(2,1)} %get-tuple-element.76) | copy-start | bytes 786436
  203.2 10.1 %collective-permute-start.4 = (f32[5,129,128]{2,1,0:T(8,128)S(1)}, f32[5,129,128]{2,1,0:T(8,128)S(1)}, u32[]{:S(2)}, u32[]{:S(2)}) collective-permute-start(f32[5,129,128]{2,1,0:T(8,128)S(1)} %select_add_fusion), channel_id=1, source_target_pairs={{0,64},{4,68},{8,72},{12,76},{16,80},{20,84},{24,88},{28,92},{32,9... | collective-permute-start | bytes 990728 | tf_op jit(solution)/shard_map/ppermute | solution.py:111
  228.8 19.7 %copy-start.10 = (bf16[1024,1,128]{2,1,0:T(2,128)(2,1)S(1)}, bf16[1024,1,128]{2,1,0:T(2,128)(2,1)}, u32[]{:S(2)}) copy-start(bf16[1024,1,128]{2,1,0:T(2,128)(2,1)} %get-tuple-element.117) | copy-start | bytes 786436
  228.8 42.6 %all-to-all-start.3 = ((bf16[32,48,640]{2,1,0:T(8,128)(2,1)}), bf16[32,48,640]{2,1,0:T(8,128)(2,1)S(1)}, u32[]{:S(2)}, u32[]{:S(2)}) async-start(bf16[32,48,640]{2,1,0:T(8,128)(2,1)} %bitcast.232), calls=%async_computation.3 | async-start | bytes 3932160 | tf_op jit(solution)/shard_map/all_to_all | solution.py:134
  244.5 123.1 %all-gather.5.cloned.1.call-start = ((), (), s32[]{:S(2)}) async-start(), calls=%async_computation.5 | async-start | bytes 6553600 | tf_op jit(solution)/shard_map/all_gather | solution.py:136
  244.8 4.5 %copy-start.11 = (bf16[1024,1,128]{2,1,0:T(2,128)(2,1)S(1)}, bf16[1024,1,128]{2,1,0:T(2,128)(2,1)}, u32[]{:S(2)}) copy-start(bf16[1024,1,128]{2,1,0:T(2,128)(2,1)} %get-tuple-element.125) | copy-start | bytes 786436
  253.1 27.3 %collective-permute-start.5 = (f32[3,129,128]{2,1,0:T(8,128)S(1)}, f32[3,129,128]{2,1,0:T(8,128)}, u32[]{:S(2)}, u32[]{:S(2)}) collective-permute-start(f32[3,129,128]{2,1,0:T(8,128)S(1)} %pad_maximum_fusion.1), channel_id=1, source_target_pairs={{0,4},{4,8},{8,12},{12,16},{16,20},{20,24},{24,28},{28,32},{32,36}... | collective-permute-start | bytes 594440 | tf_op jit(solution)/shard_map/ppermute | solution.py:111
  276.6 2.4 copy-start.20
  276.6 119.8 %all-gather.7.cloned.1.call-start = ((), (), s32[]{:S(2)}) async-start(), calls=%async_computation.6 | async-start | bytes 3932160 | tf_op jit(solution)/shard_map/all_gather | solution.py:136
  279.0 3.8 copy-start.9
  281.5 4.9 %collective-permute-start.6 = (f32[3,129,128]{2,1,0:T(8,128)S(1)}, f32[3,129,128]{2,1,0:T(8,128)S(1)}, u32[]{:S(2)}, u32[]{:S(2)}) collective-permute-start(f32[3,129,128]{2,1,0:T(8,128)S(1)} %select_add_fusion.7), channel_id=1, source_target_pairs={{0,8},{4,12},{8,16},{12,20},{16,24},{20,28},{24,32},{28,36},{32,40... | collective-permute-start | bytes 594440 | tf_op jit(solution)/shard_map/ppermute | solution.py:111
  286.4 6.7 %copy-start.19 = (bf16[1024,1,128]{0,2,1:T(8,128)(2,1)S(1)}, bf16[1024,1,128]{0,2,1:T(8,128)(2,1)}, u32[]{:S(2)}) copy-start(bf16[1024,1,128]{0,2,1:T(8,128)(2,1)} %get-tuple-element.92) | copy-start | bytes 786436
  286.5 8.2 %collective-permute-start.7 = (f32[3,129,128]{2,1,0:T(8,128)S(1)}, f32[3,129,128]{2,1,0:T(8,128)S(1)}, u32[]{:S(2)}, u32[]{:S(2)}) collective-permute-start(f32[3,129,128]{2,1,0:T(8,128)S(1)} %select_add_fusion.6), channel_id=1, source_target_pairs={{0,16},{4,20},{8,24},{12,28},{16,32},{20,36},{24,40},{28,44},{32,4... | collective-permute-start | bytes 594440 | tf_op jit(solution)/shard_map/ppermute | solution.py:111
  293.1 8.2 %copy-start.29 = (f32[8]{0:T(128)S(1)}, f32[8]{0:T(128)}, u32[]{:S(2)}) copy-start(f32[8]{0:T(128)} %copy-done.28) | copy-start | bytes 100
  293.1 8.2 %copy-start.6 = (bf16[128,8,8,128]{3,2,1,0:T(8,128)(2,1)S(1)}, bf16[128,8,8,128]{3,2,1,0:T(8,128)(2,1)}, u32[]{:S(2)}) copy-start(bf16[128,8,8,128]{3,2,1,0:T(8,128)(2,1)} %copy-done.5) | copy-start | bytes 6291460
  293.1 8.8 %copy-start.8 = (bf16[1024,1,128]{2,1,0:T(2,128)(2,1)S(1)}, bf16[1024,1,128]{2,1,0:T(2,128)(2,1)}, u32[]{:S(2)}) copy-start(bf16[1024,1,128]{2,1,0:T(2,128)(2,1)} %get-tuple-element.115) | copy-start | bytes 786436
  294.7 9.3 %collective-permute-start.8 = (f32[3,129,128]{2,1,0:T(8,128)S(1)}, f32[3,129,128]{2,1,0:T(8,128)S(1)}, u32[]{:S(2)}, u32[]{:S(2)}) collective-permute-start(f32[3,129,128]{2,1,0:T(8,128)S(1)} %select_add_fusion.5), channel_id=1, source_target_pairs={{0,32},{4,36},{8,40},{12,44},{16,48},{20,52},{24,56},{28,60},{32,6... | collective-permute-start | bytes 594440 | tf_op jit(solution)/shard_map/ppermute | solution.py:111
  304.0 10.7 %copy-start.18 = (bf16[1024,1,128]{0,2,1:T(8,128)(2,1)S(1)}, bf16[1024,1,128]{0,2,1:T(8,128)(2,1)}, u32[]{:S(2)}) copy-start(bf16[1024,1,128]{0,2,1:T(8,128)(2,1)} %get-tuple-element.98) | copy-start | bytes 786436
  304.1 12.2 %collective-permute-start.9 = (f32[3,129,128]{2,1,0:T(8,128)S(1)}, f32[3,129,128]{2,1,0:T(8,128)S(1)}, u32[]{:S(2)}, u32[]{:S(2)}) collective-permute-start(f32[3,129,128]{2,1,0:T(8,128)S(1)} %select_add_fusion.4), channel_id=1, source_target_pairs={{0,64},{4,68},{8,72},{12,76},{16,80},{20,84},{24,88},{28,92},{32,9... | collective-permute-start | bytes 594440 | tf_op jit(solution)/shard_map/ppermute | solution.py:111
  396.4 8.9 %copy-start.1 = (bf16[1024,1024]{1,0:T(8,128)(2,1)S(1)}, bf16[1024,1024]{1,0:T(8,128)(2,1)}, u32[]{:S(2)}) copy-start(bf16[1024,1024]{1,0:T(8,128)(2,1)} %param.9) | copy-start | bytes 6291460
Sparse Core Ops, SparseCore 0:
  276.7 55.6 all-gather.4
  358.2 38.1 all-gather.6
